TPU v7x, 512 devices: a whole 4x8x8 slice. The times are simulated.
512 devices in a mesh: ctx: 32 (over z, x), tp: 16 (over y, core).
Axes of the slice: x: 4, y: 8, z: 8, core: 2. Of those that a mesh axis runs over, the one named last changes fastest.
Arguments:
- hidden: bfloat16 [8192, 2048], P(('ctx', 'tp')), may hold values from -14 to 14
- in_weight: bfloat16 [2048, 2, 4096], P(None, None, 'tp'), may hold values from -0.125 to 0.125
- step_weight: bfloat16 [2048, 64], P(None, 'tp'), may hold values from -0.125 to 0.125
- group_weight: bfloat16 [256, 4, 2048], P('tp'), may hold values from -0.125 to 0.125
- conv_inner: float32 [4, 4096], P(None, 'tp'), may hold values from -3 to 3
- inner_bias: float32 [4096], P('tp'), may hold values from -2.5 to 2.5
- conv_group: float32 [4, 1024], replicated, may hold values from -3 to 3
- group_bias: float32 [1024], replicated, may hold values from -2.5 to 2.5
- step_bias: float32 [64], P('tp'), may hold values from -9.5 to 0
- log_rate: float32 [64], P('tp'), may hold values from -2.5 to -0.5
- skip_weight: float32 [64], P('tp'), may hold values from 0.25 to 1
- norm_gain: float32 [4096], P('tp'), may hold values from 0.1 to 1.9
- out_weight: bfloat16 [4096, 2048], P('tp'), may hold values from -0.09375 to 0.09375
Outputs:
- mixed: bfloat16 [8192, 2048], P(('ctx', 'tp'))
All inputs are finite; a program needn't handle non-finite values.
Results may differ from a plain program's by a relative error of at most 0.024.
Values may be sent and summed in bfloat16 or wider, within the bound.
No kernel may reach another device: no remote copies, remote signals or barrier semaphores. Data moves between devices by JAX's collectives and lax.ppermute only.
A program may use at most 64 MiB of HBM per device.

v0:
```python
import jax
import jax.numpy as jnp
from jax import lax
from jax.sharding import PartitionSpec as P

HEADS = 64
HEAD_DIM = 64
STATE = 128
GROUPS = 4
BLOCK = 256
KERNEL = 4


def shifted(x, axis, by):
    peers = lax.axis_size(axis)
    pairs = [(i, i + by) for i in range(peers) if 0 <= i + by < peers]
    return lax.ppermute(x, axis, pairs)


def entering(x, axis, combine, identity):
    peers, place = (lax.axis_size(axis), lax.axis_index(axis))
    everything = jax.tree.map(lambda part: lax.all_gather(part, axis), x)
    start = jax.tree.map(
        lambda part, zero: jnp.broadcast_to(jnp.asarray(zero, part.dtype), part.shape), x, identity
    )

    def turn(k, before):
        reached = k < place
        new = combine(before, jax.tree.map(lambda part: part[k], everything))
        return jax.tree.map(lambda a, b: jnp.where(reached, a, b), new, before)

    return lax.fori_loop(0, peers, turn, start)


def causal_conv(prior_rows, raw_rows, conv_weight, conv_bias):
    joined = jnp.concatenate([prior_rows, raw_rows], axis=0).astype(jnp.float32)
    length = raw_rows.shape[0]
    running = jnp.broadcast_to(conv_bias[None, :], raw_rows.shape)
    for offset in range(conv_weight.shape[0]):
        running = running + conv_weight[offset][None, :] * joined[offset : offset + length]
    return jax.nn.silu(running).astype(jnp.bfloat16)


def combine_states(earlier, latter):
    return (earlier[0] * latter[0], latter[0][:, None, None] * earlier[1] + latter[1])


def body(
    hidden,
    in_weight,
    step_weight,
    group_weight,
    conv_inner,
    inner_bias,
    conv_group,
    group_bias,
    step_bias,
    log_rate,
    skip_weight,
    norm_gain,
    out_weight,
):
    heads_dev = log_rate.shape[0]
    inner_dev = in_weight.shape[2]
    group_cols = 2 * STATE
    group_index = lax.axis_index("tp") * heads_dev // (HEADS // GROUPS)
    zx_weight = in_weight.reshape(in_weight.shape[0], 2 * inner_dev)
    full_weight = lax.all_gather(group_weight, "tp", axis=0, tiled=True)
    map_weight = lax.dynamic_slice_in_dim(full_weight, group_index, 1, 1)[:, 0, :]
    shard_rows = lax.all_gather(hidden, "tp", axis=0, tiled=True)
    projected = jnp.concatenate(
        [
            jnp.dot(shard_rows, zx_weight, preferred_element_type=jnp.float32),
            lax.dot_general(
                shard_rows, map_weight, (((1,), (1,)), ((), ())), preferred_element_type=jnp.float32
            ),
            jnp.dot(shard_rows, step_weight, preferred_element_type=jnp.float32),
        ],
        axis=1,
    ).astype(jnp.bfloat16)
    gate_raw = projected[:, :inner_dev]
    inner_raw = projected[:, inner_dev : 2 * inner_dev]
    map_part = projected[:, 2 * inner_dev : projected.shape[1] - heads_dev]
    step_raw = projected[:, projected.shape[1] - heads_dev :]
    border_rows = KERNEL - 1
    length = inner_raw.shape[0]
    inner_prior, map_prior = shifted(
        (inner_raw[length - border_rows :], map_part[length - border_rows :]), "ctx", 1
    )
    x_conv = causal_conv(inner_prior, inner_raw, conv_inner, inner_bias)
    own_taps = lax.dynamic_slice_in_dim(conv_group, group_index * group_cols, group_cols, 1)
    own_bias = lax.dynamic_slice_in_dim(group_bias, group_index * group_cols, group_cols, 0)
    maps = causal_conv(map_prior, map_part, own_taps, own_bias)
    step_size = jax.nn.softplus(step_raw.astype(jnp.float32) + step_bias[None, :])
    decay_rate = -jnp.exp(log_rate)
    blocks = length // BLOCK
    x_blocks = x_conv.reshape(blocks, BLOCK, heads_dev, HEAD_DIM)
    input_map = maps[:, :STATE].reshape(blocks, BLOCK, STATE)
    output_map = maps[:, STATE:].reshape(blocks, BLOCK, STATE)
    step_blocks = jnp.swapaxes(step_size.reshape(blocks, BLOCK, heads_dev), 1, 2)
    cumulative = jnp.cumsum(step_blocks * decay_rate[None, :, None], axis=2)
    scores = jnp.einsum("kin,kjn->kij", output_map, input_map, preferred_element_type=jnp.float32)
    causal = jnp.arange(BLOCK)[:, None] >= jnp.arange(BLOCK)[None, :]
    exponent = jnp.where(causal, cumulative[..., :, None] - cumulative[..., None, :], -jnp.inf)
    mixing = (scores[:, None] * jnp.exp(exponent) * step_blocks[..., None, :]).astype(jnp.bfloat16)
    within = jnp.einsum("khij,kjhp->kihp", mixing, x_blocks, preferred_element_type=jnp.float32)
    weight = jnp.exp(cumulative[..., BLOCK - 1 :] - cumulative) * step_blocks
    x_float = x_blocks.astype(jnp.float32)
    weighted = (x_float * jnp.swapaxes(weight, 1, 2)[..., None]).astype(jnp.bfloat16)
    block_state = jnp.einsum(
        "kjhp,kjn->khpn", weighted, input_map, preferred_element_type=jnp.float32
    )
    block_decay = jnp.exp(cumulative[..., BLOCK - 1])

    def advance(carry, item):
        running, product = carry
        block_stop_index, state_here = item
        return (
            (block_stop_index[:, None, None] * running + state_here, product * block_stop_index),
            (running, product),
        )

    empty_state = jnp.zeros((heads_dev, HEAD_DIM, STATE), jnp.float32)
    (dev_state, dev_decay), (local_starts, prefixes) = lax.scan(
        advance, (empty_state, jnp.ones((heads_dev,), jnp.float32)), (block_decay, block_state)
    )
    decay_in, incoming = entering(
        (dev_decay, dev_state),
        "ctx",
        combine_states,
        (jnp.ones_like(dev_decay), jnp.zeros_like(dev_state)),
    )
    starting = local_starts + prefixes[:, :, None, None] * incoming[None]
    carried = jnp.einsum(
        "kin,khpn->kihp",
        output_map,
        starting.astype(jnp.bfloat16),
        preferred_element_type=jnp.float32,
    )
    carried = carried * jnp.swapaxes(jnp.exp(cumulative), 1, 2)[..., None]
    result_heads = within + carried + skip_weight[None, None, :, None] * x_float
    result_heads = result_heads.reshape(length, inner_dev)
    gated = result_heads * jax.nn.silu(gate_raw.astype(jnp.float32))
    squares = jnp.sum(gated * gated, axis=1)
    own_slot = (jnp.arange(GROUPS) == group_index)[:, None]
    group_sums = lax.psum(jnp.where(own_slot, squares[None, :], 0.0), "tp")
    own_total = jnp.sum(jnp.where(own_slot, group_sums, 0.0), axis=0)
    inverse = lax.rsqrt(own_total / (HEADS * HEAD_DIM // GROUPS) + 1e-05)
    normed = (gated * inverse[:, None] * norm_gain[None, :]).astype(jnp.bfloat16)
    mixed = lax.psum_scatter(
        jnp.dot(normed, out_weight, preferred_element_type=jnp.float32),
        "tp",
        scatter_dimension=0,
        tiled=True,
    )
    return mixed.astype(jnp.bfloat16)


def solution(mesh):
    placed = (
        P(("ctx", "tp"), None),
        P(None, None, "tp"),
        P(None, "tp"),
        P("tp", None, None),
        P(None, "tp"),
        P("tp"),
        P(),
        P(),
        P("tp"),
        P("tp"),
        P("tp"),
        P("tp"),
        P("tp", None),
    )
    return jax.shard_map(
        body, mesh=mesh, in_specs=placed, out_specs=P(("ctx", "tp"), None), check_vma=False
    )
```

profile of v0, /device:TPU:1, one launch (start us, length us, event | category | flops | bytes accessed | tf_op | source)
XLA Modules:
  0.0 322.7 jit_solution(4867282855328708421)
XLA Ops:
  7.3 1.8 copy.45
  9.3 2.1 copy.56
  13.1 43.0 %all-gather.6.cloned.1.call-done = bf16[256,2048]{1,0:T(8,128)(2,1)} async-done(((bf16[16,2048]{1,0:T(8,128)(2,1)}), bf16[256,2048]{1,0:T(8,128)(2,1)}) %all-gather.6.cloned.1.call-update) | async-done | bytes 1048592 | tf_op jit(solution)/shard_map/all_gather | solution.py:70
  56.1 1.6 bitcast_multiply_fusion.1
  57.7 1.2 reduce-window.6
  59.4 1.9 convolution_convert_fusion
  61.3 3.1 collective-permute-start
  65.2 36.7 %all-gather.8.cloned.1.call-done = bf16[256,4,2048]{2,0,1:T(8,128)(2,1)} async-done(((bf16[16,4,2048]{2,0,1:T(8,128)(2,1)}), bf16[256,4,2048]{2,0,1:T(8,128)(2,1)}) %all-gather.8.cloned.1.call-update) | async-done | bytes 4194320 | tf_op jit(solution)/shard_map/all_gather | solution.py:68
  101.8 2.0 fusion.4
  103.9 3.1 collective-permute-start.1
  109.0 34.9 %all-gather = f32[32,4,1]{1,2,0:T(1,128)S(1)} all-gather(f32[1,4,1]{1,2,0:T(1,128)S(1)} %copy.48), channel_id=2, replica_groups=mesh['ctx'=32,'tp'=16] {'ctx'}, dimensions={0}, use_global_device_ids=true | all-gather | bytes 528 | tf_op jit(solution)/shard_map/all_gather | solution.py:22
  144.3 49.8 %all-gather.10.cloned.1.call-done = f32[128,64,128]{2,1,0:T(8,128)} async-done(((f32[4,64,128]{2,1,0:T(8,128)}), f32[128,64,128]{2,1,0:T(8,128)}) %all-gather.10.cloned.1.call-update) | async-done | bytes 4194320 | tf_op jit(solution)/shard_map/all_gather | solution.py:22
  194.2 33.1 %while.9 = (s32[]{:T(128)}, f32[4,64,128]{2,1,0:T(8,128)S(1)}, s32[]{:T(128)}, f32[32,4]{1,0:T(8,128)S(1)}, f32[32,4,64,128]{3,2,1,0:T(8,128)}, /*index=5*/s32[]{:T(128)}, s32[]{:T(128)}) while((s32[]{:T(128)}, f32[4,64,128]{2,1,0:T(8,128)S(1)}, s32[]{:T(128)}, f32[32,4]{1,0:T(8,128)S(1)}, f32[32,4,64,128]{3,2,1,0:T(8,128)}, ...), condition=%wide.region_3.4_spmd.clone, body=%wide.region_2.3_spmd.clone.sunk | while | flops 131076 | bytes 393369 | solution.py:32
  195.2 1.0 fusion.52
  196.2 1.0 fusion.52
  197.3 1.0 fusion.52
  198.3 1.0 fusion.52
  199.3 1.0 fusion.52
  200.4 1.0 fusion.52
  202.4 1.0 fusion.52
  204.5 1.0 fusion.52
  205.5 1.0 fusion.52
  206.6 1.0 fusion.52
  207.6 1.0 fusion.52
  208.7 1.0 fusion.52
  209.7 1.0 fusion.52
  210.7 1.0 fusion.52
  211.8 1.0 fusion.52
  228.3 27.2 %psum.7 = f32[4,256]{1,0:T(4,128)S(1)} all-reduce(f32[4,256]{1,0:T(4,128)S(1)} %broadcast_select_fusion), channel_id=1, replica_groups=mesh['ctx'=32,'tp'=16] {'tp'}, use_global_device_ids=true, to_apply=%region_5.6 | all-reduce | flops 1024 | bytes 8192 | tf_op jit(solution)/shard_map/psum | solution.py:146
  255.7 1.8 fusion.27
  257.5 57.1 %reduce-scatter.2.cloned.1.call-done = f32[16,2048]{1,0:T(8,128)} async-done(((f32[256,2048]{1,0:T(8,128)}), f32[16,2048]{1,0:T(8,128)}) %reduce-scatter.2.cloned.1.call-update) | async-done | bytes 131088 | tf_op jit(solution)/shard_map/reduce_scatter | solution.py:150
  314.7 1.5 convert_element_type.77
  (119 shorter events, 24.4 us)
Async XLA Ops:
  6.5 249.1 %copy-start = (bf16[256,2048]{1,0:T(8,128)(2,1)S(1)}, bf16[256,2048]{1,0:T(8,128)(2,1)}, u32[]{:S(2)}) copy-start(bf16[256,2048]{1,0:T(8,128)(2,1)} %param.27) | copy-start | bytes 3145732
  6.5 49.5 %all-gather.6.cloned.1.call-start = ((), (), s32[]{:S(2)}) async-start(), calls=%async_computation.1 | async-start | bytes 1114112 | tf_op jit(solution)/shard_map/all_gather | solution.py:70
  7.3 94.6 %all-gather.8.cloned.1.call-start = ((), (), s32[]{:S(2)}) async-start(), calls=%async_computation.2 | async-start | bytes 4456448 | tf_op jit(solution)/shard_map/all_gather | solution.py:68
  9.2 185.0 %all-gather.10.cloned.1.call-start = ((), (), s32[]{:S(2)}) async-start(), calls=%async_computation.4 | async-start | bytes 4325376 | tf_op jit(solution)/shard_map/all_gather | solution.py:22
  9.2 3.8 %copy-start.5 = (f32[4]{0:T(128)S(1)}, f32[4]{0:T(128)}, u32[]{:S(2)}) copy-start(f32[4]{0:T(128)} %param.24) | copy-start | bytes 52
  9.2 3.8 %copy-start.1 = (f32[4,256]{1,0:T(4,128)S(1)}, f32[4,256]{1,0:T(4,128)}, u32[]{:S(2)}) copy-start(f32[4,256]{1,0:T(4,128)} %param.19) | copy-start | bytes 12292
  9.3 46.8 %copy-start.4 = (bf16[2048,4]{0,1:T(4,128)(2,1)S(1)}, bf16[2048,4]{0,1:T(4,128)(2,1)}, u32[]{:S(2)}) copy-start(bf16[2048,4]{0,1:T(4,128)(2,1)} %param.17) | copy-start | bytes 49156
  9.3 46.8 %copy-start.6 = (f32[4]{0:T(128)S(1)}, f32[4]{0:T(128)}, u32[]{:S(2)}) copy-start(f32[4]{0:T(128)} %param.23) | copy-start | bytes 52
  61.3 45.7 %copy-start.3 = (f32[256]{0:T(256)S(1)}, f32[256]{0:T(256)}, u32[]{:S(2)}) copy-start(f32[256]{0:T(256)} %param.20) | copy-start | bytes 3076
  61.3 3.8 %collective-permute-start = (bf16[3,256]{1,0:T(4,128)(2,1)S(1)}, bf16[3,256]{1,0:T(4,128)(2,1)S(1)}, u32[]{:S(2)}, u32[]{:S(2)}) collective-permute-start(bf16[3,256]{1,0:T(4,128)(2,1)S(1)} %slice.112), channel_id=1, source_target_pairs={{0,16},{16,32},{32,48},{48,64},{64,80},{80,96},{96,112},{112,128},... | collective-permute-start | bytes 4616 | tf_op jit(solution)/shard_map/ppermute | solution.py:17
  103.9 3.8 %collective-permute-start.1 = (bf16[3,256]{1,0:T(4,128)(2,1)S(1)}, bf16[3,256]{1,0:T(4,128)(2,1)S(1)}, u32[]{:S(2)}, u32[]{:S(2)}) collective-permute-start(bf16[3,256]{1,0:T(4,128)(2,1)S(1)} %slice.118), channel_id=1, source_target_pairs={{0,16},{16,32},{32,48},{48,64},{64,80},{80,96},{96,112},{112,128},... | collective-permute-start | bytes 4616 | tf_op jit(solution)/shard_map/ppermute | solution.py:17
  107.9 119.5 %copy-start.7 = (f32[4]{0:T(128)S(1)}, f32[4]{0:T(128)}, u32[]{:S(2)}) copy-start(f32[4]{0:T(128)} %param.25) | copy-start | bytes 52
  108.8 205.9 %reduce-scatter.2.cloned.1.call-start = ((), (), s32[]{:S(2)}) async-start(), calls=%async_computation.3 | async-start | bytes 2228224 | tf_op jit(solution)/shard_map/reduce_scatter | solution.py:150
  227.2 28.4 %copy-start.2 = (f32[256]{0:T(256)S(1)}, f32[256]{0:T(256)}, u32[]{:S(2)}) copy-start(f32[256]{0:T(256)} %param.26) | copy-start | bytes 3076
Sparse Core Ops, SparseCore 0:
  9.5 46.5 all-gather.5
  58.2 43.5 all-gather.7
  108.9 85.2 all-gather.9
  257.6 56.9 reduce-scatter.1
where the time goes:
time: 325 us; the launch traced here: 323 us
  waiting for transfers between devices  188 us (58%)
  blocking collectives  62.1 us (19%)
  other arithmetic  35.5 us (11%)
  between operations  13.5 us (4%)
  matrix products  9.06 us (3%)
  local copies, waits for them, and re-layouts  7.25 us (2%)
  starting transfers between devices  6.31 us (2%)
    reduce_scatter x1, waiting for transfers between devices, body(): lax.psum_scatter(jnp.dot(normed, out_weight, preferred_element_type=jnp.f...  57.1 us
    all_gather x1, waiting for transfers between devices, entering(): everything = jax.tree.map(lambda part: lax.all_gather(part, axis), x)  49.8 us
    all_gather x1, waiting for transfers between devices, body(): shard_rows = lax.all_gather(hidden, 'tp', axis=0, tiled=True)  43 us
    all_gather x1, waiting for transfers between devices, body(): full_weight = lax.all_gather(group_weight, 'tp', axis=0, tiled=True)  36.7 us
    all_gather x1, blocking collectives, entering(): everything = jax.tree.map(lambda part: lax.all_gather(part, axis), x)  34.9 us
    select_n x32, other arithmetic, turn(): return jax.tree.map(lambda a, b: jnp.where(reached, a, b), new, before)  31.8 us
    psum x1, blocking collectives, body(): group_sums = lax.psum(jnp.where(own_slot, squares[None, :], 0.0), 'tp')  27.2 us
  transfers between devices with their start and end apart: 6, of which 6 were waited for; matrix products, arithmetic and copies ran while one was open for 4% of the time, Pallas kernels for 0%

commit v1 on v0

--- a/solution.py
+++ b/solution.py
@@ -17,19 +17,36 @@
     return lax.ppermute(x, axis, pairs)
 
 
-def entering(x, axis, combine, identity):
-    peers, place = (lax.axis_size(axis), lax.axis_index(axis))
-    everything = jax.tree.map(lambda part: lax.all_gather(part, axis), x)
-    start = jax.tree.map(
-        lambda part, zero: jnp.broadcast_to(jnp.asarray(zero, part.dtype), part.shape), x, identity
-    )
-
-    def turn(k, before):
-        reached = k < place
-        new = combine(before, jax.tree.map(lambda part: part[k], everything))
-        return jax.tree.map(lambda a, b: jnp.where(reached, a, b), new, before)
-
-    return lax.fori_loop(0, peers, turn, start)
+def swapped(x, axis, bit):
+    peers = lax.axis_size(axis)
+    return lax.ppermute(x, axis, [(i, i ^ bit) for i in range(peers)])
+
+
+def gather_rows(rows, axis, bits):
+    place = lax.axis_index(axis)
+    peers = lax.axis_size(axis)
+    held = rows
+    for bit in reversed(bits):
+        other = swapped(held, axis, bit)
+        low = (place & bit) == 0
+        held = jnp.where(low, jnp.stack([held, other]), jnp.stack([other, held]))
+    order = tuple(reversed(range(len(bits)))) + tuple(range(len(bits), held.ndim))
+    held = jnp.transpose(held, order)
+    return held.reshape((peers * rows.shape[0],) + rows.shape[1:])
+
+
+def scatter_sum(full, axis, bits):
+    place = lax.axis_index(axis)
+    peers = lax.axis_size(axis)
+    per = full.shape[0] // peers
+    held = full.reshape((2,) * len(bits) + (per,) + full.shape[1:])
+    for bit in bits:
+        at = held.ndim - len(full.shape) - 1
+        mine = (place // bit) % 2
+        keep = lax.dynamic_index_in_dim(held, mine, at, keepdims=False)
+        give = lax.dynamic_index_in_dim(held, 1 - mine, at, keepdims=False)
+        held = keep + swapped(give, axis, bit)
+    return held.reshape((per,) + full.shape[1:])
 
 
 def causal_conv(prior_rows, raw_rows, conv_weight, conv_bias):
@@ -39,10 +56,6 @@
     for offset in range(conv_weight.shape[0]):
         running = running + conv_weight[offset][None, :] * joined[offset : offset + length]
     return jax.nn.silu(running).astype(jnp.bfloat16)
-
-
-def combine_states(earlier, latter):
-    return (earlier[0] * latter[0], latter[0][:, None, None] * earlier[1] + latter[1])
 
 
 def body(
@@ -60,33 +73,41 @@
     norm_gain,
     out_weight,
 ):
+    tp_size = lax.axis_size("tp")
+    tp_bits = [1 << k for k in range(tp_size.bit_length() - 1)]
     heads_dev = log_rate.shape[0]
     inner_dev = in_weight.shape[2]
     group_cols = 2 * STATE
-    group_index = lax.axis_index("tp") * heads_dev // (HEADS // GROUPS)
+    per_group_dev = (HEADS // GROUPS) // heads_dev
+    group_index = lax.axis_index("tp") // per_group_dev
     zx_weight = in_weight.reshape(in_weight.shape[0], 2 * inner_dev)
-    full_weight = lax.all_gather(group_weight, "tp", axis=0, tiled=True)
-    map_weight = lax.dynamic_slice_in_dim(full_weight, group_index, 1, 1)[:, 0, :]
-    shard_rows = lax.all_gather(hidden, "tp", axis=0, tiled=True)
+    shard_rows = gather_rows(hidden, "tp", tp_bits)
+    length = shard_rows.shape[0]
     projected = jnp.concatenate(
         [
             jnp.dot(shard_rows, zx_weight, preferred_element_type=jnp.float32),
-            lax.dot_general(
-                shard_rows, map_weight, (((1,), (1,)), ((), ())), preferred_element_type=jnp.float32
-            ),
             jnp.dot(shard_rows, step_weight, preferred_element_type=jnp.float32),
         ],
         axis=1,
     ).astype(jnp.bfloat16)
     gate_raw = projected[:, :inner_dev]
     inner_raw = projected[:, inner_dev : 2 * inner_dev]
-    map_part = projected[:, 2 * inner_dev : projected.shape[1] - heads_dev]
-    step_raw = projected[:, projected.shape[1] - heads_dev :]
+    step_raw = projected[:, 2 * inner_dev :]
+    dest_groups = [q // per_group_dev for q in range(tp_size)]
+    spread = jnp.take(group_weight, jnp.array(dest_groups), axis=1)
+    own_maps = jnp.einsum(
+        "td,sqd->qts", shard_rows, spread, preferred_element_type=jnp.float32
+    ).astype(jnp.bfloat16)
+    got_maps = lax.all_to_all(own_maps, "tp", 0, 0, tiled=True)
+    map_part = jnp.transpose(got_maps, (1, 0, 2)).reshape(length, group_cols)
     border_rows = KERNEL - 1
-    length = inner_raw.shape[0]
-    inner_prior, map_prior = shifted(
-        (inner_raw[length - border_rows :], map_part[length - border_rows :]), "ctx", 1
-    )
+    prior = shifted(
+        jnp.concatenate([inner_raw[length - border_rows :], map_part[length - border_rows :]], axis=1),
+        "ctx",
+        1,
+    )
+    inner_prior = prior[:, :inner_dev]
+    map_prior = prior[:, inner_dev:]
     x_conv = causal_conv(inner_prior, inner_raw, conv_inner, inner_bias)
     own_taps = lax.dynamic_slice_in_dim(conv_group, group_index * group_cols, group_cols, 1)
     own_bias = lax.dynamic_slice_in_dim(group_bias, group_index * group_cols, group_cols, 0)
@@ -124,12 +145,27 @@
     (dev_state, dev_decay), (local_starts, prefixes) = lax.scan(
         advance, (empty_state, jnp.ones((heads_dev,), jnp.float32)), (block_decay, block_state)
     )
-    decay_in, incoming = entering(
-        (dev_decay, dev_state),
-        "ctx",
-        combine_states,
-        (jnp.ones_like(dev_decay), jnp.zeros_like(dev_state)),
-    )
+    ctx_size = lax.axis_size("ctx")
+    place = lax.axis_index("ctx")
+    in_decay = jnp.ones_like(dev_decay)
+    in_state = jnp.zeros_like(dev_state)
+    run_decay = dev_decay
+    run_state = dev_state
+    reach = 1
+    while reach < ctx_size:
+        packed = jnp.concatenate(
+            [run_state, jnp.broadcast_to(run_decay[:, None, None], (heads_dev, 1, STATE))], axis=1
+        )
+        got = shifted(packed, "ctx", reach)
+        valid = place >= reach
+        got_state = jnp.where(valid, got[:, :HEAD_DIM], 0.0)
+        got_decay = jnp.where(valid, got[:, HEAD_DIM, 0], 1.0)
+        in_state = in_decay[:, None, None] * got_state + in_state
+        in_decay = got_decay * in_decay
+        run_state = run_decay[:, None, None] * got_state + run_state
+        run_decay = got_decay * run_decay
+        reach *= 2
+    incoming = in_state
     starting = local_starts + prefixes[:, :, None, None] * incoming[None]
     carried = jnp.einsum(
         "kin,khpn->kihp",
@@ -141,17 +177,15 @@
     result_heads = within + carried + skip_weight[None, None, :, None] * x_float
     result_heads = result_heads.reshape(length, inner_dev)
     gated = result_heads * jax.nn.silu(gate_raw.astype(jnp.float32))
-    squares = jnp.sum(gated * gated, axis=1)
-    own_slot = (jnp.arange(GROUPS) == group_index)[:, None]
-    group_sums = lax.psum(jnp.where(own_slot, squares[None, :], 0.0), "tp")
-    own_total = jnp.sum(jnp.where(own_slot, group_sums, 0.0), axis=0)
-    inverse = lax.rsqrt(own_total / (HEADS * HEAD_DIM // GROUPS) + 1e-05)
+    total = jnp.sum(gated * gated, axis=1)
+    bit = 1
+    while bit < per_group_dev:
+        total = total + swapped(total, "tp", bit)
+        bit *= 2
+    inverse = lax.rsqrt(total / (HEADS * HEAD_DIM // GROUPS) + 1e-05)
     normed = (gated * inverse[:, None] * norm_gain[None, :]).astype(jnp.bfloat16)
-    mixed = lax.psum_scatter(
-        jnp.dot(normed, out_weight, preferred_element_type=jnp.float32),
-        "tp",
-        scatter_dimension=0,
-        tiled=True,
+    mixed = scatter_sum(
+        jnp.dot(normed, out_weight, preferred_element_type=jnp.float32), "tp", tp_bits
     )
     return mixed.astype(jnp.bfloat16)
 

time: 325 us -> 188 us (0.58)
  waiting for transfers between devices: 188 us -> 77.9 us
  starting transfers between devices: 6.31 us -> 85.2 us
  blocking collectives: 62.1 us -> 0 us
  other arithmetic: 35.5 us -> 5.42 us
  between operations: 13.5 us -> 0.86 us
  local copies, waits for them, and re-layouts: 7.25 us -> 13.6 us
  matrix products: 9.06 us -> 4.72 us
    all_gather x3 -> x0, waiting for transfers between devices: 130 us -> none  [the longest x1 49.8 us: entering(): everything = jax.tree.map(lambda part: lax.all_gather(part, axis), x)]
    ppermute x0 -> x10, waiting for transfers between devices: none -> 58.8 us  [swapped(): return lax.ppermute(x, axis, [(i, i ^ bit) for i in range(peers)])]
    reduce_scatter x1 -> x0, waiting for transfers between devices: 57.1 us -> none  [body(): lax.psum_scatter(jnp.dot(normed, out_weight, preferred_element_type=jnp.f...]
    ppermute x0 -> x10, starting transfers between devices: none -> 38.2 us  [swapped(): return lax.ppermute(x, axis, [(i, i ^ bit) for i in range(peers)])]
    ppermute x2 -> x6, starting transfers between devices: 6.19 us -> 43.3 us  [shifted(): return lax.ppermute(x, axis, pairs)]
    all_gather x1 -> x0, blocking collectives: 34.9 us -> none  [entering(): everything = jax.tree.map(lambda part: lax.all_gather(part, axis), x)]
    select_n x33 -> x7, other arithmetic: 31.9 us -> 0.29 us  [gather_rows(): held = jnp.where(low, jnp.stack([held, other]), jnp.stack([other, held]))]
    psum x1 -> x0, blocking collectives: 27.2 us -> none  [body(): group_sums = lax.psum(jnp.where(own_slot, squares[None, :], 0.0), 'tp')]
  transfers between devices with their start and end apart: 6 -> 17, of which waited for: 6 -> 16; matrix products, arithmetic and copies ran while one was open for 4% -> 5% of each run, Pallas kernels for 0% -> 0%
where the time goes in v1:
time: 188 us
  starting transfers between devices  85.2 us (45%)
  waiting for transfers between devices  77.9 us (41%)
  local copies, waits for them, and re-layouts  13.6 us (7%)
  other arithmetic  5.42 us (3%)
  matrix products  4.72 us (3%)
    ppermute x10, waiting for transfers between devices, swapped(): return lax.ppermute(x, axis, [(i, i ^ bit) for i in range(peers)])  58.8 us
    ppermute x6, starting transfers between devices, shifted(): return lax.ppermute(x, axis, pairs)  43.3 us
    ppermute x10, starting transfers between devices, swapped(): return lax.ppermute(x, axis, [(i, i ^ bit) for i in range(peers)])  38.2 us
    ppermute x6, waiting for transfers between devices, shifted(): return lax.ppermute(x, axis, pairs)  10.6 us
    all_to_all x1, waiting for transfers between devices, body(): got_maps = lax.all_to_all(own_maps, 'tp', 0, 0, tiled=True)  8.57 us
    unnamed x26, local copies, waits for them, and re-layouts  4.53 us
  transfers between devices with their start and end apart: 17, of which 16 were waited for; matrix products, arithmetic and copies ran while one was open for 5% of the time, Pallas kernels for 0%

profile of v1, /device:TPU:1, one launch (start us, length us, event | category | flops | bytes accessed | tf_op | source)
XLA Modules:
  0.0 187.7 jit_solution(17517786153588576919)
XLA Ops:
  0.0 8.4 %collective-permute-start = (bf16[16,2048]{1,0:T(8,128)(2,1)}, bf16[16,2048]{1,0:T(8,128)(2,1)S(1)}, u32[]{:S(2)}, u32[]{:S(2)}) collective-permute-start(bf16[16,2048]{1,0:T(8,128)(2,1)} %param.14), channel_id=1, source_target_pairs={{0,8},{1,9},{2,10},{3,11},{4,12},{5,13},{6,14},{7,15},{8,0},{9,1},... | collective-permute-start | bytes 196616 | tf_op jit(solution)/shard_map/ppermute | solution.py:22
  8.5 3.4 %copy.64 = bf16[256,8,2,256]{3,1,2,0:T(8,128)(2,1)} copy(bf16[256,8,2,256]{3,2,1,0:T(2,128)(2,1)} %bitcast.131) | data formatting | bytes 4194304
  12.0 3.5 %gather_fusion = bf16[16,16,2048]{2,0,1:T(8,128)(2,1)S(1)} fusion(bf16[16,4,2048]{2,1,0:T(4,128)(2,1)S(1)} %copy-done.1, s32[1024]{0:T(1024)S(1)} %pad_clamp_fusion), kind=kCustom, calls=%fused_computation | custom fusion | bytes 2097216 | tf_op jit(solution)/shard_map/jit(_take)/gather | solution.py:97
  17.3 2.4 %collective-permute-start.1 = (bf16[2,16,2048]{2,1,0:T(8,128)(2,1)S(1)}, bf16[2,16,2048]{2,1,0:T(8,128)(2,1)S(1)}, u32[]{:S(2)}, u32[]{:S(2)}) collective-permute-start(bf16[2,16,2048]{2,1,0:T(8,128)(2,1)S(1)} %maximum_select_fusion.3), channel_id=1, source_target_pairs={{0,4},{1,5},{2,6},{3,7},{4,0},{5,1},{6,2},{7,3},{8,12},{9,13},{10,... | collective-permute-start | bytes 393224 | tf_op jit(solution)/shard_map/ppermute | solution.py:22
  19.7 8.4 %collective-permute-done.1 = bf16[2,16,2048]{2,1,0:T(8,128)(2,1)S(1)} collective-permute-done((bf16[2,16,2048]{2,1,0:T(8,128)(2,1)S(1)}, bf16[2,16,2048]{2,1,0:T(8,128)(2,1)S(1)}, u32[]{:S(2)}, u32[]{:S(2)}) %collective-permute-start.1) | collective-permute-done | bytes 131104 | tf_op jit(solution)/shard_map/ppermute | solution.py:22
  28.2 1.9 %collective-permute-start.2 = (bf16[2,2,16,2048]{3,2,0,1:T(8,128)(2,1)S(1)}, bf16[2,2,16,2048]{3,2,0,1:T(8,128)(2,1)S(1)}, u32[]{:S(2)}, u32[]{:S(2)}) collective-permute-start(bf16[2,2,16,2048]{3,2,0,1:T(8,128)(2,1)S(1)} %maximum_select_fusion.2), channel_id=1, source_target_pairs={{0,2},{1,3},{2,0},{3,1},{4,6},{5,7},{6,4},{7,5},{8,10},{9,11},{10,... | collective-permute-start | bytes 786440 | tf_op jit(solution)/shard_map/ppermute | solution.py:22
  30.2 7.1 %collective-permute-done.2 = bf16[2,2,16,2048]{3,2,0,1:T(8,128)(2,1)S(1)} collective-permute-done((bf16[2,2,16,2048]{3,2,0,1:T(8,128)(2,1)S(1)}, bf16[2,2,16,2048]{3,2,0,1:T(8,128)(2,1)S(1)}, u32[]{:S(2)}, u32[]{:S(2)}) %collective-permute-start.2) | collective-permute-done | bytes 262176 | tf_op jit(solution)/shard_map/ppermute | solution.py:22
  37.4 3.4 %collective-permute-start.3 = (bf16[2,2,2,16,2048]{4,3,0,1,2:T(8,128)(2,1)S(1)}, bf16[2,2,2,16,2048]{4,3,0,1,2:T(8,128)(2,1)S(1)}, u32[]{:S(2)}, u32[]{:S(2)}) collective-permute-start(bf16[2,2,2,16,2048]{4,3,0,1,2:T(8,128)(2,1)S(1)} %maximum_select_fusion.1), channel_id=1, source_target_pairs={{0,1},{1,0},{2,3},{3,2},{4,5},{5,4},{6,7},{7,6},{8,9},{9,8},{10,11... | collective-permute-start | bytes 1572872 | tf_op jit(solution)/shard_map/ppermute | solution.py:22
  44.1 2.3 %convolution_convert_fusion = bf16[256,512]{1,0:T(8,128)(2,1)S(1)} fusion(bf16[256,2048]{1,0:T(8,128)(2,1)S(1)} %bitcast.128, bf16[2048,512]{1,0:T(8,128)(2,1)} %bitcast.132), kind=kOutput, calls=%fused_computation.1 | convolution fusion | flops 537001984 | bytes 3407872 | tf_op jit(solution)/shard_map/dot_general | solution.py:88
  47.6 3.7 %all-to-all-start = ((bf16[16,256,16]{1,2,0:T(8,128)(2,1)}), bf16[16,256,16]{1,2,0:T(8,128)(2,1)S(1)}, u32[]{:S(2)}, u32[]{:S(2)}) async-start(bf16[16,256,16]{1,2,0:T(8,128)(2,1)} %copy.50), calls=%async_computation | async-start | bytes 262144 | tf_op jit(solution)/shard_map/all_to_all | solution.py:101
  51.9 8.6 %all-to-all-done = bf16[16,256,16]{1,2,0:T(8,128)(2,1)S(1)} async-done(((bf16[16,256,16]{1,2,0:T(8,128)(2,1)}), bf16[16,256,16]{1,2,0:T(8,128)(2,1)S(1)}, u32[]{:S(2)}, u32[]{:S(2)}) %all-to-all-start) | async-done | bytes 131104 | tf_op jit(solution)/shard_map/all_to_all | solution.py:101
  60.7 3.1 %collective-permute-start.4 = (bf16[3,512]{1,0:T(4,128)(2,1)S(1)}, bf16[3,512]{1,0:T(4,128)(2,1)S(1)}, u32[]{:S(2)}, u32[]{:S(2)}) collective-permute-start(bf16[3,512]{1,0:T(4,128)(2,1)S(1)} %pad_maximum_fusion.9), channel_id=1, source_target_pairs={{0,16},{16,32},{32,48},{48,64},{64,80},{80,96},{96,112},{112,128},... | collective-permute-start | bytes 9224 | tf_op jit(solution)/shard_map/ppermute | solution.py:17
  65.4 3.6 %collective-permute-start.5 = (f32[4,65,128]{2,1,0:T(8,128)S(1)}, f32[4,65,128]{2,1,0:T(8,128)S(1)}, u32[]{:S(2)}, u32[]{:S(2)}) collective-permute-start(f32[4,65,128]{2,1,0:T(8,128)S(1)} %pad_maximum_fusion.4), channel_id=1, source_target_pairs={{0,16},{16,32},{32,48},{48,64},{64,80},{80,96},{96,112},{112,128},... | collective-permute-start | bytes 399368 | tf_op jit(solution)/shard_map/ppermute | solution.py:17
  69.0 2.4 %collective-permute-done.5 = f32[4,65,128]{2,1,0:T(8,128)S(1)} collective-permute-done((f32[4,65,128]{2,1,0:T(8,128)S(1)}, f32[4,65,128]{2,1,0:T(8,128)S(1)}, u32[]{:S(2)}, u32[]{:S(2)}) %collective-permute-start.5) | collective-permute-done | bytes 133152 | tf_op jit(solution)/shard_map/ppermute | solution.py:17
  71.7 5.6 %collective-permute-start.6 = (f32[4,65,128]{2,1,0:T(8,128)S(1)}, f32[4,65,128]{2,1,0:T(8,128)S(1)}, u32[]{:S(2)}, u32[]{:S(2)}) collective-permute-start(f32[4,65,128]{2,1,0:T(8,128)S(1)} %pad_maximum_fusion.5), channel_id=1, source_target_pairs={{0,32},{16,48},{32,64},{48,80},{64,96},{80,112},{96,128},{112,144}... | collective-permute-start | bytes 399368 | tf_op jit(solution)/shard_map/ppermute | solution.py:17
  77.4 2.0 %collective-permute-done.6 = f32[4,65,128]{2,1,0:T(8,128)S(1)} collective-permute-done((f32[4,65,128]{2,1,0:T(8,128)S(1)}, f32[4,65,128]{2,1,0:T(8,128)S(1)}, u32[]{:S(2)}, u32[]{:S(2)}) %collective-permute-start.6) | collective-permute-done | bytes 133152 | tf_op jit(solution)/shard_map/ppermute | solution.py:17
  79.7 9.8 %collective-permute-start.7 = (f32[4,65,128]{2,1,0:T(8,128)S(1)}, f32[4,65,128]{2,1,0:T(8,128)S(1)}, u32[]{:S(2)}, u32[]{:S(2)}) collective-permute-start(f32[4,65,128]{2,1,0:T(8,128)S(1)} %pad_maximum_fusion.6), channel_id=1, source_target_pairs={{0,64},{16,80},{32,96},{48,112},{64,128},{80,144},{96,160},{112,17... | collective-permute-start | bytes 399368 | tf_op jit(solution)/shard_map/ppermute | solution.py:17
  89.6 2.0 %collective-permute-done.7 = f32[4,65,128]{2,1,0:T(8,128)S(1)} collective-permute-done((f32[4,65,128]{2,1,0:T(8,128)S(1)}, f32[4,65,128]{2,1,0:T(8,128)S(1)}, u32[]{:S(2)}, u32[]{:S(2)}) %collective-permute-start.7) | collective-permute-done | bytes 133152 | tf_op jit(solution)/shard_map/ppermute | solution.py:17
  91.9 5.8 %collective-permute-start.8 = (f32[4,65,128]{2,1,0:T(8,128)S(1)}, f32[4,65,128]{2,1,0:T(8,128)S(1)}, u32[]{:S(2)}, u32[]{:S(2)}) collective-permute-start(f32[4,65,128]{2,1,0:T(8,128)S(1)} %pad_maximum_fusion.7), channel_id=1, source_target_pairs={{0,128},{16,144},{32,160},{48,176},{64,192},{80,208},{96,224},{112... | collective-permute-start | bytes 399368 | tf_op jit(solution)/shard_map/ppermute | solution.py:17
  100.1 15.4 %collective-permute-start.9 = (f32[4,65,128]{2,1,0:T(8,128)S(1)}, f32[4,65,128]{2,1,0:T(8,128)S(1)}, u32[]{:S(2)}, u32[]{:S(2)}) collective-permute-start(f32[4,65,128]{2,1,0:T(8,128)S(1)} %pad_maximum_fusion.8), channel_id=1, source_target_pairs={{0,256},{16,272},{32,288},{48,304},{64,320},{80,336},{96,352},{112... | collective-permute-start | bytes 399368 | tf_op jit(solution)/shard_map/ppermute | solution.py:17
  115.7 1.9 %collective-permute-done.9 = f32[4,65,128]{2,1,0:T(8,128)S(1)} collective-permute-done((f32[4,65,128]{2,1,0:T(8,128)S(1)}, f32[4,65,128]{2,1,0:T(8,128)S(1)}, u32[]{:S(2)}, u32[]{:S(2)}) %collective-permute-start.9) | collective-permute-done | bytes 133152 | tf_op jit(solution)/shard_map/ppermute | solution.py:17
  118.6 7.9 %collective-permute-start.10 = (f32[256]{0:T(256)S(1)}, f32[256]{0:T(256)S(1)}, u32[]{:S(2)}, u32[]{:S(2)}) collective-permute-start(f32[256]{0:T(256)S(1)} %multiply_reduce_fusion), channel_id=1, source_target_pairs={{0,1},{1,0},{2,3},{3,2},{4,5},{5,4},{6,7},{7,6},{8,9},{9,8},{10,11... | collective-permute-start | bytes 3080 | tf_op jit(solution)/shard_map/ppermute | solution.py:22
  127.3 1.9 %collective-permute-start.11 = (f32[256]{0:T(256)S(1)}, f32[256]{0:T(256)S(1)}, u32[]{:S(2)}, u32[]{:S(2)}) collective-permute-start(f32[256]{0:T(256)S(1)} %add.191), channel_id=1, source_target_pairs={{0,2},{1,3},{2,0},{3,1},{4,6},{5,7},{6,4},{7,5},{8,10},{9,11},{10,... | collective-permute-start | bytes 3080 | tf_op jit(solution)/shard_map/ppermute | solution.py:22
  129.2 2.4 %collective-permute-done.11 = f32[256]{0:T(256)S(1)} collective-permute-done((f32[256]{0:T(256)S(1)}, f32[256]{0:T(256)S(1)}, u32[]{:S(2)}, u32[]{:S(2)}) %collective-permute-start.11) | collective-permute-done | bytes 1056 | tf_op jit(solution)/shard_map/ppermute | solution.py:22
  133.4 3.4 %collective-permute-start.12 = (f32[2,2,2,16,2048]{4,3,1,0,2:T(8,128)}, f32[2,2,2,16,2048]{4,3,1,0,2:T(8,128)S(1)}, u32[]{:S(2)}, u32[]{:S(2)}) collective-permute-start(f32[2,2,2,16,2048]{4,3,1,0,2:T(8,128)} %bitcast.125), channel_id=1, source_target_pairs={{0,1},{1,0},{2,3},{3,2},{4,5},{5,4},{6,7},{7,6},{8,9},{9,8},{10,11... | collective-permute-start | bytes 3145736 | tf_op jit(solution)/shard_map/ppermute | solution.py:22
  136.8 2.4 %collective-permute-done.12 = f32[2,2,2,16,2048]{4,3,1,0,2:T(8,128)S(1)} collective-permute-done((f32[2,2,2,16,2048]{4,3,1,0,2:T(8,128)}, f32[2,2,2,16,2048]{4,3,1,0,2:T(8,128)S(1)}, u32[]{:S(2)}, u32[]{:S(2)}) %collective-permute-start.12) | collective-permute-done | bytes 1048608 | tf_op jit(solution)/shard_map/ppermute | solution.py:22
  141.6 1.9 %collective-permute-start.13 = (f32[2,2,16,2048]{3,2,1,0:T(8,128)S(1)}, f32[2,2,16,2048]{3,2,1,0:T(8,128)S(1)}, u32[]{:S(2)}, u32[]{:S(2)}) collective-permute-start(f32[2,2,16,2048]{3,2,1,0:T(8,128)S(1)} %dynamic-slice_bitcast_fusion), channel_id=1, source_target_pairs={{0,2},{1,3},{2,0},{3,1},{4,6},{5,7},{6,4},{7,5},{8,10},{9,11},{10,... | collective-permute-start | bytes 1572872 | tf_op jit(solution)/shard_map/ppermute | solution.py:22
  143.6 13.0 %collective-permute-done.13 = f32[2,2,16,2048]{3,2,1,0:T(8,128)S(1)} collective-permute-done((f32[2,2,16,2048]{3,2,1,0:T(8,128)S(1)}, f32[2,2,16,2048]{3,2,1,0:T(8,128)S(1)}, u32[]{:S(2)}, u32[]{:S(2)}) %collective-permute-start.13) | collective-permute-done | bytes 524320 | tf_op jit(solution)/shard_map/ppermute | solution.py:22
  156.7 2.1 %collective-permute-start.14 = (f32[2,16,2048]{2,1,0:T(8,128)S(1)}, f32[2,16,2048]{2,1,0:T(8,128)S(1)}, u32[]{:S(2)}, u32[]{:S(2)}) collective-permute-start(f32[2,16,2048]{2,1,0:T(8,128)S(1)} %dynamic-slice_bitcast_fusion.1), channel_id=1, source_target_pairs={{0,4},{1,5},{2,6},{3,7},{4,0},{5,1},{6,2},{7,3},{8,12},{9,13},{10,... | collective-permute-start | bytes 786440 | tf_op jit(solution)/shard_map/ppermute | solution.py:22
  158.9 14.2 %collective-permute-done.14 = f32[2,16,2048]{2,1,0:T(8,128)S(1)} collective-permute-done((f32[2,16,2048]{2,1,0:T(8,128)S(1)}, f32[2,16,2048]{2,1,0:T(8,128)S(1)}, u32[]{:S(2)}, u32[]{:S(2)}) %collective-permute-start.14) | collective-permute-done | bytes 262176 | tf_op jit(solution)/shard_map/ppermute | solution.py:22
  173.2 4.8 %collective-permute-start.15 = (f32[16,2048]{1,0:T(8,128)S(1)}, f32[16,2048]{1,0:T(8,128)S(1)}, u32[]{:S(2)}, u32[]{:S(2)}) collective-permute-start(f32[16,2048]{1,0:T(8,128)S(1)} %dynamic-slice_bitcast_fusion.2), channel_id=1, source_target_pairs={{0,8},{1,9},{2,10},{3,11},{4,12},{5,13},{6,14},{7,15},{8,0},{9,1},... | collective-permute-start | bytes 393224 | tf_op jit(solution)/shard_map/ppermute | solution.py:22
  178.0 9.0 %collective-permute-done.15 = f32[16,2048]{1,0:T(8,128)S(1)} collective-permute-done((f32[16,2048]{1,0:T(8,128)S(1)}, f32[16,2048]{1,0:T(8,128)S(1)}, u32[]{:S(2)}, u32[]{:S(2)}) %collective-permute-start.15) | collective-permute-done | bytes 131104 | tf_op jit(solution)/shard_map/ppermute | solution.py:22
  (117 shorter events, 18.9 us)
Async XLA Ops:
  0.0 131.6 %copy-start = (bf16[256,2048]{1,0:T(8,128)(2,1)S(1)}, bf16[256,2048]{1,0:T(8,128)(2,1)}, u32[]{:S(2)}) copy-start(bf16[256,2048]{1,0:T(8,128)(2,1)} %param.26) | copy-start | bytes 3145732
  0.0 17.2 %collective-permute-start = (bf16[16,2048]{1,0:T(8,128)(2,1)}, bf16[16,2048]{1,0:T(8,128)(2,1)S(1)}, u32[]{:S(2)}, u32[]{:S(2)}) collective-permute-start(bf16[16,2048]{1,0:T(8,128)(2,1)} %param.14), channel_id=1, source_target_pairs={{0,8},{1,9},{2,10},{3,11},{4,12},{5,13},{6,14},{7,15},{8,0},{9,1},... | collective-permute-start | bytes 196616 | tf_op jit(solution)/shard_map/ppermute | solution.py:22
  8.4 3.5 %copy-start.7 = (s32[16]{0:T(128)S(1)}, s32[16]{0:T(128)}, u32[]{:S(2)}) copy-start(s32[16]{0:T(128)} %constant.178) | copy-start | bytes 196
  8.4 3.5 %copy-start.9 = (f32[4]{0:T(128)S(1)}, f32[4]{0:T(128)}, u32[]{:S(2)}) copy-start(f32[4]{0:T(128)} %param.23) | copy-start | bytes 52
  8.4 3.5 %copy-start.4 = (f32[4,256]{1,0:T(4,128)S(1)}, f32[4,256]{1,0:T(4,128)}, u32[]{:S(2)}) copy-start(f32[4,256]{1,0:T(4,128)} %param.18) | copy-start | bytes 12292
  8.5 3.5 %copy-start.1 = (bf16[16,4,2048]{2,1,0:T(4,128)(2,1)S(1)}, bf16[16,4,2048]{2,1,0:T(4,128)(2,1)}, u32[]{:S(2)}) copy-start(bf16[16,4,2048]{2,1,0:T(4,128)(2,1)} %param.17) | copy-start | bytes 786436
  12.0 5.3 %copy-start.3 = (bf16[16,2048]{1,0:T(8,128)(2,1)S(1)}, bf16[16,2048]{1,0:T(8,128)(2,1)}, u32[]{:S(2)}) copy-start(bf16[16,2048]{1,0:T(8,128)(2,1)} %param.14) | copy-start | bytes 196612
  17.3 10.9 %collective-permute-start.1 = (bf16[2,16,2048]{2,1,0:T(8,128)(2,1)S(1)}, bf16[2,16,2048]{2,1,0:T(8,128)(2,1)S(1)}, u32[]{:S(2)}, u32[]{:S(2)}) collective-permute-start(bf16[2,16,2048]{2,1,0:T(8,128)(2,1)S(1)} %maximum_select_fusion.3), channel_id=1, source_target_pairs={{0,4},{1,5},{2,6},{3,7},{4,0},{5,1},{6,2},{7,3},{8,12},{9,13},{10,... | collective-permute-start | bytes 393224 | tf_op jit(solution)/shard_map/ppermute | solution.py:22
  28.2 9.2 %collective-permute-start.2 = (bf16[2,2,16,2048]{3,2,0,1:T(8,128)(2,1)S(1)}, bf16[2,2,16,2048]{3,2,0,1:T(8,128)(2,1)S(1)}, u32[]{:S(2)}, u32[]{:S(2)}) collective-permute-start(bf16[2,2,16,2048]{3,2,0,1:T(8,128)(2,1)S(1)} %maximum_select_fusion.2), channel_id=1, source_target_pairs={{0,2},{1,3},{2,0},{3,1},{4,6},{5,7},{6,4},{7,5},{8,10},{9,11},{10,... | collective-permute-start | bytes 786440 | tf_op jit(solution)/shard_map/ppermute | solution.py:22
  37.4 4.9 %collective-permute-start.3 = (bf16[2,2,2,16,2048]{4,3,0,1,2:T(8,128)(2,1)S(1)}, bf16[2,2,2,16,2048]{4,3,0,1,2:T(8,128)(2,1)S(1)}, u32[]{:S(2)}, u32[]{:S(2)}) collective-permute-start(bf16[2,2,2,16,2048]{4,3,0,1,2:T(8,128)(2,1)S(1)} %maximum_select_fusion.1), channel_id=1, source_target_pairs={{0,1},{1,0},{2,3},{3,2},{4,5},{5,4},{6,7},{7,6},{8,9},{9,8},{10,11... | collective-permute-start | bytes 1572872 | tf_op jit(solution)/shard_map/ppermute | solution.py:22
  40.9 1.5 copy-start.8
  40.9 1.5 copy-start.10
  46.5 18.2 %copy-start.6 = (f32[256]{0:T(256)S(1)}, f32[256]{0:T(256)}, u32[]{:S(2)}) copy-start(f32[256]{0:T(256)} %param.19) | copy-start | bytes 3076
  47.6 12.9 %all-to-all-start = ((bf16[16,256,16]{1,2,0:T(8,128)(2,1)}), bf16[16,256,16]{1,2,0:T(8,128)(2,1)S(1)}, u32[]{:S(2)}, u32[]{:S(2)}) async-start(bf16[16,256,16]{1,2,0:T(8,128)(2,1)} %copy.50), calls=%async_computation | async-start | bytes 262144 | tf_op jit(solution)/shard_map/all_to_all | solution.py:101
  60.7 3.9 %collective-permute-start.4 = (bf16[3,512]{1,0:T(4,128)(2,1)S(1)}, bf16[3,512]{1,0:T(4,128)(2,1)S(1)}, u32[]{:S(2)}, u32[]{:S(2)}) collective-permute-start(bf16[3,512]{1,0:T(4,128)(2,1)S(1)} %pad_maximum_fusion.9), channel_id=1, source_target_pairs={{0,16},{16,32},{32,48},{48,64},{64,80},{80,96},{96,112},{112,128},... | collective-permute-start | bytes 9224 | tf_op jit(solution)/shard_map/ppermute | solution.py:17
  65.4 6.0 %collective-permute-start.5 = (f32[4,65,128]{2,1,0:T(8,128)S(1)}, f32[4,65,128]{2,1,0:T(8,128)S(1)}, u32[]{:S(2)}, u32[]{:S(2)}) collective-permute-start(f32[4,65,128]{2,1,0:T(8,128)S(1)} %pad_maximum_fusion.4), channel_id=1, source_target_pairs={{0,16},{16,32},{32,48},{48,64},{64,80},{80,96},{96,112},{112,128},... | collective-permute-start | bytes 399368 | tf_op jit(solution)/shard_map/ppermute | solution.py:17
  71.7 7.7 %collective-permute-start.6 = (f32[4,65,128]{2,1,0:T(8,128)S(1)}, f32[4,65,128]{2,1,0:T(8,128)S(1)}, u32[]{:S(2)}, u32[]{:S(2)}) collective-permute-start(f32[4,65,128]{2,1,0:T(8,128)S(1)} %pad_maximum_fusion.5), channel_id=1, source_target_pairs={{0,32},{16,48},{32,64},{48,80},{64,96},{80,112},{96,128},{112,144}... | collective-permute-start | bytes 399368 | tf_op jit(solution)/shard_map/ppermute | solution.py:17
  77.3 40.5 %copy-start.11 = (f32[4]{0:T(128)S(1)}, f32[4]{0:T(128)}, u32[]{:S(2)}) copy-start(f32[4]{0:T(128)} %param.24) | copy-start | bytes 52
  79.7 11.9 %collective-permute-start.7 = (f32[4,65,128]{2,1,0:T(8,128)S(1)}, f32[4,65,128]{2,1,0:T(8,128)S(1)}, u32[]{:S(2)}, u32[]{:S(2)}) collective-permute-start(f32[4,65,128]{2,1,0:T(8,128)S(1)} %pad_maximum_fusion.6), channel_id=1, source_target_pairs={{0,64},{16,80},{32,96},{48,112},{64,128},{80,144},{96,160},{112,17... | collective-permute-start | bytes 399368 | tf_op jit(solution)/shard_map/ppermute | solution.py:17
  91.9 7.9 %collective-permute-start.8 = (f32[4,65,128]{2,1,0:T(8,128)S(1)}, f32[4,65,128]{2,1,0:T(8,128)S(1)}, u32[]{:S(2)}, u32[]{:S(2)}) collective-permute-start(f32[4,65,128]{2,1,0:T(8,128)S(1)} %pad_maximum_fusion.7), channel_id=1, source_target_pairs={{0,128},{16,144},{32,160},{48,176},{64,192},{80,208},{96,224},{112... | collective-permute-start | bytes 399368 | tf_op jit(solution)/shard_map/ppermute | solution.py:17
  100.1 31.5 %copy-start.5 = (f32[256]{0:T(256)S(1)}, f32[256]{0:T(256)}, u32[]{:S(2)}) copy-start(f32[256]{0:T(256)} %param.25) | copy-start | bytes 3076
  100.1 17.5 %collective-permute-start.9 = (f32[4,65,128]{2,1,0:T(8,128)S(1)}, f32[4,65,128]{2,1,0:T(8,128)S(1)}, u32[]{:S(2)}, u32[]{:S(2)}) collective-permute-start(f32[4,65,128]{2,1,0:T(8,128)S(1)} %pad_maximum_fusion.8), channel_id=1, source_target_pairs={{0,256},{16,272},{32,288},{48,304},{64,320},{80,336},{96,352},{112... | collective-permute-start | bytes 399368 | tf_op jit(solution)/shard_map/ppermute | solution.py:17
  118.6 8.7 %collective-permute-start.10 = (f32[256]{0:T(256)S(1)}, f32[256]{0:T(256)S(1)}, u32[]{:S(2)}, u32[]{:S(2)}) collective-permute-start(f32[256]{0:T(256)S(1)} %multiply_reduce_fusion), channel_id=1, source_target_pairs={{0,1},{1,0},{2,3},{3,2},{4,5},{5,4},{6,7},{7,6},{8,9},{9,8},{10,11... | collective-permute-start | bytes 3080 | tf_op jit(solution)/shard_map/ppermute | solution.py:22
  127.3 4.3 %collective-permute-start.11 = (f32[256]{0:T(256)S(1)}, f32[256]{0:T(256)S(1)}, u32[]{:S(2)}, u32[]{:S(2)}) collective-permute-start(f32[256]{0:T(256)S(1)} %add.191), channel_id=1, source_target_pairs={{0,2},{1,3},{2,0},{3,1},{4,6},{5,7},{6,4},{7,5},{8,10},{9,11},{10,... | collective-permute-start | bytes 3080 | tf_op jit(solution)/shard_map/ppermute | solution.py:22
  133.4 5.9 %collective-permute-start.12 = (f32[2,2,2,16,2048]{4,3,1,0,2:T(8,128)}, f32[2,2,2,16,2048]{4,3,1,0,2:T(8,128)S(1)}, u32[]{:S(2)}, u32[]{:S(2)}) collective-permute-start(f32[2,2,2,16,2048]{4,3,1,0,2:T(8,128)} %bitcast.125), channel_id=1, source_target_pairs={{0,1},{1,0},{2,3},{3,2},{4,5},{5,4},{6,7},{7,6},{8,9},{9,8},{10,11... | collective-permute-start | bytes 3145736 | tf_op jit(solution)/shard_map/ppermute | solution.py:22
  139.3 1.0 copy-start.2
  141.6 15.0 %collective-permute-start.13 = (f32[2,2,16,2048]{3,2,1,0:T(8,128)S(1)}, f32[2,2,16,2048]{3,2,1,0:T(8,128)S(1)}, u32[]{:S(2)}, u32[]{:S(2)}) collective-permute-start(f32[2,2,16,2048]{3,2,1,0:T(8,128)S(1)} %dynamic-slice_bitcast_fusion), channel_id=1, source_target_pairs={{0,2},{1,3},{2,0},{3,1},{4,6},{5,7},{6,4},{7,5},{8,10},{9,11},{10,... | collective-permute-start | bytes 1572872 | tf_op jit(solution)/shard_map/ppermute | solution.py:22
  156.7 16.4 %collective-permute-start.14 = (f32[2,16,2048]{2,1,0:T(8,128)S(1)}, f32[2,16,2048]{2,1,0:T(8,128)S(1)}, u32[]{:S(2)}, u32[]{:S(2)}) collective-permute-start(f32[2,16,2048]{2,1,0:T(8,128)S(1)} %dynamic-slice_bitcast_fusion.1), channel_id=1, source_target_pairs={{0,4},{1,5},{2,6},{3,7},{4,0},{5,1},{6,2},{7,3},{8,12},{9,13},{10,... | collective-permute-start | bytes 786440 | tf_op jit(solution)/shard_map/ppermute | solution.py:22
  173.2 13.9 %collective-permute-start.15 = (f32[16,2048]{1,0:T(8,128)S(1)}, f32[16,2048]{1,0:T(8,128)S(1)}, u32[]{:S(2)}, u32[]{:S(2)}) collective-permute-start(f32[16,2048]{1,0:T(8,128)S(1)} %dynamic-slice_bitcast_fusion.2), channel_id=1, source_target_pairs={{0,8},{1,9},{2,10},{3,11},{4,12},{5,13},{6,14},{7,15},{8,0},{9,1},... | collective-permute-start | bytes 393224 | tf_op jit(solution)/shard_map/ppermute | solution.py:22

commit v2 on v1

--- a/solution.py
+++ b/solution.py
@@ -35,18 +35,18 @@
     return held.reshape((peers * rows.shape[0],) + rows.shape[1:])
 
 
-def scatter_sum(full, axis, bits):
+def halve(full, axis, bits, levels):
     place = lax.axis_index(axis)
-    peers = lax.axis_size(axis)
-    per = full.shape[0] // peers
-    held = full.reshape((2,) * len(bits) + (per,) + full.shape[1:])
+    held = full
+    if full.ndim < levels + 2:
+        held = full.reshape((2,) * levels + (full.shape[0] >> levels,) + full.shape[1:])
     for bit in bits:
-        at = held.ndim - len(full.shape) - 1
+        at = held.ndim - 3
         mine = (place // bit) % 2
         keep = lax.dynamic_index_in_dim(held, mine, at, keepdims=False)
         give = lax.dynamic_index_in_dim(held, 1 - mine, at, keepdims=False)
-        held = keep + swapped(give, axis, bit)
-    return held.reshape((per,) + full.shape[1:])
+        held = keep + swapped(give.astype(jnp.bfloat16), axis, bit).astype(jnp.float32)
+    return held
 
 
 def causal_conv(prior_rows, raw_rows, conv_weight, conv_bias):
@@ -177,16 +177,18 @@
     result_heads = within + carried + skip_weight[None, None, :, None] * x_float
     result_heads = result_heads.reshape(length, inner_dev)
     gated = result_heads * jax.nn.silu(gate_raw.astype(jnp.float32))
-    total = jnp.sum(gated * gated, axis=1)
-    bit = 1
-    while bit < per_group_dev:
-        total = total + swapped(total, "tp", bit)
-        bit *= 2
-    inverse = lax.rsqrt(total / (HEADS * HEAD_DIM // GROUPS) + 1e-05)
-    normed = (gated * inverse[:, None] * norm_gain[None, :]).astype(jnp.bfloat16)
-    mixed = scatter_sum(
-        jnp.dot(normed, out_weight, preferred_element_type=jnp.float32), "tp", tp_bits
-    )
+    squares = jnp.sum(gated * gated, axis=1)
+    scaled = (gated * norm_gain[None, :]).astype(jnp.bfloat16)
+    partial = jnp.dot(scaled, out_weight, preferred_element_type=jnp.float32)
+    width = partial.shape[1]
+    packed = jnp.concatenate([partial, jnp.broadcast_to(squares[:, None], (length, 128))], axis=1)
+    within_bits = [bit for bit in tp_bits if bit < per_group_dev]
+    across_bits = [bit for bit in tp_bits if bit >= per_group_dev]
+    held = halve(packed, "tp", within_bits, len(tp_bits))
+    inverse = lax.rsqrt(held[..., width] / (HEADS * HEAD_DIM // GROUPS) + 1e-05)
+    held = held[..., :width] * inverse[..., None]
+    held = halve(held, "tp", across_bits, len(across_bits))
+    mixed = held.reshape(length // tp_size, width)
     return mixed.astype(jnp.bfloat16)
 
 

time: 188 us -> 180 us (0.957)
  waiting for transfers between devices: 77.9 us -> 47.1 us
  local copies, waits for them, and re-layouts: 13.6 us -> 31.8 us
  other arithmetic: 5.42 us -> 14.3 us
  starting transfers between devices: 85.2 us -> 80.3 us
    ppermute x10 -> x8, waiting for transfers between devices: 58.8 us -> 29.9 us  [swapped(): return lax.ppermute(x, axis, [(i, i ^ bit) for i in range(peers)])]
    dynamic_slice x2 -> x4, local copies, waits for them, and re-layouts: 1.28 us -> 9.64 us  [halve(): keep = lax.dynamic_index_in_dim(held, mine, at, keepdims=False)]
    convert_element_type x0 -> x6, local copies, waits for them, and re-layouts: none -> 8.06 us  [the longest x1 4.21 us: halve(): swapped(give.astype(jnp.bfloat16), axis, bit).astype(jnp.float32)]
    add x4 -> x3, other arithmetic: 1.43 us -> 7.29 us  [halve(): keep + swapped(give.astype(jnp.bfloat16), axis, bit).astype(jnp.float32)]
    ppermute x10 -> x8, starting transfers between devices: 38.2 us -> 33.3 us  [swapped(): return lax.ppermute(x, axis, [(i, i ^ bit) for i in range(peers)])]
    all_to_all x1, waiting for transfers between devices: 8.57 us -> 6.59 us  [body(): got_maps = lax.all_to_all(own_maps, 'tp', 0, 0, tiled=True)]
    unnamed x26 -> x20, local copies, waits for them, and re-layouts: 4.53 us -> 5.41 us
  transfers between devices with their start and end apart: 17 -> 15, of which waited for: 16 -> 14; matrix products, arithmetic and copies ran while one was open for 5% -> 13% of each run, Pallas kernels for 0% -> 0%
where the time goes in v2:
time: 180 us; the launch traced here: 179 us
  starting transfers between devices  80.3 us (45%)
  waiting for transfers between devices  47.1 us (26%)
  local copies, waits for them, and re-layouts  31.8 us (18%)
  other arithmetic  14.3 us (8%)
  matrix products  4.72 us (3%)
    ppermute x6, starting transfers between devices, shifted(): return lax.ppermute(x, axis, pairs)  43.3 us
    ppermute x8, starting transfers between devices, swapped(): return lax.ppermute(x, axis, [(i, i ^ bit) for i in range(peers)])  33.3 us
    ppermute x8, waiting for transfers between devices, swapped(): return lax.ppermute(x, axis, [(i, i ^ bit) for i in range(peers)])  29.9 us
    ppermute x6, waiting for transfers between devices, shifted(): return lax.ppermute(x, axis, pairs)  10.6 us
    dynamic_slice x4, local copies, waits for them, and re-layouts, halve(): keep = lax.dynamic_index_in_dim(held, mine, at, keepdims=False)  9.64 us
    add x3, other arithmetic, halve(): keep + swapped(give.astype(jnp.bfloat16), axis, bit).astype(jnp.float32)  7.29 us
    all_to_all x1, waiting for transfers between devices, body(): got_maps = lax.all_to_all(own_maps, 'tp', 0, 0, tiled=True)  6.59 us
    unnamed x20, local copies, waits for them, and re-layouts  5.41 us
  transfers between devices with their start and end apart: 15, of which 14 were waited for; matrix products, arithmetic and copies ran while one was open for 13% of the time, Pallas kernels for 0%

profile of v2, /device:TPU:1, one launch (start us, length us, event | category | flops | bytes accessed | tf_op | source)
XLA Modules:
  0.0 178.9 jit_solution(810448333160662064)
XLA Ops:
  0.0 8.4 %collective-permute-start = (bf16[16,2048]{1,0:T(8,128)(2,1)}, bf16[16,2048]{1,0:T(8,128)(2,1)S(1)}, u32[]{:S(2)}, u32[]{:S(2)}) collective-permute-start(bf16[16,2048]{1,0:T(8,128)(2,1)} %param.14), channel_id=1, source_target_pairs={{0,8},{1,9},{2,10},{3,11},{4,12},{5,13},{6,14},{7,15},{8,0},{9,1},... | collective-permute-start | bytes 196616 | tf_op jit(solution)/shard_map/ppermute | solution.py:22
  10.6 3.4 %copy.152 = bf16[256,8,2,256]{3,1,2,0:T(8,128)(2,1)} copy(bf16[256,8,2,256]{3,2,1,0:T(2,128)(2,1)} %bitcast.132) | data formatting | bytes 4194304
  14.8 3.5 %gather_fusion = bf16[16,16,2048]{2,0,1:T(8,128)(2,1)S(1)} fusion(bf16[16,4,2048]{2,1,0:T(4,128)(2,1)S(1)} %copy-done.1, s32[1024]{0:T(1024)S(1)} %pad_clamp_fusion), kind=kCustom, calls=%fused_computation | custom fusion | bytes 2097216 | tf_op jit(solution)/shard_map/jit(_take)/gather | solution.py:97
  19.3 2.4 %collective-permute-start.1 = (bf16[2,16,2048]{2,1,0:T(8,128)(2,1)S(1)}, bf16[2,16,2048]{2,1,0:T(8,128)(2,1)S(1)}, u32[]{:S(2)}, u32[]{:S(2)}) collective-permute-start(bf16[2,16,2048]{2,1,0:T(8,128)(2,1)S(1)} %maximum_select_fusion.3), channel_id=1, source_target_pairs={{0,4},{1,5},{2,6},{3,7},{4,0},{5,1},{6,2},{7,3},{8,12},{9,13},{10,... | collective-permute-start | bytes 393224 | tf_op jit(solution)/shard_map/ppermute | solution.py:22
  21.7 8.4 %collective-permute-done.1 = bf16[2,16,2048]{2,1,0:T(8,128)(2,1)S(1)} collective-permute-done((bf16[2,16,2048]{2,1,0:T(8,128)(2,1)S(1)}, bf16[2,16,2048]{2,1,0:T(8,128)(2,1)S(1)}, u32[]{:S(2)}, u32[]{:S(2)}) %collective-permute-start.1) | collective-permute-done | bytes 131104 | tf_op jit(solution)/shard_map/ppermute | solution.py:22
  30.2 1.9 %collective-permute-start.2 = (bf16[2,2,16,2048]{3,2,0,1:T(8,128)(2,1)S(1)}, bf16[2,2,16,2048]{3,2,0,1:T(8,128)(2,1)S(1)}, u32[]{:S(2)}, u32[]{:S(2)}) collective-permute-start(bf16[2,2,16,2048]{3,2,0,1:T(8,128)(2,1)S(1)} %maximum_select_fusion.2), channel_id=1, source_target_pairs={{0,2},{1,3},{2,0},{3,1},{4,6},{5,7},{6,4},{7,5},{8,10},{9,11},{10,... | collective-permute-start | bytes 786440 | tf_op jit(solution)/shard_map/ppermute | solution.py:22
  32.2 7.1 %collective-permute-done.2 = bf16[2,2,16,2048]{3,2,0,1:T(8,128)(2,1)S(1)} collective-permute-done((bf16[2,2,16,2048]{3,2,0,1:T(8,128)(2,1)S(1)}, bf16[2,2,16,2048]{3,2,0,1:T(8,128)(2,1)S(1)}, u32[]{:S(2)}, u32[]{:S(2)}) %collective-permute-start.2) | collective-permute-done | bytes 262176 | tf_op jit(solution)/shard_map/ppermute | solution.py:22
  39.4 3.4 %collective-permute-start.3 = (bf16[2,2,2,16,2048]{4,3,0,1,2:T(8,128)(2,1)S(1)}, bf16[2,2,2,16,2048]{4,3,0,1,2:T(8,128)(2,1)S(1)}, u32[]{:S(2)}, u32[]{:S(2)}) collective-permute-start(bf16[2,2,2,16,2048]{4,3,0,1,2:T(8,128)(2,1)S(1)} %maximum_select_fusion.1), channel_id=1, source_target_pairs={{0,1},{1,0},{2,3},{3,2},{4,5},{5,4},{6,7},{7,6},{8,9},{9,8},{10,11... | collective-permute-start | bytes 1572872 | tf_op jit(solution)/shard_map/ppermute | solution.py:22
  47.7 3.7 %all-to-all-start = ((bf16[16,256,16]{1,2,0:T(8,128)(2,1)}), bf16[16,256,16]{1,2,0:T(8,128)(2,1)S(1)}, u32[]{:S(2)}, u32[]{:S(2)}) async-start(bf16[16,256,16]{1,2,0:T(8,128)(2,1)} %copy.136), calls=%async_computation | async-start | bytes 262144 | tf_op jit(solution)/shard_map/all_to_all | solution.py:101
  51.3 2.3 %convolution_convert_fusion = bf16[256,512]{1,0:T(8,128)(2,1)S(1)} fusion(bf16[256,2048]{1,0:T(8,128)(2,1)S(1)} %bitcast.130, bf16[2048,512]{1,0:T(8,128)(2,1)} %bitcast.133), kind=kOutput, calls=%fused_computation.5 | convolution fusion | flops 537001984 | bytes 3407872 | tf_op jit(solution)/shard_map/dot_general | solution.py:88
  53.9 6.6 %all-to-all-done = bf16[16,256,16]{1,2,0:T(8,128)(2,1)S(1)} async-done(((bf16[16,256,16]{1,2,0:T(8,128)(2,1)}), bf16[16,256,16]{1,2,0:T(8,128)(2,1)S(1)}, u32[]{:S(2)}, u32[]{:S(2)}) %all-to-all-start) | async-done | bytes 131104 | tf_op jit(solution)/shard_map/all_to_all | solution.py:101
  60.7 3.1 %collective-permute-start.4 = (bf16[3,512]{1,0:T(4,128)(2,1)S(1)}, bf16[3,512]{1,0:T(4,128)(2,1)S(1)}, u32[]{:S(2)}, u32[]{:S(2)}) collective-permute-start(bf16[3,512]{1,0:T(4,128)(2,1)S(1)} %pad_maximum_fusion.10), channel_id=1, source_target_pairs={{0,16},{16,32},{32,48},{48,64},{64,80},{80,96},{96,112},{112,128},... | collective-permute-start | bytes 9224 | tf_op jit(solution)/shard_map/ppermute | solution.py:17
  65.4 3.6 %collective-permute-start.5 = (f32[4,65,128]{2,1,0:T(8,128)S(1)}, f32[4,65,128]{2,1,0:T(8,128)S(1)}, u32[]{:S(2)}, u32[]{:S(2)}) collective-permute-start(f32[4,65,128]{2,1,0:T(8,128)S(1)} %pad_maximum_fusion.5), channel_id=1, source_target_pairs={{0,16},{16,32},{32,48},{48,64},{64,80},{80,96},{96,112},{112,128},... | collective-permute-start | bytes 399368 | tf_op jit(solution)/shard_map/ppermute | solution.py:17
  69.0 2.4 %collective-permute-done.5 = f32[4,65,128]{2,1,0:T(8,128)S(1)} collective-permute-done((f32[4,65,128]{2,1,0:T(8,128)S(1)}, f32[4,65,128]{2,1,0:T(8,128)S(1)}, u32[]{:S(2)}, u32[]{:S(2)}) %collective-permute-start.5) | collective-permute-done | bytes 133152 | tf_op jit(solution)/shard_map/ppermute | solution.py:17
  71.7 5.6 %collective-permute-start.6 = (f32[4,65,128]{2,1,0:T(8,128)S(1)}, f32[4,65,128]{2,1,0:T(8,128)S(1)}, u32[]{:S(2)}, u32[]{:S(2)}) collective-permute-start(f32[4,65,128]{2,1,0:T(8,128)S(1)} %pad_maximum_fusion.6), channel_id=1, source_target_pairs={{0,32},{16,48},{32,64},{48,80},{64,96},{80,112},{96,128},{112,144}... | collective-permute-start | bytes 399368 | tf_op jit(solution)/shard_map/ppermute | solution.py:17
  77.4 2.0 %collective-permute-done.6 = f32[4,65,128]{2,1,0:T(8,128)S(1)} collective-permute-done((f32[4,65,128]{2,1,0:T(8,128)S(1)}, f32[4,65,128]{2,1,0:T(8,128)S(1)}, u32[]{:S(2)}, u32[]{:S(2)}) %collective-permute-start.6) | collective-permute-done | bytes 133152 | tf_op jit(solution)/shard_map/ppermute | solution.py:17
  79.8 9.8 %collective-permute-start.7 = (f32[4,65,128]{2,1,0:T(8,128)S(1)}, f32[4,65,128]{2,1,0:T(8,128)S(1)}, u32[]{:S(2)}, u32[]{:S(2)}) collective-permute-start(f32[4,65,128]{2,1,0:T(8,128)S(1)} %pad_maximum_fusion.7), channel_id=1, source_target_pairs={{0,64},{16,80},{32,96},{48,112},{64,128},{80,144},{96,160},{112,17... | collective-permute-start | bytes 399368 | tf_op jit(solution)/shard_map/ppermute | solution.py:17
  89.6 2.0 %collective-permute-done.7 = f32[4,65,128]{2,1,0:T(8,128)S(1)} collective-permute-done((f32[4,65,128]{2,1,0:T(8,128)S(1)}, f32[4,65,128]{2,1,0:T(8,128)S(1)}, u32[]{:S(2)}, u32[]{:S(2)}) %collective-permute-start.7) | collective-permute-done | bytes 133152 | tf_op jit(solution)/shard_map/ppermute | solution.py:17
  91.9 5.8 %collective-permute-start.8 = (f32[4,65,128]{2,1,0:T(8,128)S(1)}, f32[4,65,128]{2,1,0:T(8,128)S(1)}, u32[]{:S(2)}, u32[]{:S(2)}) collective-permute-start(f32[4,65,128]{2,1,0:T(8,128)S(1)} %pad_maximum_fusion.8), channel_id=1, source_target_pairs={{0,128},{16,144},{32,160},{48,176},{64,192},{80,208},{96,224},{112... | collective-permute-start | bytes 399368 | tf_op jit(solution)/shard_map/ppermute | solution.py:17
  100.1 15.4 %collective-permute-start.9 = (f32[4,65,128]{2,1,0:T(8,128)S(1)}, f32[4,65,128]{2,1,0:T(8,128)S(1)}, u32[]{:S(2)}, u32[]{:S(2)}) collective-permute-start(f32[4,65,128]{2,1,0:T(8,128)S(1)} %pad_maximum_fusion.9), channel_id=1, source_target_pairs={{0,256},{16,272},{32,288},{48,304},{64,320},{80,336},{96,352},{112... | collective-permute-start | bytes 399368 | tf_op jit(solution)/shard_map/ppermute | solution.py:17
  120.3 7.9 %collective-permute-start.10 = (bf16[2,2,2,16,2176]{4,3,2,1,0:T(8,128)(2,1)}, bf16[2,2,2,16,2176]{4,3,2,1,0:T(8,128)(2,1)}, u32[]{:S(2)}, u32[]{:S(2)}) collective-permute-start(bf16[2,2,2,16,2176]{4,3,2,1,0:T(8,128)(2,1)} %fusion.7), channel_id=1, source_target_pairs={{0,1},{1,0},{2,3},{3,2},{4,5},{5,4},{6,7},{7,6},{8,9},{9,8},{10,11... | collective-permute-start | bytes 1671176 | tf_op jit(solution)/shard_map/ppermute | solution.py:22
  131.3 2.1 %collective-permute-start.11 = (bf16[2,2,16,2176]{3,2,1,0:T(8,128)(2,1)S(1)}, bf16[2,2,16,2176]{3,2,1,0:T(8,128)(2,1)S(1)}, u32[]{:S(2)}, u32[]{:S(2)}) collective-permute-start(bf16[2,2,16,2176]{3,2,1,0:T(8,128)(2,1)S(1)} %fusion.14), channel_id=1, source_target_pairs={{0,2},{1,3},{2,0},{3,1},{4,6},{5,7},{6,4},{7,5},{8,10},{9,11},{10,... | collective-permute-start | bytes 835592 | tf_op jit(solution)/shard_map/ppermute | solution.py:22
  133.4 4.7 %copy.147 = f32[2,2,1,16,2176]{3,1,4,0,2:T(2,128)} copy(f32[2,2,1,16,2176]{4,3,2,1,0:T(8,128)S(1)} %constant_dynamic-slice_fusion.2) | data formatting | bytes 1114112 | tf_op jit(solution)/shard_map/jit(dynamic_index_in_dim)/dynamic_slice | solution.py:46
  138.1 2.9 %collective-permute-done.11 = bf16[2,2,16,2176]{3,2,1,0:T(8,128)(2,1)S(1)} collective-permute-done((bf16[2,2,16,2176]{3,2,1,0:T(8,128)(2,1)S(1)}, bf16[2,2,16,2176]{3,2,1,0:T(8,128)(2,1)S(1)}, u32[]{:S(2)}, u32[]{:S(2)}) %collective-permute-start.11) | collective-permute-done | bytes 278560 | tf_op jit(solution)/shard_map/ppermute | solution.py:22
  141.0 4.2 %copy.148 = f32[2,2,16,2176]{2,1,3,0:T(2,128)} copy(bf16[2,2,16,2176]{3,2,1,0:T(8,128)(2,1)S(1)} %collective-permute-done.11) | data formatting | bytes 835584 | tf_op jit(solution)/shard_map/convert_element_type | solution.py:48
  145.2 5.2 %bitcast_add_fusion = f32[2,2,16,2176]{2,1,3,0:T(2,128)S(1)} fusion(f32[2,2,16,2176]{2,1,3,0:T(2,128)} %copy.148, f32[2,2,1,16,2176]{3,1,4,0,2:T(2,128)} %copy.147), kind=kLoop, calls=%fused_computation.1 | loop fusion | flops 139264 | bytes 1671168 | tf_op jit(solution)/shard_map/add | solution.py:48
  153.9 2.0 %dynamic-slice_convert_fusion = bf16[2,1,16,2048]{2,1,3,0:T(2,128)(2,1)S(1)} fusion(f32[2,2,16,2048]{2,1,3,0:T(2,128)S(1)} %slice_multiply_fusion, s32[]{:T(128)S(6)} %select_n.303), kind=kLoop, calls=%fused_computation.4 | loop fusion | bytes 262148 | tf_op jit(solution)/shard_map/convert_element_type | solution.py:48
  156.9 2.2 %collective-permute-start.12 = (bf16[2,16,2048]{2,1,0:T(8,128)(2,1)S(1)}, bf16[2,16,2048]{2,1,0:T(8,128)(2,1)}, u32[]{:S(2)}, u32[]{:S(2)}) collective-permute-start(bf16[2,16,2048]{2,1,0:T(8,128)(2,1)S(1)} %bitcast.152), channel_id=1, source_target_pairs={{0,4},{1,5},{2,6},{3,7},{4,0},{5,1},{6,2},{7,3},{8,12},{9,13},{10,... | collective-permute-start | bytes 393224 | tf_op jit(solution)/shard_map/ppermute | solution.py:22
  159.0 3.9 %constant_dynamic-slice_fusion.1 = f32[2,1,16,2048]{2,1,3,0:T(1,128)S(1)} fusion(f32[2,2,16,2048]{2,1,3,0:T(2,128)} %copy-done.2, s32[]{:T(128)S(6)} %select_n.302), kind=kLoop, calls=%fused_computation.127 | loop fusion | bytes 524292 | tf_op jit(solution)/shard_map/jit(dynamic_index_in_dim)/dynamic_slice | solution.py:46
  164.0 3.6 %collective-permute-done.12 = bf16[2,16,2048]{2,1,0:T(8,128)(2,1)} collective-permute-done((bf16[2,16,2048]{2,1,0:T(8,128)(2,1)S(1)}, bf16[2,16,2048]{2,1,0:T(8,128)(2,1)}, u32[]{:S(2)}, u32[]{:S(2)}) %collective-permute-start.12) | collective-permute-done | bytes 131104 | tf_op jit(solution)/shard_map/ppermute | solution.py:22
  168.5 5.0 %collective-permute-start.13 = (bf16[16,2048]{1,0:T(8,128)(2,1)S(1)}, bf16[16,2048]{1,0:T(8,128)(2,1)S(1)}, u32[]{:S(2)}, u32[]{:S(2)}) collective-permute-start(bf16[16,2048]{1,0:T(8,128)(2,1)S(1)} %fusion.34), channel_id=1, source_target_pairs={{0,8},{1,9},{2,10},{3,11},{4,12},{5,13},{6,14},{7,15},{8,0},{9,1},... | collective-permute-start | bytes 196616 | tf_op jit(solution)/shard_map/ppermute | solution.py:22
  173.6 4.7 %collective-permute-done.13 = bf16[16,2048]{1,0:T(8,128)(2,1)S(1)} collective-permute-done((bf16[16,2048]{1,0:T(8,128)(2,1)S(1)}, bf16[16,2048]{1,0:T(8,128)(2,1)S(1)}, u32[]{:S(2)}, u32[]{:S(2)}) %collective-permute-start.13) | collective-permute-done | bytes 65568 | tf_op jit(solution)/shard_map/ppermute | solution.py:22
  (114 shorter events, 28.9 us)
Async XLA Ops:
  0.0 118.6 %copy-start = (bf16[256,2048]{1,0:T(8,128)(2,1)S(1)}, bf16[256,2048]{1,0:T(8,128)(2,1)}, u32[]{:S(2)}) copy-start(bf16[256,2048]{1,0:T(8,128)(2,1)} %param.26) | copy-start | bytes 3145732
  0.0 14.8 %copy-start.1 = (bf16[16,4,2048]{2,1,0:T(4,128)(2,1)S(1)}, bf16[16,4,2048]{2,1,0:T(4,128)(2,1)}, u32[]{:S(2)}) copy-start(bf16[16,4,2048]{2,1,0:T(4,128)(2,1)} %param.17) | copy-start | bytes 786436
  0.0 19.2 %collective-permute-start = (bf16[16,2048]{1,0:T(8,128)(2,1)}, bf16[16,2048]{1,0:T(8,128)(2,1)S(1)}, u32[]{:S(2)}, u32[]{:S(2)}) collective-permute-start(bf16[16,2048]{1,0:T(8,128)(2,1)} %param.14), channel_id=1, source_target_pairs={{0,8},{1,9},{2,10},{3,11},{4,12},{5,13},{6,14},{7,15},{8,0},{9,1},... | collective-permute-start | bytes 196616 | tf_op jit(solution)/shard_map/ppermute | solution.py:22
  14.8 4.5 %copy-start.3 = (bf16[16,2048]{1,0:T(8,128)(2,1)S(1)}, bf16[16,2048]{1,0:T(8,128)(2,1)}, u32[]{:S(2)}) copy-start(bf16[16,2048]{1,0:T(8,128)(2,1)} %param.14) | copy-start | bytes 196612
  19.3 10.9 %collective-permute-start.1 = (bf16[2,16,2048]{2,1,0:T(8,128)(2,1)S(1)}, bf16[2,16,2048]{2,1,0:T(8,128)(2,1)S(1)}, u32[]{:S(2)}, u32[]{:S(2)}) collective-permute-start(bf16[2,16,2048]{2,1,0:T(8,128)(2,1)S(1)} %maximum_select_fusion.3), channel_id=1, source_target_pairs={{0,4},{1,5},{2,6},{3,7},{4,0},{5,1},{6,2},{7,3},{8,12},{9,13},{10,... | collective-permute-start | bytes 393224 | tf_op jit(solution)/shard_map/ppermute | solution.py:22
  30.2 9.2 %collective-permute-start.2 = (bf16[2,2,16,2048]{3,2,0,1:T(8,128)(2,1)S(1)}, bf16[2,2,16,2048]{3,2,0,1:T(8,128)(2,1)S(1)}, u32[]{:S(2)}, u32[]{:S(2)}) collective-permute-start(bf16[2,2,16,2048]{3,2,0,1:T(8,128)(2,1)S(1)} %maximum_select_fusion.2), channel_id=1, source_target_pairs={{0,2},{1,3},{2,0},{3,1},{4,6},{5,7},{6,4},{7,5},{8,10},{9,11},{10,... | collective-permute-start | bytes 786440 | tf_op jit(solution)/shard_map/ppermute | solution.py:22
  39.4 4.9 %collective-permute-start.3 = (bf16[2,2,2,16,2048]{4,3,0,1,2:T(8,128)(2,1)S(1)}, bf16[2,2,2,16,2048]{4,3,0,1,2:T(8,128)(2,1)S(1)}, u32[]{:S(2)}, u32[]{:S(2)}) collective-permute-start(bf16[2,2,2,16,2048]{4,3,0,1,2:T(8,128)(2,1)S(1)} %maximum_select_fusion.1), channel_id=1, source_target_pairs={{0,1},{1,0},{2,3},{3,2},{4,5},{5,4},{6,7},{7,6},{8,9},{9,8},{10,11... | collective-permute-start | bytes 1572872 | tf_op jit(solution)/shard_map/ppermute | solution.py:22
  42.9 1.5 copy-start.6
  42.9 1.5 copy-start.7
  47.7 12.9 %all-to-all-start = ((bf16[16,256,16]{1,2,0:T(8,128)(2,1)}), bf16[16,256,16]{1,2,0:T(8,128)(2,1)S(1)}, u32[]{:S(2)}, u32[]{:S(2)}) async-start(bf16[16,256,16]{1,2,0:T(8,128)(2,1)} %copy.136), calls=%async_computation | async-start | bytes 262144 | tf_op jit(solution)/shard_map/all_to_all | solution.py:101
  51.3 13.3 %copy-start.4 = (f32[256]{0:T(256)S(1)}, f32[256]{0:T(256)}, u32[]{:S(2)}) copy-start(f32[256]{0:T(256)} %param.19) | copy-start | bytes 3076
  60.7 3.9 %collective-permute-start.4 = (bf16[3,512]{1,0:T(4,128)(2,1)S(1)}, bf16[3,512]{1,0:T(4,128)(2,1)S(1)}, u32[]{:S(2)}, u32[]{:S(2)}) collective-permute-start(bf16[3,512]{1,0:T(4,128)(2,1)S(1)} %pad_maximum_fusion.10), channel_id=1, source_target_pairs={{0,16},{16,32},{32,48},{48,64},{64,80},{80,96},{96,112},{112,128},... | collective-permute-start | bytes 9224 | tf_op jit(solution)/shard_map/ppermute | solution.py:17
  65.4 6.0 %collective-permute-start.5 = (f32[4,65,128]{2,1,0:T(8,128)S(1)}, f32[4,65,128]{2,1,0:T(8,128)S(1)}, u32[]{:S(2)}, u32[]{:S(2)}) collective-permute-start(f32[4,65,128]{2,1,0:T(8,128)S(1)} %pad_maximum_fusion.5), channel_id=1, source_target_pairs={{0,16},{16,32},{32,48},{48,64},{64,80},{80,96},{96,112},{112,128},... | collective-permute-start | bytes 399368 | tf_op jit(solution)/shard_map/ppermute | solution.py:17
  71.7 46.2 %copy-start.8 = (f32[4]{0:T(128)S(1)}, f32[4]{0:T(128)}, u32[]{:S(2)}) copy-start(f32[4]{0:T(128)} %param.24) | copy-start | bytes 52
  71.7 7.7 %collective-permute-start.6 = (f32[4,65,128]{2,1,0:T(8,128)S(1)}, f32[4,65,128]{2,1,0:T(8,128)S(1)}, u32[]{:S(2)}, u32[]{:S(2)}) collective-permute-start(f32[4,65,128]{2,1,0:T(8,128)S(1)} %pad_maximum_fusion.6), channel_id=1, source_target_pairs={{0,32},{16,48},{32,64},{48,80},{64,96},{80,112},{96,128},{112,144}... | collective-permute-start | bytes 399368 | tf_op jit(solution)/shard_map/ppermute | solution.py:17
  79.8 11.9 %collective-permute-start.7 = (f32[4,65,128]{2,1,0:T(8,128)S(1)}, f32[4,65,128]{2,1,0:T(8,128)S(1)}, u32[]{:S(2)}, u32[]{:S(2)}) collective-permute-start(f32[4,65,128]{2,1,0:T(8,128)S(1)} %pad_maximum_fusion.7), channel_id=1, source_target_pairs={{0,64},{16,80},{32,96},{48,112},{64,128},{80,144},{96,160},{112,17... | collective-permute-start | bytes 399368 | tf_op jit(solution)/shard_map/ppermute | solution.py:17
  91.9 7.9 %collective-permute-start.8 = (f32[4,65,128]{2,1,0:T(8,128)S(1)}, f32[4,65,128]{2,1,0:T(8,128)S(1)}, u32[]{:S(2)}, u32[]{:S(2)}) collective-permute-start(f32[4,65,128]{2,1,0:T(8,128)S(1)} %pad_maximum_fusion.8), channel_id=1, source_target_pairs={{0,128},{16,144},{32,160},{48,176},{64,192},{80,208},{96,224},{112... | collective-permute-start | bytes 399368 | tf_op jit(solution)/shard_map/ppermute | solution.py:17
  100.1 18.5 %copy-start.5 = (f32[256]{0:T(256)S(1)}, f32[256]{0:T(256)}, u32[]{:S(2)}) copy-start(f32[256]{0:T(256)} %param.25) | copy-start | bytes 3076
  100.1 17.5 %collective-permute-start.9 = (f32[4,65,128]{2,1,0:T(8,128)S(1)}, f32[4,65,128]{2,1,0:T(8,128)S(1)}, u32[]{:S(2)}, u32[]{:S(2)}) collective-permute-start(f32[4,65,128]{2,1,0:T(8,128)S(1)} %pad_maximum_fusion.9), channel_id=1, source_target_pairs={{0,256},{16,272},{32,288},{48,304},{64,320},{80,336},{96,352},{112... | collective-permute-start | bytes 399368 | tf_op jit(solution)/shard_map/ppermute | solution.py:17
  120.3 9.8 %collective-permute-start.10 = (bf16[2,2,2,16,2176]{4,3,2,1,0:T(8,128)(2,1)}, bf16[2,2,2,16,2176]{4,3,2,1,0:T(8,128)(2,1)}, u32[]{:S(2)}, u32[]{:S(2)}) collective-permute-start(bf16[2,2,2,16,2176]{4,3,2,1,0:T(8,128)(2,1)} %fusion.7), channel_id=1, source_target_pairs={{0,1},{1,0},{2,3},{3,2},{4,5},{5,4},{6,7},{7,6},{8,9},{9,8},{10,11... | collective-permute-start | bytes 1671176 | tf_op jit(solution)/shard_map/ppermute | solution.py:22
  131.3 9.8 %collective-permute-start.11 = (bf16[2,2,16,2176]{3,2,1,0:T(8,128)(2,1)S(1)}, bf16[2,2,16,2176]{3,2,1,0:T(8,128)(2,1)S(1)}, u32[]{:S(2)}, u32[]{:S(2)}) collective-permute-start(bf16[2,2,16,2176]{3,2,1,0:T(8,128)(2,1)S(1)} %fusion.14), channel_id=1, source_target_pairs={{0,2},{1,3},{2,0},{3,1},{4,6},{5,7},{6,4},{7,5},{8,10},{9,11},{10,... | collective-permute-start | bytes 835592 | tf_op jit(solution)/shard_map/ppermute | solution.py:22
  152.0 1.9 %copy-start.2 = (f32[2,2,16,2048]{2,1,3,0:T(2,128)}, f32[2,2,16,2048]{2,1,3,0:T(2,128)S(1)}, u32[]{:S(2)}) copy-start(f32[2,2,16,2048]{2,1,3,0:T(2,128)S(1)} %slice_multiply_fusion) | copy-start | bytes 1572868
  156.9 10.7 %collective-permute-start.12 = (bf16[2,16,2048]{2,1,0:T(8,128)(2,1)S(1)}, bf16[2,16,2048]{2,1,0:T(8,128)(2,1)}, u32[]{:S(2)}, u32[]{:S(2)}) collective-permute-start(bf16[2,16,2048]{2,1,0:T(8,128)(2,1)S(1)} %bitcast.152), channel_id=1, source_target_pairs={{0,4},{1,5},{2,6},{3,7},{4,0},{5,1},{6,2},{7,3},{8,12},{9,13},{10,... | collective-permute-start | bytes 393224 | tf_op jit(solution)/shard_map/ppermute | solution.py:22
  168.5 9.8 %collective-permute-start.13 = (bf16[16,2048]{1,0:T(8,128)(2,1)S(1)}, bf16[16,2048]{1,0:T(8,128)(2,1)S(1)}, u32[]{:S(2)}, u32[]{:S(2)}) collective-permute-start(bf16[16,2048]{1,0:T(8,128)(2,1)S(1)} %fusion.34), channel_id=1, source_target_pairs={{0,8},{1,9},{2,10},{3,11},{4,12},{5,13},{6,14},{7,15},{8,0},{9,1},... | collective-permute-start | bytes 196616 | tf_op jit(solution)/shard_map/ppermute | solution.py:22

commit v3 on v1

--- a/solution.py
+++ b/solution.py
@@ -30,23 +30,17 @@
         other = swapped(held, axis, bit)
         low = (place & bit) == 0
         held = jnp.where(low, jnp.stack([held, other]), jnp.stack([other, held]))
-    order = tuple(reversed(range(len(bits)))) + tuple(range(len(bits), held.ndim))
-    held = jnp.transpose(held, order)
-    return held.reshape((peers * rows.shape[0],) + rows.shape[1:])
-
-
-def scatter_sum(full, axis, bits):
+    return held
+
+
+def halve(held, axis, bits):
     place = lax.axis_index(axis)
-    peers = lax.axis_size(axis)
-    per = full.shape[0] // peers
-    held = full.reshape((2,) * len(bits) + (per,) + full.shape[1:])
     for bit in bits:
-        at = held.ndim - len(full.shape) - 1
         mine = (place // bit) % 2
-        keep = lax.dynamic_index_in_dim(held, mine, at, keepdims=False)
-        give = lax.dynamic_index_in_dim(held, 1 - mine, at, keepdims=False)
-        held = keep + swapped(give, axis, bit)
-    return held.reshape((per,) + full.shape[1:])
+        keep = lax.dynamic_index_in_dim(held, mine, 0, keepdims=False)
+        give = lax.dynamic_index_in_dim(held, 1 - mine, 0, keepdims=False)
+        held = keep + swapped(give.astype(jnp.bfloat16), axis, bit).astype(jnp.float32)
+    return held
 
 
 def causal_conv(prior_rows, raw_rows, conv_weight, conv_bias):
@@ -81,23 +75,31 @@
     per_group_dev = (HEADS // GROUPS) // heads_dev
     group_index = lax.axis_index("tp") // per_group_dev
     zx_weight = in_weight.reshape(in_weight.shape[0], 2 * inner_dev)
-    shard_rows = gather_rows(hidden, "tp", tp_bits)
-    length = shard_rows.shape[0]
+    stacked = gather_rows(hidden, "tp", tp_bits)
+    levels = len(tp_bits)
+    length = tp_size * hidden.shape[0]
+    flipped = tuple(reversed(range(levels)))
+
+    def in_order(rows):
+        rows = jnp.transpose(rows, flipped + tuple(range(levels, rows.ndim)))
+        return rows.reshape((length,) + rows.shape[levels + 1 :])
+
     projected = jnp.concatenate(
         [
-            jnp.dot(shard_rows, zx_weight, preferred_element_type=jnp.float32),
-            jnp.dot(shard_rows, step_weight, preferred_element_type=jnp.float32),
+            in_order(jnp.einsum("...d,dn->...n", stacked, zx_weight, preferred_element_type=jnp.float32)),
+            in_order(jnp.einsum("...d,dn->...n", stacked, step_weight, preferred_element_type=jnp.float32)),
         ],
         axis=1,
     ).astype(jnp.bfloat16)
     gate_raw = projected[:, :inner_dev]
     inner_raw = projected[:, inner_dev : 2 * inner_dev]
     step_raw = projected[:, 2 * inner_dev :]
-    dest_groups = [q // per_group_dev for q in range(tp_size)]
-    spread = jnp.take(group_weight, jnp.array(dest_groups), axis=1)
     own_maps = jnp.einsum(
-        "td,sqd->qts", shard_rows, spread, preferred_element_type=jnp.float32
+        "...d,sgd->...gs", stacked, group_weight, preferred_element_type=jnp.float32
     ).astype(jnp.bfloat16)
+    own_maps = jnp.moveaxis(in_order(own_maps), 1, 0)
+    own_maps = jnp.broadcast_to(own_maps[:, None], (GROUPS, per_group_dev) + own_maps.shape[1:])
+    own_maps = own_maps.reshape((tp_size,) + own_maps.shape[2:])
     got_maps = lax.all_to_all(own_maps, "tp", 0, 0, tiled=True)
     map_part = jnp.transpose(got_maps, (1, 0, 2)).reshape(length, group_cols)
     border_rows = KERNEL - 1
@@ -182,11 +184,20 @@
     while bit < per_group_dev:
         total = total + swapped(total, "tp", bit)
         bit *= 2
+    scaled = (gated * norm_gain[None, :]).astype(jnp.bfloat16)
+    scaled = scaled.reshape((2,) * levels + (length // tp_size, inner_dev))
+    scaled = jnp.transpose(scaled, flipped + (levels, levels + 1))
+    partial = jnp.einsum("...c,cn->...n", scaled, out_weight, preferred_element_type=jnp.float32)
+    within_bits = [bit for bit in tp_bits if bit < per_group_dev]
+    across_bits = [bit for bit in tp_bits if bit >= per_group_dev]
+    held = halve(partial, "tp", within_bits)
     inverse = lax.rsqrt(total / (HEADS * HEAD_DIM // GROUPS) + 1e-05)
-    normed = (gated * inverse[:, None] * norm_gain[None, :]).astype(jnp.bfloat16)
-    mixed = scatter_sum(
-        jnp.dot(normed, out_weight, preferred_element_type=jnp.float32), "tp", tp_bits
-    )
+    inverse = jnp.transpose(inverse.reshape((2,) * levels + (length // tp_size,)), flipped + (levels,))
+    for bit in within_bits:
+        inverse = lax.dynamic_index_in_dim(inverse, (lax.axis_index("tp") // bit) % 2, 0, keepdims=False)
+    held = held * inverse[..., None]
+    held = halve(held, "tp", across_bits)
+    mixed = held
     return mixed.astype(jnp.bfloat16)
 
 

time: 188 us -> 165 us (0.88)
  waiting for transfers between devices: 77.9 us -> 48.7 us
  starting transfers between devices: 85.2 us -> 90.8 us
  local copies, waits for them, and re-layouts: 13.6 us -> 10.9 us
    ppermute x10, waiting for transfers between devices: 58.8 us -> 29.9 us  [swapped(): return lax.ppermute(x, axis, [(i, i ^ bit) for i in range(peers)])]
    ppermute x10, starting transfers between devices: 38.2 us -> 42.7 us  [swapped(): return lax.ppermute(x, axis, [(i, i ^ bit) for i in range(peers)])]
    gather x1 -> x0, local copies, waits for them, and re-layouts: 3.55 us -> none  [body(): spread = jnp.take(group_weight, jnp.array(dest_groups), axis=1)]
    reshape x1 -> x4, local copies, waits for them, and re-layouts: 0.01 us -> 3.53 us  [the longest x1 3.19 us: body(): zx_weight = in_weight.reshape(in_weight.shape[0], 2 * inner_dev)]
    unnamed x26 -> x27, local copies, waits for them, and re-layouts: 4.53 us -> 1.09 us
  transfers between devices with their start and end apart: 17 -> 17, of which waited for: 16 -> 14; matrix products, arithmetic and copies ran while one was open for 5% -> 6% of each run, Pallas kernels for 0% -> 0%
where the time goes in v3:
time: 165 us; the launch traced here: 164 us
  starting transfers between devices  90.8 us (55%)
  waiting for transfers between devices  48.7 us (30%)
  local copies, waits for them, and re-layouts  10.9 us (7%)
  other arithmetic  7.02 us (4%)
  matrix products  5.89 us (4%)
    ppermute x6, starting transfers between devices, shifted(): return lax.ppermute(x, axis, pairs)  44.1 us
    ppermute x10, starting transfers between devices, swapped(): return lax.ppermute(x, axis, [(i, i ^ bit) for i in range(peers)])  42.7 us
    ppermute x10, waiting for transfers between devices, swapped(): return lax.ppermute(x, axis, [(i, i ^ bit) for i in range(peers)])  29.9 us
    ppermute x6, waiting for transfers between devices, shifted(): return lax.ppermute(x, axis, pairs)  10.5 us
    all_to_all x1, waiting for transfers between devices, body(): got_maps = lax.all_to_all(own_maps, 'tp', 0, 0, tiled=True)  8.23 us
    all_to_all x1, starting transfers between devices, body(): got_maps = lax.all_to_all(own_maps, 'tp', 0, 0, tiled=True)  4.03 us
  transfers between devices with their start and end apart: 17, of which 14 were waited for; matrix products, arithmetic and copies ran while one was open for 6% of the time, Pallas kernels for 0%

profile of v3, /device:TPU:1, one launch (start us, length us, event | category | flops | bytes accessed | tf_op | source)
XLA Modules:
  0.0 164.1 jit_solution(3025558798690898863)
XLA Ops:
  0.0 8.4 %collective-permute-start = (bf16[16,2048]{1,0:T(8,128)(2,1)}, bf16[16,2048]{1,0:T(8,128)(2,1)S(1)}, u32[]{:S(2)}, u32[]{:S(2)}) collective-permute-start(bf16[16,2048]{1,0:T(8,128)(2,1)} %param.13), channel_id=1, source_target_pairs={{0,8},{1,9},{2,10},{3,11},{4,12},{5,13},{6,14},{7,15},{8,0},{9,1},... | collective-permute-start | bytes 196616 | tf_op jit(solution)/shard_map/ppermute | solution.py:22
  9.9 3.2 %reshape.614 = bf16[2048,512,1,1,1,1]{1,0,2,3,4,5:T(8,128)(2,1)S(1)} reshape(bf16[2048,2,256]{2,1,0:T(2,128)(2,1)} %param.14) | data formatting | bytes 4194304 | tf_op jit(solution)/shard_map/reshape | solution.py:77
  13.9 2.4 %collective-permute-start.1 = (bf16[2,16,2048]{2,1,0:T(8,128)(2,1)S(1)}, bf16[2,16,2048]{2,1,0:T(8,128)(2,1)S(1)}, u32[]{:S(2)}, u32[]{:S(2)}) collective-permute-start(bf16[2,16,2048]{2,1,0:T(8,128)(2,1)S(1)} %maximum_select_fusion.6), channel_id=1, source_target_pairs={{0,4},{1,5},{2,6},{3,7},{4,0},{5,1},{6,2},{7,3},{8,12},{9,13},{10,... | collective-permute-start | bytes 393224 | tf_op jit(solution)/shard_map/ppermute | solution.py:22
  16.4 7.7 %collective-permute-done.1 = bf16[2,16,2048]{2,1,0:T(8,128)(2,1)S(1)} collective-permute-done((bf16[2,16,2048]{2,1,0:T(8,128)(2,1)S(1)}, bf16[2,16,2048]{2,1,0:T(8,128)(2,1)S(1)}, u32[]{:S(2)}, u32[]{:S(2)}) %collective-permute-start.1) | collective-permute-done | bytes 131104 | tf_op jit(solution)/shard_map/ppermute | solution.py:22
  24.1 1.9 %collective-permute-start.2 = (bf16[2,2,16,2048]{3,2,1,0:T(8,128)(2,1)S(1)}, bf16[2,2,16,2048]{3,2,1,0:T(8,128)(2,1)S(1)}, u32[]{:S(2)}, u32[]{:S(2)}) collective-permute-start(bf16[2,2,16,2048]{3,2,1,0:T(8,128)(2,1)S(1)} %maximum_select_fusion.4), channel_id=1, source_target_pairs={{0,2},{1,3},{2,0},{3,1},{4,6},{5,7},{6,4},{7,5},{8,10},{9,11},{10,... | collective-permute-start | bytes 786440 | tf_op jit(solution)/shard_map/ppermute | solution.py:22
  26.0 6.4 %collective-permute-done.2 = bf16[2,2,16,2048]{3,2,1,0:T(8,128)(2,1)S(1)} collective-permute-done((bf16[2,2,16,2048]{3,2,1,0:T(8,128)(2,1)S(1)}, bf16[2,2,16,2048]{3,2,1,0:T(8,128)(2,1)S(1)}, u32[]{:S(2)}, u32[]{:S(2)}) %collective-permute-start.2) | collective-permute-done | bytes 262176 | tf_op jit(solution)/shard_map/ppermute | solution.py:22
  32.5 4.2 %collective-permute-start.3 = (bf16[2,2,2,16,2048]{4,3,2,1,0:T(8,128)(2,1)S(1)}, bf16[2,2,2,16,2048]{4,3,2,1,0:T(8,128)(2,1)S(1)}, u32[]{:S(2)}, u32[]{:S(2)}) collective-permute-start(bf16[2,2,2,16,2048]{4,3,2,1,0:T(8,128)(2,1)S(1)} %maximum_select_fusion.2), channel_id=1, source_target_pairs={{0,1},{1,0},{2,3},{3,2},{4,5},{5,4},{6,7},{7,6},{8,9},{9,8},{10,11... | collective-permute-start | bytes 1572872 | tf_op jit(solution)/shard_map/ppermute | solution.py:22
  38.2 1.3 fusion.13
  39.8 1.2 reduce-window.6
  41.1 2.3 %fusion.9 = bf16[2,2,2,2,16,512]{5,4,0,1,2,3:T(8,128)(2,1)S(1)} fusion(bf16[2048,512,1,1,1,1]{1,0,2,3,4,5:T(8,128)(2,1)S(1)} %reshape.614, bf16[1,2,2,2,16,2048]{5,4,3,2,1,0:T(8,128)(2,1)} %bitcast.179, bf16[1,2,2,2,16,2048]{5,4,3,2,1,0:T(8,128)(2,1)} %copy-done.3, pred[]{:T(512)S(6)} %eq.19), kind=kOutput, calls=%fused_computation.10 | convolution fusion | flops 538574848 | bytes 3407873 | tf_op jit(solution)/shard_map/...d,dn->...n/dot_general | solution.py:89
  45.4 4.0 %all-to-all-start = ((bf16[16,256,16]{1,2,0:T(8,128)(2,1)}), bf16[16,256,16]{1,2,0:T(8,128)(2,1)S(1)}, u32[]{:S(2)}, u32[]{:S(2)}) async-start(bf16[16,256,16]{1,2,0:T(8,128)(2,1)} %bitcast.20), calls=%async_computation | async-start | bytes 262144 | tf_op jit(solution)/shard_map/all_to_all | solution.py:103
  50.1 8.2 %all-to-all-done = bf16[16,256,16]{1,2,0:T(8,128)(2,1)S(1)} async-done(((bf16[16,256,16]{1,2,0:T(8,128)(2,1)}), bf16[16,256,16]{1,2,0:T(8,128)(2,1)S(1)}, u32[]{:S(2)}, u32[]{:S(2)}) %all-to-all-start) | async-done | bytes 131104 | tf_op jit(solution)/shard_map/all_to_all | solution.py:103
  58.5 3.8 %collective-permute-start.4 = (bf16[3,512]{1,0:T(4,128)(2,1)S(1)}, bf16[3,512]{1,0:T(4,128)(2,1)S(1)}, u32[]{:S(2)}, u32[]{:S(2)}) collective-permute-start(bf16[3,512]{1,0:T(4,128)(2,1)S(1)} %pad_maximum_fusion.5), channel_id=1, source_target_pairs={{0,16},{16,32},{32,48},{48,64},{64,80},{80,96},{96,112},{112,128},... | collective-permute-start | bytes 9224 | tf_op jit(solution)/shard_map/ppermute | solution.py:17
  64.0 3.6 %collective-permute-start.5 = (f32[4,65,128]{2,1,0:T(8,128)S(1)}, f32[4,65,128]{2,1,0:T(8,128)S(1)}, u32[]{:S(2)}, u32[]{:S(2)}) collective-permute-start(f32[4,65,128]{2,1,0:T(8,128)S(1)} %pad_maximum_fusion), channel_id=1, source_target_pairs={{0,16},{16,32},{32,48},{48,64},{64,80},{80,96},{96,112},{112,128},... | collective-permute-start | bytes 399368 | tf_op jit(solution)/shard_map/ppermute | solution.py:17
  67.6 2.3 %collective-permute-done.5 = f32[4,65,128]{2,1,0:T(8,128)S(1)} collective-permute-done((f32[4,65,128]{2,1,0:T(8,128)S(1)}, f32[4,65,128]{2,1,0:T(8,128)S(1)}, u32[]{:S(2)}, u32[]{:S(2)}) %collective-permute-start.5) | collective-permute-done | bytes 133152 | tf_op jit(solution)/shard_map/ppermute | solution.py:17
  70.3 5.6 %collective-permute-start.6 = (f32[4,65,128]{2,1,0:T(8,128)S(1)}, f32[4,65,128]{2,1,0:T(8,128)S(1)}, u32[]{:S(2)}, u32[]{:S(2)}) collective-permute-start(f32[4,65,128]{2,1,0:T(8,128)S(1)} %pad_maximum_fusion.1), channel_id=1, source_target_pairs={{0,32},{16,48},{32,64},{48,80},{64,96},{80,112},{96,128},{112,144}... | collective-permute-start | bytes 399368 | tf_op jit(solution)/shard_map/ppermute | solution.py:17
  76.0 2.0 %collective-permute-done.6 = f32[4,65,128]{2,1,0:T(8,128)S(1)} collective-permute-done((f32[4,65,128]{2,1,0:T(8,128)S(1)}, f32[4,65,128]{2,1,0:T(8,128)S(1)}, u32[]{:S(2)}, u32[]{:S(2)}) %collective-permute-start.6) | collective-permute-done | bytes 133152 | tf_op jit(solution)/shard_map/ppermute | solution.py:17
  78.3 9.8 %collective-permute-start.7 = (f32[4,65,128]{2,1,0:T(8,128)S(1)}, f32[4,65,128]{2,1,0:T(8,128)S(1)}, u32[]{:S(2)}, u32[]{:S(2)}) collective-permute-start(f32[4,65,128]{2,1,0:T(8,128)S(1)} %pad_maximum_fusion.2), channel_id=1, source_target_pairs={{0,64},{16,80},{32,96},{48,112},{64,128},{80,144},{96,160},{112,17... | collective-permute-start | bytes 399368 | tf_op jit(solution)/shard_map/ppermute | solution.py:17
  88.1 2.1 %collective-permute-done.7 = f32[4,65,128]{2,1,0:T(8,128)S(1)} collective-permute-done((f32[4,65,128]{2,1,0:T(8,128)S(1)}, f32[4,65,128]{2,1,0:T(8,128)S(1)}, u32[]{:S(2)}, u32[]{:S(2)}) %collective-permute-start.7) | collective-permute-done | bytes 133152 | tf_op jit(solution)/shard_map/ppermute | solution.py:17
  90.5 5.8 %collective-permute-start.8 = (f32[4,65,128]{2,1,0:T(8,128)S(1)}, f32[4,65,128]{2,1,0:T(8,128)S(1)}, u32[]{:S(2)}, u32[]{:S(2)}) collective-permute-start(f32[4,65,128]{2,1,0:T(8,128)S(1)} %pad_maximum_fusion.3), channel_id=1, source_target_pairs={{0,128},{16,144},{32,160},{48,176},{64,192},{80,208},{96,224},{112... | collective-permute-start | bytes 399368 | tf_op jit(solution)/shard_map/ppermute | solution.py:17
  96.6 1.8 %collective-permute-done.8 = f32[4,65,128]{2,1,0:T(8,128)S(1)} collective-permute-done((f32[4,65,128]{2,1,0:T(8,128)S(1)}, f32[4,65,128]{2,1,0:T(8,128)S(1)}, u32[]{:S(2)}, u32[]{:S(2)}) %collective-permute-start.8) | collective-permute-done | bytes 133152 | tf_op jit(solution)/shard_map/ppermute | solution.py:17
  98.7 15.4 %collective-permute-start.9 = (f32[4,65,128]{2,1,0:T(8,128)S(1)}, f32[4,65,128]{2,1,0:T(8,128)S(1)}, u32[]{:S(2)}, u32[]{:S(2)}) collective-permute-start(f32[4,65,128]{2,1,0:T(8,128)S(1)} %pad_maximum_fusion.4), channel_id=1, source_target_pairs={{0,256},{16,272},{32,288},{48,304},{64,320},{80,336},{96,352},{112... | collective-permute-start | bytes 399368 | tf_op jit(solution)/shard_map/ppermute | solution.py:17
  114.2 1.9 %collective-permute-done.9 = f32[4,65,128]{2,1,0:T(8,128)S(1)} collective-permute-done((f32[4,65,128]{2,1,0:T(8,128)S(1)}, f32[4,65,128]{2,1,0:T(8,128)S(1)}, u32[]{:S(2)}, u32[]{:S(2)}) %collective-permute-start.9) | collective-permute-done | bytes 133152 | tf_op jit(solution)/shard_map/ppermute | solution.py:17
  118.5 7.9 %collective-permute-start.10 = (bf16[2,2,2,16,2048]{4,3,2,1,0:T(8,128)(2,1)}, bf16[2,2,2,16,2048]{4,3,2,1,0:T(8,128)(2,1)}, u32[]{:S(2)}, u32[]{:S(2)}) collective-permute-start(bf16[2,2,2,16,2048]{4,3,2,1,0:T(8,128)(2,1)} %fusion.17), channel_id=1, source_target_pairs={{0,1},{1,0},{2,3},{3,2},{4,5},{5,4},{6,7},{7,6},{8,9},{9,8},{10,11... | collective-permute-start | bytes 1572872 | tf_op jit(solution)/shard_map/ppermute | solution.py:22
  126.4 1.9 %collective-permute-start.12 = (f32[256]{0:T(256)S(1)}, f32[256]{0:T(256)S(1)}, u32[]{:S(2)}, u32[]{:S(2)}) collective-permute-start(f32[256]{0:T(256)S(1)} %get-tuple-element.43), channel_id=1, source_target_pairs={{0,1},{1,0},{2,3},{3,2},{4,5},{5,4},{6,7},{7,6},{8,9},{9,8},{10,11... | collective-permute-start | bytes 3080 | tf_op jit(solution)/shard_map/ppermute | solution.py:22
  129.5 1.9 %collective-permute-start.13 = (f32[256]{0:T(256)S(1)}, f32[256]{0:T(256)S(1)}, u32[]{:S(2)}, u32[]{:S(2)}) collective-permute-start(f32[256]{0:T(256)S(1)} %add.205), channel_id=1, source_target_pairs={{0,2},{1,3},{2,0},{3,1},{4,6},{5,7},{6,4},{7,5},{8,10},{9,11},{10,... | collective-permute-start | bytes 3080 | tf_op jit(solution)/shard_map/ppermute | solution.py:22
  133.6 3.4 %collective-permute-start.11 = (bf16[2,2,16,2048]{3,2,1,0:T(8,128)(2,1)S(1)}, bf16[2,2,16,2048]{3,2,1,0:T(8,128)(2,1)S(1)}, u32[]{:S(2)}, u32[]{:S(2)}) collective-permute-start(bf16[2,2,16,2048]{3,2,1,0:T(8,128)(2,1)S(1)} %fusion.29), channel_id=1, source_target_pairs={{0,2},{1,3},{2,0},{3,1},{4,6},{5,7},{6,4},{7,5},{8,10},{9,11},{10,... | collective-permute-start | bytes 786440 | tf_op jit(solution)/shard_map/ppermute | solution.py:22
  137.1 5.8 %collective-permute-done.11 = bf16[2,2,16,2048]{3,2,1,0:T(8,128)(2,1)S(1)} collective-permute-done((bf16[2,2,16,2048]{3,2,1,0:T(8,128)(2,1)S(1)}, bf16[2,2,16,2048]{3,2,1,0:T(8,128)(2,1)S(1)}, u32[]{:S(2)}, u32[]{:S(2)}) %collective-permute-start.11) | collective-permute-done | bytes 262176 | tf_op jit(solution)/shard_map/ppermute | solution.py:22
  144.1 2.9 %collective-permute-start.14 = (bf16[2,16,2048]{2,1,0:T(8,128)(2,1)S(1)}, bf16[2,16,2048]{2,1,0:T(8,128)(2,1)S(1)}, u32[]{:S(2)}, u32[]{:S(2)}) collective-permute-start(bf16[2,16,2048]{2,1,0:T(8,128)(2,1)S(1)} %fusion.39), channel_id=1, source_target_pairs={{0,4},{1,5},{2,6},{3,7},{4,0},{5,1},{6,2},{7,3},{8,12},{9,13},{10,... | collective-permute-start | bytes 393224 | tf_op jit(solution)/shard_map/ppermute | solution.py:22
  147.0 6.9 %collective-permute-done.14 = bf16[2,16,2048]{2,1,0:T(8,128)(2,1)S(1)} collective-permute-done((bf16[2,16,2048]{2,1,0:T(8,128)(2,1)S(1)}, bf16[2,16,2048]{2,1,0:T(8,128)(2,1)S(1)}, u32[]{:S(2)}, u32[]{:S(2)}) %collective-permute-start.14) | collective-permute-done | bytes 131104 | tf_op jit(solution)/shard_map/ppermute | solution.py:22
  154.0 7.8 %collective-permute-start.15 = (bf16[16,2048]{1,0:T(8,128)(2,1)S(1)}, bf16[16,2048]{1,0:T(8,128)(2,1)S(1)}, u32[]{:S(2)}, u32[]{:S(2)}) collective-permute-start(bf16[16,2048]{1,0:T(8,128)(2,1)S(1)} %fusion.46), channel_id=1, source_target_pairs={{0,8},{1,9},{2,10},{3,11},{4,12},{5,13},{6,14},{7,15},{8,0},{9,1},... | collective-permute-start | bytes 196616 | tf_op jit(solution)/shard_map/ppermute | solution.py:22
  161.8 1.6 collective-permute-done.15
  (124 shorter events, 17.8 us)
Async XLA Ops:
  0.0 117.2 %copy-start = (bf16[256,2048]{1,0:T(8,128)(2,1)S(1)}, bf16[256,2048]{1,0:T(8,128)(2,1)}, u32[]{:S(2)}) copy-start(bf16[256,2048]{1,0:T(8,128)(2,1)} %param.25) | copy-start | bytes 3145732
  0.0 13.9 %collective-permute-start = (bf16[16,2048]{1,0:T(8,128)(2,1)}, bf16[16,2048]{1,0:T(8,128)(2,1)S(1)}, u32[]{:S(2)}, u32[]{:S(2)}) collective-permute-start(bf16[16,2048]{1,0:T(8,128)(2,1)} %param.13), channel_id=1, source_target_pairs={{0,8},{1,9},{2,10},{3,11},{4,12},{5,13},{6,14},{7,15},{8,0},{9,1},... | collective-permute-start | bytes 196616 | tf_op jit(solution)/shard_map/ppermute | solution.py:22
  9.9 4.0 %copy-start.2 = (bf16[16,2048]{1,0:T(8,128)(2,1)S(1)}, bf16[16,2048]{1,0:T(8,128)(2,1)}, u32[]{:S(2)}) copy-start(bf16[16,2048]{1,0:T(8,128)(2,1)} %param.13) | copy-start | bytes 196612
  13.9 10.1 %collective-permute-start.1 = (bf16[2,16,2048]{2,1,0:T(8,128)(2,1)S(1)}, bf16[2,16,2048]{2,1,0:T(8,128)(2,1)S(1)}, u32[]{:S(2)}, u32[]{:S(2)}) collective-permute-start(bf16[2,16,2048]{2,1,0:T(8,128)(2,1)S(1)} %maximum_select_fusion.6), channel_id=1, source_target_pairs={{0,4},{1,5},{2,6},{3,7},{4,0},{5,1},{6,2},{7,3},{8,12},{9,13},{10,... | collective-permute-start | bytes 393224 | tf_op jit(solution)/shard_map/ppermute | solution.py:22
  16.3 21.8 %copy-start.11 = (bf16[2048,4]{0,1:T(4,128)(2,1)S(1)}, bf16[2048,4]{0,1:T(4,128)(2,1)}, u32[]{:S(2)}) copy-start(bf16[2048,4]{0,1:T(4,128)(2,1)} %param.15) | copy-start | bytes 49156
  24.1 8.4 %collective-permute-start.2 = (bf16[2,2,16,2048]{3,2,1,0:T(8,128)(2,1)S(1)}, bf16[2,2,16,2048]{3,2,1,0:T(8,128)(2,1)S(1)}, u32[]{:S(2)}, u32[]{:S(2)}) collective-permute-start(bf16[2,2,16,2048]{3,2,1,0:T(8,128)(2,1)S(1)} %maximum_select_fusion.4), channel_id=1, source_target_pairs={{0,2},{1,3},{2,0},{3,1},{4,6},{5,7},{6,4},{7,5},{8,10},{9,11},{10,... | collective-permute-start | bytes 786440 | tf_op jit(solution)/shard_map/ppermute | solution.py:22
  32.5 5.7 %collective-permute-start.3 = (bf16[2,2,2,16,2048]{4,3,2,1,0:T(8,128)(2,1)S(1)}, bf16[2,2,2,16,2048]{4,3,2,1,0:T(8,128)(2,1)S(1)}, u32[]{:S(2)}, u32[]{:S(2)}) collective-permute-start(bf16[2,2,2,16,2048]{4,3,2,1,0:T(8,128)(2,1)S(1)} %maximum_select_fusion.2), channel_id=1, source_target_pairs={{0,1},{1,0},{2,3},{3,2},{4,5},{5,4},{6,7},{7,6},{8,9},{9,8},{10,11... | collective-permute-start | bytes 1572872 | tf_op jit(solution)/shard_map/ppermute | solution.py:22
  37.7 1.8 %copy-start.3 = (bf16[1,2,2,2,16,2048]{5,4,3,2,1,0:T(8,128)(2,1)}, bf16[1,2,2,2,16,2048]{5,4,3,2,1,0:T(8,128)(2,1)S(1)}, u32[]{:S(2)}) copy-start(bf16[1,2,2,2,16,2048]{5,4,3,2,1,0:T(8,128)(2,1)S(1)} %maximum_select_fusion.1) | copy-start | bytes 1572868
  38.2 1.3 copy-start.8
  38.2 1.5 copy-start.5
  41.1 2.3 %copy-start.4 = (bf16[1,2,2,2,16,2048]{5,4,3,2,1,0:T(8,128)(2,1)S(1)}, bf16[1,2,2,2,16,2048]{5,4,3,2,1,0:T(8,128)(2,1)}, u32[]{:S(2)}) copy-start(bf16[1,2,2,2,16,2048]{5,4,3,2,1,0:T(8,128)(2,1)} %copy-done.3) | copy-start | bytes 1572868
  41.1 2.4 %copy-start.9 = (bf16[2,2,2,16,2048]{4,3,2,1,0:T(8,128)(2,1)S(1)}, bf16[2,2,2,16,2048]{4,3,2,1,0:T(8,128)(2,1)}, u32[]{:S(2)}) copy-start(bf16[2,2,2,16,2048]{4,3,2,1,0:T(8,128)(2,1)} %copy-done.8) | copy-start | bytes 1572868
  41.1 2.4 %copy-start.10 = (bf16[16,4,2048]{2,1,0:T(4,128)(2,1)S(1)}, bf16[16,4,2048]{2,1,0:T(4,128)(2,1)}, u32[]{:S(2)}) copy-start(bf16[16,4,2048]{2,1,0:T(4,128)(2,1)} %param.16) | copy-start | bytes 786436
  44.2 18.9 %copy-start.7 = (f32[256]{0:T(256)S(1)}, f32[256]{0:T(256)}, u32[]{:S(2)}) copy-start(f32[256]{0:T(256)} %param.18) | copy-start | bytes 3076
  45.4 12.9 %all-to-all-start = ((bf16[16,256,16]{1,2,0:T(8,128)(2,1)}), bf16[16,256,16]{1,2,0:T(8,128)(2,1)S(1)}, u32[]{:S(2)}, u32[]{:S(2)}) async-start(bf16[16,256,16]{1,2,0:T(8,128)(2,1)} %bitcast.20), calls=%async_computation | async-start | bytes 262144 | tf_op jit(solution)/shard_map/all_to_all | solution.py:103
  58.5 4.6 %collective-permute-start.4 = (bf16[3,512]{1,0:T(4,128)(2,1)S(1)}, bf16[3,512]{1,0:T(4,128)(2,1)S(1)}, u32[]{:S(2)}, u32[]{:S(2)}) collective-permute-start(bf16[3,512]{1,0:T(4,128)(2,1)S(1)} %pad_maximum_fusion.5), channel_id=1, source_target_pairs={{0,16},{16,32},{32,48},{48,64},{64,80},{80,96},{96,112},{112,128},... | collective-permute-start | bytes 9224 | tf_op jit(solution)/shard_map/ppermute | solution.py:17
  64.0 6.0 %collective-permute-start.5 = (f32[4,65,128]{2,1,0:T(8,128)S(1)}, f32[4,65,128]{2,1,0:T(8,128)S(1)}, u32[]{:S(2)}, u32[]{:S(2)}) collective-permute-start(f32[4,65,128]{2,1,0:T(8,128)S(1)} %pad_maximum_fusion), channel_id=1, source_target_pairs={{0,16},{16,32},{32,48},{48,64},{64,80},{80,96},{96,112},{112,128},... | collective-permute-start | bytes 399368 | tf_op jit(solution)/shard_map/ppermute | solution.py:17
  70.3 46.1 %copy-start.12 = (f32[4]{0:T(128)S(1)}, f32[4]{0:T(128)}, u32[]{:S(2)}) copy-start(f32[4]{0:T(128)} %param.23) | copy-start | bytes 52
  70.3 7.7 %collective-permute-start.6 = (f32[4,65,128]{2,1,0:T(8,128)S(1)}, f32[4,65,128]{2,1,0:T(8,128)S(1)}, u32[]{:S(2)}, u32[]{:S(2)}) collective-permute-start(f32[4,65,128]{2,1,0:T(8,128)S(1)} %pad_maximum_fusion.1), channel_id=1, source_target_pairs={{0,32},{16,48},{32,64},{48,80},{64,96},{80,112},{96,128},{112,144}... | collective-permute-start | bytes 399368 | tf_op jit(solution)/shard_map/ppermute | solution.py:17
  78.3 11.9 %collective-permute-start.7 = (f32[4,65,128]{2,1,0:T(8,128)S(1)}, f32[4,65,128]{2,1,0:T(8,128)S(1)}, u32[]{:S(2)}, u32[]{:S(2)}) collective-permute-start(f32[4,65,128]{2,1,0:T(8,128)S(1)} %pad_maximum_fusion.2), channel_id=1, source_target_pairs={{0,64},{16,80},{32,96},{48,112},{64,128},{80,144},{96,160},{112,17... | collective-permute-start | bytes 399368 | tf_op jit(solution)/shard_map/ppermute | solution.py:17
  90.5 7.9 %collective-permute-start.8 = (f32[4,65,128]{2,1,0:T(8,128)S(1)}, f32[4,65,128]{2,1,0:T(8,128)S(1)}, u32[]{:S(2)}, u32[]{:S(2)}) collective-permute-start(f32[4,65,128]{2,1,0:T(8,128)S(1)} %pad_maximum_fusion.3), channel_id=1, source_target_pairs={{0,128},{16,144},{32,160},{48,176},{64,192},{80,208},{96,224},{112... | collective-permute-start | bytes 399368 | tf_op jit(solution)/shard_map/ppermute | solution.py:17
  98.6 18.4 %copy-start.6 = (f32[256]{0:T(256)S(1)}, f32[256]{0:T(256)}, u32[]{:S(2)}) copy-start(f32[256]{0:T(256)} %param.24) | copy-start | bytes 3076
  98.7 17.5 %collective-permute-start.9 = (f32[4,65,128]{2,1,0:T(8,128)S(1)}, f32[4,65,128]{2,1,0:T(8,128)S(1)}, u32[]{:S(2)}, u32[]{:S(2)}) collective-permute-start(f32[4,65,128]{2,1,0:T(8,128)S(1)} %pad_maximum_fusion.4), channel_id=1, source_target_pairs={{0,256},{16,272},{32,288},{48,304},{64,320},{80,336},{96,352},{112... | collective-permute-start | bytes 399368 | tf_op jit(solution)/shard_map/ppermute | solution.py:17
  118.5 12.9 %collective-permute-start.10 = (bf16[2,2,2,16,2048]{4,3,2,1,0:T(8,128)(2,1)}, bf16[2,2,2,16,2048]{4,3,2,1,0:T(8,128)(2,1)}, u32[]{:S(2)}, u32[]{:S(2)}) collective-permute-start(bf16[2,2,2,16,2048]{4,3,2,1,0:T(8,128)(2,1)} %fusion.17), channel_id=1, source_target_pairs={{0,1},{1,0},{2,3},{3,2},{4,5},{5,4},{6,7},{7,6},{8,9},{9,8},{10,11... | collective-permute-start | bytes 1572872 | tf_op jit(solution)/shard_map/ppermute | solution.py:22
  126.4 3.1 %collective-permute-start.12 = (f32[256]{0:T(256)S(1)}, f32[256]{0:T(256)S(1)}, u32[]{:S(2)}, u32[]{:S(2)}) collective-permute-start(f32[256]{0:T(256)S(1)} %get-tuple-element.43), channel_id=1, source_target_pairs={{0,1},{1,0},{2,3},{3,2},{4,5},{5,4},{6,7},{7,6},{8,9},{9,8},{10,11... | collective-permute-start | bytes 3080 | tf_op jit(solution)/shard_map/ppermute | solution.py:22
  129.5 7.5 %collective-permute-start.13 = (f32[256]{0:T(256)S(1)}, f32[256]{0:T(256)S(1)}, u32[]{:S(2)}, u32[]{:S(2)}) collective-permute-start(f32[256]{0:T(256)S(1)} %add.205), channel_id=1, source_target_pairs={{0,2},{1,3},{2,0},{3,1},{4,6},{5,7},{6,4},{7,5},{8,10},{9,11},{10,... | collective-permute-start | bytes 3080 | tf_op jit(solution)/shard_map/ppermute | solution.py:22
  132.6 1.0 copy-start.1
  133.6 9.3 %collective-permute-start.11 = (bf16[2,2,16,2048]{3,2,1,0:T(8,128)(2,1)S(1)}, bf16[2,2,16,2048]{3,2,1,0:T(8,128)(2,1)S(1)}, u32[]{:S(2)}, u32[]{:S(2)}) collective-permute-start(bf16[2,2,16,2048]{3,2,1,0:T(8,128)(2,1)S(1)} %fusion.29), channel_id=1, source_target_pairs={{0,2},{1,3},{2,0},{3,1},{4,6},{5,7},{6,4},{7,5},{8,10},{9,11},{10,... | collective-permute-start | bytes 786440 | tf_op jit(solution)/shard_map/ppermute | solution.py:22
  144.1 9.9 %collective-permute-start.14 = (bf16[2,16,2048]{2,1,0:T(8,128)(2,1)S(1)}, bf16[2,16,2048]{2,1,0:T(8,128)(2,1)S(1)}, u32[]{:S(2)}, u32[]{:S(2)}) collective-permute-start(bf16[2,16,2048]{2,1,0:T(8,128)(2,1)S(1)} %fusion.39), channel_id=1, source_target_pairs={{0,4},{1,5},{2,6},{3,7},{4,0},{5,1},{6,2},{7,3},{8,12},{9,13},{10,... | collective-permute-start | bytes 393224 | tf_op jit(solution)/shard_map/ppermute | solution.py:22
  154.0 9.5 %collective-permute-start.15 = (bf16[16,2048]{1,0:T(8,128)(2,1)S(1)}, bf16[16,2048]{1,0:T(8,128)(2,1)S(1)}, u32[]{:S(2)}, u32[]{:S(2)}) collective-permute-start(bf16[16,2048]{1,0:T(8,128)(2,1)S(1)} %fusion.46), channel_id=1, source_target_pairs={{0,8},{1,9},{2,10},{3,11},{4,12},{5,13},{6,14},{7,15},{8,0},{9,1},... | collective-permute-start | bytes 196616 | tf_op jit(solution)/shard_map/ppermute | solution.py:22

commit v4 on v3

--- a/solution.py
+++ b/solution.py
@@ -94,22 +94,23 @@
     gate_raw = projected[:, :inner_dev]
     inner_raw = projected[:, inner_dev : 2 * inner_dev]
     step_raw = projected[:, 2 * inner_dev :]
-    own_maps = jnp.einsum(
-        "...d,sgd->...gs", stacked, group_weight, preferred_element_type=jnp.float32
-    ).astype(jnp.bfloat16)
-    own_maps = jnp.moveaxis(in_order(own_maps), 1, 0)
-    own_maps = jnp.broadcast_to(own_maps[:, None], (GROUPS, per_group_dev) + own_maps.shape[1:])
-    own_maps = own_maps.reshape((tp_size,) + own_maps.shape[2:])
-    got_maps = lax.all_to_all(own_maps, "tp", 0, 0, tiled=True)
-    map_part = jnp.transpose(got_maps, (1, 0, 2)).reshape(length, group_cols)
+    own_group = jnp.broadcast_to(
+        jnp.swapaxes(group_weight, 0, 1)[:, None], (GROUPS, per_group_dev) + group_weight[:, 0].shape
+    ).reshape((tp_size,) + group_weight[:, 0].shape)
+    map_weight = lax.all_to_all(own_group, "tp", 0, 0, tiled=True)
+    map_weight = map_weight.reshape((-1,) + map_weight.shape[2:])
+    map_part = in_order(
+        jnp.einsum("...d,sd->...s", stacked, map_weight, preferred_element_type=jnp.float32)
+    ).astype(jnp.bfloat16)
     border_rows = KERNEL - 1
-    prior = shifted(
-        jnp.concatenate([inner_raw[length - border_rows :], map_part[length - border_rows :]], axis=1),
-        "ctx",
-        1,
-    )
-    inner_prior = prior[:, :inner_dev]
-    map_prior = prior[:, inner_dev:]
+    last_rows = stacked[(1,) * levels][hidden.shape[0] - border_rows :]
+    before = shifted(last_rows, "ctx", 1)
+    inner_prior = jnp.dot(
+        before, zx_weight[:, inner_dev:], preferred_element_type=jnp.float32
+    ).astype(jnp.bfloat16)
+    map_prior = lax.dot_general(
+        before, map_weight, (((1,), (1,)), ((), ())), preferred_element_type=jnp.float32
+    ).astype(jnp.bfloat16)
     x_conv = causal_conv(inner_prior, inner_raw, conv_inner, inner_bias)
     own_taps = lax.dynamic_slice_in_dim(conv_group, group_index * group_cols, group_cols, 1)
     own_bias = lax.dynamic_slice_in_dim(group_bias, group_index * group_cols, group_cols, 0)

time: 165 us -> 180 us (1.091)
  local copies, waits for them, and re-layouts: 10.9 us -> 23 us
  starting transfers between devices: 90.8 us -> 84.6 us
  waiting for transfers between devices: 48.7 us -> 52.3 us
  matrix products: 5.89 us -> 9.06 us
  other arithmetic: 7.02 us -> 9.04 us
    ppermute x10, waiting for transfers between devices: 29.9 us -> 42.7 us  [swapped(): return lax.ppermute(x, axis, [(i, i ^ bit) for i in range(peers)])]
    all_to_all x1, waiting for transfers between devices: 8.23 us -> 0.01 us  [body(): map_weight = lax.all_to_all(own_group, 'tp', 0, 0, tiled=True)]
    ppermute x6, starting transfers between devices: 44.1 us -> 38.5 us  [shifted(): return lax.ppermute(x, axis, pairs)]
    ppermute x10, starting transfers between devices: 42.7 us -> 38.5 us  [swapped(): return lax.ppermute(x, axis, [(i, i ^ bit) for i in range(peers)])]
    unnamed x27 -> x60, local copies, waits for them, and re-layouts: 1.09 us -> 5.09 us
    all_to_all x1, starting transfers between devices: 4.03 us -> 7.68 us  [body(): map_weight = lax.all_to_all(own_group, 'tp', 0, 0, tiled=True)]
  transfers between devices with their start and end apart: 17 -> 17, of which waited for: 14 -> 11; matrix products, arithmetic and copies ran while one was open for 6% -> 18% of each run, Pallas kernels for 0% -> 0%
where the time goes in v4:
time: 180 us; the launch traced here: 179 us
  starting transfers between devices  84.6 us (47%)
  waiting for transfers between devices  52.3 us (29%)
  local copies, waits for them, and re-layouts  23 us (13%)
  matrix products  9.06 us (5%)
  other arithmetic  9.04 us (5%)
    ppermute x10, waiting for transfers between devices, swapped(): return lax.ppermute(x, axis, [(i, i ^ bit) for i in range(peers)])  42.7 us
    ppermute x6, starting transfers between devices, shifted(): return lax.ppermute(x, axis, pairs)  38.5 us
    ppermute x10, starting transfers between devices, swapped(): return lax.ppermute(x, axis, [(i, i ^ bit) for i in range(peers)])  38.5 us
    ppermute x6, waiting for transfers between devices, shifted(): return lax.ppermute(x, axis, pairs)  9.64 us
    all_to_all x1, starting transfers between devices, body(): map_weight = lax.all_to_all(own_group, 'tp', 0, 0, tiled=True)  7.68 us
    unnamed x60, local copies, waits for them, and re-layouts  5.09 us
    reshape x1, local copies, waits for them, and re-layouts, body(): zx_weight = in_weight.reshape(in_weight.shape[0], 2 * inner_dev)  4.41 us
  transfers between devices with their start and end apart: 17, of which 11 were waited for; matrix products, arithmetic and copies ran while one was open for 18% of the time, Pallas kernels for 0%

profile of v4, /device:TPU:1, one launch (start us, length us, event | category | flops | bytes accessed | tf_op | source)
XLA Modules:
  0.0 179.0 jit_solution(1537605189500640299)
XLA Ops:
  0.0 8.4 %collective-permute-start = (bf16[16,2048]{1,0:T(8,128)(2,1)}, bf16[16,2048]{1,0:T(8,128)(2,1)S(1)}, u32[]{:S(2)}, u32[]{:S(2)}) collective-permute-start(bf16[16,2048]{1,0:T(8,128)(2,1)} %param.13), channel_id=1, source_target_pairs={{0,8},{1,9},{2,10},{3,11},{4,12},{5,13},{6,14},{7,15},{8,0},{9,1},... | collective-permute-start | bytes 196616 | tf_op jit(solution)/shard_map/ppermute | solution.py:22
  10.6 7.7 %all-to-all-start = ((bf16[16,16,2048]{2,1,0:T(8,128)(2,1)}), bf16[16,16,2048]{2,1,0:T(8,128)(2,1)S(1)}, u32[]{:S(2)}, u32[]{:S(2)}) async-start(bf16[16,16,2048]{2,1,0:T(8,128)(2,1)} %bitcast.22), calls=%async_computation | async-start | bytes 2097152 | tf_op jit(solution)/shard_map/all_to_all | solution.py:100
  19.0 4.4 %reshape.612 = bf16[2048,512,1,1,1,1]{1,0,2,3,4,5:T(8,128)(2,1)} reshape(bf16[2048,2,256]{2,1,0:T(2,128)(2,1)} %param.14) | data formatting | bytes 4194304 | tf_op jit(solution)/shard_map/reshape | solution.py:77
  23.4 3.4 %copy.59 = bf16[256,8,2,256]{3,1,2,0:T(8,128)(2,1)} copy(bf16[256,8,2,256]{3,2,1,0:T(2,128)(2,1)} %bitcast.150) | data formatting | bytes 4194304
  28.1 4.2 %collective-permute-start.1 = (bf16[2,16,2048]{2,1,0:T(8,128)(2,1)S(1)}, bf16[2,16,2048]{2,1,0:T(8,128)(2,1)S(1)}, u32[]{:S(2)}, u32[]{:S(2)}) collective-permute-start(bf16[2,16,2048]{2,1,0:T(8,128)(2,1)S(1)} %maximum_select_fusion.6), channel_id=1, source_target_pairs={{0,4},{1,5},{2,6},{3,7},{4,0},{5,1},{6,2},{7,3},{8,12},{9,13},{10,... | collective-permute-start | bytes 393224 | tf_op jit(solution)/shard_map/ppermute | solution.py:22
  32.3 17.3 %collective-permute-done.1 = bf16[2,16,2048]{2,1,0:T(8,128)(2,1)S(1)} collective-permute-done((bf16[2,16,2048]{2,1,0:T(8,128)(2,1)S(1)}, bf16[2,16,2048]{2,1,0:T(8,128)(2,1)S(1)}, u32[]{:S(2)}, u32[]{:S(2)}) %collective-permute-start.1) | collective-permute-done | bytes 131104 | tf_op jit(solution)/shard_map/ppermute | solution.py:22
  49.6 1.9 %collective-permute-start.2 = (bf16[2,2,16,2048]{3,2,1,0:T(8,128)(2,1)S(1)}, bf16[2,2,16,2048]{3,2,1,0:T(8,128)(2,1)S(1)}, u32[]{:S(2)}, u32[]{:S(2)}) collective-permute-start(bf16[2,2,16,2048]{3,2,1,0:T(8,128)(2,1)S(1)} %maximum_select_fusion.4), channel_id=1, source_target_pairs={{0,2},{1,3},{2,0},{3,1},{4,6},{5,7},{6,4},{7,5},{8,10},{9,11},{10,... | collective-permute-start | bytes 786440 | tf_op jit(solution)/shard_map/ppermute | solution.py:22
  51.6 6.8 %collective-permute-done.2 = bf16[2,2,16,2048]{3,2,1,0:T(8,128)(2,1)S(1)} collective-permute-done((bf16[2,2,16,2048]{3,2,1,0:T(8,128)(2,1)S(1)}, bf16[2,2,16,2048]{3,2,1,0:T(8,128)(2,1)S(1)}, u32[]{:S(2)}, u32[]{:S(2)}) %collective-permute-start.2) | collective-permute-done | bytes 262176 | tf_op jit(solution)/shard_map/ppermute | solution.py:22
  58.5 3.7 %collective-permute-start.3 = (bf16[2,2,2,16,2048]{4,3,2,1,0:T(8,128)(2,1)S(1)}, bf16[2,2,2,16,2048]{4,3,2,1,0:T(8,128)(2,1)S(1)}, u32[]{:S(2)}, u32[]{:S(2)}) collective-permute-start(bf16[2,2,2,16,2048]{4,3,2,1,0:T(8,128)(2,1)S(1)} %maximum_select_fusion.2), channel_id=1, source_target_pairs={{0,1},{1,0},{2,3},{3,2},{4,5},{5,4},{6,7},{7,6},{8,9},{9,8},{10,11... | collective-permute-start | bytes 1572872 | tf_op jit(solution)/shard_map/ppermute | solution.py:22
  62.3 1.5 constant_dynamic-slice_fusion
  71.2 3.0 %fusion.8 = bf16[2,2,2,2,16,512]{5,4,0,1,2,3:T(8,128)(2,1)} fusion(bf16[2,2,2,2,16,2048]{5,4,3,2,1,0:T(8,128)(2,1)S(1)} %maximum_select_fusion, bf16[2048,512,1,1,1,1]{1,0,2,3,4,5:T(8,128)(2,1)} %reshape.612), kind=kOutput, calls=%fused_computation.8 | convolution fusion | flops 537001984 | bytes 3407872 | tf_op jit(solution)/shard_map/...d,dn->...n/dot_general | solution.py:89
  76.7 1.5 convolution_convert_fusion.3
  78.3 1.5 multiply_convert_fusion.3
  79.8 1.7 copy.49
  83.0 1.7 collective-permute-start.5
  84.8 2.6 %collective-permute-done.5 = f32[4,65,128]{2,1,0:T(8,128)S(1)} collective-permute-done((f32[4,65,128]{2,1,0:T(8,128)S(1)}, f32[4,65,128]{2,1,0:T(8,128)S(1)}, u32[]{:S(2)}, u32[]{:S(2)}) %collective-permute-start.5) | collective-permute-done | bytes 133152 | tf_op jit(solution)/shard_map/ppermute | solution.py:17
  87.7 5.3 %collective-permute-start.6 = (f32[4,65,128]{2,1,0:T(8,128)S(1)}, f32[4,65,128]{2,1,0:T(8,128)S(1)}, u32[]{:S(2)}, u32[]{:S(2)}) collective-permute-start(f32[4,65,128]{2,1,0:T(8,128)S(1)} %pad_maximum_fusion.1), channel_id=1, source_target_pairs={{0,32},{16,48},{32,64},{48,80},{64,96},{80,112},{96,128},{112,144}... | collective-permute-start | bytes 399368 | tf_op jit(solution)/shard_map/ppermute | solution.py:17
  93.2 2.0 %collective-permute-done.6 = f32[4,65,128]{2,1,0:T(8,128)S(1)} collective-permute-done((f32[4,65,128]{2,1,0:T(8,128)S(1)}, f32[4,65,128]{2,1,0:T(8,128)S(1)}, u32[]{:S(2)}, u32[]{:S(2)}) %collective-permute-start.6) | collective-permute-done | bytes 133152 | tf_op jit(solution)/shard_map/ppermute | solution.py:17
  95.5 8.0 %collective-permute-start.7 = (f32[4,65,128]{2,1,0:T(8,128)S(1)}, f32[4,65,128]{2,1,0:T(8,128)S(1)}, u32[]{:S(2)}, u32[]{:S(2)}) collective-permute-start(f32[4,65,128]{2,1,0:T(8,128)S(1)} %pad_maximum_fusion.2), channel_id=1, source_target_pairs={{0,64},{16,80},{32,96},{48,112},{64,128},{80,144},{96,160},{112,17... | collective-permute-start | bytes 399368 | tf_op jit(solution)/shard_map/ppermute | solution.py:17
  103.5 2.1 %collective-permute-done.7 = f32[4,65,128]{2,1,0:T(8,128)S(1)} collective-permute-done((f32[4,65,128]{2,1,0:T(8,128)S(1)}, f32[4,65,128]{2,1,0:T(8,128)S(1)}, u32[]{:S(2)}, u32[]{:S(2)}) %collective-permute-start.7) | collective-permute-done | bytes 133152 | tf_op jit(solution)/shard_map/ppermute | solution.py:17
  105.8 5.8 %collective-permute-start.8 = (f32[4,65,128]{2,1,0:T(8,128)S(1)}, f32[4,65,128]{2,1,0:T(8,128)S(1)}, u32[]{:S(2)}, u32[]{:S(2)}) collective-permute-start(f32[4,65,128]{2,1,0:T(8,128)S(1)} %pad_maximum_fusion.3), channel_id=1, source_target_pairs={{0,128},{16,144},{32,160},{48,176},{64,192},{80,208},{96,224},{112... | collective-permute-start | bytes 399368 | tf_op jit(solution)/shard_map/ppermute | solution.py:17
  114.0 16.4 %collective-permute-start.9 = (f32[4,65,128]{2,1,0:T(8,128)S(1)}, f32[4,65,128]{2,1,0:T(8,128)S(1)}, u32[]{:S(2)}, u32[]{:S(2)}) collective-permute-start(f32[4,65,128]{2,1,0:T(8,128)S(1)} %pad_maximum_fusion.4), channel_id=1, source_target_pairs={{0,256},{16,272},{32,288},{48,304},{64,320},{80,336},{96,352},{112... | collective-permute-start | bytes 399368 | tf_op jit(solution)/shard_map/ppermute | solution.py:17
  130.6 1.9 %collective-permute-done.9 = f32[4,65,128]{2,1,0:T(8,128)S(1)} collective-permute-done((f32[4,65,128]{2,1,0:T(8,128)S(1)}, f32[4,65,128]{2,1,0:T(8,128)S(1)}, u32[]{:S(2)}, u32[]{:S(2)}) %collective-permute-start.9) | collective-permute-done | bytes 133152 | tf_op jit(solution)/shard_map/ppermute | solution.py:17
  135.8 5.4 %collective-permute-start.10 = (bf16[2,2,2,16,2048]{4,3,2,1,0:T(8,128)(2,1)}, bf16[2,2,2,16,2048]{4,3,2,1,0:T(8,128)(2,1)}, u32[]{:S(2)}, u32[]{:S(2)}) collective-permute-start(bf16[2,2,2,16,2048]{4,3,2,1,0:T(8,128)(2,1)} %fusion.17), channel_id=1, source_target_pairs={{0,1},{1,0},{2,3},{3,2},{4,5},{5,4},{6,7},{7,6},{8,9},{9,8},{10,11... | collective-permute-start | bytes 1572872 | tf_op jit(solution)/shard_map/ppermute | solution.py:22
  141.2 1.9 %collective-permute-start.12 = (f32[256]{0:T(256)S(1)}, f32[256]{0:T(256)S(1)}, u32[]{:S(2)}, u32[]{:S(2)}) collective-permute-start(f32[256]{0:T(256)S(1)} %get-tuple-element.43), channel_id=1, source_target_pairs={{0,1},{1,0},{2,3},{3,2},{4,5},{5,4},{6,7},{7,6},{8,9},{9,8},{10,11... | collective-permute-start | bytes 3080 | tf_op jit(solution)/shard_map/ppermute | solution.py:22
  144.2 1.9 %collective-permute-start.13 = (f32[256]{0:T(256)S(1)}, f32[256]{0:T(256)S(1)}, u32[]{:S(2)}, u32[]{:S(2)}) collective-permute-start(f32[256]{0:T(256)S(1)} %add.205), channel_id=1, source_target_pairs={{0,2},{1,3},{2,0},{3,1},{4,6},{5,7},{6,4},{7,5},{8,10},{9,11},{10,... | collective-permute-start | bytes 3080 | tf_op jit(solution)/shard_map/ppermute | solution.py:22
  148.4 3.4 %collective-permute-start.11 = (bf16[2,2,16,2048]{3,2,1,0:T(8,128)(2,1)S(1)}, bf16[2,2,16,2048]{3,2,1,0:T(8,128)(2,1)S(1)}, u32[]{:S(2)}, u32[]{:S(2)}) collective-permute-start(bf16[2,2,16,2048]{3,2,1,0:T(8,128)(2,1)S(1)} %fusion.29), channel_id=1, source_target_pairs={{0,2},{1,3},{2,0},{3,1},{4,6},{5,7},{6,4},{7,5},{8,10},{9,11},{10,... | collective-permute-start | bytes 786440 | tf_op jit(solution)/shard_map/ppermute | solution.py:22
  151.9 5.8 %collective-permute-done.11 = bf16[2,2,16,2048]{3,2,1,0:T(8,128)(2,1)S(1)} collective-permute-done((bf16[2,2,16,2048]{3,2,1,0:T(8,128)(2,1)S(1)}, bf16[2,2,16,2048]{3,2,1,0:T(8,128)(2,1)S(1)}, u32[]{:S(2)}, u32[]{:S(2)}) %collective-permute-start.11) | collective-permute-done | bytes 262176 | tf_op jit(solution)/shard_map/ppermute | solution.py:22
  158.9 3.6 %collective-permute-start.14 = (bf16[2,16,2048]{2,1,0:T(8,128)(2,1)S(1)}, bf16[2,16,2048]{2,1,0:T(8,128)(2,1)S(1)}, u32[]{:S(2)}, u32[]{:S(2)}) collective-permute-start(bf16[2,16,2048]{2,1,0:T(8,128)(2,1)S(1)} %fusion.38), channel_id=1, source_target_pairs={{0,4},{1,5},{2,6},{3,7},{4,0},{5,1},{6,2},{7,3},{8,12},{9,13},{10,... | collective-permute-start | bytes 393224 | tf_op jit(solution)/shard_map/ppermute | solution.py:22
  162.5 6.2 %collective-permute-done.14 = bf16[2,16,2048]{2,1,0:T(8,128)(2,1)S(1)} collective-permute-done((bf16[2,16,2048]{2,1,0:T(8,128)(2,1)S(1)}, bf16[2,16,2048]{2,1,0:T(8,128)(2,1)S(1)}, u32[]{:S(2)}, u32[]{:S(2)}) %collective-permute-start.14) | collective-permute-done | bytes 131104 | tf_op jit(solution)/shard_map/ppermute | solution.py:22
  168.8 4.0 %collective-permute-start.15 = (bf16[16,2048]{1,0:T(8,128)(2,1)S(1)}, bf16[16,2048]{1,0:T(8,128)(2,1)S(1)}, u32[]{:S(2)}, u32[]{:S(2)}) collective-permute-start(bf16[16,2048]{1,0:T(8,128)(2,1)S(1)} %fusion.45), channel_id=1, source_target_pairs={{0,8},{1,9},{2,10},{3,11},{4,12},{5,13},{6,14},{7,15},{8,0},{9,1},... | collective-permute-start | bytes 196616 | tf_op jit(solution)/shard_map/ppermute | solution.py:22
  172.8 5.6 %collective-permute-done.15 = bf16[16,2048]{1,0:T(8,128)(2,1)S(1)} collective-permute-done((bf16[16,2048]{1,0:T(8,128)(2,1)S(1)}, bf16[16,2048]{1,0:T(8,128)(2,1)S(1)}, u32[]{:S(2)}, u32[]{:S(2)}) %collective-permute-start.15) | collective-permute-done | bytes 65568 | tf_op jit(solution)/shard_map/ppermute | solution.py:22
  (156 shorter events, 27.6 us)
Async XLA Ops:
  0.0 134.5 %copy-start = (bf16[256,2048]{1,0:T(8,128)(2,1)S(1)}, bf16[256,2048]{1,0:T(8,128)(2,1)}, u32[]{:S(2)}) copy-start(bf16[256,2048]{1,0:T(8,128)(2,1)} %param.25) | copy-start | bytes 3145732
  0.0 18.3 %copy-start.18 = (f32[4,256]{1,0:T(4,128)S(1)}, f32[4,256]{1,0:T(4,128)}, u32[]{:S(2)}) copy-start(f32[4,256]{1,0:T(4,128)} %param.17) | copy-start | bytes 12292
  0.0 18.9 %copy-start.27 = (f32[4]{0:T(128)S(1)}, f32[4]{0:T(128)}, u32[]{:S(2)}) copy-start(f32[4]{0:T(128)} %param.22) | copy-start | bytes 52
  0.0 28.1 %collective-permute-start = (bf16[16,2048]{1,0:T(8,128)(2,1)}, bf16[16,2048]{1,0:T(8,128)(2,1)S(1)}, u32[]{:S(2)}, u32[]{:S(2)}) collective-permute-start(bf16[16,2048]{1,0:T(8,128)(2,1)} %param.13), channel_id=1, source_target_pairs={{0,8},{1,9},{2,10},{3,11},{4,12},{5,13},{6,14},{7,15},{8,0},{9,1},... | collective-permute-start | bytes 196616 | tf_op jit(solution)/shard_map/ppermute | solution.py:22
  10.6 70.8 %all-to-all-start = ((bf16[16,16,2048]{2,1,0:T(8,128)(2,1)}), bf16[16,16,2048]{2,1,0:T(8,128)(2,1)S(1)}, u32[]{:S(2)}, u32[]{:S(2)}) async-start(bf16[16,16,2048]{2,1,0:T(8,128)(2,1)} %bitcast.22), calls=%async_computation | async-start | bytes 2097152 | tf_op jit(solution)/shard_map/all_to_all | solution.py:100
  28.1 21.5 %collective-permute-start.1 = (bf16[2,16,2048]{2,1,0:T(8,128)(2,1)S(1)}, bf16[2,16,2048]{2,1,0:T(8,128)(2,1)S(1)}, u32[]{:S(2)}, u32[]{:S(2)}) collective-permute-start(bf16[2,16,2048]{2,1,0:T(8,128)(2,1)S(1)} %maximum_select_fusion.6), channel_id=1, source_target_pairs={{0,4},{1,5},{2,6},{3,7},{4,0},{5,1},{6,2},{7,3},{8,12},{9,13},{10,... | collective-permute-start | bytes 393224 | tf_op jit(solution)/shard_map/ppermute | solution.py:22
  49.6 8.8 %collective-permute-start.2 = (bf16[2,2,16,2048]{3,2,1,0:T(8,128)(2,1)S(1)}, bf16[2,2,16,2048]{3,2,1,0:T(8,128)(2,1)S(1)}, u32[]{:S(2)}, u32[]{:S(2)}) collective-permute-start(bf16[2,2,16,2048]{3,2,1,0:T(8,128)(2,1)S(1)} %maximum_select_fusion.4), channel_id=1, source_target_pairs={{0,2},{1,3},{2,0},{3,1},{4,6},{5,7},{6,4},{7,5},{8,10},{9,11},{10,... | collective-permute-start | bytes 786440 | tf_op jit(solution)/shard_map/ppermute | solution.py:22
  58.5 6.2 %copy-start.11 = (bf16[2048,4]{0,1:T(4,128)(2,1)S(1)}, bf16[2048,4]{0,1:T(4,128)(2,1)}, u32[]{:S(2)}) copy-start(bf16[2048,4]{0,1:T(4,128)(2,1)} %param.15) | copy-start | bytes 49156
  58.5 5.4 %collective-permute-start.3 = (bf16[2,2,2,16,2048]{4,3,2,1,0:T(8,128)(2,1)S(1)}, bf16[2,2,2,16,2048]{4,3,2,1,0:T(8,128)(2,1)S(1)}, u32[]{:S(2)}, u32[]{:S(2)}) collective-permute-start(bf16[2,2,2,16,2048]{4,3,2,1,0:T(8,128)(2,1)S(1)} %maximum_select_fusion.2), channel_id=1, source_target_pairs={{0,1},{1,0},{2,3},{3,2},{4,5},{5,4},{6,7},{7,6},{8,9},{9,8},{10,11... | collective-permute-start | bytes 1572872 | tf_op jit(solution)/shard_map/ppermute | solution.py:22
  66.2 8.1 %copy-start.5 = (f32[256,4]{0,1:T(4,128)}, f32[256,4]{0,1:T(4,128)S(1)}, u32[]{:S(2)}) copy-start(f32[256,4]{0,1:T(4,128)S(1)} %reshape.610) | copy-start | bytes 12292
  67.5 6.7 %copy-start.7 = (f32[1,4,2,128]{3,2,1,0:T(2,128)}, f32[1,4,2,128]{3,2,1,0:T(2,128)S(1)}, u32[]{:S(2)}) copy-start(f32[1,4,2,128]{3,2,1,0:T(2,128)S(1)} %reduce-window.6) | copy-start | bytes 12292
  67.6 9.1 %collective-permute-start.4 = (bf16[3,2048]{1,0:T(4,128)(2,1)}, bf16[3,2048]{1,0:T(4,128)(2,1)S(1)}, u32[]{:S(2)}, u32[]{:S(2)}) collective-permute-start(bf16[3,2048]{1,0:T(4,128)(2,1)} %slice_bitcast_fusion), channel_id=1, source_target_pairs={{0,16},{16,32},{32,48},{48,64},{64,80},{80,96},{96,112},{112,128},... | collective-permute-start | bytes 36872 | tf_op jit(solution)/shard_map/ppermute | solution.py:17
  82.0 5.5 %copy-start.13 = (f32[1,4,1]{2,1,0:T(4,128)S(1)}, f32[1,4,1]{2,1,0:T(4,128)}, u32[]{:S(2)}) copy-start(f32[1,4,1]{2,1,0:T(4,128)} %get-tuple-element.55) | copy-start | bytes 52
  82.0 11.1 %copy-start.10 = (f32[4,2]{1,0:T(4,128)S(1)}, f32[4,2]{1,0:T(4,128)}, u32[]{:S(2)}) copy-start(f32[4,2]{1,0:T(4,128)} %copy-done.9) | copy-start | bytes 100
  82.0 13.2 %copy-start.17 = (f32[4]{0:T(128)S(1)}, f32[4]{0:T(128)}, u32[]{:S(2)}) copy-start(f32[4]{0:T(128)} %copy-done.16) | copy-start | bytes 52
  82.4 21.0 %copy-start.8 = (f32[1,4,2,128]{3,2,1,0:T(2,128)S(1)}, f32[1,4,2,128]{3,2,1,0:T(2,128)}, u32[]{:S(2)}) copy-start(f32[1,4,2,128]{3,2,1,0:T(2,128)} %copy-done.7) | copy-start | bytes 12292
  82.5 29.2 %copy-start.6 = (f32[256,4]{0,1:T(4,128)S(1)}, f32[256,4]{0,1:T(4,128)}, u32[]{:S(2)}) copy-start(f32[256,4]{0,1:T(4,128)} %copy-done.5) | copy-start | bytes 12292
  82.5 29.2 %copy-start.15 = (f32[4]{0:T(128)S(1)}, f32[4]{0:T(128)}, u32[]{:S(2)}) copy-start(f32[4]{0:T(128)} %param.21) | copy-start | bytes 52
  83.0 49.5 %copy-start.12 = (f32[256,4]{0,1:T(4,128)S(1)}, f32[256,4]{0,1:T(4,128)}, u32[]{:S(2)}) copy-start(f32[256,4]{0,1:T(4,128)} %get-tuple-element.41) | copy-start | bytes 12292
  83.0 4.4 %collective-permute-start.5 = (f32[4,65,128]{2,1,0:T(8,128)S(1)}, f32[4,65,128]{2,1,0:T(8,128)S(1)}, u32[]{:S(2)}, u32[]{:S(2)}) collective-permute-start(f32[4,65,128]{2,1,0:T(8,128)S(1)} %pad_maximum_fusion), channel_id=1, source_target_pairs={{0,16},{16,32},{32,48},{48,64},{64,80},{80,96},{96,112},{112,128},... | collective-permute-start | bytes 399368 | tf_op jit(solution)/shard_map/ppermute | solution.py:17
  87.7 45.0 %copy-start.28 = (f32[4]{0:T(128)S(1)}, f32[4]{0:T(128)}, u32[]{:S(2)}) copy-start(f32[4]{0:T(128)} %param.23) | copy-start | bytes 52
  87.7 7.4 %collective-permute-start.6 = (f32[4,65,128]{2,1,0:T(8,128)S(1)}, f32[4,65,128]{2,1,0:T(8,128)S(1)}, u32[]{:S(2)}, u32[]{:S(2)}) collective-permute-start(f32[4,65,128]{2,1,0:T(8,128)S(1)} %pad_maximum_fusion.1), channel_id=1, source_target_pairs={{0,32},{16,48},{32,64},{48,80},{64,96},{80,112},{96,128},{112,144}... | collective-permute-start | bytes 399368 | tf_op jit(solution)/shard_map/ppermute | solution.py:17
  95.5 10.0 %collective-permute-start.7 = (f32[4,65,128]{2,1,0:T(8,128)S(1)}, f32[4,65,128]{2,1,0:T(8,128)S(1)}, u32[]{:S(2)}, u32[]{:S(2)}) collective-permute-start(f32[4,65,128]{2,1,0:T(8,128)S(1)} %pad_maximum_fusion.2), channel_id=1, source_target_pairs={{0,64},{16,80},{32,96},{48,112},{64,128},{80,144},{96,160},{112,17... | collective-permute-start | bytes 399368 | tf_op jit(solution)/shard_map/ppermute | solution.py:17
  105.8 7.9 %collective-permute-start.8 = (f32[4,65,128]{2,1,0:T(8,128)S(1)}, f32[4,65,128]{2,1,0:T(8,128)S(1)}, u32[]{:S(2)}, u32[]{:S(2)}) collective-permute-start(f32[4,65,128]{2,1,0:T(8,128)S(1)} %pad_maximum_fusion.3), channel_id=1, source_target_pairs={{0,128},{16,144},{32,160},{48,176},{64,192},{80,208},{96,224},{112... | collective-permute-start | bytes 399368 | tf_op jit(solution)/shard_map/ppermute | solution.py:17
  114.0 20.3 %copy-start.25 = (f32[256]{0:T(256)S(1)}, f32[256]{0:T(256)}, u32[]{:S(2)}) copy-start(f32[256]{0:T(256)} %param.24) | copy-start | bytes 3076
  114.0 18.5 %collective-permute-start.9 = (f32[4,65,128]{2,1,0:T(8,128)S(1)}, f32[4,65,128]{2,1,0:T(8,128)S(1)}, u32[]{:S(2)}, u32[]{:S(2)}) collective-permute-start(f32[4,65,128]{2,1,0:T(8,128)S(1)} %pad_maximum_fusion.4), channel_id=1, source_target_pairs={{0,256},{16,272},{32,288},{48,304},{64,320},{80,336},{96,352},{112... | collective-permute-start | bytes 399368 | tf_op jit(solution)/shard_map/ppermute | solution.py:17
  135.8 10.4 %collective-permute-start.10 = (bf16[2,2,2,16,2048]{4,3,2,1,0:T(8,128)(2,1)}, bf16[2,2,2,16,2048]{4,3,2,1,0:T(8,128)(2,1)}, u32[]{:S(2)}, u32[]{:S(2)}) collective-permute-start(bf16[2,2,2,16,2048]{4,3,2,1,0:T(8,128)(2,1)} %fusion.17), channel_id=1, source_target_pairs={{0,1},{1,0},{2,3},{3,2},{4,5},{5,4},{6,7},{7,6},{8,9},{9,8},{10,11... | collective-permute-start | bytes 1572872 | tf_op jit(solution)/shard_map/ppermute | solution.py:22
  141.2 3.1 %collective-permute-start.12 = (f32[256]{0:T(256)S(1)}, f32[256]{0:T(256)S(1)}, u32[]{:S(2)}, u32[]{:S(2)}) collective-permute-start(f32[256]{0:T(256)S(1)} %get-tuple-element.43), channel_id=1, source_target_pairs={{0,1},{1,0},{2,3},{3,2},{4,5},{5,4},{6,7},{7,6},{8,9},{9,8},{10,11... | collective-permute-start | bytes 3080 | tf_op jit(solution)/shard_map/ppermute | solution.py:22
  144.2 7.5 %collective-permute-start.13 = (f32[256]{0:T(256)S(1)}, f32[256]{0:T(256)S(1)}, u32[]{:S(2)}, u32[]{:S(2)}) collective-permute-start(f32[256]{0:T(256)S(1)} %add.205), channel_id=1, source_target_pairs={{0,2},{1,3},{2,0},{3,1},{4,6},{5,7},{6,4},{7,5},{8,10},{9,11},{10,... | collective-permute-start | bytes 3080 | tf_op jit(solution)/shard_map/ppermute | solution.py:22
  148.4 9.3 %collective-permute-start.11 = (bf16[2,2,16,2048]{3,2,1,0:T(8,128)(2,1)S(1)}, bf16[2,2,16,2048]{3,2,1,0:T(8,128)(2,1)S(1)}, u32[]{:S(2)}, u32[]{:S(2)}) collective-permute-start(bf16[2,2,16,2048]{3,2,1,0:T(8,128)(2,1)S(1)} %fusion.29), channel_id=1, source_target_pairs={{0,2},{1,3},{2,0},{3,1},{4,6},{5,7},{6,4},{7,5},{8,10},{9,11},{10,... | collective-permute-start | bytes 786440 | tf_op jit(solution)/shard_map/ppermute | solution.py:22
  158.9 9.9 %collective-permute-start.14 = (bf16[2,16,2048]{2,1,0:T(8,128)(2,1)S(1)}, bf16[2,16,2048]{2,1,0:T(8,128)(2,1)S(1)}, u32[]{:S(2)}, u32[]{:S(2)}) collective-permute-start(bf16[2,16,2048]{2,1,0:T(8,128)(2,1)S(1)} %fusion.38), channel_id=1, source_target_pairs={{0,4},{1,5},{2,6},{3,7},{4,0},{5,1},{6,2},{7,3},{8,12},{9,13},{10,... | collective-permute-start | bytes 393224 | tf_op jit(solution)/shard_map/ppermute | solution.py:22
  168.8 9.6 %collective-permute-start.15 = (bf16[16,2048]{1,0:T(8,128)(2,1)S(1)}, bf16[16,2048]{1,0:T(8,128)(2,1)S(1)}, u32[]{:S(2)}, u32[]{:S(2)}) collective-permute-start(bf16[16,2048]{1,0:T(8,128)(2,1)S(1)} %fusion.45), channel_id=1, source_target_pairs={{0,8},{1,9},{2,10},{3,11},{4,12},{5,13},{6,14},{7,15},{8,0},{9,1},... | collective-permute-start | bytes 196616 | tf_op jit(solution)/shard_map/ppermute | solution.py:22
  (14 other events, 23.1 us)

commit v5 on v3

--- a/solution.py
+++ b/solution.py
@@ -17,29 +17,42 @@
     return lax.ppermute(x, axis, pairs)
 
 
-def swapped(x, axis, bit):
+def swapped(x, axis, offset):
     peers = lax.axis_size(axis)
-    return lax.ppermute(x, axis, [(i, i ^ bit) for i in range(peers)])
-
-
-def gather_rows(rows, axis, bits):
+    return lax.ppermute(x, axis, [(i, i ^ offset) for i in range(peers)])
+
+
+def digits_of(size, shift=0):
+    found = []
+    while size > 1:
+        radix = 4 if size % 4 == 0 else 2
+        found.append((shift, radix))
+        shift += radix.bit_length() - 1
+        size //= radix
+    return found
+
+
+def gather_rows(rows, axis, digits):
     place = lax.axis_index(axis)
-    peers = lax.axis_size(axis)
     held = rows
-    for bit in reversed(bits):
-        other = swapped(held, axis, bit)
-        low = (place & bit) == 0
-        held = jnp.where(low, jnp.stack([held, other]), jnp.stack([other, held]))
+    for shift, radix in reversed(digits):
+        mine = (place >> shift) % radix
+        by_offset = jnp.stack([held] + [swapped(held, axis, o << shift) for o in range(1, radix)])
+        held = jnp.stack(
+            [lax.dynamic_index_in_dim(by_offset, j ^ mine, 0, keepdims=False) for j in range(radix)]
+        )
     return held
 
 
-def halve(held, axis, bits):
+def scatter_sum(held, axis, digits):
     place = lax.axis_index(axis)
-    for bit in bits:
-        mine = (place // bit) % 2
-        keep = lax.dynamic_index_in_dim(held, mine, 0, keepdims=False)
-        give = lax.dynamic_index_in_dim(held, 1 - mine, 0, keepdims=False)
-        held = keep + swapped(give.astype(jnp.bfloat16), axis, bit).astype(jnp.float32)
+    for shift, radix in digits:
+        mine = (place >> shift) % radix
+        total = lax.dynamic_index_in_dim(held, mine, 0, keepdims=False)
+        for o in range(1, radix):
+            give = lax.dynamic_index_in_dim(held, mine ^ o, 0, keepdims=False)
+            total = total + swapped(give.astype(jnp.bfloat16), axis, o << shift).astype(jnp.float32)
+        held = total
     return held
 
 
@@ -68,15 +81,17 @@
     out_weight,
 ):
     tp_size = lax.axis_size("tp")
-    tp_bits = [1 << k for k in range(tp_size.bit_length() - 1)]
     heads_dev = log_rate.shape[0]
     inner_dev = in_weight.shape[2]
     group_cols = 2 * STATE
     per_group_dev = (HEADS // GROUPS) // heads_dev
+    within_digits = digits_of(per_group_dev)
+    across_digits = digits_of(tp_size // per_group_dev, per_group_dev.bit_length() - 1)
+    tp_digits = within_digits + across_digits
     group_index = lax.axis_index("tp") // per_group_dev
     zx_weight = in_weight.reshape(in_weight.shape[0], 2 * inner_dev)
-    stacked = gather_rows(hidden, "tp", tp_bits)
-    levels = len(tp_bits)
+    stacked = gather_rows(hidden, "tp", tp_digits)
+    levels = len(tp_digits)
     length = tp_size * hidden.shape[0]
     flipped = tuple(reversed(range(levels)))
 
@@ -155,18 +170,20 @@
     run_state = dev_state
     reach = 1
     while reach < ctx_size:
+        radix = 4 if (ctx_size // reach) % 4 == 0 else 2
         packed = jnp.concatenate(
             [run_state, jnp.broadcast_to(run_decay[:, None, None], (heads_dev, 1, STATE))], axis=1
         )
-        got = shifted(packed, "ctx", reach)
-        valid = place >= reach
-        got_state = jnp.where(valid, got[:, :HEAD_DIM], 0.0)
-        got_decay = jnp.where(valid, got[:, HEAD_DIM, 0], 1.0)
-        in_state = in_decay[:, None, None] * got_state + in_state
-        in_decay = got_decay * in_decay
-        run_state = run_decay[:, None, None] * got_state + run_state
-        run_decay = got_decay * run_decay
-        reach *= 2
+        arrived = [shifted(packed, "ctx", m * reach) for m in range(1, radix)]
+        for m, got in zip(range(1, radix), arrived):
+            valid = place >= m * reach
+            got_state = jnp.where(valid, got[:, :HEAD_DIM], 0.0)
+            got_decay = jnp.where(valid, got[:, HEAD_DIM, 0], 1.0)
+            in_state = in_decay[:, None, None] * got_state + in_state
+            in_decay = got_decay * in_decay
+            run_state = run_decay[:, None, None] * got_state + run_state
+            run_decay = got_decay * run_decay
+        reach *= radix
     incoming = in_state
     starting = local_starts + prefixes[:, :, None, None] * incoming[None]
     carried = jnp.einsum(
@@ -179,25 +196,23 @@
     result_heads = within + carried + skip_weight[None, None, :, None] * x_float
     result_heads = result_heads.reshape(length, inner_dev)
     gated = result_heads * jax.nn.silu(gate_raw.astype(jnp.float32))
-    total = jnp.sum(gated * gated, axis=1)
-    bit = 1
-    while bit < per_group_dev:
-        total = total + swapped(total, "tp", bit)
-        bit *= 2
+    squares = jnp.sum(gated * gated, axis=1)
+    total = squares
+    for shift, radix in within_digits:
+        total = total + sum(swapped(total, "tp", o << shift) for o in range(1, radix))
+    radices = tuple(radix for _, radix in reversed(tp_digits))
     scaled = (gated * norm_gain[None, :]).astype(jnp.bfloat16)
-    scaled = scaled.reshape((2,) * levels + (length // tp_size, inner_dev))
+    scaled = scaled.reshape(radices + (length // tp_size, inner_dev))
     scaled = jnp.transpose(scaled, flipped + (levels, levels + 1))
     partial = jnp.einsum("...c,cn->...n", scaled, out_weight, preferred_element_type=jnp.float32)
-    within_bits = [bit for bit in tp_bits if bit < per_group_dev]
-    across_bits = [bit for bit in tp_bits if bit >= per_group_dev]
-    held = halve(partial, "tp", within_bits)
+    held = scatter_sum(partial, "tp", within_digits)
     inverse = lax.rsqrt(total / (HEADS * HEAD_DIM // GROUPS) + 1e-05)
-    inverse = jnp.transpose(inverse.reshape((2,) * levels + (length // tp_size,)), flipped + (levels,))
-    for bit in within_bits:
-        inverse = lax.dynamic_index_in_dim(inverse, (lax.axis_index("tp") // bit) % 2, 0, keepdims=False)
+    inverse = jnp.transpose(inverse.reshape(radices + (length // tp_size,)), flipped + (levels,))
+    for shift, radix in within_digits:
+        mine = (lax.axis_index("tp") >> shift) % radix
+        inverse = lax.dynamic_index_in_dim(inverse, mine, 0, keepdims=False)
     held = held * inverse[..., None]
-    held = halve(held, "tp", across_bits)
-    mixed = held
+    mixed = scatter_sum(held, "tp", across_digits)
     return mixed.astype(jnp.bfloat16)
 
 

time: 165 us -> 173 us (1.048)
  the two profiles are of different devices: /device:TPU:1 before, /device:TPU:73 now
where the time goes in v5:
time: 173 us; the launch traced here: 172 us
  starting transfers between devices  96.9 us (56%)
  waiting for transfers between devices  43.8 us (25%)
  local copies, waits for them, and re-layouts  12.9 us (7%)
  other arithmetic  9.46 us (5%)
  matrix products  8.23 us (5%)
    ppermute x15, starting transfers between devices, swapped(): return lax.ppermute(x, axis, [(i, i ^ offset) for i in range(peers)])  53 us
    ppermute x8, starting transfers between devices, shifted(): return lax.ppermute(x, axis, pairs)  37.9 us
    ppermute x15, waiting for transfers between devices, swapped(): return lax.ppermute(x, axis, [(i, i ^ offset) for i in range(peers)])  23.5 us
    ppermute x8, waiting for transfers between devices, shifted(): return lax.ppermute(x, axis, pairs)  17.5 us
    all_to_all x1, starting transfers between devices, body(): got_maps = lax.all_to_all(own_maps, 'tp', 0, 0, tiled=True)  6.07 us
  transfers between devices with their start and end apart: 24, of which 14 were waited for; matrix products, arithmetic and copies ran while one was open for 8% of the time, Pallas kernels for 0%

profile of v5, /device:TPU:73, one launch (start us, length us, event | category | flops | bytes accessed | tf_op | source)
XLA Modules:
  0.0 172.2 jit_solution(17480232931705584873)
XLA Ops:
  0.0 4.5 %collective-permute-start = (bf16[16,2048]{1,0:T(8,128)(2,1)}, bf16[16,2048]{1,0:T(8,128)(2,1)S(1)}, u32[]{:S(2)}, u32[]{:S(2)}) collective-permute-start(bf16[16,2048]{1,0:T(8,128)(2,1)} %param.13), channel_id=1, source_target_pairs={{0,4},{1,5},{2,6},{3,7},{4,0},{5,1},{6,2},{7,3},{8,12},{9,13},{10,... | collective-permute-start | bytes 196616 | tf_op jit(solution)/shard_map/ppermute | solution.py:22
  4.5 4.8 %collective-permute-start.1 = (bf16[16,2048]{1,0:T(8,128)(2,1)}, bf16[16,2048]{1,0:T(8,128)(2,1)S(1)}, u32[]{:S(2)}, u32[]{:S(2)}) collective-permute-start(bf16[16,2048]{1,0:T(8,128)(2,1)} %param.13), channel_id=1, source_target_pairs={{0,8},{1,9},{2,10},{3,11},{4,12},{5,13},{6,14},{7,15},{8,0},{9,1},... | collective-permute-start | bytes 196616 | tf_op jit(solution)/shard_map/ppermute | solution.py:22
  18.2 4.3 %collective-permute-start.3 = (bf16[4,16,2048]{2,1,0:T(8,128)(2,1)}, bf16[4,16,2048]{2,1,0:T(8,128)(2,1)}, u32[]{:S(2)}, u32[]{:S(2)}) collective-permute-start(bf16[4,16,2048]{2,1,0:T(8,128)(2,1)} %get-tuple-element.60), channel_id=1, source_target_pairs={{0,1},{1,0},{2,3},{3,2},{4,5},{5,4},{6,7},{7,6},{8,9},{9,8},{10,11... | collective-permute-start | bytes 786440 | tf_op jit(solution)/shard_map/ppermute | solution.py:22
  22.5 3.0 %collective-permute-start.4 = (bf16[4,16,2048]{2,1,0:T(8,128)(2,1)}, bf16[4,16,2048]{2,1,0:T(8,128)(2,1)}, u32[]{:S(2)}, u32[]{:S(2)}) collective-permute-start(bf16[4,16,2048]{2,1,0:T(8,128)(2,1)} %get-tuple-element.60), channel_id=1, source_target_pairs={{0,2},{1,3},{2,0},{3,1},{4,6},{5,7},{6,4},{7,5},{8,10},{9,11},{10,... | collective-permute-start | bytes 786440 | tf_op jit(solution)/shard_map/ppermute | solution.py:22
  29.5 2.6 %reshape.321 = bf16[2048,512,1,1]{1,0,2,3:T(8,128)(2,1)} reshape(bf16[2048,2,256]{2,1,0:T(2,128)(2,1)S(1)} %copy-done.1) | data formatting | bytes 4194304 | tf_op jit(solution)/shard_map/reshape | solution.py:92
  34.1 4.3 %collective-permute-done.5 = bf16[4,16,2048]{2,1,0:T(8,128)(2,1)} collective-permute-done((bf16[4,16,2048]{2,1,0:T(8,128)(2,1)}, bf16[4,16,2048]{2,1,0:T(8,128)(2,1)}, u32[]{:S(2)}, u32[]{:S(2)}) %collective-permute-start.5) | collective-permute-done | bytes 262176 | tf_op jit(solution)/shard_map/ppermute | solution.py:22
  43.3 2.8 %fusion.8 = bf16[4,4,16,4,16]{4,2,3,0,1:T(8,128)(2,1)} fusion(bf16[16,4,2048,1,1]{2,1,0,4,3:T(4,128)(2,1)} %bitcast.171, bf16[1,4,16,2048]{3,2,1,0:T(8,128)(2,1)} %copy-done.4, bf16[1,4,16,2048]{3,2,1,0:T(8,128)(2,1)} %copy-done.5, bf16[1,4,16,2048]{3,2,1,0:T(8,128)(2,1)} %copy-done.6, bf16[1,4,16,2048]{3,2,1,0:T(8,128)(2,1)S(1)} %get-tuple-element.48), kind=kOutput, calls=%fused_computation.9 | convolution fusion | flops 71319552 | bytes 1343488 | tf_op jit(solution)/shard_map/...d,sgd->...gs/dot_general | solution.py:112
  48.2 6.1 %all-to-all-start = ((bf16[16,256,16]{1,2,0:T(8,128)(2,1)}), bf16[16,256,16]{1,2,0:T(8,128)(2,1)S(1)}, u32[]{:S(2)}, u32[]{:S(2)}) async-start(bf16[16,256,16]{1,2,0:T(8,128)(2,1)} %bitcast.17), calls=%async_computation | async-start | bytes 262144 | tf_op jit(solution)/shard_map/all_to_all | solution.py:118
  54.3 2.6 %fusion.9 = bf16[4,4,16,512]{3,2,0,1:T(8,128)(2,1)} fusion(bf16[2048,512,1,1]{1,0,2,3:T(8,128)(2,1)S(1)} %copy-done.2, bf16[1,4,16,2048]{3,2,1,0:T(8,128)(2,1)} %copy-done.4, bf16[1,4,16,2048]{3,2,1,0:T(8,128)(2,1)} %copy-done.5, bf16[1,4,16,2048]{3,2,1,0:T(8,128)(2,1)} %copy-done.6, bf16[1,4,16,2048]{3,2,1,0:T(8,128)(2,1)} %copy-done.3), kind=kOutput, calls=%fused_computation.10 | convolution fusion | flops 538574848 | bytes 3407872 | tf_op jit(solution)/shard_map/...d,dn->...n/dot_general | solution.py:104
  59.2 2.8 %all-to-all-done = bf16[16,256,16]{1,2,0:T(8,128)(2,1)S(1)} async-done(((bf16[16,256,16]{1,2,0:T(8,128)(2,1)}), bf16[16,256,16]{1,2,0:T(8,128)(2,1)S(1)}, u32[]{:S(2)}, u32[]{:S(2)}) %all-to-all-start) | async-done | bytes 131104 | tf_op jit(solution)/shard_map/all_to_all | solution.py:118
  62.3 3.1 %collective-permute-start.6 = (bf16[3,512]{1,0:T(4,128)(2,1)S(1)}, bf16[3,512]{1,0:T(4,128)(2,1)S(1)}, u32[]{:S(2)}, u32[]{:S(2)}) collective-permute-start(bf16[3,512]{1,0:T(4,128)(2,1)S(1)} %pad_maximum_fusion.7), channel_id=1, source_target_pairs={{0,16},{16,32},{32,48},{48,64},{64,80},{80,96},{96,112},{112,128},... | collective-permute-start | bytes 9224 | tf_op jit(solution)/shard_map/ppermute | solution.py:17
  65.7 3.0 %collective-permute-done.6 = bf16[3,512]{1,0:T(4,128)(2,1)S(1)} collective-permute-done((bf16[3,512]{1,0:T(4,128)(2,1)S(1)}, bf16[3,512]{1,0:T(4,128)(2,1)S(1)}, u32[]{:S(2)}, u32[]{:S(2)}) %collective-permute-start.6) | collective-permute-done | bytes 3104 | tf_op jit(solution)/shard_map/ppermute | solution.py:17
  69.7 2.5 %collective-permute-start.7 = (f32[4,65,128]{2,1,0:T(8,128)S(1)}, f32[4,65,128]{2,1,0:T(8,128)S(1)}, u32[]{:S(2)}, u32[]{:S(2)}) collective-permute-start(f32[4,65,128]{2,1,0:T(8,128)S(1)} %pad_maximum_fusion.4), channel_id=1, source_target_pairs={{0,32},{16,48},{32,64},{48,80},{64,96},{80,112},{96,128},{112,144}... | collective-permute-start | bytes 399368 | tf_op jit(solution)/shard_map/ppermute | solution.py:17
  72.2 2.5 %collective-permute-start.8 = (f32[4,65,128]{2,1,0:T(8,128)S(1)}, f32[4,65,128]{2,1,0:T(8,128)S(1)}, u32[]{:S(2)}, u32[]{:S(2)}) collective-permute-start(f32[4,65,128]{2,1,0:T(8,128)S(1)} %pad_maximum_fusion.4), channel_id=1, source_target_pairs={{0,16},{16,32},{32,48},{48,64},{64,80},{80,96},{96,112},{112,128},... | collective-permute-start | bytes 399368 | tf_op jit(solution)/shard_map/ppermute | solution.py:17
  74.8 5.8 %collective-permute-start.9 = (f32[4,65,128]{2,1,0:T(8,128)S(1)}, f32[4,65,128]{2,1,0:T(8,128)S(1)}, u32[]{:S(2)}, u32[]{:S(2)}) collective-permute-start(f32[4,65,128]{2,1,0:T(8,128)S(1)} %pad_maximum_fusion.4), channel_id=1, source_target_pairs={{0,48},{16,64},{32,80},{48,96},{64,112},{80,128},{96,144},{112,160... | collective-permute-start | bytes 399368 | tf_op jit(solution)/shard_map/ppermute | solution.py:17
  83.0 4.0 %collective-permute-start.12 = (f32[4,65,128]{2,1,0:T(8,128)S(1)}, f32[4,65,128]{2,1,0:T(8,128)S(1)}, u32[]{:S(2)}, u32[]{:S(2)}) collective-permute-start(f32[4,65,128]{2,1,0:T(8,128)S(1)} %pad_maximum_fusion.5), channel_id=1, source_target_pairs={{0,64},{16,80},{32,96},{48,112},{64,128},{80,144},{96,160},{112,17... | collective-permute-start | bytes 399368 | tf_op jit(solution)/shard_map/ppermute | solution.py:17
  87.0 8.3 %collective-permute-start.10 = (f32[4,65,128]{2,1,0:T(8,128)S(1)}, f32[4,65,128]{2,1,0:T(8,128)S(1)}, u32[]{:S(2)}, u32[]{:S(2)}) collective-permute-start(f32[4,65,128]{2,1,0:T(8,128)S(1)} %pad_maximum_fusion.5), channel_id=1, source_target_pairs={{0,192},{16,208},{32,224},{48,240},{64,256},{80,272},{96,288},{112... | collective-permute-start | bytes 399368 | tf_op jit(solution)/shard_map/ppermute | solution.py:17
  95.3 2.8 %collective-permute-start.11 = (f32[4,65,128]{2,1,0:T(8,128)S(1)}, f32[4,65,128]{2,1,0:T(8,128)S(1)}, u32[]{:S(2)}, u32[]{:S(2)}) collective-permute-start(f32[4,65,128]{2,1,0:T(8,128)S(1)} %pad_maximum_fusion.5), channel_id=1, source_target_pairs={{0,128},{16,144},{32,160},{48,176},{64,192},{80,208},{96,224},{112... | collective-permute-start | bytes 399368 | tf_op jit(solution)/shard_map/ppermute | solution.py:17
  98.1 4.3 %collective-permute-done.10 = f32[4,65,128]{2,1,0:T(8,128)S(1)} collective-permute-done((f32[4,65,128]{2,1,0:T(8,128)S(1)}, f32[4,65,128]{2,1,0:T(8,128)S(1)}, u32[]{:S(2)}, u32[]{:S(2)}) %collective-permute-start.10) | collective-permute-done | bytes 133152 | tf_op jit(solution)/shard_map/ppermute | solution.py:17
  102.5 4.9 %collective-permute-done.11 = f32[4,65,128]{2,1,0:T(8,128)S(1)} collective-permute-done((f32[4,65,128]{2,1,0:T(8,128)S(1)}, f32[4,65,128]{2,1,0:T(8,128)S(1)}, u32[]{:S(2)}, u32[]{:S(2)}) %collective-permute-start.11) | collective-permute-done | bytes 133152 | tf_op jit(solution)/shard_map/ppermute | solution.py:17
  107.7 8.9 %collective-permute-start.13 = (f32[4,65,128]{2,1,0:T(8,128)S(1)}, f32[4,65,128]{2,1,0:T(8,128)S(1)}, u32[]{:S(2)}, u32[]{:S(2)}) collective-permute-start(f32[4,65,128]{2,1,0:T(8,128)S(1)} %pad_maximum_fusion.6), channel_id=1, source_target_pairs={{0,256},{16,272},{32,288},{48,304},{64,320},{80,336},{96,352},{112... | collective-permute-start | bytes 399368 | tf_op jit(solution)/shard_map/ppermute | solution.py:17
  116.8 3.5 %collective-permute-done.13 = f32[4,65,128]{2,1,0:T(8,128)S(1)} collective-permute-done((f32[4,65,128]{2,1,0:T(8,128)S(1)}, f32[4,65,128]{2,1,0:T(8,128)S(1)}, u32[]{:S(2)}, u32[]{:S(2)}) %collective-permute-start.13) | collective-permute-done | bytes 133152 | tf_op jit(solution)/shard_map/ppermute | solution.py:17
  121.3 6.9 %collective-permute-start.17 = (f32[256]{0:T(256)S(1)}, f32[256]{0:T(256)S(1)}, u32[]{:S(2)}, u32[]{:S(2)}) collective-permute-start(f32[256]{0:T(256)S(1)} %get-tuple-element.55), channel_id=1, source_target_pairs={{0,1},{1,0},{2,3},{3,2},{4,5},{5,4},{6,7},{7,6},{8,9},{9,8},{10,11... | collective-permute-start | bytes 3080 | tf_op jit(solution)/shard_map/ppermute | solution.py:22
  128.2 3.1 %collective-permute-start.18 = (f32[256]{0:T(256)S(1)}, f32[256]{0:T(256)S(1)}, u32[]{:S(2)}, u32[]{:S(2)}) collective-permute-start(f32[256]{0:T(256)S(1)} %get-tuple-element.55), channel_id=1, source_target_pairs={{0,2},{1,3},{2,0},{3,1},{4,6},{5,7},{6,4},{7,5},{8,10},{9,11},{10,... | collective-permute-start | bytes 3080 | tf_op jit(solution)/shard_map/ppermute | solution.py:22
  137.2 3.1 %collective-permute-start.15 = (bf16[4,16,2048]{2,1,0:T(8,128)(2,1)}, bf16[4,16,2048]{2,1,0:T(8,128)(2,1)}, u32[]{:S(2)}, u32[]{:S(2)}) collective-permute-start(bf16[4,16,2048]{2,1,0:T(8,128)(2,1)} %get-tuple-element.47), channel_id=1, source_target_pairs={{0,2},{1,3},{2,0},{3,1},{4,6},{5,7},{6,4},{7,5},{8,10},{9,11},{10,... | collective-permute-start | bytes 786440 | tf_op jit(solution)/shard_map/ppermute | solution.py:22
  140.3 2.6 %collective-permute-start.16 = (bf16[4,16,2048]{2,1,0:T(8,128)(2,1)S(1)}, bf16[4,16,2048]{2,1,0:T(8,128)(2,1)}, u32[]{:S(2)}, u32[]{:S(2)}) collective-permute-start(bf16[4,16,2048]{2,1,0:T(8,128)(2,1)S(1)} %get-tuple-element.46), channel_id=1, source_target_pairs={{0,3},{1,2},{2,1},{3,0},{4,7},{5,6},{6,5},{7,4},{8,11},{9,10},{10,... | collective-permute-start | bytes 786440 | tf_op jit(solution)/shard_map/ppermute | solution.py:22
  143.1 3.9 %collective-permute-done.15 = bf16[4,16,2048]{2,1,0:T(8,128)(2,1)} collective-permute-done((bf16[4,16,2048]{2,1,0:T(8,128)(2,1)}, bf16[4,16,2048]{2,1,0:T(8,128)(2,1)}, u32[]{:S(2)}, u32[]{:S(2)}) %collective-permute-start.15) | collective-permute-done | bytes 262176 | tf_op jit(solution)/shard_map/ppermute | solution.py:22
  147.0 6.1 %collective-permute-done.16 = bf16[4,16,2048]{2,1,0:T(8,128)(2,1)} collective-permute-done((bf16[4,16,2048]{2,1,0:T(8,128)(2,1)S(1)}, bf16[4,16,2048]{2,1,0:T(8,128)(2,1)}, u32[]{:S(2)}, u32[]{:S(2)}) %collective-permute-start.16) | collective-permute-done | bytes 262176 | tf_op jit(solution)/shard_map/ppermute | solution.py:22
  154.4 2.5 %collective-permute-start.20 = (bf16[16,2048]{1,0:T(8,128)(2,1)S(1)}, bf16[16,2048]{1,0:T(8,128)(2,1)S(1)}, u32[]{:S(2)}, u32[]{:S(2)}) collective-permute-start(bf16[16,2048]{1,0:T(8,128)(2,1)S(1)} %get-tuple-element.52), channel_id=1, source_target_pairs={{0,4},{1,5},{2,6},{3,7},{4,0},{5,1},{6,2},{7,3},{8,12},{9,13},{10,... | collective-permute-start | bytes 196616 | tf_op jit(solution)/shard_map/ppermute | solution.py:22
  156.9 4.3 %collective-permute-start.21 = (bf16[16,2048]{1,0:T(8,128)(2,1)S(1)}, bf16[16,2048]{1,0:T(8,128)(2,1)S(1)}, u32[]{:S(2)}, u32[]{:S(2)}) collective-permute-start(bf16[16,2048]{1,0:T(8,128)(2,1)S(1)} %get-tuple-element.54), channel_id=1, source_target_pairs={{0,8},{1,9},{2,10},{3,11},{4,12},{5,13},{6,14},{7,15},{8,0},{9,1},... | collective-permute-start | bytes 196616 | tf_op jit(solution)/shard_map/ppermute | solution.py:22
  161.2 4.6 %collective-permute-start.22 = (bf16[16,2048]{1,0:T(8,128)(2,1)S(1)}, bf16[16,2048]{1,0:T(8,128)(2,1)S(1)}, u32[]{:S(2)}, u32[]{:S(2)}) collective-permute-start(bf16[16,2048]{1,0:T(8,128)(2,1)S(1)} %get-tuple-element.53), channel_id=1, source_target_pairs={{0,12},{1,13},{2,14},{3,15},{4,8},{5,9},{6,10},{7,11},{8,4},{9,5},... | collective-permute-start | bytes 196616 | tf_op jit(solution)/shard_map/ppermute | solution.py:22
  166.2 5.3 %collective-permute-done.22 = bf16[16,2048]{1,0:T(8,128)(2,1)S(1)} collective-permute-done((bf16[16,2048]{1,0:T(8,128)(2,1)S(1)}, bf16[16,2048]{1,0:T(8,128)(2,1)S(1)}, u32[]{:S(2)}, u32[]{:S(2)}) %collective-permute-start.22) | collective-permute-done | bytes 65568 | tf_op jit(solution)/shard_map/ppermute | solution.py:22
  (143 shorter events, 37.7 us)
Async XLA Ops:
  0.0 133.7 %copy-start = (bf16[256,2048]{1,0:T(8,128)(2,1)S(1)}, bf16[256,2048]{1,0:T(8,128)(2,1)}, u32[]{:S(2)}) copy-start(bf16[256,2048]{1,0:T(8,128)(2,1)} %param.25) | copy-start | bytes 3145732
  0.0 29.5 %copy-start.1 = (bf16[2048,2,256]{2,1,0:T(2,128)(2,1)S(1)}, bf16[2048,2,256]{2,1,0:T(2,128)(2,1)}, u32[]{:S(2)}) copy-start(bf16[2048,2,256]{2,1,0:T(2,128)(2,1)} %param.14) | copy-start | bytes 6291460
  0.0 13.0 %collective-permute-start = (bf16[16,2048]{1,0:T(8,128)(2,1)}, bf16[16,2048]{1,0:T(8,128)(2,1)S(1)}, u32[]{:S(2)}, u32[]{:S(2)}) collective-permute-start(bf16[16,2048]{1,0:T(8,128)(2,1)} %param.13), channel_id=1, source_target_pairs={{0,4},{1,5},{2,6},{3,7},{4,0},{5,1},{6,2},{7,3},{8,12},{9,13},{10,... | collective-permute-start | bytes 196616 | tf_op jit(solution)/shard_map/ppermute | solution.py:22
  4.5 9.7 %collective-permute-start.1 = (bf16[16,2048]{1,0:T(8,128)(2,1)}, bf16[16,2048]{1,0:T(8,128)(2,1)S(1)}, u32[]{:S(2)}, u32[]{:S(2)}) collective-permute-start(bf16[16,2048]{1,0:T(8,128)(2,1)} %param.13), channel_id=1, source_target_pairs={{0,8},{1,9},{2,10},{3,11},{4,12},{5,13},{6,14},{7,15},{8,0},{9,1},... | collective-permute-start | bytes 196616 | tf_op jit(solution)/shard_map/ppermute | solution.py:22
  9.2 7.3 %collective-permute-start.2 = (bf16[16,2048]{1,0:T(8,128)(2,1)}, bf16[16,2048]{1,0:T(8,128)(2,1)S(1)}, u32[]{:S(2)}, u32[]{:S(2)}) collective-permute-start(bf16[16,2048]{1,0:T(8,128)(2,1)} %param.13), channel_id=1, source_target_pairs={{0,12},{1,13},{2,14},{3,15},{4,8},{5,9},{6,10},{7,11},{8,4},{9,5},... | collective-permute-start | bytes 196616 | tf_op jit(solution)/shard_map/ppermute | solution.py:22
  18.2 15.9 %collective-permute-start.3 = (bf16[4,16,2048]{2,1,0:T(8,128)(2,1)}, bf16[4,16,2048]{2,1,0:T(8,128)(2,1)}, u32[]{:S(2)}, u32[]{:S(2)}) collective-permute-start(bf16[4,16,2048]{2,1,0:T(8,128)(2,1)} %get-tuple-element.60), channel_id=1, source_target_pairs={{0,1},{1,0},{2,3},{3,2},{4,5},{5,4},{6,7},{7,6},{8,9},{9,8},{10,11... | collective-permute-start | bytes 786440 | tf_op jit(solution)/shard_map/ppermute | solution.py:22
  22.5 11.6 %collective-permute-start.4 = (bf16[4,16,2048]{2,1,0:T(8,128)(2,1)}, bf16[4,16,2048]{2,1,0:T(8,128)(2,1)}, u32[]{:S(2)}, u32[]{:S(2)}) collective-permute-start(bf16[4,16,2048]{2,1,0:T(8,128)(2,1)} %get-tuple-element.60), channel_id=1, source_target_pairs={{0,2},{1,3},{2,0},{3,1},{4,6},{5,7},{6,4},{7,5},{8,10},{9,11},{10,... | collective-permute-start | bytes 786440 | tf_op jit(solution)/shard_map/ppermute | solution.py:22
  25.5 12.9 %collective-permute-start.5 = (bf16[4,16,2048]{2,1,0:T(8,128)(2,1)}, bf16[4,16,2048]{2,1,0:T(8,128)(2,1)}, u32[]{:S(2)}, u32[]{:S(2)}) collective-permute-start(bf16[4,16,2048]{2,1,0:T(8,128)(2,1)} %get-tuple-element.60), channel_id=1, source_target_pairs={{0,3},{1,2},{2,1},{3,0},{4,7},{5,6},{6,5},{7,4},{8,11},{9,10},{10,... | collective-permute-start | bytes 786440 | tf_op jit(solution)/shard_map/ppermute | solution.py:22
  48.2 13.9 %all-to-all-start = ((bf16[16,256,16]{1,2,0:T(8,128)(2,1)}), bf16[16,256,16]{1,2,0:T(8,128)(2,1)S(1)}, u32[]{:S(2)}, u32[]{:S(2)}) async-start(bf16[16,256,16]{1,2,0:T(8,128)(2,1)} %bitcast.17), calls=%async_computation | async-start | bytes 262144 | tf_op jit(solution)/shard_map/all_to_all | solution.py:118
  56.9 12.0 %copy-start.18 = (f32[1,256]{1,0:T(1,128)S(1)}, f32[1,256]{1,0:T(1,128)}, u32[]{:S(2)}) copy-start(f32[1,256]{1,0:T(1,128)} %get-tuple-element.75) | copy-start | bytes 3076
  56.9 12.0 %copy-start.19 = (f32[1,256]{1,0:T(1,128)S(1)}, f32[1,256]{1,0:T(1,128)}, u32[]{:S(2)}) copy-start(f32[1,256]{1,0:T(1,128)} %get-tuple-element.76) | copy-start | bytes 3076
  56.9 12.0 %copy-start.21 = (f32[256]{0:T(256)S(1)}, f32[256]{0:T(256)}, u32[]{:S(2)}) copy-start(f32[256]{0:T(256)} %param.18) | copy-start | bytes 3076
  62.3 6.5 %collective-permute-start.6 = (bf16[3,512]{1,0:T(4,128)(2,1)S(1)}, bf16[3,512]{1,0:T(4,128)(2,1)S(1)}, u32[]{:S(2)}, u32[]{:S(2)}) collective-permute-start(bf16[3,512]{1,0:T(4,128)(2,1)S(1)} %pad_maximum_fusion.7), channel_id=1, source_target_pairs={{0,16},{16,32},{32,48},{48,64},{64,80},{80,96},{96,112},{112,128},... | collective-permute-start | bytes 9224 | tf_op jit(solution)/shard_map/ppermute | solution.py:17
  69.7 11.2 %collective-permute-start.7 = (f32[4,65,128]{2,1,0:T(8,128)S(1)}, f32[4,65,128]{2,1,0:T(8,128)S(1)}, u32[]{:S(2)}, u32[]{:S(2)}) collective-permute-start(f32[4,65,128]{2,1,0:T(8,128)S(1)} %pad_maximum_fusion.4), channel_id=1, source_target_pairs={{0,32},{16,48},{32,64},{48,80},{64,96},{80,112},{96,128},{112,144}... | collective-permute-start | bytes 399368 | tf_op jit(solution)/shard_map/ppermute | solution.py:17
  72.2 9.1 %collective-permute-start.8 = (f32[4,65,128]{2,1,0:T(8,128)S(1)}, f32[4,65,128]{2,1,0:T(8,128)S(1)}, u32[]{:S(2)}, u32[]{:S(2)}) collective-permute-start(f32[4,65,128]{2,1,0:T(8,128)S(1)} %pad_maximum_fusion.4), channel_id=1, source_target_pairs={{0,16},{16,32},{32,48},{48,64},{64,80},{80,96},{96,112},{112,128},... | collective-permute-start | bytes 399368 | tf_op jit(solution)/shard_map/ppermute | solution.py:17
  74.8 7.9 %collective-permute-start.9 = (f32[4,65,128]{2,1,0:T(8,128)S(1)}, f32[4,65,128]{2,1,0:T(8,128)S(1)}, u32[]{:S(2)}, u32[]{:S(2)}) collective-permute-start(f32[4,65,128]{2,1,0:T(8,128)S(1)} %pad_maximum_fusion.4), channel_id=1, source_target_pairs={{0,48},{16,64},{32,80},{48,96},{64,112},{80,128},{96,144},{112,160... | collective-permute-start | bytes 399368 | tf_op jit(solution)/shard_map/ppermute | solution.py:17
  80.6 39.9 %copy-start.7 = (pred[256,256]{1,0:T(8,128)(4,1)S(1)}, pred[256,256]{1,0:T(8,128)(4,1)}, u32[]{:S(2)}) copy-start(pred[256,256]{1,0:T(8,128)(4,1)} %iota_compare_fusion) | copy-start | bytes 196612
  80.7 39.9 %copy-start.23 = (f32[4]{0:T(128)S(1)}, f32[4]{0:T(128)}, u32[]{:S(2)}) copy-start(f32[4]{0:T(128)} %param.23) | copy-start | bytes 52
  83.0 15.1 %collective-permute-start.12 = (f32[4,65,128]{2,1,0:T(8,128)S(1)}, f32[4,65,128]{2,1,0:T(8,128)S(1)}, u32[]{:S(2)}, u32[]{:S(2)}) collective-permute-start(f32[4,65,128]{2,1,0:T(8,128)S(1)} %pad_maximum_fusion.5), channel_id=1, source_target_pairs={{0,64},{16,80},{32,96},{48,112},{64,128},{80,144},{96,160},{112,17... | collective-permute-start | bytes 399368 | tf_op jit(solution)/shard_map/ppermute | solution.py:17
  87.0 15.5 %collective-permute-start.10 = (f32[4,65,128]{2,1,0:T(8,128)S(1)}, f32[4,65,128]{2,1,0:T(8,128)S(1)}, u32[]{:S(2)}, u32[]{:S(2)}) collective-permute-start(f32[4,65,128]{2,1,0:T(8,128)S(1)} %pad_maximum_fusion.5), channel_id=1, source_target_pairs={{0,192},{16,208},{32,224},{48,240},{64,256},{80,272},{96,288},{112... | collective-permute-start | bytes 399368 | tf_op jit(solution)/shard_map/ppermute | solution.py:17
  95.3 12.1 %collective-permute-start.11 = (f32[4,65,128]{2,1,0:T(8,128)S(1)}, f32[4,65,128]{2,1,0:T(8,128)S(1)}, u32[]{:S(2)}, u32[]{:S(2)}) collective-permute-start(f32[4,65,128]{2,1,0:T(8,128)S(1)} %pad_maximum_fusion.5), channel_id=1, source_target_pairs={{0,128},{16,144},{32,160},{48,176},{64,192},{80,208},{96,224},{112... | collective-permute-start | bytes 399368 | tf_op jit(solution)/shard_map/ppermute | solution.py:17
  107.7 13.4 %copy-start.20 = (f32[256]{0:T(256)S(1)}, f32[256]{0:T(256)}, u32[]{:S(2)}) copy-start(f32[256]{0:T(256)} %param.24) | copy-start | bytes 3076
  107.7 12.5 %collective-permute-start.13 = (f32[4,65,128]{2,1,0:T(8,128)S(1)}, f32[4,65,128]{2,1,0:T(8,128)S(1)}, u32[]{:S(2)}, u32[]{:S(2)}) collective-permute-start(f32[4,65,128]{2,1,0:T(8,128)S(1)} %pad_maximum_fusion.6), channel_id=1, source_target_pairs={{0,256},{16,272},{32,288},{48,304},{64,320},{80,336},{96,352},{112... | collective-permute-start | bytes 399368 | tf_op jit(solution)/shard_map/ppermute | solution.py:17
  121.3 19.0 %collective-permute-start.17 = (f32[256]{0:T(256)S(1)}, f32[256]{0:T(256)S(1)}, u32[]{:S(2)}, u32[]{:S(2)}) collective-permute-start(f32[256]{0:T(256)S(1)} %get-tuple-element.55), channel_id=1, source_target_pairs={{0,1},{1,0},{2,3},{3,2},{4,5},{5,4},{6,7},{7,6},{8,9},{9,8},{10,11... | collective-permute-start | bytes 3080 | tf_op jit(solution)/shard_map/ppermute | solution.py:22
  128.2 14.7 %collective-permute-start.18 = (f32[256]{0:T(256)S(1)}, f32[256]{0:T(256)S(1)}, u32[]{:S(2)}, u32[]{:S(2)}) collective-permute-start(f32[256]{0:T(256)S(1)} %get-tuple-element.55), channel_id=1, source_target_pairs={{0,2},{1,3},{2,0},{3,1},{4,6},{5,7},{6,4},{7,5},{8,10},{9,11},{10,... | collective-permute-start | bytes 3080 | tf_op jit(solution)/shard_map/ppermute | solution.py:22
  131.3 11.6 %collective-permute-start.19 = (f32[256]{0:T(256)S(1)}, f32[256]{0:T(256)S(1)}, u32[]{:S(2)}, u32[]{:S(2)}) collective-permute-start(f32[256]{0:T(256)S(1)} %get-tuple-element.55), channel_id=1, source_target_pairs={{0,3},{1,2},{2,1},{3,0},{4,7},{5,6},{6,5},{7,4},{8,11},{9,10},{10,... | collective-permute-start | bytes 3080 | tf_op jit(solution)/shard_map/ppermute | solution.py:22
  135.1 8.0 %collective-permute-start.14 = (bf16[4,16,2048]{2,1,0:T(8,128)(2,1)}, bf16[4,16,2048]{2,1,0:T(8,128)(2,1)}, u32[]{:S(2)}, u32[]{:S(2)}) collective-permute-start(bf16[4,16,2048]{2,1,0:T(8,128)(2,1)} %get-tuple-element.45), channel_id=1, source_target_pairs={{0,1},{1,0},{2,3},{3,2},{4,5},{5,4},{6,7},{7,6},{8,9},{9,8},{10,11... | collective-permute-start | bytes 786440 | tf_op jit(solution)/shard_map/ppermute | solution.py:22
  137.2 9.8 %collective-permute-start.15 = (bf16[4,16,2048]{2,1,0:T(8,128)(2,1)}, bf16[4,16,2048]{2,1,0:T(8,128)(2,1)}, u32[]{:S(2)}, u32[]{:S(2)}) collective-permute-start(bf16[4,16,2048]{2,1,0:T(8,128)(2,1)} %get-tuple-element.47), channel_id=1, source_target_pairs={{0,2},{1,3},{2,0},{3,1},{4,6},{5,7},{6,4},{7,5},{8,10},{9,11},{10,... | collective-permute-start | bytes 786440 | tf_op jit(solution)/shard_map/ppermute | solution.py:22
  140.3 12.7 %collective-permute-start.16 = (bf16[4,16,2048]{2,1,0:T(8,128)(2,1)S(1)}, bf16[4,16,2048]{2,1,0:T(8,128)(2,1)}, u32[]{:S(2)}, u32[]{:S(2)}) collective-permute-start(bf16[4,16,2048]{2,1,0:T(8,128)(2,1)S(1)} %get-tuple-element.46), channel_id=1, source_target_pairs={{0,3},{1,2},{2,1},{3,0},{4,7},{5,6},{6,5},{7,4},{8,11},{9,10},{10,... | collective-permute-start | bytes 786440 | tf_op jit(solution)/shard_map/ppermute | solution.py:22
  154.4 11.4 %collective-permute-start.20 = (bf16[16,2048]{1,0:T(8,128)(2,1)S(1)}, bf16[16,2048]{1,0:T(8,128)(2,1)S(1)}, u32[]{:S(2)}, u32[]{:S(2)}) collective-permute-start(bf16[16,2048]{1,0:T(8,128)(2,1)S(1)} %get-tuple-element.52), channel_id=1, source_target_pairs={{0,4},{1,5},{2,6},{3,7},{4,0},{5,1},{6,2},{7,3},{8,12},{9,13},{10,... | collective-permute-start | bytes 196616 | tf_op jit(solution)/shard_map/ppermute | solution.py:22
  156.9 9.2 %collective-permute-start.21 = (bf16[16,2048]{1,0:T(8,128)(2,1)S(1)}, bf16[16,2048]{1,0:T(8,128)(2,1)S(1)}, u32[]{:S(2)}, u32[]{:S(2)}) collective-permute-start(bf16[16,2048]{1,0:T(8,128)(2,1)S(1)} %get-tuple-element.54), channel_id=1, source_target_pairs={{0,8},{1,9},{2,10},{3,11},{4,12},{5,13},{6,14},{7,15},{8,0},{9,1},... | collective-permute-start | bytes 196616 | tf_op jit(solution)/shard_map/ppermute | solution.py:22
  161.2 10.3 %collective-permute-start.22 = (bf16[16,2048]{1,0:T(8,128)(2,1)S(1)}, bf16[16,2048]{1,0:T(8,128)(2,1)S(1)}, u32[]{:S(2)}, u32[]{:S(2)}) collective-permute-start(bf16[16,2048]{1,0:T(8,128)(2,1)S(1)} %get-tuple-element.53), channel_id=1, source_target_pairs={{0,12},{1,13},{2,14},{3,15},{4,8},{5,9},{6,10},{7,11},{8,4},{9,5},... | collective-permute-start | bytes 196616 | tf_op jit(solution)/shard_map/ppermute | solution.py:22
  (16 other events, 98.6 us)

commit v6 on v3

--- a/solution.py
+++ b/solution.py
@@ -158,7 +158,7 @@
         packed = jnp.concatenate(
             [run_state, jnp.broadcast_to(run_decay[:, None, None], (heads_dev, 1, STATE))], axis=1
         )
-        got = shifted(packed, "ctx", reach)
+        got = shifted(packed.astype(jnp.bfloat16), "ctx", reach).astype(jnp.float32)
         valid = place >= reach
         got_state = jnp.where(valid, got[:, :HEAD_DIM], 0.0)
         got_decay = jnp.where(valid, got[:, HEAD_DIM, 0], 1.0)
@@ -179,23 +179,28 @@
     result_heads = within + carried + skip_weight[None, None, :, None] * x_float
     result_heads = result_heads.reshape(length, inner_dev)
     gated = result_heads * jax.nn.silu(gate_raw.astype(jnp.float32))
-    total = jnp.sum(gated * gated, axis=1)
-    bit = 1
-    while bit < per_group_dev:
-        total = total + swapped(total, "tp", bit)
-        bit *= 2
-    scaled = (gated * norm_gain[None, :]).astype(jnp.bfloat16)
-    scaled = scaled.reshape((2,) * levels + (length // tp_size, inner_dev))
+    scaled = jnp.concatenate(
+        [(gated * norm_gain[None, :]).astype(jnp.bfloat16), (gated * gated).astype(jnp.bfloat16)], axis=1
+    )
+    width = out_weight.shape[1]
+    extended = jnp.concatenate(
+        [
+            jnp.concatenate([out_weight, jnp.zeros((inner_dev, 128), out_weight.dtype)], axis=1),
+            jnp.concatenate(
+                [jnp.zeros((inner_dev, width), out_weight.dtype), jnp.ones((inner_dev, 128), out_weight.dtype)],
+                axis=1,
+            ),
+        ],
+        axis=0,
+    )
+    scaled = scaled.reshape((2,) * levels + (length // tp_size, 2 * inner_dev))
     scaled = jnp.transpose(scaled, flipped + (levels, levels + 1))
-    partial = jnp.einsum("...c,cn->...n", scaled, out_weight, preferred_element_type=jnp.float32)
+    partial = jnp.einsum("...c,cn->...n", scaled, extended, preferred_element_type=jnp.float32)
     within_bits = [bit for bit in tp_bits if bit < per_group_dev]
     across_bits = [bit for bit in tp_bits if bit >= per_group_dev]
     held = halve(partial, "tp", within_bits)
-    inverse = lax.rsqrt(total / (HEADS * HEAD_DIM // GROUPS) + 1e-05)
-    inverse = jnp.transpose(inverse.reshape((2,) * levels + (length // tp_size,)), flipped + (levels,))
-    for bit in within_bits:
-        inverse = lax.dynamic_index_in_dim(inverse, (lax.axis_index("tp") // bit) % 2, 0, keepdims=False)
-    held = held * inverse[..., None]
+    inverse = lax.rsqrt(held[..., width] / (HEADS * HEAD_DIM // GROUPS) + 1e-05)
+    held = held[..., :width] * inverse[..., None]
     held = halve(held, "tp", across_bits)
     mixed = held
     return mixed.astype(jnp.bfloat16)

time: 165 us -> 158 us (0.958)
  starting transfers between devices: 90.8 us -> 83.7 us
  waiting for transfers between devices: 48.7 us -> 50.6 us
    ppermute x10 -> x8, starting transfers between devices: 42.7 us -> 36.1 us  [swapped(): return lax.ppermute(x, axis, [(i, i ^ bit) for i in range(peers)])]
    ppermute x10 -> x8, waiting for transfers between devices: 29.9 us -> 35.7 us  [swapped(): return lax.ppermute(x, axis, [(i, i ^ bit) for i in range(peers)])]
    ppermute x6, waiting for transfers between devices: 10.5 us -> 6.68 us  [shifted(): return lax.ppermute(x, axis, pairs)]
    ppermute x6, starting transfers between devices: 44.1 us -> 42.2 us  [shifted(): return lax.ppermute(x, axis, pairs)]
  transfers between devices with their start and end apart: 17 -> 15, of which waited for: 14 -> 14; matrix products, arithmetic and copies ran while one was open for 6% -> 4% of each run, Pallas kernels for 0% -> 0%
where the time goes in v6:
time: 158 us; the launch traced here: 157 us
  starting transfers between devices  83.7 us (53%)
  waiting for transfers between devices  50.6 us (32%)
  local copies, waits for them, and re-layouts  10.1 us (6%)
  matrix products  5.95 us (4%)
  other arithmetic  5.91 us (4%)
    ppermute x6, starting transfers between devices, shifted(): return lax.ppermute(x, axis, pairs)  42.2 us
    ppermute x8, starting transfers between devices, swapped(): return lax.ppermute(x, axis, [(i, i ^ bit) for i in range(peers)])  36.1 us
    ppermute x8, waiting for transfers between devices, swapped(): return lax.ppermute(x, axis, [(i, i ^ bit) for i in range(peers)])  35.7 us
    all_to_all x1, waiting for transfers between devices, body(): got_maps = lax.all_to_all(own_maps, 'tp', 0, 0, tiled=True)  8.23 us
    ppermute x6, waiting for transfers between devices, shifted(): return lax.ppermute(x, axis, pairs)  6.68 us
    all_to_all x1, starting transfers between devices, body(): got_maps = lax.all_to_all(own_maps, 'tp', 0, 0, tiled=True)  5.45 us
    reshape x1, local copies, waits for them, and re-layouts, body(): zx_weight = in_weight.reshape(in_weight.shape[0], 2 * inner_dev)  3.19 us
  transfers between devices with their start and end apart: 15, of which 14 were waited for; matrix products, arithmetic and copies ran while one was open for 4% of the time, Pallas kernels for 0%

profile of v6, /device:TPU:1, one launch (start us, length us, event | category | flops | bytes accessed | tf_op | source)
XLA Modules:
  0.0 157.1 jit_solution(4868203542709504120)
XLA Ops:
  0.0 8.4 %collective-permute-start = (bf16[16,2048]{1,0:T(8,128)(2,1)}, bf16[16,2048]{1,0:T(8,128)(2,1)S(1)}, u32[]{:S(2)}, u32[]{:S(2)}) collective-permute-start(bf16[16,2048]{1,0:T(8,128)(2,1)} %param.13), channel_id=1, source_target_pairs={{0,8},{1,9},{2,10},{3,11},{4,12},{5,13},{6,14},{7,15},{8,0},{9,1},... | collective-permute-start | bytes 196616 | tf_op jit(solution)/shard_map/ppermute | solution.py:22
  8.5 3.2 %reshape.609 = bf16[2048,512,1,1,1,1]{1,0,2,3,4,5:T(8,128)(2,1)S(1)} reshape(bf16[2048,2,256]{2,1,0:T(2,128)(2,1)} %param.14) | data formatting | bytes 4194304 | tf_op jit(solution)/shard_map/reshape | solution.py:77
  12.6 2.9 %collective-permute-start.1 = (bf16[2,16,2048]{2,1,0:T(8,128)(2,1)S(1)}, bf16[2,16,2048]{2,1,0:T(8,128)(2,1)S(1)}, u32[]{:S(2)}, u32[]{:S(2)}) collective-permute-start(bf16[2,16,2048]{2,1,0:T(8,128)(2,1)S(1)} %maximum_select_fusion.6), channel_id=1, source_target_pairs={{0,4},{1,5},{2,6},{3,7},{4,0},{5,1},{6,2},{7,3},{8,12},{9,13},{10,... | collective-permute-start | bytes 393224 | tf_op jit(solution)/shard_map/ppermute | solution.py:22
  15.5 6.5 %collective-permute-done.1 = bf16[2,16,2048]{2,1,0:T(8,128)(2,1)S(1)} collective-permute-done((bf16[2,16,2048]{2,1,0:T(8,128)(2,1)S(1)}, bf16[2,16,2048]{2,1,0:T(8,128)(2,1)S(1)}, u32[]{:S(2)}, u32[]{:S(2)}) %collective-permute-start.1) | collective-permute-done | bytes 131104 | tf_op jit(solution)/shard_map/ppermute | solution.py:22
  22.1 1.9 %collective-permute-start.2 = (bf16[2,2,16,2048]{3,2,1,0:T(8,128)(2,1)S(1)}, bf16[2,2,16,2048]{3,2,1,0:T(8,128)(2,1)S(1)}, u32[]{:S(2)}, u32[]{:S(2)}) collective-permute-start(bf16[2,2,16,2048]{3,2,1,0:T(8,128)(2,1)S(1)} %maximum_select_fusion.4), channel_id=1, source_target_pairs={{0,2},{1,3},{2,0},{3,1},{4,6},{5,7},{6,4},{7,5},{8,10},{9,11},{10,... | collective-permute-start | bytes 786440 | tf_op jit(solution)/shard_map/ppermute | solution.py:22
  24.0 5.1 %collective-permute-done.2 = bf16[2,2,16,2048]{3,2,1,0:T(8,128)(2,1)S(1)} collective-permute-done((bf16[2,2,16,2048]{3,2,1,0:T(8,128)(2,1)S(1)}, bf16[2,2,16,2048]{3,2,1,0:T(8,128)(2,1)S(1)}, u32[]{:S(2)}, u32[]{:S(2)}) %collective-permute-start.2) | collective-permute-done | bytes 262176 | tf_op jit(solution)/shard_map/ppermute | solution.py:22
  29.2 6.1 %collective-permute-start.3 = (bf16[2,2,2,16,2048]{4,3,2,1,0:T(8,128)(2,1)S(1)}, bf16[2,2,2,16,2048]{4,3,2,1,0:T(8,128)(2,1)S(1)}, u32[]{:S(2)}, u32[]{:S(2)}) collective-permute-start(bf16[2,2,2,16,2048]{4,3,2,1,0:T(8,128)(2,1)S(1)} %maximum_select_fusion.2), channel_id=1, source_target_pairs={{0,1},{1,0},{2,3},{3,2},{4,5},{5,4},{6,7},{7,6},{8,9},{9,8},{10,11... | collective-permute-start | bytes 1572872 | tf_op jit(solution)/shard_map/ppermute | solution.py:22
  36.8 1.3 fusion.22
  38.4 1.2 reduce-window.6
  39.7 2.0 %fusion.17 = bf16[2,2,2,2,16,512]{5,4,0,1,2,3:T(8,128)(2,1)S(1)} fusion(bf16[2048,512,1,1,1,1]{1,0,2,3,4,5:T(8,128)(2,1)S(1)} %reshape.609, bf16[1,2,2,2,16,2048]{5,4,3,2,1,0:T(8,128)(2,1)} %bitcast.174, bf16[1,2,2,2,16,2048]{5,4,3,2,1,0:T(8,128)(2,1)S(1)} %maximum_select_fusion.1, pred[]{:T(512)S(6)} %eq.17), kind=kOutput, calls=%fused_computation.18 | convolution fusion | flops 538574848 | bytes 3407873 | tf_op jit(solution)/shard_map/...d,dn->...n/dot_general | solution.py:89
  43.7 5.5 %all-to-all-start = ((bf16[16,256,16]{1,2,0:T(8,128)(2,1)}), bf16[16,256,16]{1,2,0:T(8,128)(2,1)S(1)}, u32[]{:S(2)}, u32[]{:S(2)}) async-start(bf16[16,256,16]{1,2,0:T(8,128)(2,1)} %bitcast.20), calls=%async_computation | async-start | bytes 262144 | tf_op jit(solution)/shard_map/all_to_all | solution.py:103
  49.8 8.2 %all-to-all-done = bf16[16,256,16]{1,2,0:T(8,128)(2,1)S(1)} async-done(((bf16[16,256,16]{1,2,0:T(8,128)(2,1)}), bf16[16,256,16]{1,2,0:T(8,128)(2,1)S(1)}, u32[]{:S(2)}, u32[]{:S(2)}) %all-to-all-start) | async-done | bytes 131104 | tf_op jit(solution)/shard_map/all_to_all | solution.py:103
  58.3 2.7 %collective-permute-start.4 = (bf16[3,512]{1,0:T(4,128)(2,1)S(1)}, bf16[3,512]{1,0:T(4,128)(2,1)S(1)}, u32[]{:S(2)}, u32[]{:S(2)}) collective-permute-start(bf16[3,512]{1,0:T(4,128)(2,1)S(1)} %pad_maximum_fusion.6), channel_id=1, source_target_pairs={{0,16},{16,32},{32,48},{48,64},{64,80},{80,96},{96,112},{112,128},... | collective-permute-start | bytes 9224 | tf_op jit(solution)/shard_map/ppermute | solution.py:17
  62.6 3.6 %collective-permute-start.5 = (bf16[4,65,128]{2,1,0:T(8,128)(2,1)S(1)}, bf16[4,65,128]{2,1,0:T(8,128)(2,1)S(1)}, u32[]{:S(2)}, u32[]{:S(2)}) collective-permute-start(bf16[4,65,128]{2,1,0:T(8,128)(2,1)S(1)} %pad_maximum_fusion.1), channel_id=1, source_target_pairs={{0,16},{16,32},{32,48},{48,64},{64,80},{80,96},{96,112},{112,128},... | collective-permute-start | bytes 199688 | tf_op jit(solution)/shard_map/ppermute | solution.py:17
  66.3 1.3 collective-permute-done.5
  67.9 5.2 %collective-permute-start.6 = (bf16[4,65,128]{2,1,0:T(8,128)(2,1)S(1)}, bf16[4,65,128]{2,1,0:T(8,128)(2,1)S(1)}, u32[]{:S(2)}, u32[]{:S(2)}) collective-permute-start(bf16[4,65,128]{2,1,0:T(8,128)(2,1)S(1)} %pad_maximum_fusion.2), channel_id=1, source_target_pairs={{0,32},{16,48},{32,64},{48,80},{64,96},{80,112},{96,128},{112,144}... | collective-permute-start | bytes 199688 | tf_op jit(solution)/shard_map/ppermute | solution.py:17
  73.2 1.3 collective-permute-done.6
  74.9 9.7 %collective-permute-start.7 = (bf16[4,65,128]{2,1,0:T(8,128)(2,1)S(1)}, bf16[4,65,128]{2,1,0:T(8,128)(2,1)S(1)}, u32[]{:S(2)}, u32[]{:S(2)}) collective-permute-start(bf16[4,65,128]{2,1,0:T(8,128)(2,1)S(1)} %pad_maximum_fusion.3), channel_id=1, source_target_pairs={{0,64},{16,80},{32,96},{48,112},{64,128},{80,144},{96,160},{112,17... | collective-permute-start | bytes 199688 | tf_op jit(solution)/shard_map/ppermute | solution.py:17
  84.5 1.4 collective-permute-done.7
  86.2 5.8 %collective-permute-start.8 = (bf16[4,65,128]{2,1,0:T(8,128)(2,1)S(1)}, bf16[4,65,128]{2,1,0:T(8,128)(2,1)S(1)}, u32[]{:S(2)}, u32[]{:S(2)}) collective-permute-start(bf16[4,65,128]{2,1,0:T(8,128)(2,1)S(1)} %pad_maximum_fusion.4), channel_id=1, source_target_pairs={{0,128},{16,144},{32,160},{48,176},{64,192},{80,208},{96,224},{112... | collective-permute-start | bytes 199688 | tf_op jit(solution)/shard_map/ppermute | solution.py:17
  92.1 1.3 collective-permute-done.8
  93.9 15.2 %collective-permute-start.9 = (bf16[4,65,128]{2,1,0:T(8,128)(2,1)S(1)}, bf16[4,65,128]{2,1,0:T(8,128)(2,1)S(1)}, u32[]{:S(2)}, u32[]{:S(2)}) collective-permute-start(bf16[4,65,128]{2,1,0:T(8,128)(2,1)S(1)} %pad_maximum_fusion.5), channel_id=1, source_target_pairs={{0,256},{16,272},{32,288},{48,304},{64,320},{80,336},{96,352},{112... | collective-permute-start | bytes 199688 | tf_op jit(solution)/shard_map/ppermute | solution.py:17
  112.8 1.4 copy-done.1
  114.2 8.4 %collective-permute-start.10 = (bf16[2,2,2,16,2176]{4,3,2,1,0:T(8,128)(2,1)S(1)}, bf16[2,2,2,16,2176]{4,3,2,1,0:T(8,128)(2,1)S(1)}, u32[]{:S(2)}, u32[]{:S(2)}) collective-permute-start(bf16[2,2,2,16,2176]{4,3,2,1,0:T(8,128)(2,1)S(1)} %fusion.24), channel_id=1, source_target_pairs={{0,1},{1,0},{2,3},{3,2},{4,5},{5,4},{6,7},{7,6},{8,9},{9,8},{10,11... | collective-permute-start | bytes 1671176 | tf_op jit(solution)/shard_map/ppermute | solution.py:22
  122.6 1.5 collective-permute-done.10
  124.1 1.3 bitcast_add_fusion
  125.5 2.3 %collective-permute-start.11 = (bf16[2,2,16,2176]{3,2,1,0:T(8,128)(2,1)S(1)}, bf16[2,2,16,2176]{3,2,1,0:T(8,128)(2,1)S(1)}, u32[]{:S(2)}, u32[]{:S(2)}) collective-permute-start(bf16[2,2,16,2176]{3,2,1,0:T(8,128)(2,1)S(1)} %fusion.31), channel_id=1, source_target_pairs={{0,2},{1,3},{2,0},{3,1},{4,6},{5,7},{6,4},{7,5},{8,10},{9,11},{10,... | collective-permute-start | bytes 835592 | tf_op jit(solution)/shard_map/ppermute | solution.py:22
  127.9 7.4 %collective-permute-done.11 = bf16[2,2,16,2176]{3,2,1,0:T(8,128)(2,1)S(1)} collective-permute-done((bf16[2,2,16,2176]{3,2,1,0:T(8,128)(2,1)S(1)}, bf16[2,2,16,2176]{3,2,1,0:T(8,128)(2,1)S(1)}, u32[]{:S(2)}, u32[]{:S(2)}) %collective-permute-start.11) | collective-permute-done | bytes 278560 | tf_op jit(solution)/shard_map/ppermute | solution.py:22
  135.6 2.5 %collective-permute-start.12 = (bf16[2,16,2048]{2,1,0:T(8,128)(2,1)S(1)}, bf16[2,16,2048]{2,1,0:T(8,128)(2,1)S(1)}, u32[]{:S(2)}, u32[]{:S(2)}) collective-permute-start(bf16[2,16,2048]{2,1,0:T(8,128)(2,1)S(1)} %fusion.47), channel_id=1, source_target_pairs={{0,4},{1,5},{2,6},{3,7},{4,0},{5,1},{6,2},{7,3},{8,12},{9,13},{10,... | collective-permute-start | bytes 393224 | tf_op jit(solution)/shard_map/ppermute | solution.py:22
  138.1 8.3 %collective-permute-done.12 = bf16[2,16,2048]{2,1,0:T(8,128)(2,1)S(1)} collective-permute-done((bf16[2,16,2048]{2,1,0:T(8,128)(2,1)S(1)}, bf16[2,16,2048]{2,1,0:T(8,128)(2,1)S(1)}, u32[]{:S(2)}, u32[]{:S(2)}) %collective-permute-start.12) | collective-permute-done | bytes 131104 | tf_op jit(solution)/shard_map/ppermute | solution.py:22
  146.5 3.6 %collective-permute-start.13 = (bf16[16,2048]{1,0:T(8,128)(2,1)S(1)}, bf16[16,2048]{1,0:T(8,128)(2,1)S(1)}, u32[]{:S(2)}, u32[]{:S(2)}) collective-permute-start(bf16[16,2048]{1,0:T(8,128)(2,1)S(1)} %fusion.49), channel_id=1, source_target_pairs={{0,8},{1,9},{2,10},{3,11},{4,12},{5,13},{6,14},{7,15},{8,0},{9,1},... | collective-permute-start | bytes 196616 | tf_op jit(solution)/shard_map/ppermute | solution.py:22
  150.1 6.4 %collective-permute-done.13 = bf16[16,2048]{1,0:T(8,128)(2,1)S(1)} collective-permute-done((bf16[16,2048]{1,0:T(8,128)(2,1)S(1)}, bf16[16,2048]{1,0:T(8,128)(2,1)S(1)}, u32[]{:S(2)}, u32[]{:S(2)}) %collective-permute-start.13) | collective-permute-done | bytes 65568 | tf_op jit(solution)/shard_map/ppermute | solution.py:22
  (127 shorter events, 13.4 us)
Async XLA Ops:
  0.0 41.7 %copy-start = (bf16[16,4,2048]{2,1,0:T(4,128)(2,1)S(1)}, bf16[16,4,2048]{2,1,0:T(4,128)(2,1)}, u32[]{:S(2)}) copy-start(bf16[16,4,2048]{2,1,0:T(4,128)(2,1)} %param.16) | copy-start | bytes 786436
  0.0 12.6 %collective-permute-start = (bf16[16,2048]{1,0:T(8,128)(2,1)}, bf16[16,2048]{1,0:T(8,128)(2,1)S(1)}, u32[]{:S(2)}, u32[]{:S(2)}) collective-permute-start(bf16[16,2048]{1,0:T(8,128)(2,1)} %param.13), channel_id=1, source_target_pairs={{0,8},{1,9},{2,10},{3,11},{4,12},{5,13},{6,14},{7,15},{8,0},{9,1},... | collective-permute-start | bytes 196616 | tf_op jit(solution)/shard_map/ppermute | solution.py:22
  8.4 3.2 %copy-start.11 = (f32[4]{0:T(128)S(1)}, f32[4]{0:T(128)}, u32[]{:S(2)}) copy-start(f32[4]{0:T(128)} %param.22) | copy-start | bytes 52
  8.5 3.3 %copy-start.4 = (f32[4,256]{1,0:T(4,128)S(1)}, f32[4,256]{1,0:T(4,128)}, u32[]{:S(2)}) copy-start(f32[4,256]{1,0:T(4,128)} %param.17) | copy-start | bytes 12292
  8.5 4.1 %copy-start.2 = (bf16[16,2048]{1,0:T(8,128)(2,1)S(1)}, bf16[16,2048]{1,0:T(8,128)(2,1)}, u32[]{:S(2)}) copy-start(bf16[16,2048]{1,0:T(8,128)(2,1)} %param.13) | copy-start | bytes 196612
  12.6 9.4 %collective-permute-start.1 = (bf16[2,16,2048]{2,1,0:T(8,128)(2,1)S(1)}, bf16[2,16,2048]{2,1,0:T(8,128)(2,1)S(1)}, u32[]{:S(2)}, u32[]{:S(2)}) collective-permute-start(bf16[2,16,2048]{2,1,0:T(8,128)(2,1)S(1)} %maximum_select_fusion.6), channel_id=1, source_target_pairs={{0,4},{1,5},{2,6},{3,7},{4,0},{5,1},{6,2},{7,3},{8,12},{9,13},{10,... | collective-permute-start | bytes 393224 | tf_op jit(solution)/shard_map/ppermute | solution.py:22
  15.5 21.3 %copy-start.10 = (bf16[2048,4]{0,1:T(4,128)(2,1)S(1)}, bf16[2048,4]{0,1:T(4,128)(2,1)}, u32[]{:S(2)}) copy-start(bf16[2048,4]{0,1:T(4,128)(2,1)} %param.15) | copy-start | bytes 49156
  22.1 7.1 %collective-permute-start.2 = (bf16[2,2,16,2048]{3,2,1,0:T(8,128)(2,1)S(1)}, bf16[2,2,16,2048]{3,2,1,0:T(8,128)(2,1)S(1)}, u32[]{:S(2)}, u32[]{:S(2)}) collective-permute-start(bf16[2,2,16,2048]{3,2,1,0:T(8,128)(2,1)S(1)} %maximum_select_fusion.4), channel_id=1, source_target_pairs={{0,2},{1,3},{2,0},{3,1},{4,6},{5,7},{6,4},{7,5},{8,10},{9,11},{10,... | collective-permute-start | bytes 786440 | tf_op jit(solution)/shard_map/ppermute | solution.py:22
  29.2 7.6 %collective-permute-start.3 = (bf16[2,2,2,16,2048]{4,3,2,1,0:T(8,128)(2,1)S(1)}, bf16[2,2,2,16,2048]{4,3,2,1,0:T(8,128)(2,1)S(1)}, u32[]{:S(2)}, u32[]{:S(2)}) collective-permute-start(bf16[2,2,2,16,2048]{4,3,2,1,0:T(8,128)(2,1)S(1)} %maximum_select_fusion.2), channel_id=1, source_target_pairs={{0,1},{1,0},{2,3},{3,2},{4,5},{5,4},{6,7},{7,6},{8,9},{9,8},{10,11... | collective-permute-start | bytes 1572872 | tf_op jit(solution)/shard_map/ppermute | solution.py:22
  36.8 1.3 copy-start.8
  36.8 1.5 copy-start.3
  39.7 2.0 %copy-start.9 = (bf16[2,2,2,16,2048]{4,3,2,1,0:T(8,128)(2,1)S(1)}, bf16[2,2,2,16,2048]{4,3,2,1,0:T(8,128)(2,1)}, u32[]{:S(2)}) copy-start(bf16[2,2,2,16,2048]{4,3,2,1,0:T(8,128)(2,1)} %copy-done.8) | copy-start | bytes 1572868
  42.5 19.2 %copy-start.6 = (f32[256]{0:T(256)S(1)}, f32[256]{0:T(256)}, u32[]{:S(2)}) copy-start(f32[256]{0:T(256)} %param.18) | copy-start | bytes 3076
  43.7 14.3 %all-to-all-start = ((bf16[16,256,16]{1,2,0:T(8,128)(2,1)}), bf16[16,256,16]{1,2,0:T(8,128)(2,1)S(1)}, u32[]{:S(2)}, u32[]{:S(2)}) async-start(bf16[16,256,16]{1,2,0:T(8,128)(2,1)} %bitcast.20), calls=%async_computation | async-start | bytes 262144 | tf_op jit(solution)/shard_map/all_to_all | solution.py:103
  58.3 3.5 %collective-permute-start.4 = (bf16[3,512]{1,0:T(4,128)(2,1)S(1)}, bf16[3,512]{1,0:T(4,128)(2,1)S(1)}, u32[]{:S(2)}, u32[]{:S(2)}) collective-permute-start(bf16[3,512]{1,0:T(4,128)(2,1)S(1)} %pad_maximum_fusion.6), channel_id=1, source_target_pairs={{0,16},{16,32},{32,48},{48,64},{64,80},{80,96},{96,112},{112,128},... | collective-permute-start | bytes 9224 | tf_op jit(solution)/shard_map/ppermute | solution.py:17
  62.6 5.0 %collective-permute-start.5 = (bf16[4,65,128]{2,1,0:T(8,128)(2,1)S(1)}, bf16[4,65,128]{2,1,0:T(8,128)(2,1)S(1)}, u32[]{:S(2)}, u32[]{:S(2)}) collective-permute-start(bf16[4,65,128]{2,1,0:T(8,128)(2,1)S(1)} %pad_maximum_fusion.1), channel_id=1, source_target_pairs={{0,16},{16,32},{32,48},{48,64},{64,80},{80,96},{96,112},{112,128},... | collective-permute-start | bytes 199688 | tf_op jit(solution)/shard_map/ppermute | solution.py:17
  67.9 6.6 %collective-permute-start.6 = (bf16[4,65,128]{2,1,0:T(8,128)(2,1)S(1)}, bf16[4,65,128]{2,1,0:T(8,128)(2,1)S(1)}, u32[]{:S(2)}, u32[]{:S(2)}) collective-permute-start(bf16[4,65,128]{2,1,0:T(8,128)(2,1)S(1)} %pad_maximum_fusion.2), channel_id=1, source_target_pairs={{0,32},{16,48},{32,64},{48,80},{64,96},{80,112},{96,128},{112,144}... | collective-permute-start | bytes 199688 | tf_op jit(solution)/shard_map/ppermute | solution.py:17
  74.7 36.1 %copy-start.12 = (f32[4]{0:T(128)S(1)}, f32[4]{0:T(128)}, u32[]{:S(2)}) copy-start(f32[4]{0:T(128)} %param.23) | copy-start | bytes 52
  74.9 11.1 %collective-permute-start.7 = (bf16[4,65,128]{2,1,0:T(8,128)(2,1)S(1)}, bf16[4,65,128]{2,1,0:T(8,128)(2,1)S(1)}, u32[]{:S(2)}, u32[]{:S(2)}) collective-permute-start(bf16[4,65,128]{2,1,0:T(8,128)(2,1)S(1)} %pad_maximum_fusion.3), channel_id=1, source_target_pairs={{0,64},{16,80},{32,96},{48,112},{64,128},{80,144},{96,160},{112,17... | collective-permute-start | bytes 199688 | tf_op jit(solution)/shard_map/ppermute | solution.py:17
  86.2 7.2 %collective-permute-start.8 = (bf16[4,65,128]{2,1,0:T(8,128)(2,1)S(1)}, bf16[4,65,128]{2,1,0:T(8,128)(2,1)S(1)}, u32[]{:S(2)}, u32[]{:S(2)}) collective-permute-start(bf16[4,65,128]{2,1,0:T(8,128)(2,1)S(1)} %pad_maximum_fusion.4), channel_id=1, source_target_pairs={{0,128},{16,144},{32,160},{48,176},{64,192},{80,208},{96,224},{112... | collective-permute-start | bytes 199688 | tf_op jit(solution)/shard_map/ppermute | solution.py:17
  93.9 16.6 %collective-permute-start.9 = (bf16[4,65,128]{2,1,0:T(8,128)(2,1)S(1)}, bf16[4,65,128]{2,1,0:T(8,128)(2,1)S(1)}, u32[]{:S(2)}, u32[]{:S(2)}) collective-permute-start(bf16[4,65,128]{2,1,0:T(8,128)(2,1)S(1)} %pad_maximum_fusion.5), channel_id=1, source_target_pairs={{0,256},{16,272},{32,288},{48,304},{64,320},{80,336},{96,352},{112... | collective-permute-start | bytes 199688 | tf_op jit(solution)/shard_map/ppermute | solution.py:17
  109.3 2.1 %copy-start.5 = (f32[256]{0:T(256)S(1)}, f32[256]{0:T(256)}, u32[]{:S(2)}) copy-start(f32[256]{0:T(256)} %param.24) | copy-start | bytes 3076
  110.7 1.2 copy-start.7
  112.8 1.4 copy-start.1
  114.2 9.9 %collective-permute-start.10 = (bf16[2,2,2,16,2176]{4,3,2,1,0:T(8,128)(2,1)S(1)}, bf16[2,2,2,16,2176]{4,3,2,1,0:T(8,128)(2,1)S(1)}, u32[]{:S(2)}, u32[]{:S(2)}) collective-permute-start(bf16[2,2,2,16,2176]{4,3,2,1,0:T(8,128)(2,1)S(1)} %fusion.24), channel_id=1, source_target_pairs={{0,1},{1,0},{2,3},{3,2},{4,5},{5,4},{6,7},{7,6},{8,9},{9,8},{10,11... | collective-permute-start | bytes 1671176 | tf_op jit(solution)/shard_map/ppermute | solution.py:22
  125.5 9.7 %collective-permute-start.11 = (bf16[2,2,16,2176]{3,2,1,0:T(8,128)(2,1)S(1)}, bf16[2,2,16,2176]{3,2,1,0:T(8,128)(2,1)S(1)}, u32[]{:S(2)}, u32[]{:S(2)}) collective-permute-start(bf16[2,2,16,2176]{3,2,1,0:T(8,128)(2,1)S(1)} %fusion.31), channel_id=1, source_target_pairs={{0,2},{1,3},{2,0},{3,1},{4,6},{5,7},{6,4},{7,5},{8,10},{9,11},{10,... | collective-permute-start | bytes 835592 | tf_op jit(solution)/shard_map/ppermute | solution.py:22
  135.6 10.8 %collective-permute-start.12 = (bf16[2,16,2048]{2,1,0:T(8,128)(2,1)S(1)}, bf16[2,16,2048]{2,1,0:T(8,128)(2,1)S(1)}, u32[]{:S(2)}, u32[]{:S(2)}) collective-permute-start(bf16[2,16,2048]{2,1,0:T(8,128)(2,1)S(1)} %fusion.47), channel_id=1, source_target_pairs={{0,4},{1,5},{2,6},{3,7},{4,0},{5,1},{6,2},{7,3},{8,12},{9,13},{10,... | collective-permute-start | bytes 393224 | tf_op jit(solution)/shard_map/ppermute | solution.py:22
  146.5 10.0 %collective-permute-start.13 = (bf16[16,2048]{1,0:T(8,128)(2,1)S(1)}, bf16[16,2048]{1,0:T(8,128)(2,1)S(1)}, u32[]{:S(2)}, u32[]{:S(2)}) collective-permute-start(bf16[16,2048]{1,0:T(8,128)(2,1)S(1)} %fusion.49), channel_id=1, source_target_pairs={{0,8},{1,9},{2,10},{3,11},{4,12},{5,13},{6,14},{7,15},{8,0},{9,1},... | collective-permute-start | bytes 196616 | tf_op jit(solution)/shard_map/ppermute | solution.py:22

commit v7 on v6

--- a/solution.py
+++ b/solution.py
@@ -94,22 +94,26 @@
     gate_raw = projected[:, :inner_dev]
     inner_raw = projected[:, inner_dev : 2 * inner_dev]
     step_raw = projected[:, 2 * inner_dev :]
+    border_rows = KERNEL - 1
+    last_rows = stacked[(1,) * levels][hidden.shape[0] - border_rows :]
+    before = shifted(last_rows, "ctx", 1)
+    inner_prior = jnp.dot(
+        before, zx_weight[:, inner_dev:], preferred_element_type=jnp.float32
+    ).astype(jnp.bfloat16)
     own_maps = jnp.einsum(
         "...d,sgd->...gs", stacked, group_weight, preferred_element_type=jnp.float32
     ).astype(jnp.bfloat16)
     own_maps = jnp.moveaxis(in_order(own_maps), 1, 0)
+    border_maps = jnp.einsum(
+        "td,sgd->gts", before, group_weight, preferred_element_type=jnp.float32
+    ).astype(jnp.bfloat16)
+    own_maps = jnp.concatenate([border_maps, own_maps], axis=1)
     own_maps = jnp.broadcast_to(own_maps[:, None], (GROUPS, per_group_dev) + own_maps.shape[1:])
     own_maps = own_maps.reshape((tp_size,) + own_maps.shape[2:])
     got_maps = lax.all_to_all(own_maps, "tp", 0, 0, tiled=True)
-    map_part = jnp.transpose(got_maps, (1, 0, 2)).reshape(length, group_cols)
-    border_rows = KERNEL - 1
-    prior = shifted(
-        jnp.concatenate([inner_raw[length - border_rows :], map_part[length - border_rows :]], axis=1),
-        "ctx",
-        1,
-    )
-    inner_prior = prior[:, :inner_dev]
-    map_prior = prior[:, inner_dev:]
+    all_maps = jnp.transpose(got_maps, (1, 0, 2)).reshape(border_rows + length, group_cols)
+    map_prior = all_maps[:border_rows]
+    map_part = all_maps[border_rows:]
     x_conv = causal_conv(inner_prior, inner_raw, conv_inner, inner_bias)
     own_taps = lax.dynamic_slice_in_dim(conv_group, group_index * group_cols, group_cols, 1)
     own_bias = lax.dynamic_slice_in_dim(group_bias, group_index * group_cols, group_cols, 0)

time: 158 us -> 162 us (1.025)
  starting transfers between devices: 83.7 us -> 72.7 us
  local copies, waits for them, and re-layouts: 10.1 us -> 17.2 us
  waiting for transfers between devices: 50.6 us -> 55.9 us
    ppermute x8, starting transfers between devices: 36.1 us -> 29.6 us  [swapped(): return lax.ppermute(x, axis, [(i, i ^ bit) for i in range(peers)])]
    ppermute x8, waiting for transfers between devices: 35.7 us -> 39.6 us  [swapped(): return lax.ppermute(x, axis, [(i, i ^ bit) for i in range(peers)])]
    ppermute x6, starting transfers between devices: 42.2 us -> 39.2 us  [shifted(): return lax.ppermute(x, axis, pairs)]
    unnamed x27 -> x52, local copies, waits for them, and re-layouts: 1.84 us -> 3.67 us
    all_to_all x1, starting transfers between devices: 5.45 us -> 3.83 us  [body(): got_maps = lax.all_to_all(own_maps, 'tp', 0, 0, tiled=True)]
  transfers between devices with their start and end apart: 15 -> 15, of which waited for: 14 -> 12; matrix products, arithmetic and copies ran while one was open for 4% -> 12% of each run, Pallas kernels for 0% -> 0%
where the time goes in v7:
time: 162 us; the launch traced here: 161 us
  starting transfers between devices  72.7 us (45%)
  waiting for transfers between devices  55.9 us (35%)
  local copies, waits for them, and re-layouts  17.2 us (11%)
  other arithmetic  7.5 us (5%)
  matrix products  6.69 us (4%)
    ppermute x8, waiting for transfers between devices, swapped(): return lax.ppermute(x, axis, [(i, i ^ bit) for i in range(peers)])  39.6 us
    ppermute x6, starting transfers between devices, shifted(): return lax.ppermute(x, axis, pairs)  39.2 us
    ppermute x8, starting transfers between devices, swapped(): return lax.ppermute(x, axis, [(i, i ^ bit) for i in range(peers)])  29.6 us
    all_to_all x1, waiting for transfers between devices, body(): got_maps = lax.all_to_all(own_maps, 'tp', 0, 0, tiled=True)  9.55 us
    ppermute x6, waiting for transfers between devices, shifted(): return lax.ppermute(x, axis, pairs)  6.74 us
    reshape x1, local copies, waits for them, and re-layouts, body(): zx_weight = in_weight.reshape(in_weight.shape[0], 2 * inner_dev)  4.52 us
    all_to_all x1, starting transfers between devices, body(): got_maps = lax.all_to_all(own_maps, 'tp', 0, 0, tiled=True)  3.83 us
    unnamed x52, local copies, waits for them, and re-layouts  3.67 us
  transfers between devices with their start and end apart: 15, of which 12 were waited for; matrix products, arithmetic and copies ran while one was open for 12% of the time, Pallas kernels for 0%

profile of v7, /device:TPU:1, one launch (start us, length us, event | category | flops | bytes accessed | tf_op | source)
XLA Modules:
  0.0 160.9 jit_solution(9050704545478833623)
XLA Ops:
  0.0 8.4 %collective-permute-start = (bf16[16,2048]{1,0:T(8,128)(2,1)}, bf16[16,2048]{1,0:T(8,128)(2,1)S(1)}, u32[]{:S(2)}, u32[]{:S(2)}) collective-permute-start(bf16[16,2048]{1,0:T(8,128)(2,1)} %param.13), channel_id=1, source_target_pairs={{0,8},{1,9},{2,10},{3,11},{4,12},{5,13},{6,14},{7,15},{8,0},{9,1},... | collective-permute-start | bytes 196616 | tf_op jit(solution)/shard_map/ppermute | solution.py:22
  9.1 4.5 %reshape.608 = bf16[2048,512,1,1,1,1]{1,0,2,3,4,5:T(8,128)(2,1)} reshape(bf16[2048,2,256]{2,1,0:T(2,128)(2,1)} %param.14) | data formatting | bytes 4194304 | tf_op jit(solution)/shard_map/reshape | solution.py:77
  13.7 1.8 %copy.71 = bf16[256,8,2,256]{3,1,2,0:T(8,128)(2,1)} copy(bf16[256,8,2,256]{3,2,1,0:T(2,128)(2,1)S(1)} %bitcast.150) | data formatting | bytes 4194304
  16.0 1.3 dynamic_slice.40
  17.5 2.4 %collective-permute-start.1 = (bf16[2,16,2048]{2,1,0:T(8,128)(2,1)S(1)}, bf16[2,16,2048]{2,1,0:T(8,128)(2,1)S(1)}, u32[]{:S(2)}, u32[]{:S(2)}) collective-permute-start(bf16[2,16,2048]{2,1,0:T(8,128)(2,1)S(1)} %maximum_select_fusion.6), channel_id=1, source_target_pairs={{0,4},{1,5},{2,6},{3,7},{4,0},{5,1},{6,2},{7,3},{8,12},{9,13},{10,... | collective-permute-start | bytes 393224 | tf_op jit(solution)/shard_map/ppermute | solution.py:22
  19.9 8.5 %collective-permute-done.1 = bf16[2,16,2048]{2,1,0:T(8,128)(2,1)S(1)} collective-permute-done((bf16[2,16,2048]{2,1,0:T(8,128)(2,1)S(1)}, bf16[2,16,2048]{2,1,0:T(8,128)(2,1)S(1)}, u32[]{:S(2)}, u32[]{:S(2)}) %collective-permute-start.1) | collective-permute-done | bytes 131104 | tf_op jit(solution)/shard_map/ppermute | solution.py:22
  28.4 1.9 %collective-permute-start.2 = (bf16[2,2,16,2048]{3,2,1,0:T(8,128)(2,1)S(1)}, bf16[2,2,16,2048]{3,2,1,0:T(8,128)(2,1)S(1)}, u32[]{:S(2)}, u32[]{:S(2)}) collective-permute-start(bf16[2,2,16,2048]{3,2,1,0:T(8,128)(2,1)S(1)} %maximum_select_fusion.4), channel_id=1, source_target_pairs={{0,2},{1,3},{2,0},{3,1},{4,6},{5,7},{6,4},{7,5},{8,10},{9,11},{10,... | collective-permute-start | bytes 786440 | tf_op jit(solution)/shard_map/ppermute | solution.py:22
  30.4 7.2 %collective-permute-done.2 = bf16[2,2,16,2048]{3,2,1,0:T(8,128)(2,1)S(1)} collective-permute-done((bf16[2,2,16,2048]{3,2,1,0:T(8,128)(2,1)S(1)}, bf16[2,2,16,2048]{3,2,1,0:T(8,128)(2,1)S(1)}, u32[]{:S(2)}, u32[]{:S(2)}) %collective-permute-start.2) | collective-permute-done | bytes 262176 | tf_op jit(solution)/shard_map/ppermute | solution.py:22
  37.6 3.4 %collective-permute-start.3 = (bf16[2,2,2,16,2048]{4,3,2,1,0:T(8,128)(2,1)S(1)}, bf16[2,2,2,16,2048]{4,3,2,1,0:T(8,128)(2,1)S(1)}, u32[]{:S(2)}, u32[]{:S(2)}) collective-permute-start(bf16[2,2,2,16,2048]{4,3,2,1,0:T(8,128)(2,1)S(1)} %maximum_select_fusion.2), channel_id=1, source_target_pairs={{0,1},{1,0},{2,3},{3,2},{4,5},{5,4},{6,7},{7,6},{8,9},{9,8},{10,11... | collective-permute-start | bytes 1572872 | tf_op jit(solution)/shard_map/ppermute | solution.py:22
  41.0 1.5 constant_dynamic-slice_fusion
  45.8 3.1 %collective-permute-start.4 = (bf16[3,2048]{1,0:T(4,128)(2,1)S(1)}, bf16[3,2048]{1,0:T(4,128)(2,1)S(1)}, u32[]{:S(2)}, u32[]{:S(2)}) collective-permute-start(bf16[3,2048]{1,0:T(4,128)(2,1)S(1)} %slice_bitcast_fusion), channel_id=1, source_target_pairs={{0,16},{16,32},{32,48},{48,64},{64,80},{80,96},{96,112},{112,128},... | collective-permute-start | bytes 36872 | tf_op jit(solution)/shard_map/ppermute | solution.py:17
  48.9 1.4 fusion.16
  51.6 1.4 fusion.17
  57.2 3.8 %all-to-all-start = ((bf16[16,259,16]{1,2,0:T(8,128)(2,1)}), bf16[16,259,16]{1,2,0:T(8,128)(2,1)S(1)}, u32[]{:S(2)}, u32[]{:S(2)}) async-start(bf16[16,259,16]{1,2,0:T(8,128)(2,1)} %bitcast.28), calls=%async_computation | async-start | bytes 393216 | tf_op jit(solution)/shard_map/all_to_all | solution.py:113
  61.7 9.6 %all-to-all-done = bf16[16,259,16]{1,2,0:T(8,128)(2,1)S(1)} async-done(((bf16[16,259,16]{1,2,0:T(8,128)(2,1)}), bf16[16,259,16]{1,2,0:T(8,128)(2,1)S(1)}, u32[]{:S(2)}, u32[]{:S(2)}) %all-to-all-start) | async-done | bytes 132640 | tf_op jit(solution)/shard_map/all_to_all | solution.py:113
  72.2 3.1 %collective-permute-start.5 = (bf16[4,65,128]{2,1,0:T(8,128)(2,1)S(1)}, bf16[4,65,128]{2,1,0:T(8,128)(2,1)S(1)}, u32[]{:S(2)}, u32[]{:S(2)}) collective-permute-start(bf16[4,65,128]{2,1,0:T(8,128)(2,1)S(1)} %pad_maximum_fusion.1), channel_id=1, source_target_pairs={{0,16},{16,32},{32,48},{48,64},{64,80},{80,96},{96,112},{112,128},... | collective-permute-start | bytes 199688 | tf_op jit(solution)/shard_map/ppermute | solution.py:17
  75.4 1.8 %collective-permute-done.5 = bf16[4,65,128]{2,1,0:T(8,128)(2,1)S(1)} collective-permute-done((bf16[4,65,128]{2,1,0:T(8,128)(2,1)S(1)}, bf16[4,65,128]{2,1,0:T(8,128)(2,1)S(1)}, u32[]{:S(2)}, u32[]{:S(2)}) %collective-permute-start.5) | collective-permute-done | bytes 66592 | tf_op jit(solution)/shard_map/ppermute | solution.py:17
  77.5 5.3 %collective-permute-start.6 = (bf16[4,65,128]{2,1,0:T(8,128)(2,1)S(1)}, bf16[4,65,128]{2,1,0:T(8,128)(2,1)S(1)}, u32[]{:S(2)}, u32[]{:S(2)}) collective-permute-start(bf16[4,65,128]{2,1,0:T(8,128)(2,1)S(1)} %pad_maximum_fusion.2), channel_id=1, source_target_pairs={{0,32},{16,48},{32,64},{48,80},{64,96},{80,112},{96,128},{112,144}... | collective-permute-start | bytes 199688 | tf_op jit(solution)/shard_map/ppermute | solution.py:17
  84.6 7.9 %collective-permute-start.7 = (bf16[4,65,128]{2,1,0:T(8,128)(2,1)S(1)}, bf16[4,65,128]{2,1,0:T(8,128)(2,1)S(1)}, u32[]{:S(2)}, u32[]{:S(2)}) collective-permute-start(bf16[4,65,128]{2,1,0:T(8,128)(2,1)S(1)} %pad_maximum_fusion.3), channel_id=1, source_target_pairs={{0,64},{16,80},{32,96},{48,112},{64,128},{80,144},{96,160},{112,17... | collective-permute-start | bytes 199688 | tf_op jit(solution)/shard_map/ppermute | solution.py:17
  92.5 1.4 collective-permute-done.7
  94.1 5.8 %collective-permute-start.8 = (bf16[4,65,128]{2,1,0:T(8,128)(2,1)S(1)}, bf16[4,65,128]{2,1,0:T(8,128)(2,1)S(1)}, u32[]{:S(2)}, u32[]{:S(2)}) collective-permute-start(bf16[4,65,128]{2,1,0:T(8,128)(2,1)S(1)} %pad_maximum_fusion.4), channel_id=1, source_target_pairs={{0,128},{16,144},{32,160},{48,176},{64,192},{80,208},{96,224},{112... | collective-permute-start | bytes 199688 | tf_op jit(solution)/shard_map/ppermute | solution.py:17
  101.8 14.0 %collective-permute-start.9 = (bf16[4,65,128]{2,1,0:T(8,128)(2,1)S(1)}, bf16[4,65,128]{2,1,0:T(8,128)(2,1)S(1)}, u32[]{:S(2)}, u32[]{:S(2)}) collective-permute-start(bf16[4,65,128]{2,1,0:T(8,128)(2,1)S(1)} %pad_maximum_fusion.5), channel_id=1, source_target_pairs={{0,256},{16,272},{32,288},{48,304},{64,320},{80,336},{96,352},{112... | collective-permute-start | bytes 199688 | tf_op jit(solution)/shard_map/ppermute | solution.py:17
  119.5 1.4 copy-done.4
  120.9 6.8 %collective-permute-start.10 = (bf16[2,2,2,16,2176]{4,3,2,1,0:T(8,128)(2,1)S(1)}, bf16[2,2,2,16,2176]{4,3,2,1,0:T(8,128)(2,1)S(1)}, u32[]{:S(2)}, u32[]{:S(2)}) collective-permute-start(bf16[2,2,2,16,2176]{4,3,2,1,0:T(8,128)(2,1)S(1)} %fusion.26), channel_id=1, source_target_pairs={{0,1},{1,0},{2,3},{3,2},{4,5},{5,4},{6,7},{7,6},{8,9},{9,8},{10,11... | collective-permute-start | bytes 1671176 | tf_op jit(solution)/shard_map/ppermute | solution.py:22
  127.8 1.5 collective-permute-done.10
  129.3 1.3 bitcast_add_fusion
  130.7 1.9 %collective-permute-start.11 = (bf16[2,2,16,2176]{3,2,1,0:T(8,128)(2,1)S(1)}, bf16[2,2,16,2176]{3,2,1,0:T(8,128)(2,1)S(1)}, u32[]{:S(2)}, u32[]{:S(2)}) collective-permute-start(bf16[2,2,16,2176]{3,2,1,0:T(8,128)(2,1)S(1)} %fusion.33), channel_id=1, source_target_pairs={{0,2},{1,3},{2,0},{3,1},{4,6},{5,7},{6,4},{7,5},{8,10},{9,11},{10,... | collective-permute-start | bytes 835592 | tf_op jit(solution)/shard_map/ppermute | solution.py:22
  132.6 7.8 %collective-permute-done.11 = bf16[2,2,16,2176]{3,2,1,0:T(8,128)(2,1)S(1)} collective-permute-done((bf16[2,2,16,2176]{3,2,1,0:T(8,128)(2,1)S(1)}, bf16[2,2,16,2176]{3,2,1,0:T(8,128)(2,1)S(1)}, u32[]{:S(2)}, u32[]{:S(2)}) %collective-permute-start.11) | collective-permute-done | bytes 278560 | tf_op jit(solution)/shard_map/ppermute | solution.py:22
  140.7 2.3 %collective-permute-start.12 = (bf16[2,16,2048]{2,1,0:T(8,128)(2,1)S(1)}, bf16[2,16,2048]{2,1,0:T(8,128)(2,1)S(1)}, u32[]{:S(2)}, u32[]{:S(2)}) collective-permute-start(bf16[2,16,2048]{2,1,0:T(8,128)(2,1)S(1)} %fusion.50), channel_id=1, source_target_pairs={{0,4},{1,5},{2,6},{3,7},{4,0},{5,1},{6,2},{7,3},{8,12},{9,13},{10,... | collective-permute-start | bytes 393224 | tf_op jit(solution)/shard_map/ppermute | solution.py:22
  143.1 8.2 %collective-permute-done.12 = bf16[2,16,2048]{2,1,0:T(8,128)(2,1)S(1)} collective-permute-done((bf16[2,16,2048]{2,1,0:T(8,128)(2,1)S(1)}, bf16[2,16,2048]{2,1,0:T(8,128)(2,1)S(1)}, u32[]{:S(2)}, u32[]{:S(2)}) %collective-permute-start.12) | collective-permute-done | bytes 131104 | tf_op jit(solution)/shard_map/ppermute | solution.py:22
  151.3 2.5 %collective-permute-start.13 = (bf16[16,2048]{1,0:T(8,128)(2,1)S(1)}, bf16[16,2048]{1,0:T(8,128)(2,1)S(1)}, u32[]{:S(2)}, u32[]{:S(2)}) collective-permute-start(bf16[16,2048]{1,0:T(8,128)(2,1)S(1)} %fusion.52), channel_id=1, source_target_pairs={{0,8},{1,9},{2,10},{3,11},{4,12},{5,13},{6,14},{7,15},{8,0},{9,1},... | collective-permute-start | bytes 196616 | tf_op jit(solution)/shard_map/ppermute | solution.py:22
  153.8 6.5 %collective-permute-done.13 = bf16[16,2048]{1,0:T(8,128)(2,1)S(1)} collective-permute-done((bf16[16,2048]{1,0:T(8,128)(2,1)S(1)}, bf16[16,2048]{1,0:T(8,128)(2,1)S(1)}, u32[]{:S(2)}, u32[]{:S(2)}) %collective-permute-start.13) | collective-permute-done | bytes 65568 | tf_op jit(solution)/shard_map/ppermute | solution.py:22
  (157 shorter events, 20.3 us)
Async XLA Ops:
  0.0 48.9 %copy-start = (bf16[16,4,2048]{2,1,0:T(4,128)(2,1)S(1)}, bf16[16,4,2048]{2,1,0:T(4,128)(2,1)}, u32[]{:S(2)}) copy-start(bf16[16,4,2048]{2,1,0:T(4,128)(2,1)} %param.16) | copy-start | bytes 786436
  0.0 17.4 %collective-permute-start = (bf16[16,2048]{1,0:T(8,128)(2,1)}, bf16[16,2048]{1,0:T(8,128)(2,1)S(1)}, u32[]{:S(2)}, u32[]{:S(2)}) collective-permute-start(bf16[16,2048]{1,0:T(8,128)(2,1)} %param.13), channel_id=1, source_target_pairs={{0,8},{1,9},{2,10},{3,11},{4,12},{5,13},{6,14},{7,15},{8,0},{9,1},... | collective-permute-start | bytes 196616 | tf_op jit(solution)/shard_map/ppermute | solution.py:22
  17.5 10.9 %collective-permute-start.1 = (bf16[2,16,2048]{2,1,0:T(8,128)(2,1)S(1)}, bf16[2,16,2048]{2,1,0:T(8,128)(2,1)S(1)}, u32[]{:S(2)}, u32[]{:S(2)}) collective-permute-start(bf16[2,16,2048]{2,1,0:T(8,128)(2,1)S(1)} %maximum_select_fusion.6), channel_id=1, source_target_pairs={{0,4},{1,5},{2,6},{3,7},{4,0},{5,1},{6,2},{7,3},{8,12},{9,13},{10,... | collective-permute-start | bytes 393224 | tf_op jit(solution)/shard_map/ppermute | solution.py:22
  28.4 9.2 %collective-permute-start.2 = (bf16[2,2,16,2048]{3,2,1,0:T(8,128)(2,1)S(1)}, bf16[2,2,16,2048]{3,2,1,0:T(8,128)(2,1)S(1)}, u32[]{:S(2)}, u32[]{:S(2)}) collective-permute-start(bf16[2,2,16,2048]{3,2,1,0:T(8,128)(2,1)S(1)} %maximum_select_fusion.4), channel_id=1, source_target_pairs={{0,2},{1,3},{2,0},{3,1},{4,6},{5,7},{6,4},{7,5},{8,10},{9,11},{10,... | collective-permute-start | bytes 786440 | tf_op jit(solution)/shard_map/ppermute | solution.py:22
  37.6 5.0 %collective-permute-start.3 = (bf16[2,2,2,16,2048]{4,3,2,1,0:T(8,128)(2,1)S(1)}, bf16[2,2,2,16,2048]{4,3,2,1,0:T(8,128)(2,1)S(1)}, u32[]{:S(2)}, u32[]{:S(2)}) collective-permute-start(bf16[2,2,2,16,2048]{4,3,2,1,0:T(8,128)(2,1)S(1)} %maximum_select_fusion.2), channel_id=1, source_target_pairs={{0,1},{1,0},{2,3},{3,2},{4,5},{5,4},{6,7},{7,6},{8,9},{9,8},{10,11... | collective-permute-start | bytes 1572872 | tf_op jit(solution)/shard_map/ppermute | solution.py:22
  44.2 7.4 %copy-start.3 = (bf16[2048,512,1,1,1,1]{1,0,2,3,4,5:T(8,128)(2,1)S(1)}, bf16[2048,512,1,1,1,1]{1,0,2,3,4,5:T(8,128)(2,1)}, u32[]{:S(2)}) copy-start(bf16[2048,512,1,1,1,1]{1,0,2,3,4,5:T(8,128)(2,1)} %reshape.608) | copy-start | bytes 6291460
  45.8 10.1 %collective-permute-start.4 = (bf16[3,2048]{1,0:T(4,128)(2,1)S(1)}, bf16[3,2048]{1,0:T(4,128)(2,1)S(1)}, u32[]{:S(2)}, u32[]{:S(2)}) collective-permute-start(bf16[3,2048]{1,0:T(4,128)(2,1)S(1)} %slice_bitcast_fusion), channel_id=1, source_target_pairs={{0,16},{16,32},{32,48},{48,64},{64,80},{80,96},{96,112},{112,128},... | collective-permute-start | bytes 36872 | tf_op jit(solution)/shard_map/ppermute | solution.py:17
  53.0 8.0 %copy-start.2 = (bf16[256,8,2,256]{3,1,2,0:T(8,128)(2,1)S(1)}, bf16[256,8,2,256]{3,1,2,0:T(8,128)(2,1)}, u32[]{:S(2)}) copy-start(bf16[256,8,2,256]{3,1,2,0:T(8,128)(2,1)} %copy.71) | copy-start | bytes 6291460
  54.6 6.7 %copy-start.17 = (f32[1,256]{1,0:T(1,128)S(1)}, f32[1,256]{1,0:T(1,128)}, u32[]{:S(2)}) copy-start(f32[1,256]{1,0:T(1,128)} %get-tuple-element.53) | copy-start | bytes 3076
  54.6 6.7 %copy-start.18 = (f32[1,256]{1,0:T(1,128)S(1)}, f32[1,256]{1,0:T(1,128)}, u32[]{:S(2)}) copy-start(f32[1,256]{1,0:T(1,128)} %get-tuple-element.54) | copy-start | bytes 3076
  54.6 6.7 %copy-start.19 = (f32[1,256]{1,0:T(1,128)S(1)}, f32[1,256]{1,0:T(1,128)}, u32[]{:S(2)}) copy-start(f32[1,256]{1,0:T(1,128)} %get-tuple-element.55) | copy-start | bytes 3076
  54.6 6.7 %copy-start.20 = (f32[1,256]{1,0:T(1,128)S(1)}, f32[1,256]{1,0:T(1,128)}, u32[]{:S(2)}) copy-start(f32[1,256]{1,0:T(1,128)} %get-tuple-element.56) | copy-start | bytes 3076
  54.6 6.7 %copy-start.22 = (f32[256]{0:T(256)S(1)}, f32[256]{0:T(256)}, u32[]{:S(2)}) copy-start(f32[256]{0:T(256)} %param.18) | copy-start | bytes 3076
  57.2 14.1 %all-to-all-start = ((bf16[16,259,16]{1,2,0:T(8,128)(2,1)}), bf16[16,259,16]{1,2,0:T(8,128)(2,1)S(1)}, u32[]{:S(2)}, u32[]{:S(2)}) async-start(bf16[16,259,16]{1,2,0:T(8,128)(2,1)} %bitcast.28), calls=%async_computation | async-start | bytes 393216 | tf_op jit(solution)/shard_map/all_to_all | solution.py:113
  61.0 10.7 %copy-start.12 = (f32[1,256]{1,0:T(1,128)S(1)}, f32[1,256]{1,0:T(1,128)}, u32[]{:S(2)}) copy-start(f32[1,256]{1,0:T(1,128)} %get-tuple-element.47) | copy-start | bytes 3076
  61.0 10.7 %copy-start.13 = (f32[1,256]{1,0:T(1,128)S(1)}, f32[1,256]{1,0:T(1,128)}, u32[]{:S(2)}) copy-start(f32[1,256]{1,0:T(1,128)} %get-tuple-element.48) | copy-start | bytes 3076
  61.0 10.7 %copy-start.14 = (f32[1,256]{1,0:T(1,128)S(1)}, f32[1,256]{1,0:T(1,128)}, u32[]{:S(2)}) copy-start(f32[1,256]{1,0:T(1,128)} %get-tuple-element.49) | copy-start | bytes 3076
  61.0 10.7 %copy-start.15 = (f32[1,256]{1,0:T(1,128)S(1)}, f32[1,256]{1,0:T(1,128)}, u32[]{:S(2)}) copy-start(f32[1,256]{1,0:T(1,128)} %get-tuple-element.50) | copy-start | bytes 3076
  61.0 10.7 %copy-start.16 = (f32[256]{0:T(256)S(1)}, f32[256]{0:T(256)}, u32[]{:S(2)}) copy-start(f32[256]{0:T(256)} %dynamic_slice.40) | copy-start | bytes 3076
  61.6 22.8 %copy-start.8 = (f32[4]{0:T(128)S(1)}, f32[4]{0:T(128)}, u32[]{:S(2)}) copy-start(f32[4]{0:T(128)} %copy-done.7) | copy-start | bytes 52
  71.6 28.3 %copy-start.10 = (f32[4]{0:T(128)S(1)}, f32[4]{0:T(128)}, u32[]{:S(2)}) copy-start(f32[4]{0:T(128)} %param.21) | copy-start | bytes 52
  72.2 5.0 %collective-permute-start.5 = (bf16[4,65,128]{2,1,0:T(8,128)(2,1)S(1)}, bf16[4,65,128]{2,1,0:T(8,128)(2,1)S(1)}, u32[]{:S(2)}, u32[]{:S(2)}) collective-permute-start(bf16[4,65,128]{2,1,0:T(8,128)(2,1)S(1)} %pad_maximum_fusion.1), channel_id=1, source_target_pairs={{0,16},{16,32},{32,48},{48,64},{64,80},{80,96},{96,112},{112,128},... | collective-permute-start | bytes 199688 | tf_op jit(solution)/shard_map/ppermute | solution.py:17
  77.5 6.7 %collective-permute-start.6 = (bf16[4,65,128]{2,1,0:T(8,128)(2,1)S(1)}, bf16[4,65,128]{2,1,0:T(8,128)(2,1)S(1)}, u32[]{:S(2)}, u32[]{:S(2)}) collective-permute-start(bf16[4,65,128]{2,1,0:T(8,128)(2,1)S(1)} %pad_maximum_fusion.2), channel_id=1, source_target_pairs={{0,32},{16,48},{32,64},{48,80},{64,96},{80,112},{96,128},{112,144}... | collective-permute-start | bytes 199688 | tf_op jit(solution)/shard_map/ppermute | solution.py:17
  84.4 33.1 %copy-start.24 = (f32[4]{0:T(128)S(1)}, f32[4]{0:T(128)}, u32[]{:S(2)}) copy-start(f32[4]{0:T(128)} %param.23) | copy-start | bytes 52
  84.6 9.2 %collective-permute-start.7 = (bf16[4,65,128]{2,1,0:T(8,128)(2,1)S(1)}, bf16[4,65,128]{2,1,0:T(8,128)(2,1)S(1)}, u32[]{:S(2)}, u32[]{:S(2)}) collective-permute-start(bf16[4,65,128]{2,1,0:T(8,128)(2,1)S(1)} %pad_maximum_fusion.3), channel_id=1, source_target_pairs={{0,64},{16,80},{32,96},{48,112},{64,128},{80,144},{96,160},{112,17... | collective-permute-start | bytes 199688 | tf_op jit(solution)/shard_map/ppermute | solution.py:17
  94.1 7.2 %collective-permute-start.8 = (bf16[4,65,128]{2,1,0:T(8,128)(2,1)S(1)}, bf16[4,65,128]{2,1,0:T(8,128)(2,1)S(1)}, u32[]{:S(2)}, u32[]{:S(2)}) collective-permute-start(bf16[4,65,128]{2,1,0:T(8,128)(2,1)S(1)} %pad_maximum_fusion.4), channel_id=1, source_target_pairs={{0,128},{16,144},{32,160},{48,176},{64,192},{80,208},{96,224},{112... | collective-permute-start | bytes 199688 | tf_op jit(solution)/shard_map/ppermute | solution.py:17
  101.6 16.5 %copy-start.21 = (f32[256]{0:T(256)S(1)}, f32[256]{0:T(256)}, u32[]{:S(2)}) copy-start(f32[256]{0:T(256)} %param.24) | copy-start | bytes 3076
  101.8 15.4 %collective-permute-start.9 = (bf16[4,65,128]{2,1,0:T(8,128)(2,1)S(1)}, bf16[4,65,128]{2,1,0:T(8,128)(2,1)S(1)}, u32[]{:S(2)}, u32[]{:S(2)}) collective-permute-start(bf16[4,65,128]{2,1,0:T(8,128)(2,1)S(1)} %pad_maximum_fusion.5), channel_id=1, source_target_pairs={{0,256},{16,272},{32,288},{48,304},{64,320},{80,336},{96,352},{112... | collective-permute-start | bytes 199688 | tf_op jit(solution)/shard_map/ppermute | solution.py:17
  120.9 8.4 %collective-permute-start.10 = (bf16[2,2,2,16,2176]{4,3,2,1,0:T(8,128)(2,1)S(1)}, bf16[2,2,2,16,2176]{4,3,2,1,0:T(8,128)(2,1)S(1)}, u32[]{:S(2)}, u32[]{:S(2)}) collective-permute-start(bf16[2,2,2,16,2176]{4,3,2,1,0:T(8,128)(2,1)S(1)} %fusion.26), channel_id=1, source_target_pairs={{0,1},{1,0},{2,3},{3,2},{4,5},{5,4},{6,7},{7,6},{8,9},{9,8},{10,11... | collective-permute-start | bytes 1671176 | tf_op jit(solution)/shard_map/ppermute | solution.py:22
  130.7 9.7 %collective-permute-start.11 = (bf16[2,2,16,2176]{3,2,1,0:T(8,128)(2,1)S(1)}, bf16[2,2,16,2176]{3,2,1,0:T(8,128)(2,1)S(1)}, u32[]{:S(2)}, u32[]{:S(2)}) collective-permute-start(bf16[2,2,16,2176]{3,2,1,0:T(8,128)(2,1)S(1)} %fusion.33), channel_id=1, source_target_pairs={{0,2},{1,3},{2,0},{3,1},{4,6},{5,7},{6,4},{7,5},{8,10},{9,11},{10,... | collective-permute-start | bytes 835592 | tf_op jit(solution)/shard_map/ppermute | solution.py:22
  140.7 10.6 %collective-permute-start.12 = (bf16[2,16,2048]{2,1,0:T(8,128)(2,1)S(1)}, bf16[2,16,2048]{2,1,0:T(8,128)(2,1)S(1)}, u32[]{:S(2)}, u32[]{:S(2)}) collective-permute-start(bf16[2,16,2048]{2,1,0:T(8,128)(2,1)S(1)} %fusion.50), channel_id=1, source_target_pairs={{0,4},{1,5},{2,6},{3,7},{4,0},{5,1},{6,2},{7,3},{8,12},{9,13},{10,... | collective-permute-start | bytes 393224 | tf_op jit(solution)/shard_map/ppermute | solution.py:22
  151.3 9.0 %collective-permute-start.13 = (bf16[16,2048]{1,0:T(8,128)(2,1)S(1)}, bf16[16,2048]{1,0:T(8,128)(2,1)S(1)}, u32[]{:S(2)}, u32[]{:S(2)}) collective-permute-start(bf16[16,2048]{1,0:T(8,128)(2,1)S(1)} %fusion.52), channel_id=1, source_target_pairs={{0,8},{1,9},{2,10},{3,11},{4,12},{5,13},{6,14},{7,15},{8,0},{9,1},... | collective-permute-start | bytes 196616 | tf_op jit(solution)/shard_map/ppermute | solution.py:22
  (8 other events, 21.9 us)

commit v8 on v6

--- a/solution.py
+++ b/solution.py
@@ -84,20 +84,16 @@
         rows = jnp.transpose(rows, flipped + tuple(range(levels, rows.ndim)))
         return rows.reshape((length,) + rows.shape[levels + 1 :])
 
-    projected = jnp.concatenate(
-        [
-            in_order(jnp.einsum("...d,dn->...n", stacked, zx_weight, preferred_element_type=jnp.float32)),
-            in_order(jnp.einsum("...d,dn->...n", stacked, step_weight, preferred_element_type=jnp.float32)),
-        ],
-        axis=1,
+    map_cols = jnp.transpose(group_weight, (2, 1, 0)).reshape(group_weight.shape[2], -1)
+    joined = jnp.concatenate([zx_weight, step_weight, map_cols], axis=1)
+    projected = in_order(
+        jnp.einsum("...d,dn->...n", stacked, joined, preferred_element_type=jnp.float32)
     ).astype(jnp.bfloat16)
     gate_raw = projected[:, :inner_dev]
     inner_raw = projected[:, inner_dev : 2 * inner_dev]
-    step_raw = projected[:, 2 * inner_dev :]
-    own_maps = jnp.einsum(
-        "...d,sgd->...gs", stacked, group_weight, preferred_element_type=jnp.float32
-    ).astype(jnp.bfloat16)
-    own_maps = jnp.moveaxis(in_order(own_maps), 1, 0)
+    step_raw = projected[:, 2 * inner_dev : 2 * inner_dev + heads_dev]
+    own_maps = projected[:, 2 * inner_dev + heads_dev :].reshape(length, GROUPS, -1)
+    own_maps = jnp.moveaxis(own_maps, 1, 0)
     own_maps = jnp.broadcast_to(own_maps[:, None], (GROUPS, per_group_dev) + own_maps.shape[1:])
     own_maps = own_maps.reshape((tp_size,) + own_maps.shape[2:])
     got_maps = lax.all_to_all(own_maps, "tp", 0, 0, tiled=True)

time: 158 us -> 154 us (0.975)
  starting transfers between devices: 83.7 us -> 79.5 us
  waiting for transfers between devices: 50.6 us -> 54.5 us
  matrix products: 5.95 us -> 2.94 us
    ppermute x8, waiting for transfers between devices: 35.7 us -> 39.3 us  [swapped(): return lax.ppermute(x, axis, [(i, i ^ bit) for i in range(peers)])]
    unnamed x27 -> x23, local copies, waits for them, and re-layouts: 1.84 us -> 5.31 us
    reshape x3 -> x1, local copies, waits for them, and re-layouts: 3.45 us -> 0.01 us  [the longest x1 3.19 us: body(): zx_weight = in_weight.reshape(in_weight.shape[0], 2 * inner_dev)]
    ppermute x8, starting transfers between devices: 36.1 us -> 32.9 us  [swapped(): return lax.ppermute(x, axis, [(i, i ^ bit) for i in range(peers)])]
    dot_general x3 -> x1, matrix products: 4.09 us -> 1.07 us  [body(): jnp.einsum('...d,dn->...n', stacked, joined, preferred_element_type=jnp.f...]
    all_to_all x1, starting transfers between devices: 5.45 us -> 3.67 us  [body(): got_maps = lax.all_to_all(own_maps, 'tp', 0, 0, tiled=True)]
  transfers between devices with their start and end apart: 15 -> 15, of which waited for: 14 -> 14; matrix products, arithmetic and copies ran while one was open for 4% -> 5% of each run, Pallas kernels for 0% -> 0%
where the time goes in v8:
time: 154 us
  starting transfers between devices  79.5 us (52%)
  waiting for transfers between devices  54.5 us (35%)
  local copies, waits for them, and re-layouts  10.1 us (7%)
  other arithmetic  5.72 us (4%)
  matrix products  2.94 us (2%)
    ppermute x6, starting transfers between devices, shifted(): return lax.ppermute(x, axis, pairs)  43 us
    ppermute x8, waiting for transfers between devices, swapped(): return lax.ppermute(x, axis, [(i, i ^ bit) for i in range(peers)])  39.3 us
    ppermute x8, starting transfers between devices, swapped(): return lax.ppermute(x, axis, [(i, i ^ bit) for i in range(peers)])  32.9 us
    all_to_all x1, waiting for transfers between devices, body(): got_maps = lax.all_to_all(own_maps, 'tp', 0, 0, tiled=True)  8.56 us
    ppermute x6, waiting for transfers between devices, shifted(): return lax.ppermute(x, axis, pairs)  6.68 us
    unnamed x23, local copies, waits for them, and re-layouts  5.31 us
    all_to_all x1, starting transfers between devices, body(): got_maps = lax.all_to_all(own_maps, 'tp', 0, 0, tiled=True)  3.67 us
  transfers between devices with their start and end apart: 15, of which 14 were waited for; matrix products, arithmetic and copies ran while one was open for 5% of the time, Pallas kernels for 0%

profile of v8, /device:TPU:1, one launch (start us, length us, event | category | flops | bytes accessed | tf_op | source)
XLA Modules:
  0.0 153.7 jit_solution(77357436877859609)
XLA Ops:
  0.0 8.4 %collective-permute-start = (bf16[16,2048]{1,0:T(8,128)(2,1)}, bf16[16,2048]{1,0:T(8,128)(2,1)S(1)}, u32[]{:S(2)}, u32[]{:S(2)}) collective-permute-start(bf16[16,2048]{1,0:T(8,128)(2,1)} %param.13), channel_id=1, source_target_pairs={{0,8},{1,9},{2,10},{3,11},{4,12},{5,13},{6,14},{7,15},{8,0},{9,1},... | collective-permute-start | bytes 196616 | tf_op jit(solution)/shard_map/ppermute | solution.py:22
  8.5 4.8 %copy.64 = bf16[2048,2,256]{0,2,1:T(8,128)(2,1)S(1)} copy(bf16[2048,2,256]{2,1,0:T(2,128)(2,1)} %param.14) | data formatting | bytes 4194304 | tf_op args[1]
  14.4 2.4 %collective-permute-start.1 = (bf16[2,16,2048]{2,1,0:T(8,128)(2,1)S(1)}, bf16[2,16,2048]{2,1,0:T(8,128)(2,1)S(1)}, u32[]{:S(2)}, u32[]{:S(2)}) collective-permute-start(bf16[2,16,2048]{2,1,0:T(8,128)(2,1)S(1)} %maximum_select_fusion.7), channel_id=1, source_target_pairs={{0,4},{1,5},{2,6},{3,7},{4,0},{5,1},{6,2},{7,3},{8,12},{9,13},{10,... | collective-permute-start | bytes 393224 | tf_op jit(solution)/shard_map/ppermute | solution.py:22
  16.8 8.1 %collective-permute-done.1 = bf16[2,16,2048]{2,1,0:T(8,128)(2,1)S(1)} collective-permute-done((bf16[2,16,2048]{2,1,0:T(8,128)(2,1)S(1)}, bf16[2,16,2048]{2,1,0:T(8,128)(2,1)S(1)}, u32[]{:S(2)}, u32[]{:S(2)}) %collective-permute-start.1) | collective-permute-done | bytes 131104 | tf_op jit(solution)/shard_map/ppermute | solution.py:22
  24.9 1.9 %collective-permute-start.2 = (bf16[2,2,16,2048]{3,2,1,0:T(8,128)(2,1)S(1)}, bf16[2,2,16,2048]{3,2,1,0:T(8,128)(2,1)S(1)}, u32[]{:S(2)}, u32[]{:S(2)}) collective-permute-start(bf16[2,2,16,2048]{3,2,1,0:T(8,128)(2,1)S(1)} %maximum_select_fusion.5), channel_id=1, source_target_pairs={{0,2},{1,3},{2,0},{3,1},{4,6},{5,7},{6,4},{7,5},{8,10},{9,11},{10,... | collective-permute-start | bytes 786440 | tf_op jit(solution)/shard_map/ppermute | solution.py:22
  26.9 6.8 %collective-permute-done.2 = bf16[2,2,16,2048]{3,2,1,0:T(8,128)(2,1)S(1)} collective-permute-done((bf16[2,2,16,2048]{3,2,1,0:T(8,128)(2,1)S(1)}, bf16[2,2,16,2048]{3,2,1,0:T(8,128)(2,1)S(1)}, u32[]{:S(2)}, u32[]{:S(2)}) %collective-permute-start.2) | collective-permute-done | bytes 262176 | tf_op jit(solution)/shard_map/ppermute | solution.py:22
  33.8 3.7 %collective-permute-start.3 = (bf16[2,2,2,16,2048]{4,3,2,1,0:T(8,128)(2,1)S(1)}, bf16[2,2,2,16,2048]{4,3,2,1,0:T(8,128)(2,1)S(1)}, u32[]{:S(2)}, u32[]{:S(2)}) collective-permute-start(bf16[2,2,2,16,2048]{4,3,2,1,0:T(8,128)(2,1)S(1)} %maximum_select_fusion.3), channel_id=1, source_target_pairs={{0,1},{1,0},{2,3},{3,2},{4,5},{5,4},{6,7},{7,6},{8,9},{9,8},{10,11... | collective-permute-start | bytes 1572872 | tf_op jit(solution)/shard_map/ppermute | solution.py:22
  37.6 0.9 constant_dynamic-slice_fusion
  39.1 1.1 fusion.14
  40.5 1.2 reduce-window.6
  42.6 3.7 %all-to-all-start = ((bf16[16,256,16]{1,2,0:T(8,128)(2,1)}), bf16[16,256,16]{1,2,0:T(8,128)(2,1)S(1)}, u32[]{:S(2)}, u32[]{:S(2)}) async-start(bf16[16,256,16]{1,2,0:T(8,128)(2,1)} %bitcast.21), calls=%async_computation | async-start | bytes 262144 | tf_op jit(solution)/shard_map/all_to_all | solution.py:99
  46.9 8.6 %all-to-all-done = bf16[16,256,16]{1,2,0:T(8,128)(2,1)S(1)} async-done(((bf16[16,256,16]{1,2,0:T(8,128)(2,1)}), bf16[16,256,16]{1,2,0:T(8,128)(2,1)S(1)}, u32[]{:S(2)}, u32[]{:S(2)}) %all-to-all-start) | async-done | bytes 131104 | tf_op jit(solution)/shard_map/all_to_all | solution.py:99
  55.7 3.5 %collective-permute-start.4 = (bf16[3,512]{1,0:T(4,128)(2,1)S(1)}, bf16[3,512]{1,0:T(4,128)(2,1)S(1)}, u32[]{:S(2)}, u32[]{:S(2)}) collective-permute-start(bf16[3,512]{1,0:T(4,128)(2,1)S(1)} %pad_maximum_fusion.6), channel_id=1, source_target_pairs={{0,16},{16,32},{32,48},{48,64},{64,80},{80,96},{96,112},{112,128},... | collective-permute-start | bytes 9224 | tf_op jit(solution)/shard_map/ppermute | solution.py:17
  60.7 3.6 %collective-permute-start.5 = (bf16[4,65,128]{2,1,0:T(8,128)(2,1)S(1)}, bf16[4,65,128]{2,1,0:T(8,128)(2,1)S(1)}, u32[]{:S(2)}, u32[]{:S(2)}) collective-permute-start(bf16[4,65,128]{2,1,0:T(8,128)(2,1)S(1)} %pad_maximum_fusion.1), channel_id=1, source_target_pairs={{0,16},{16,32},{32,48},{48,64},{64,80},{80,96},{96,112},{112,128},... | collective-permute-start | bytes 199688 | tf_op jit(solution)/shard_map/ppermute | solution.py:17
  64.4 1.3 collective-permute-done.5
  66.0 5.2 %collective-permute-start.6 = (bf16[4,65,128]{2,1,0:T(8,128)(2,1)S(1)}, bf16[4,65,128]{2,1,0:T(8,128)(2,1)S(1)}, u32[]{:S(2)}, u32[]{:S(2)}) collective-permute-start(bf16[4,65,128]{2,1,0:T(8,128)(2,1)S(1)} %pad_maximum_fusion.2), channel_id=1, source_target_pairs={{0,32},{16,48},{32,64},{48,80},{64,96},{80,112},{96,128},{112,144}... | collective-permute-start | bytes 199688 | tf_op jit(solution)/shard_map/ppermute | solution.py:17
  71.4 1.3 collective-permute-done.6
  73.0 9.7 %collective-permute-start.7 = (bf16[4,65,128]{2,1,0:T(8,128)(2,1)S(1)}, bf16[4,65,128]{2,1,0:T(8,128)(2,1)S(1)}, u32[]{:S(2)}, u32[]{:S(2)}) collective-permute-start(bf16[4,65,128]{2,1,0:T(8,128)(2,1)S(1)} %pad_maximum_fusion.3), channel_id=1, source_target_pairs={{0,64},{16,80},{32,96},{48,112},{64,128},{80,144},{96,160},{112,17... | collective-permute-start | bytes 199688 | tf_op jit(solution)/shard_map/ppermute | solution.py:17
  82.7 1.4 collective-permute-done.7
  84.4 5.8 %collective-permute-start.8 = (bf16[4,65,128]{2,1,0:T(8,128)(2,1)S(1)}, bf16[4,65,128]{2,1,0:T(8,128)(2,1)S(1)}, u32[]{:S(2)}, u32[]{:S(2)}) collective-permute-start(bf16[4,65,128]{2,1,0:T(8,128)(2,1)S(1)} %pad_maximum_fusion.4), channel_id=1, source_target_pairs={{0,128},{16,144},{32,160},{48,176},{64,192},{80,208},{96,224},{112... | collective-permute-start | bytes 199688 | tf_op jit(solution)/shard_map/ppermute | solution.py:17
  90.3 1.3 collective-permute-done.8
  92.1 15.2 %collective-permute-start.9 = (bf16[4,65,128]{2,1,0:T(8,128)(2,1)S(1)}, bf16[4,65,128]{2,1,0:T(8,128)(2,1)S(1)}, u32[]{:S(2)}, u32[]{:S(2)}) collective-permute-start(bf16[4,65,128]{2,1,0:T(8,128)(2,1)S(1)} %pad_maximum_fusion.5), channel_id=1, source_target_pairs={{0,256},{16,272},{32,288},{48,304},{64,320},{80,336},{96,352},{112... | collective-permute-start | bytes 199688 | tf_op jit(solution)/shard_map/ppermute | solution.py:17
  107.6 1.0 collective-permute-done.9
  111.0 8.2 %collective-permute-start.10 = (bf16[2,2,2,16,2176]{4,3,2,1,0:T(8,128)(2,1)S(1)}, bf16[2,2,2,16,2176]{4,3,2,1,0:T(8,128)(2,1)}, u32[]{:S(2)}, u32[]{:S(2)}) collective-permute-start(bf16[2,2,2,16,2176]{4,3,2,1,0:T(8,128)(2,1)S(1)} %fusion.25), channel_id=1, source_target_pairs={{0,1},{1,0},{2,3},{3,2},{4,5},{5,4},{6,7},{7,6},{8,9},{9,8},{10,11... | collective-permute-start | bytes 1671176 | tf_op jit(solution)/shard_map/ppermute | solution.py:22
  119.2 1.7 %collective-permute-done.10 = bf16[2,2,2,16,2176]{4,3,2,1,0:T(8,128)(2,1)} collective-permute-done((bf16[2,2,2,16,2176]{4,3,2,1,0:T(8,128)(2,1)S(1)}, bf16[2,2,2,16,2176]{4,3,2,1,0:T(8,128)(2,1)}, u32[]{:S(2)}, u32[]{:S(2)}) %collective-permute-start.10) | collective-permute-done | bytes 557088 | tf_op jit(solution)/shard_map/ppermute | solution.py:22
  120.9 1.1 bitcast_add_fusion
  122.1 2.2 %collective-permute-start.11 = (bf16[2,2,16,2176]{3,2,1,0:T(8,128)(2,1)S(1)}, bf16[2,2,16,2176]{3,2,1,0:T(8,128)(2,1)S(1)}, u32[]{:S(2)}, u32[]{:S(2)}) collective-permute-start(bf16[2,2,16,2176]{3,2,1,0:T(8,128)(2,1)S(1)} %fusion.32), channel_id=1, source_target_pairs={{0,2},{1,3},{2,0},{3,1},{4,6},{5,7},{6,4},{7,5},{8,10},{9,11},{10,... | collective-permute-start | bytes 835592 | tf_op jit(solution)/shard_map/ppermute | solution.py:22
  124.3 7.5 %collective-permute-done.11 = bf16[2,2,16,2176]{3,2,1,0:T(8,128)(2,1)S(1)} collective-permute-done((bf16[2,2,16,2176]{3,2,1,0:T(8,128)(2,1)S(1)}, bf16[2,2,16,2176]{3,2,1,0:T(8,128)(2,1)S(1)}, u32[]{:S(2)}, u32[]{:S(2)}) %collective-permute-start.11) | collective-permute-done | bytes 278560 | tf_op jit(solution)/shard_map/ppermute | solution.py:22
  132.1 2.5 %collective-permute-start.12 = (bf16[2,16,2048]{2,1,0:T(8,128)(2,1)S(1)}, bf16[2,16,2048]{2,1,0:T(8,128)(2,1)S(1)}, u32[]{:S(2)}, u32[]{:S(2)}) collective-permute-start(bf16[2,16,2048]{2,1,0:T(8,128)(2,1)S(1)} %fusion.47), channel_id=1, source_target_pairs={{0,4},{1,5},{2,6},{3,7},{4,0},{5,1},{6,2},{7,3},{8,12},{9,13},{10,... | collective-permute-start | bytes 393224 | tf_op jit(solution)/shard_map/ppermute | solution.py:22
  134.6 8.3 %collective-permute-done.12 = bf16[2,16,2048]{2,1,0:T(8,128)(2,1)S(1)} collective-permute-done((bf16[2,16,2048]{2,1,0:T(8,128)(2,1)S(1)}, bf16[2,16,2048]{2,1,0:T(8,128)(2,1)S(1)}, u32[]{:S(2)}, u32[]{:S(2)}) %collective-permute-start.12) | collective-permute-done | bytes 131104 | tf_op jit(solution)/shard_map/ppermute | solution.py:22
  143.0 3.6 %collective-permute-start.13 = (bf16[16,2048]{1,0:T(8,128)(2,1)S(1)}, bf16[16,2048]{1,0:T(8,128)(2,1)S(1)}, u32[]{:S(2)}, u32[]{:S(2)}) collective-permute-start(bf16[16,2048]{1,0:T(8,128)(2,1)S(1)} %fusion.49), channel_id=1, source_target_pairs={{0,8},{1,9},{2,10},{3,11},{4,12},{5,13},{6,14},{7,15},{8,0},{9,1},... | collective-permute-start | bytes 196616 | tf_op jit(solution)/shard_map/ppermute | solution.py:22
  146.6 6.4 %collective-permute-done.13 = bf16[16,2048]{1,0:T(8,128)(2,1)S(1)} collective-permute-done((bf16[16,2048]{1,0:T(8,128)(2,1)S(1)}, bf16[16,2048]{1,0:T(8,128)(2,1)S(1)}, u32[]{:S(2)}, u32[]{:S(2)}) %collective-permute-start.13) | collective-permute-done | bytes 65568 | tf_op jit(solution)/shard_map/ppermute | solution.py:22
  (120 shorter events, 10.5 us)
Async XLA Ops:
  0.0 13.2 %copy-start.1 = (bf16[16,4,2048]{2,1,0:T(4,128)(2,1)S(1)}, bf16[16,4,2048]{2,1,0:T(4,128)(2,1)}, u32[]{:S(2)}) copy-start(bf16[16,4,2048]{2,1,0:T(4,128)(2,1)} %param.16) | copy-start | bytes 786436
  0.0 14.3 %collective-permute-start = (bf16[16,2048]{1,0:T(8,128)(2,1)}, bf16[16,2048]{1,0:T(8,128)(2,1)S(1)}, u32[]{:S(2)}, u32[]{:S(2)}) collective-permute-start(bf16[16,2048]{1,0:T(8,128)(2,1)} %param.13), channel_id=1, source_target_pairs={{0,8},{1,9},{2,10},{3,11},{4,12},{5,13},{6,14},{7,15},{8,0},{9,1},... | collective-permute-start | bytes 196616 | tf_op jit(solution)/shard_map/ppermute | solution.py:22
  8.4 5.0 %copy-start.8 = (f32[4]{0:T(128)S(1)}, f32[4]{0:T(128)}, u32[]{:S(2)}) copy-start(f32[4]{0:T(128)} %param.22) | copy-start | bytes 52
  8.5 5.0 %copy-start.3 = (f32[4,256]{1,0:T(4,128)S(1)}, f32[4,256]{1,0:T(4,128)}, u32[]{:S(2)}) copy-start(f32[4,256]{1,0:T(4,128)} %param.17) | copy-start | bytes 12292
  8.5 5.9 %copy-start = (bf16[16,2048]{1,0:T(8,128)(2,1)S(1)}, bf16[16,2048]{1,0:T(8,128)(2,1)}, u32[]{:S(2)}) copy-start(bf16[16,2048]{1,0:T(8,128)(2,1)} %param.13) | copy-start | bytes 196612
  14.3 24.8 %copy-start.7 = (bf16[2048,4]{0,1:T(4,128)(2,1)S(1)}, bf16[2048,4]{0,1:T(4,128)(2,1)}, u32[]{:S(2)}) copy-start(bf16[2048,4]{0,1:T(4,128)(2,1)} %param.15) | copy-start | bytes 49156
  14.4 10.6 %collective-permute-start.1 = (bf16[2,16,2048]{2,1,0:T(8,128)(2,1)S(1)}, bf16[2,16,2048]{2,1,0:T(8,128)(2,1)S(1)}, u32[]{:S(2)}, u32[]{:S(2)}) collective-permute-start(bf16[2,16,2048]{2,1,0:T(8,128)(2,1)S(1)} %maximum_select_fusion.7), channel_id=1, source_target_pairs={{0,4},{1,5},{2,6},{3,7},{4,0},{5,1},{6,2},{7,3},{8,12},{9,13},{10,... | collective-permute-start | bytes 393224 | tf_op jit(solution)/shard_map/ppermute | solution.py:22
  24.9 8.8 %collective-permute-start.2 = (bf16[2,2,16,2048]{3,2,1,0:T(8,128)(2,1)S(1)}, bf16[2,2,16,2048]{3,2,1,0:T(8,128)(2,1)S(1)}, u32[]{:S(2)}, u32[]{:S(2)}) collective-permute-start(bf16[2,2,16,2048]{3,2,1,0:T(8,128)(2,1)S(1)} %maximum_select_fusion.5), channel_id=1, source_target_pairs={{0,2},{1,3},{2,0},{3,1},{4,6},{5,7},{6,4},{7,5},{8,10},{9,11},{10,... | collective-permute-start | bytes 786440 | tf_op jit(solution)/shard_map/ppermute | solution.py:22
  33.8 5.2 %collective-permute-start.3 = (bf16[2,2,2,16,2048]{4,3,2,1,0:T(8,128)(2,1)S(1)}, bf16[2,2,2,16,2048]{4,3,2,1,0:T(8,128)(2,1)S(1)}, u32[]{:S(2)}, u32[]{:S(2)}) collective-permute-start(bf16[2,2,2,16,2048]{4,3,2,1,0:T(8,128)(2,1)S(1)} %maximum_select_fusion.3), channel_id=1, source_target_pairs={{0,1},{1,0},{2,3},{3,2},{4,5},{5,4},{6,7},{7,6},{8,9},{9,8},{10,11... | collective-permute-start | bytes 1572872 | tf_op jit(solution)/shard_map/ppermute | solution.py:22
  39.1 1.3 copy-start.2
  40.2 19.8 %copy-start.5 = (f32[256]{0:T(256)S(1)}, f32[256]{0:T(256)}, u32[]{:S(2)}) copy-start(f32[256]{0:T(256)} %param.18) | copy-start | bytes 3076
  42.6 12.9 %all-to-all-start = ((bf16[16,256,16]{1,2,0:T(8,128)(2,1)}), bf16[16,256,16]{1,2,0:T(8,128)(2,1)S(1)}, u32[]{:S(2)}, u32[]{:S(2)}) async-start(bf16[16,256,16]{1,2,0:T(8,128)(2,1)} %bitcast.21), calls=%async_computation | async-start | bytes 262144 | tf_op jit(solution)/shard_map/all_to_all | solution.py:99
  55.7 4.2 %collective-permute-start.4 = (bf16[3,512]{1,0:T(4,128)(2,1)S(1)}, bf16[3,512]{1,0:T(4,128)(2,1)S(1)}, u32[]{:S(2)}, u32[]{:S(2)}) collective-permute-start(bf16[3,512]{1,0:T(4,128)(2,1)S(1)} %pad_maximum_fusion.6), channel_id=1, source_target_pairs={{0,16},{16,32},{32,48},{48,64},{64,80},{80,96},{96,112},{112,128},... | collective-permute-start | bytes 9224 | tf_op jit(solution)/shard_map/ppermute | solution.py:17
  60.7 5.0 %collective-permute-start.5 = (bf16[4,65,128]{2,1,0:T(8,128)(2,1)S(1)}, bf16[4,65,128]{2,1,0:T(8,128)(2,1)S(1)}, u32[]{:S(2)}, u32[]{:S(2)}) collective-permute-start(bf16[4,65,128]{2,1,0:T(8,128)(2,1)S(1)} %pad_maximum_fusion.1), channel_id=1, source_target_pairs={{0,16},{16,32},{32,48},{48,64},{64,80},{80,96},{96,112},{112,128},... | collective-permute-start | bytes 199688 | tf_op jit(solution)/shard_map/ppermute | solution.py:17
  66.0 6.6 %collective-permute-start.6 = (bf16[4,65,128]{2,1,0:T(8,128)(2,1)S(1)}, bf16[4,65,128]{2,1,0:T(8,128)(2,1)S(1)}, u32[]{:S(2)}, u32[]{:S(2)}) collective-permute-start(bf16[4,65,128]{2,1,0:T(8,128)(2,1)S(1)} %pad_maximum_fusion.2), channel_id=1, source_target_pairs={{0,32},{16,48},{32,64},{48,80},{64,96},{80,112},{96,128},{112,144}... | collective-permute-start | bytes 199688 | tf_op jit(solution)/shard_map/ppermute | solution.py:17
  71.4 37.5 %copy-start.9 = (f32[4]{0:T(128)S(1)}, f32[4]{0:T(128)}, u32[]{:S(2)}) copy-start(f32[4]{0:T(128)} %param.23) | copy-start | bytes 52
  73.0 11.1 %collective-permute-start.7 = (bf16[4,65,128]{2,1,0:T(8,128)(2,1)S(1)}, bf16[4,65,128]{2,1,0:T(8,128)(2,1)S(1)}, u32[]{:S(2)}, u32[]{:S(2)}) collective-permute-start(bf16[4,65,128]{2,1,0:T(8,128)(2,1)S(1)} %pad_maximum_fusion.3), channel_id=1, source_target_pairs={{0,64},{16,80},{32,96},{48,112},{64,128},{80,144},{96,160},{112,17... | collective-permute-start | bytes 199688 | tf_op jit(solution)/shard_map/ppermute | solution.py:17
  84.4 7.2 %collective-permute-start.8 = (bf16[4,65,128]{2,1,0:T(8,128)(2,1)S(1)}, bf16[4,65,128]{2,1,0:T(8,128)(2,1)S(1)}, u32[]{:S(2)}, u32[]{:S(2)}) collective-permute-start(bf16[4,65,128]{2,1,0:T(8,128)(2,1)S(1)} %pad_maximum_fusion.4), channel_id=1, source_target_pairs={{0,128},{16,144},{32,160},{48,176},{64,192},{80,208},{96,224},{112... | collective-permute-start | bytes 199688 | tf_op jit(solution)/shard_map/ppermute | solution.py:17
  92.0 17.5 %copy-start.4 = (f32[256]{0:T(256)S(1)}, f32[256]{0:T(256)}, u32[]{:S(2)}) copy-start(f32[256]{0:T(256)} %param.24) | copy-start | bytes 3076
  92.1 16.6 %collective-permute-start.9 = (bf16[4,65,128]{2,1,0:T(8,128)(2,1)S(1)}, bf16[4,65,128]{2,1,0:T(8,128)(2,1)S(1)}, u32[]{:S(2)}, u32[]{:S(2)}) collective-permute-start(bf16[4,65,128]{2,1,0:T(8,128)(2,1)S(1)} %pad_maximum_fusion.5), channel_id=1, source_target_pairs={{0,256},{16,272},{32,288},{48,304},{64,320},{80,336},{96,352},{112... | collective-permute-start | bytes 199688 | tf_op jit(solution)/shard_map/ppermute | solution.py:17
  108.9 1.2 copy-start.6
  111.0 9.9 %collective-permute-start.10 = (bf16[2,2,2,16,2176]{4,3,2,1,0:T(8,128)(2,1)S(1)}, bf16[2,2,2,16,2176]{4,3,2,1,0:T(8,128)(2,1)}, u32[]{:S(2)}, u32[]{:S(2)}) collective-permute-start(bf16[2,2,2,16,2176]{4,3,2,1,0:T(8,128)(2,1)S(1)} %fusion.25), channel_id=1, source_target_pairs={{0,1},{1,0},{2,3},{3,2},{4,5},{5,4},{6,7},{7,6},{8,9},{9,8},{10,11... | collective-permute-start | bytes 1671176 | tf_op jit(solution)/shard_map/ppermute | solution.py:22
  122.1 9.7 %collective-permute-start.11 = (bf16[2,2,16,2176]{3,2,1,0:T(8,128)(2,1)S(1)}, bf16[2,2,16,2176]{3,2,1,0:T(8,128)(2,1)S(1)}, u32[]{:S(2)}, u32[]{:S(2)}) collective-permute-start(bf16[2,2,16,2176]{3,2,1,0:T(8,128)(2,1)S(1)} %fusion.32), channel_id=1, source_target_pairs={{0,2},{1,3},{2,0},{3,1},{4,6},{5,7},{6,4},{7,5},{8,10},{9,11},{10,... | collective-permute-start | bytes 835592 | tf_op jit(solution)/shard_map/ppermute | solution.py:22
  132.1 10.8 %collective-permute-start.12 = (bf16[2,16,2048]{2,1,0:T(8,128)(2,1)S(1)}, bf16[2,16,2048]{2,1,0:T(8,128)(2,1)S(1)}, u32[]{:S(2)}, u32[]{:S(2)}) collective-permute-start(bf16[2,16,2048]{2,1,0:T(8,128)(2,1)S(1)} %fusion.47), channel_id=1, source_target_pairs={{0,4},{1,5},{2,6},{3,7},{4,0},{5,1},{6,2},{7,3},{8,12},{9,13},{10,... | collective-permute-start | bytes 393224 | tf_op jit(solution)/shard_map/ppermute | solution.py:22
  143.0 10.0 %collective-permute-start.13 = (bf16[16,2048]{1,0:T(8,128)(2,1)S(1)}, bf16[16,2048]{1,0:T(8,128)(2,1)S(1)}, u32[]{:S(2)}, u32[]{:S(2)}) collective-permute-start(bf16[16,2048]{1,0:T(8,128)(2,1)S(1)} %fusion.49), channel_id=1, source_target_pairs={{0,8},{1,9},{2,10},{3,11},{4,12},{5,13},{6,14},{7,15},{8,0},{9,1},... | collective-permute-start | bytes 196616 | tf_op jit(solution)/shard_map/ppermute | solution.py:22

commit v9 on v8

--- a/solution.py
+++ b/solution.py
@@ -1,7 +1,7 @@
 import jax
 import jax.numpy as jnp
 from jax import lax
-from jax.sharding import PartitionSpec as P
+from jax.sharding import Mesh, PartitionSpec as P
 
 HEADS = 64
 HEAD_DIM = 64
@@ -101,7 +101,7 @@
     border_rows = KERNEL - 1
     prior = shifted(
         jnp.concatenate([inner_raw[length - border_rows :], map_part[length - border_rows :]], axis=1),
-        "ctx",
+        ("z", "x"),
         1,
     )
     inner_prior = prior[:, :inner_dev]
@@ -143,26 +143,47 @@
     (dev_state, dev_decay), (local_starts, prefixes) = lax.scan(
         advance, (empty_state, jnp.ones((heads_dev,), jnp.float32)), (block_decay, block_state)
     )
-    ctx_size = lax.axis_size("ctx")
-    place = lax.axis_index("ctx")
+    x_peers = lax.axis_size("x")
+    x_place = lax.axis_index("x")
+    packed = jnp.concatenate(
+        [dev_state, jnp.broadcast_to(dev_decay[:, None, None], (heads_dev, 1, STATE))], axis=1
+    ).astype(jnp.bfloat16)
+    row = lax.all_to_all(
+        jnp.broadcast_to(packed[None], (x_peers,) + packed.shape), "x", 0, 0, tiled=True
+    ).astype(jnp.float32)
+    row_decay = jnp.ones_like(dev_decay)
+    row_state = jnp.zeros_like(dev_state)
     in_decay = jnp.ones_like(dev_decay)
     in_state = jnp.zeros_like(dev_state)
-    run_decay = dev_decay
-    run_state = dev_state
+    for k in reversed(range(x_peers)):
+        got_state = row[k, :, :HEAD_DIM]
+        got_decay = row[k, :, HEAD_DIM, 0]
+        earlier = k < x_place
+        in_state = jnp.where(earlier, in_decay[:, None, None] * got_state + in_state, in_state)
+        in_decay = jnp.where(earlier, got_decay * in_decay, in_decay)
+        row_state = row_decay[:, None, None] * got_state + row_state
+        row_decay = got_decay * row_decay
+    z_peers = lax.axis_size("z")
+    z_place = lax.axis_index("z")
+    pre_decay = jnp.ones_like(dev_decay)
+    pre_state = jnp.zeros_like(dev_state)
+    run_decay = row_decay
+    run_state = row_state
     reach = 1
-    while reach < ctx_size:
+    while reach < z_peers:
         packed = jnp.concatenate(
             [run_state, jnp.broadcast_to(run_decay[:, None, None], (heads_dev, 1, STATE))], axis=1
         )
-        got = shifted(packed.astype(jnp.bfloat16), "ctx", reach).astype(jnp.float32)
-        valid = place >= reach
+        got = shifted(packed.astype(jnp.bfloat16), "z", reach).astype(jnp.float32)
+        valid = z_place >= reach
         got_state = jnp.where(valid, got[:, :HEAD_DIM], 0.0)
         got_decay = jnp.where(valid, got[:, HEAD_DIM, 0], 1.0)
-        in_state = in_decay[:, None, None] * got_state + in_state
-        in_decay = got_decay * in_decay
+        pre_state = pre_decay[:, None, None] * got_state + pre_state
+        pre_decay = got_decay * pre_decay
         run_state = run_decay[:, None, None] * got_state + run_state
         run_decay = got_decay * run_decay
         reach *= 2
+    in_state = in_decay[:, None, None] * pre_state + in_state
     incoming = in_state
     starting = local_starts + prefixes[:, :, None, None] * incoming[None]
     carried = jnp.einsum(
@@ -203,8 +224,14 @@
 
 
 def solution(mesh):
+    ctx_size = mesh.shape["ctx"]
+    x_size = 4 if ctx_size % 4 == 0 else ctx_size
+    fine = Mesh(
+        mesh.devices.reshape(ctx_size // x_size, x_size, mesh.shape["tp"]), ("z", "x", "tp")
+    )
+    rows = ("z", "x", "tp")
     placed = (
-        P(("ctx", "tp"), None),
+        P(rows, None),
         P(None, None, "tp"),
         P(None, "tp"),
         P("tp", None, None),
@@ -218,6 +245,4 @@
         P("tp"),
         P("tp", None),
     )
-    return jax.shard_map(
-        body, mesh=mesh, in_specs=placed, out_specs=P(("ctx", "tp"), None), check_vma=False
-    )
+    return jax.shard_map(body, mesh=fine, in_specs=placed, out_specs=P(rows, None), check_vma=False)

time: 154 us -> 145 us (0.942)
  starting transfers between devices: 79.5 us -> 66.1 us
  waiting for transfers between devices: 54.5 us -> 57.7 us
    ppermute x6 -> x4, starting transfers between devices: 43 us -> 27.6 us  [shifted(): return lax.ppermute(x, axis, pairs)]
    all_to_all x0 -> x1, waiting for transfers between devices: none -> 5.5 us  [body(): lax.all_to_all(jnp.broadcast_to(packed[None], (x_peers,) + packed.shape),...]
    all_to_all x0 -> x1, starting transfers between devices: none -> 4.55 us  [body(): lax.all_to_all(jnp.broadcast_to(packed[None], (x_peers,) + packed.shape),...]
    ppermute x6 -> x4, waiting for transfers between devices: 6.68 us -> 3.89 us  [shifted(): return lax.ppermute(x, axis, pairs)]
    ppermute x8, starting transfers between devices: 32.9 us -> 30.3 us  [swapped(): return lax.ppermute(x, axis, [(i, i ^ bit) for i in range(peers)])]
  transfers between devices with their start and end apart: 15 -> 14, of which waited for: 14 -> 13; matrix products, arithmetic and copies ran while one was open for 5% -> 6% of each run, Pallas kernels for 0% -> 0%
where the time goes in v9:
time: 145 us; the launch traced here: 144 us
  starting transfers between devices  66.1 us (46%)
  waiting for transfers between devices  57.7 us (40%)
  local copies, waits for them, and re-layouts  11.1 us (8%)
  other arithmetic  5.36 us (4%)
  matrix products  2.96 us (2%)
    ppermute x8, waiting for transfers between devices, swapped(): return lax.ppermute(x, axis, [(i, i ^ bit) for i in range(peers)])  39.6 us
    ppermute x8, starting transfers between devices, swapped(): return lax.ppermute(x, axis, [(i, i ^ bit) for i in range(peers)])  30.3 us
    ppermute x4, starting transfers between devices, shifted(): return lax.ppermute(x, axis, pairs)  27.6 us
    all_to_all x1, waiting for transfers between devices, body(): got_maps = lax.all_to_all(own_maps, 'tp', 0, 0, tiled=True)  8.8 us
    all_to_all x1, waiting for transfers between devices, body(): lax.all_to_all(jnp.broadcast_to(packed[None], (x_peers,) + packed.shape),...  5.5 us
    unnamed x23, local copies, waits for them, and re-layouts  5.32 us
    all_to_all x1, starting transfers between devices, body(): lax.all_to_all(jnp.broadcast_to(packed[None], (x_peers,) + packed.shape),...  4.55 us
    ppermute x4, waiting for transfers between devices, shifted(): return lax.ppermute(x, axis, pairs)  3.89 us
  transfers between devices with their start and end apart: 14, of which 13 were waited for; matrix products, arithmetic and copies ran while one was open for 6% of the time, Pallas kernels for 0%

profile of v9, /device:TPU:1, one launch (start us, length us, event | category | flops | bytes accessed | tf_op | source)
XLA Modules:
  0.0 144.2 jit_solution(2258122211047938778)
XLA Ops:
  0.0 8.4 %collective-permute-start = (bf16[16,2048]{1,0:T(8,128)(2,1)}, bf16[16,2048]{1,0:T(8,128)(2,1)S(1)}, u32[]{:S(2)}, u32[]{:S(2)}) collective-permute-start(bf16[16,2048]{1,0:T(8,128)(2,1)} %param.13), channel_id=1, source_target_pairs={{0,8},{1,9},{2,10},{3,11},{4,12},{5,13},{6,14},{7,15},{8,0},{9,1},... | collective-permute-start | bytes 196616 | tf_op jit(solution)/shard_map/ppermute | solution.py:22
  8.5 4.8 %copy.116 = bf16[2048,2,256]{0,2,1:T(8,128)(2,1)S(1)} copy(bf16[2048,2,256]{2,1,0:T(2,128)(2,1)} %param.14) | data formatting | bytes 4194304 | tf_op args[1]
  13.5 0.8 dynamic_slice.40
  14.4 2.4 %collective-permute-start.1 = (bf16[2,16,2048]{2,1,0:T(8,128)(2,1)S(1)}, bf16[2,16,2048]{2,1,0:T(8,128)(2,1)S(1)}, u32[]{:S(2)}, u32[]{:S(2)}) collective-permute-start(bf16[2,16,2048]{2,1,0:T(8,128)(2,1)S(1)} %maximum_select_fusion.7), channel_id=1, source_target_pairs={{0,4},{1,5},{2,6},{3,7},{4,0},{5,1},{6,2},{7,3},{8,12},{9,13},{10,... | collective-permute-start | bytes 393224 | tf_op jit(solution)/shard_map/ppermute | solution.py:22
  16.8 8.1 %collective-permute-done.1 = bf16[2,16,2048]{2,1,0:T(8,128)(2,1)S(1)} collective-permute-done((bf16[2,16,2048]{2,1,0:T(8,128)(2,1)S(1)}, bf16[2,16,2048]{2,1,0:T(8,128)(2,1)S(1)}, u32[]{:S(2)}, u32[]{:S(2)}) %collective-permute-start.1) | collective-permute-done | bytes 131104 | tf_op jit(solution)/shard_map/ppermute | solution.py:22
  24.9 1.9 %collective-permute-start.2 = (bf16[2,2,16,2048]{3,2,1,0:T(8,128)(2,1)S(1)}, bf16[2,2,16,2048]{3,2,1,0:T(8,128)(2,1)S(1)}, u32[]{:S(2)}, u32[]{:S(2)}) collective-permute-start(bf16[2,2,16,2048]{3,2,1,0:T(8,128)(2,1)S(1)} %maximum_select_fusion.5), channel_id=1, source_target_pairs={{0,2},{1,3},{2,0},{3,1},{4,6},{5,7},{6,4},{7,5},{8,10},{9,11},{10,... | collective-permute-start | bytes 786440 | tf_op jit(solution)/shard_map/ppermute | solution.py:22
  26.9 6.8 %collective-permute-done.2 = bf16[2,2,16,2048]{3,2,1,0:T(8,128)(2,1)S(1)} collective-permute-done((bf16[2,2,16,2048]{3,2,1,0:T(8,128)(2,1)S(1)}, bf16[2,2,16,2048]{3,2,1,0:T(8,128)(2,1)S(1)}, u32[]{:S(2)}, u32[]{:S(2)}) %collective-permute-start.2) | collective-permute-done | bytes 262176 | tf_op jit(solution)/shard_map/ppermute | solution.py:22
  33.8 3.7 %collective-permute-start.3 = (bf16[2,2,2,16,2048]{4,3,2,1,0:T(8,128)(2,1)S(1)}, bf16[2,2,2,16,2048]{4,3,2,1,0:T(8,128)(2,1)S(1)}, u32[]{:S(2)}, u32[]{:S(2)}) collective-permute-start(bf16[2,2,2,16,2048]{4,3,2,1,0:T(8,128)(2,1)S(1)} %maximum_select_fusion.3), channel_id=1, source_target_pairs={{0,1},{1,0},{2,3},{3,2},{4,5},{5,4},{6,7},{7,6},{8,9},{9,8},{10,11... | collective-permute-start | bytes 1572872 | tf_op jit(solution)/shard_map/ppermute | solution.py:22
  37.6 0.9 constant_dynamic-slice_fusion
  39.1 1.1 fusion.14
  40.5 1.2 reduce-window.6
  42.8 3.7 %all-to-all-start = ((bf16[16,256,16]{1,2,0:T(8,128)(2,1)}), bf16[16,256,16]{1,2,0:T(8,128)(2,1)S(1)}, u32[]{:S(2)}, u32[]{:S(2)}) async-start(bf16[16,256,16]{1,2,0:T(8,128)(2,1)} %bitcast.21), calls=%async_computation | async-start | bytes 262144 | tf_op jit(solution)/shard_map/all_to_all | solution.py:99
  46.9 8.8 %all-to-all-done = bf16[16,256,16]{1,2,0:T(8,128)(2,1)S(1)} async-done(((bf16[16,256,16]{1,2,0:T(8,128)(2,1)}), bf16[16,256,16]{1,2,0:T(8,128)(2,1)S(1)}, u32[]{:S(2)}, u32[]{:S(2)}) %all-to-all-start) | async-done | bytes 131104 | tf_op jit(solution)/shard_map/all_to_all | solution.py:99
  55.9 3.5 %collective-permute-start.4 = (bf16[3,512]{1,0:T(4,128)(2,1)S(1)}, bf16[3,512]{1,0:T(4,128)(2,1)S(1)}, u32[]{:S(2)}, u32[]{:S(2)}) collective-permute-start(bf16[3,512]{1,0:T(4,128)(2,1)S(1)} %pad_maximum_fusion.5), channel_id=1, source_target_pairs={{0,16},{16,32},{32,48},{48,64},{64,80},{80,96},{96,112},{112,128},... | collective-permute-start | bytes 9224 | tf_op jit(solution)/shard_map/ppermute | solution.py:17
  61.7 4.5 %all-to-all-start.1 = ((bf16[4,4,65,128]{3,1,2,0:T(4,128)(2,1)}), bf16[4,4,65,128]{3,1,2,0:T(4,128)(2,1)S(1)}, u32[]{:S(2)}, u32[]{:S(2)}) async-start(bf16[4,4,65,128]{3,1,2,0:T(4,128)(2,1)} %broadcast_in_dim.49), calls=%async_computation.1 | async-start | bytes 532480 | tf_op jit(solution)/shard_map/all_to_all | solution.py:151
  66.3 5.5 %all-to-all-done.1 = bf16[4,4,65,128]{3,1,2,0:T(4,128)(2,1)S(1)} async-done(((bf16[4,4,65,128]{3,1,2,0:T(4,128)(2,1)}), bf16[4,4,65,128]{3,1,2,0:T(4,128)(2,1)S(1)}, u32[]{:S(2)}, u32[]{:S(2)}) %all-to-all-start.1) | async-done | bytes 266272 | tf_op jit(solution)/shard_map/all_to_all | solution.py:151
  72.3 5.6 %collective-permute-start.5 = (bf16[4,65,128]{2,0,1:T(4,128)(2,1)S(1)}, bf16[4,65,128]{2,0,1:T(4,128)(2,1)S(1)}, u32[]{:S(2)}, u32[]{:S(2)}) collective-permute-start(bf16[4,65,128]{2,0,1:T(4,128)(2,1)S(1)} %pad_maximum_fusion.2), channel_id=1, source_target_pairs={{0,64},{64,128},{128,192},{192,256},{256,320},{320,384},{384,448},... | collective-permute-start | bytes 199688 | tf_op jit(solution)/shard_map/ppermute | solution.py:17
  78.0 1.3 collective-permute-done.5
  79.7 5.8 %collective-permute-start.6 = (bf16[4,65,128]{2,0,1:T(4,128)(2,1)S(1)}, bf16[4,65,128]{2,0,1:T(4,128)(2,1)S(1)}, u32[]{:S(2)}, u32[]{:S(2)}) collective-permute-start(bf16[4,65,128]{2,0,1:T(4,128)(2,1)S(1)} %pad_maximum_fusion.3), channel_id=1, source_target_pairs={{0,128},{64,192},{128,256},{192,320},{256,384},{320,448},{1,129},{... | collective-permute-start | bytes 199688 | tf_op jit(solution)/shard_map/ppermute | solution.py:17
  85.6 1.2 collective-permute-done.6
  87.3 12.7 %collective-permute-start.7 = (bf16[4,65,128]{2,0,1:T(4,128)(2,1)S(1)}, bf16[4,65,128]{2,0,1:T(4,128)(2,1)S(1)}, u32[]{:S(2)}, u32[]{:S(2)}) collective-permute-start(bf16[4,65,128]{2,0,1:T(4,128)(2,1)S(1)} %pad_maximum_fusion.4), channel_id=1, source_target_pairs={{0,256},{64,320},{128,384},{192,448},{1,257},{65,321},{129,385},{1... | collective-permute-start | bytes 199688 | tf_op jit(solution)/shard_map/ppermute | solution.py:17
  100.5 0.9 collective-permute-done.7
  103.0 0.8 fusion.8
  103.8 7.0 %collective-permute-start.8 = (bf16[2,2,2,16,2176]{4,3,2,1,0:T(8,128)(2,1)S(1)}, bf16[2,2,2,16,2176]{4,3,2,1,0:T(8,128)(2,1)}, u32[]{:S(2)}, u32[]{:S(2)}) collective-permute-start(bf16[2,2,2,16,2176]{4,3,2,1,0:T(8,128)(2,1)S(1)} %fusion.26), channel_id=1, source_target_pairs={{0,1},{1,0},{2,3},{3,2},{4,5},{5,4},{6,7},{7,6},{8,9},{9,8},{10,11... | collective-permute-start | bytes 1671176 | tf_op jit(solution)/shard_map/ppermute | solution.py:22
  110.9 1.7 %collective-permute-done.8 = bf16[2,2,2,16,2176]{4,3,2,1,0:T(8,128)(2,1)} collective-permute-done((bf16[2,2,2,16,2176]{4,3,2,1,0:T(8,128)(2,1)S(1)}, bf16[2,2,2,16,2176]{4,3,2,1,0:T(8,128)(2,1)}, u32[]{:S(2)}, u32[]{:S(2)}) %collective-permute-start.8) | collective-permute-done | bytes 557088 | tf_op jit(solution)/shard_map/ppermute | solution.py:22
  112.5 1.1 bitcast_add_fusion
  113.7 2.0 %collective-permute-start.9 = (bf16[2,2,16,2176]{3,2,1,0:T(8,128)(2,1)S(1)}, bf16[2,2,16,2176]{3,2,1,0:T(8,128)(2,1)S(1)}, u32[]{:S(2)}, u32[]{:S(2)}) collective-permute-start(bf16[2,2,16,2176]{3,2,1,0:T(8,128)(2,1)S(1)} %fusion.33), channel_id=1, source_target_pairs={{0,2},{1,3},{2,0},{3,1},{4,6},{5,7},{6,4},{7,5},{8,10},{9,11},{10,... | collective-permute-start | bytes 835592 | tf_op jit(solution)/shard_map/ppermute | solution.py:22
  115.8 7.7 %collective-permute-done.9 = bf16[2,2,16,2176]{3,2,1,0:T(8,128)(2,1)S(1)} collective-permute-done((bf16[2,2,16,2176]{3,2,1,0:T(8,128)(2,1)S(1)}, bf16[2,2,16,2176]{3,2,1,0:T(8,128)(2,1)S(1)}, u32[]{:S(2)}, u32[]{:S(2)}) %collective-permute-start.9) | collective-permute-done | bytes 278560 | tf_op jit(solution)/shard_map/ppermute | solution.py:22
  123.8 2.3 %collective-permute-start.10 = (bf16[2,16,2048]{2,1,0:T(8,128)(2,1)S(1)}, bf16[2,16,2048]{2,1,0:T(8,128)(2,1)S(1)}, u32[]{:S(2)}, u32[]{:S(2)}) collective-permute-start(bf16[2,16,2048]{2,1,0:T(8,128)(2,1)S(1)} %fusion.50), channel_id=1, source_target_pairs={{0,4},{1,5},{2,6},{3,7},{4,0},{5,1},{6,2},{7,3},{8,12},{9,13},{10,... | collective-permute-start | bytes 393224 | tf_op jit(solution)/shard_map/ppermute | solution.py:22
  126.1 8.3 %collective-permute-done.10 = bf16[2,16,2048]{2,1,0:T(8,128)(2,1)S(1)} collective-permute-done((bf16[2,16,2048]{2,1,0:T(8,128)(2,1)S(1)}, bf16[2,16,2048]{2,1,0:T(8,128)(2,1)S(1)}, u32[]{:S(2)}, u32[]{:S(2)}) %collective-permute-start.10) | collective-permute-done | bytes 131104 | tf_op jit(solution)/shard_map/ppermute | solution.py:22
  134.5 2.5 %collective-permute-start.11 = (bf16[16,2048]{1,0:T(8,128)(2,1)S(1)}, bf16[16,2048]{1,0:T(8,128)(2,1)S(1)}, u32[]{:S(2)}, u32[]{:S(2)}) collective-permute-start(bf16[16,2048]{1,0:T(8,128)(2,1)S(1)} %fusion.52), channel_id=1, source_target_pairs={{0,8},{1,9},{2,10},{3,11},{4,12},{5,13},{6,14},{7,15},{8,0},{9,1},... | collective-permute-start | bytes 196616 | tf_op jit(solution)/shard_map/ppermute | solution.py:22
  137.0 6.5 %collective-permute-done.11 = bf16[16,2048]{1,0:T(8,128)(2,1)S(1)} collective-permute-done((bf16[16,2048]{1,0:T(8,128)(2,1)S(1)}, bf16[16,2048]{1,0:T(8,128)(2,1)S(1)}, u32[]{:S(2)}, u32[]{:S(2)}) %collective-permute-start.11) | collective-permute-done | bytes 65568 | tf_op jit(solution)/shard_map/ppermute | solution.py:22
  (118 shorter events, 9.6 us)
Async XLA Ops:
  0.0 13.2 %copy-start.1 = (bf16[16,4,2048]{2,1,0:T(4,128)(2,1)S(1)}, bf16[16,4,2048]{2,1,0:T(4,128)(2,1)}, u32[]{:S(2)}) copy-start(bf16[16,4,2048]{2,1,0:T(4,128)(2,1)} %param.16) | copy-start | bytes 786436
  0.0 14.3 %collective-permute-start = (bf16[16,2048]{1,0:T(8,128)(2,1)}, bf16[16,2048]{1,0:T(8,128)(2,1)S(1)}, u32[]{:S(2)}, u32[]{:S(2)}) collective-permute-start(bf16[16,2048]{1,0:T(8,128)(2,1)} %param.13), channel_id=1, source_target_pairs={{0,8},{1,9},{2,10},{3,11},{4,12},{5,13},{6,14},{7,15},{8,0},{9,1},... | collective-permute-start | bytes 196616 | tf_op jit(solution)/shard_map/ppermute | solution.py:22
  8.4 5.0 %copy-start.8 = (f32[4]{0:T(128)S(1)}, f32[4]{0:T(128)}, u32[]{:S(2)}) copy-start(f32[4]{0:T(128)} %param.22) | copy-start | bytes 52
  8.5 5.0 %copy-start.3 = (f32[4,256]{1,0:T(4,128)S(1)}, f32[4,256]{1,0:T(4,128)}, u32[]{:S(2)}) copy-start(f32[4,256]{1,0:T(4,128)} %param.17) | copy-start | bytes 12292
  8.5 5.8 %copy-start = (bf16[16,2048]{1,0:T(8,128)(2,1)S(1)}, bf16[16,2048]{1,0:T(8,128)(2,1)}, u32[]{:S(2)}) copy-start(bf16[16,2048]{1,0:T(8,128)(2,1)} %param.13) | copy-start | bytes 196612
  14.3 24.8 %copy-start.7 = (bf16[2048,4]{0,1:T(4,128)(2,1)S(1)}, bf16[2048,4]{0,1:T(4,128)(2,1)}, u32[]{:S(2)}) copy-start(bf16[2048,4]{0,1:T(4,128)(2,1)} %param.15) | copy-start | bytes 49156
  14.4 10.6 %collective-permute-start.1 = (bf16[2,16,2048]{2,1,0:T(8,128)(2,1)S(1)}, bf16[2,16,2048]{2,1,0:T(8,128)(2,1)S(1)}, u32[]{:S(2)}, u32[]{:S(2)}) collective-permute-start(bf16[2,16,2048]{2,1,0:T(8,128)(2,1)S(1)} %maximum_select_fusion.7), channel_id=1, source_target_pairs={{0,4},{1,5},{2,6},{3,7},{4,0},{5,1},{6,2},{7,3},{8,12},{9,13},{10,... | collective-permute-start | bytes 393224 | tf_op jit(solution)/shard_map/ppermute | solution.py:22
  24.9 8.8 %collective-permute-start.2 = (bf16[2,2,16,2048]{3,2,1,0:T(8,128)(2,1)S(1)}, bf16[2,2,16,2048]{3,2,1,0:T(8,128)(2,1)S(1)}, u32[]{:S(2)}, u32[]{:S(2)}) collective-permute-start(bf16[2,2,16,2048]{3,2,1,0:T(8,128)(2,1)S(1)} %maximum_select_fusion.5), channel_id=1, source_target_pairs={{0,2},{1,3},{2,0},{3,1},{4,6},{5,7},{6,4},{7,5},{8,10},{9,11},{10,... | collective-permute-start | bytes 786440 | tf_op jit(solution)/shard_map/ppermute | solution.py:22
  33.8 5.2 %collective-permute-start.3 = (bf16[2,2,2,16,2048]{4,3,2,1,0:T(8,128)(2,1)S(1)}, bf16[2,2,2,16,2048]{4,3,2,1,0:T(8,128)(2,1)S(1)}, u32[]{:S(2)}, u32[]{:S(2)}) collective-permute-start(bf16[2,2,2,16,2048]{4,3,2,1,0:T(8,128)(2,1)S(1)} %maximum_select_fusion.3), channel_id=1, source_target_pairs={{0,1},{1,0},{2,3},{3,2},{4,5},{5,4},{6,7},{7,6},{8,9},{9,8},{10,11... | collective-permute-start | bytes 1572872 | tf_op jit(solution)/shard_map/ppermute | solution.py:22
  39.1 1.3 copy-start.2
  40.2 20.0 %copy-start.5 = (f32[256]{0:T(256)S(1)}, f32[256]{0:T(256)}, u32[]{:S(2)}) copy-start(f32[256]{0:T(256)} %param.18) | copy-start | bytes 3076
  42.8 12.9 %all-to-all-start = ((bf16[16,256,16]{1,2,0:T(8,128)(2,1)}), bf16[16,256,16]{1,2,0:T(8,128)(2,1)S(1)}, u32[]{:S(2)}, u32[]{:S(2)}) async-start(bf16[16,256,16]{1,2,0:T(8,128)(2,1)} %bitcast.21), calls=%async_computation | async-start | bytes 262144 | tf_op jit(solution)/shard_map/all_to_all | solution.py:99
  55.9 4.2 %collective-permute-start.4 = (bf16[3,512]{1,0:T(4,128)(2,1)S(1)}, bf16[3,512]{1,0:T(4,128)(2,1)S(1)}, u32[]{:S(2)}, u32[]{:S(2)}) collective-permute-start(bf16[3,512]{1,0:T(4,128)(2,1)S(1)} %pad_maximum_fusion.5), channel_id=1, source_target_pairs={{0,16},{16,32},{32,48},{48,64},{64,80},{80,96},{96,112},{112,128},... | collective-permute-start | bytes 9224 | tf_op jit(solution)/shard_map/ppermute | solution.py:17
  61.7 10.1 %all-to-all-start.1 = ((bf16[4,4,65,128]{3,1,2,0:T(4,128)(2,1)}), bf16[4,4,65,128]{3,1,2,0:T(4,128)(2,1)S(1)}, u32[]{:S(2)}, u32[]{:S(2)}) async-start(bf16[4,4,65,128]{3,1,2,0:T(4,128)(2,1)} %broadcast_in_dim.49), calls=%async_computation.1 | async-start | bytes 532480 | tf_op jit(solution)/shard_map/all_to_all | solution.py:151
  72.1 29.6 %copy-start.9 = (f32[4]{0:T(128)S(1)}, f32[4]{0:T(128)}, u32[]{:S(2)}) copy-start(f32[4]{0:T(128)} %param.23) | copy-start | bytes 52
  72.3 6.9 %collective-permute-start.5 = (bf16[4,65,128]{2,0,1:T(4,128)(2,1)S(1)}, bf16[4,65,128]{2,0,1:T(4,128)(2,1)S(1)}, u32[]{:S(2)}, u32[]{:S(2)}) collective-permute-start(bf16[4,65,128]{2,0,1:T(4,128)(2,1)S(1)} %pad_maximum_fusion.2), channel_id=1, source_target_pairs={{0,64},{64,128},{128,192},{192,256},{256,320},{320,384},{384,448},... | collective-permute-start | bytes 199688 | tf_op jit(solution)/shard_map/ppermute | solution.py:17
  79.7 7.1 %collective-permute-start.6 = (bf16[4,65,128]{2,0,1:T(4,128)(2,1)S(1)}, bf16[4,65,128]{2,0,1:T(4,128)(2,1)S(1)}, u32[]{:S(2)}, u32[]{:S(2)}) collective-permute-start(bf16[4,65,128]{2,0,1:T(4,128)(2,1)S(1)} %pad_maximum_fusion.3), channel_id=1, source_target_pairs={{0,128},{64,192},{128,256},{192,320},{256,384},{320,448},{1,129},{... | collective-permute-start | bytes 199688 | tf_op jit(solution)/shard_map/ppermute | solution.py:17
  87.3 14.1 %collective-permute-start.7 = (bf16[4,65,128]{2,0,1:T(4,128)(2,1)S(1)}, bf16[4,65,128]{2,0,1:T(4,128)(2,1)S(1)}, u32[]{:S(2)}, u32[]{:S(2)}) collective-permute-start(bf16[4,65,128]{2,0,1:T(4,128)(2,1)S(1)} %pad_maximum_fusion.4), channel_id=1, source_target_pairs={{0,256},{64,320},{128,384},{192,448},{1,257},{65,321},{129,385},{1... | collective-permute-start | bytes 199688 | tf_op jit(solution)/shard_map/ppermute | solution.py:17
  100.3 2.1 %copy-start.4 = (f32[256]{0:T(256)S(1)}, f32[256]{0:T(256)}, u32[]{:S(2)}) copy-start(f32[256]{0:T(256)} %param.24) | copy-start | bytes 3076
  101.7 1.2 copy-start.6
  103.8 8.7 %collective-permute-start.8 = (bf16[2,2,2,16,2176]{4,3,2,1,0:T(8,128)(2,1)S(1)}, bf16[2,2,2,16,2176]{4,3,2,1,0:T(8,128)(2,1)}, u32[]{:S(2)}, u32[]{:S(2)}) collective-permute-start(bf16[2,2,2,16,2176]{4,3,2,1,0:T(8,128)(2,1)S(1)} %fusion.26), channel_id=1, source_target_pairs={{0,1},{1,0},{2,3},{3,2},{4,5},{5,4},{6,7},{7,6},{8,9},{9,8},{10,11... | collective-permute-start | bytes 1671176 | tf_op jit(solution)/shard_map/ppermute | solution.py:22
  113.7 9.7 %collective-permute-start.9 = (bf16[2,2,16,2176]{3,2,1,0:T(8,128)(2,1)S(1)}, bf16[2,2,16,2176]{3,2,1,0:T(8,128)(2,1)S(1)}, u32[]{:S(2)}, u32[]{:S(2)}) collective-permute-start(bf16[2,2,16,2176]{3,2,1,0:T(8,128)(2,1)S(1)} %fusion.33), channel_id=1, source_target_pairs={{0,2},{1,3},{2,0},{3,1},{4,6},{5,7},{6,4},{7,5},{8,10},{9,11},{10,... | collective-permute-start | bytes 835592 | tf_op jit(solution)/shard_map/ppermute | solution.py:22
  123.8 10.7 %collective-permute-start.10 = (bf16[2,16,2048]{2,1,0:T(8,128)(2,1)S(1)}, bf16[2,16,2048]{2,1,0:T(8,128)(2,1)S(1)}, u32[]{:S(2)}, u32[]{:S(2)}) collective-permute-start(bf16[2,16,2048]{2,1,0:T(8,128)(2,1)S(1)} %fusion.50), channel_id=1, source_target_pairs={{0,4},{1,5},{2,6},{3,7},{4,0},{5,1},{6,2},{7,3},{8,12},{9,13},{10,... | collective-permute-start | bytes 393224 | tf_op jit(solution)/shard_map/ppermute | solution.py:22
  134.5 9.0 %collective-permute-start.11 = (bf16[16,2048]{1,0:T(8,128)(2,1)S(1)}, bf16[16,2048]{1,0:T(8,128)(2,1)S(1)}, u32[]{:S(2)}, u32[]{:S(2)}) collective-permute-start(bf16[16,2048]{1,0:T(8,128)(2,1)S(1)} %fusion.52), channel_id=1, source_target_pairs={{0,8},{1,9},{2,10},{3,11},{4,12},{5,13},{6,14},{7,15},{8,0},{9,1},... | collective-permute-start | bytes 196616 | tf_op jit(solution)/shard_map/ppermute | solution.py:22

commit v10 on v9

--- a/solution.py
+++ b/solution.py
@@ -67,22 +67,27 @@
     norm_gain,
     out_weight,
 ):
-    tp_size = lax.axis_size("tp")
-    tp_bits = [1 << k for k in range(tp_size.bit_length() - 1)]
+    tp_size = lax.axis_size(TP_AXES)
     heads_dev = log_rate.shape[0]
     inner_dev = in_weight.shape[2]
     group_cols = 2 * STATE
     per_group_dev = (HEADS // GROUPS) // heads_dev
-    group_index = lax.axis_index("tp") // per_group_dev
+    group_index = lax.axis_index("tg")
     zx_weight = in_weight.reshape(in_weight.shape[0], 2 * inner_dev)
-    stacked = gather_rows(hidden, "tp", tp_bits)
-    levels = len(tp_bits)
+    ring = ("tg", "yl")
+    ring_size = lax.axis_size(ring)
     length = tp_size * hidden.shape[0]
-    flipped = tuple(reversed(range(levels)))
+    ring_rows = lax.all_to_all(
+        jnp.broadcast_to(hidden[None], (ring_size,) + hidden.shape), ring, 0, 0, tiled=True
+    )
+    other_rows = lax.ppermute(ring_rows, "tc", [(0, 1), (1, 0)])
+    first = lax.axis_index("tc") == 0
+    stacked = jnp.where(
+        first, jnp.stack([ring_rows, other_rows], axis=1), jnp.stack([other_rows, ring_rows], axis=1)
+    ).reshape((length,) + hidden.shape[1:])
 
     def in_order(rows):
-        rows = jnp.transpose(rows, flipped + tuple(range(levels, rows.ndim)))
-        return rows.reshape((length,) + rows.shape[levels + 1 :])
+        return rows
 
     map_cols = jnp.transpose(group_weight, (2, 1, 0)).reshape(group_weight.shape[2], -1)
     joined = jnp.concatenate([zx_weight, step_weight, map_cols], axis=1)
@@ -96,7 +101,7 @@
     own_maps = jnp.moveaxis(own_maps, 1, 0)
     own_maps = jnp.broadcast_to(own_maps[:, None], (GROUPS, per_group_dev) + own_maps.shape[1:])
     own_maps = own_maps.reshape((tp_size,) + own_maps.shape[2:])
-    got_maps = lax.all_to_all(own_maps, "tp", 0, 0, tiled=True)
+    got_maps = lax.all_to_all(own_maps, TP_AXES, 0, 0, tiled=True)
     map_part = jnp.transpose(got_maps, (1, 0, 2)).reshape(length, group_cols)
     border_rows = KERNEL - 1
     prior = shifted(
@@ -210,39 +215,48 @@
         ],
         axis=0,
     )
-    scaled = scaled.reshape((2,) * levels + (length // tp_size, 2 * inner_dev))
-    scaled = jnp.transpose(scaled, flipped + (levels, levels + 1))
+    groups_here = lax.axis_size("tg")
+    per = length // tp_size
+    scaled = scaled.reshape((groups_here, 2, 2, per, 2 * inner_dev))
+    scaled = jnp.transpose(scaled, (2, 1, 0, 3, 4))
     partial = jnp.einsum("...c,cn->...n", scaled, extended, preferred_element_type=jnp.float32)
-    within_bits = [bit for bit in tp_bits if bit < per_group_dev]
-    across_bits = [bit for bit in tp_bits if bit >= per_group_dev]
-    held = halve(partial, "tp", within_bits)
-    inverse = lax.rsqrt(held[..., width] / (HEADS * HEAD_DIM // GROUPS) + 1e-05)
-    held = held[..., :width] * inverse[..., None]
-    held = halve(held, "tp", across_bits)
-    mixed = held
+    for axis in ("tc", "yl"):
+        mine = lax.axis_index(axis)
+        keep = lax.dynamic_index_in_dim(partial, mine, 0, keepdims=False)
+        give = lax.dynamic_index_in_dim(partial, 1 - mine, 0, keepdims=False)
+        partial = keep + lax.ppermute(give.astype(jnp.bfloat16), axis, [(0, 1), (1, 0)]).astype(jnp.float32)
+    inverse = lax.rsqrt(partial[..., width] / (HEADS * HEAD_DIM // GROUPS) + 1e-05)
+    held = (partial[..., :width] * inverse[..., None]).astype(jnp.bfloat16)
+    arrived = lax.all_to_all(held, "tg", 0, 0, tiled=True)
+    mixed = jnp.sum(arrived.astype(jnp.float32), axis=0)
     return mixed.astype(jnp.bfloat16)
+
+
+TP_AXES = ("tg", "yl", "tc")
 
 
 def solution(mesh):
     ctx_size = mesh.shape["ctx"]
+    tp_size = mesh.shape["tp"]
     x_size = 4 if ctx_size % 4 == 0 else ctx_size
     fine = Mesh(
-        mesh.devices.reshape(ctx_size // x_size, x_size, mesh.shape["tp"]), ("z", "x", "tp")
-    )
-    rows = ("z", "x", "tp")
+        mesh.devices.reshape(ctx_size // x_size, x_size, tp_size // 4, 2, 2), ("z", "x") + TP_AXES
+    )
+    rows = ("z", "x") + TP_AXES
+    tp = TP_AXES
     placed = (
         P(rows, None),
-        P(None, None, "tp"),
-        P(None, "tp"),
-        P("tp", None, None),
-        P(None, "tp"),
-        P("tp"),
+        P(None, None, tp),
+        P(None, tp),
+        P(tp, None, None),
+        P(None, tp),
+        P(tp),
         P(),
         P(),
-        P("tp"),
-        P("tp"),
-        P("tp"),
-        P("tp"),
-        P("tp", None),
+        P(tp),
+        P(tp),
+        P(tp),
+        P(tp),
+        P(tp, None),
     )
     return jax.shard_map(body, mesh=fine, in_specs=placed, out_specs=P(rows, None), check_vma=False)

time: 145 us -> 134 us (0.924)
  waiting for transfers between devices: 57.7 us -> 40.9 us
  blocking collectives: 0 us -> 10.9 us
  starting transfers between devices: 66.1 us -> 57.8 us
  matrix products: 2.96 us -> 5.65 us
    ppermute x8 -> x3, waiting for transfers between devices: 39.6 us -> 9.5 us  [the longest x2 9.5 us: body(): lax.ppermute(give.astype(jnp.bfloat16), axis, [(0, 1), (1, 0)])]
    ppermute x8 -> x3, starting transfers between devices: 30.3 us -> 14 us  [the longest x2 8.64 us: body(): lax.ppermute(give.astype(jnp.bfloat16), axis, [(0, 1), (1, 0)])]
    all_to_all x0 -> x1, blocking collectives: none -> 10.9 us  [body(): arrived = lax.all_to_all(held, 'tg', 0, 0, tiled=True)]
    all_to_all x1 -> x2, waiting for transfers between devices: 8.8 us -> 18.9 us  [the longest x1 10.5 us: body(): lax.all_to_all(jnp.broadcast_to(hidden[None], (ring_size,) + hidden.shape...]
    all_to_all x1 -> x2, starting transfers between devices: 3.67 us -> 11.3 us  [the longest x1 7.64 us: body(): lax.all_to_all(jnp.broadcast_to(hidden[None], (ring_size,) + hidden.shape...]
    ppermute x4, waiting for transfers between devices: 3.89 us -> 6.8 us  [shifted(): return lax.ppermute(x, axis, pairs)]
    unnamed x23 -> x22, local copies, waits for them, and re-layouts: 5.32 us -> 3.44 us
    broadcast_in_dim x0 -> x1, local copies, waits for them, and re-layouts: none -> 1.68 us  [body(): jnp.broadcast_to(hidden[None], (ring_size,) + hidden.shape)]
  transfers between devices with their start and end apart: 14 -> 10, of which waited for: 13 -> 9; matrix products, arithmetic and copies ran while one was open for 6% -> 5% of each run, Pallas kernels for 0% -> 0%
where the time goes in v10:
time: 134 us; the launch traced here: 133 us
  starting transfers between devices  57.8 us (43%)
  waiting for transfers between devices  40.9 us (31%)
  blocking collectives  10.9 us (8%)
  local copies, waits for them, and re-layouts  10.8 us (8%)
  other arithmetic  5.86 us (4%)
  matrix products  5.65 us (4%)
    ppermute x4, starting transfers between devices, shifted(): return lax.ppermute(x, axis, pairs)  27.5 us
    all_to_all x1, blocking collectives, body(): arrived = lax.all_to_all(held, 'tg', 0, 0, tiled=True)  10.9 us
    all_to_all x1, waiting for transfers between devices, body(): lax.all_to_all(jnp.broadcast_to(hidden[None], (ring_size,) + hidden.shape...  10.5 us
    ppermute x2, waiting for transfers between devices, body(): lax.ppermute(give.astype(jnp.bfloat16), axis, [(0, 1), (1, 0)])  9.5 us
    ppermute x2, starting transfers between devices, body(): lax.ppermute(give.astype(jnp.bfloat16), axis, [(0, 1), (1, 0)])  8.64 us
    all_to_all x1, waiting for transfers between devices, body(): got_maps = lax.all_to_all(own_maps, TP_AXES, 0, 0, tiled=True)  8.48 us
    all_to_all x1, starting transfers between devices, body(): lax.all_to_all(jnp.broadcast_to(hidden[None], (ring_size,) + hidden.shape...  7.64 us
    ppermute x4, waiting for transfers between devices, shifted(): return lax.ppermute(x, axis, pairs)  6.8 us
  transfers between devices with their start and end apart: 10, of which 9 were waited for; matrix products, arithmetic and copies ran while one was open for 5% of the time, Pallas kernels for 0%

profile of v10, /device:TPU:1, one launch (start us, length us, event | category | flops | bytes accessed | tf_op | source)
XLA Modules:
  0.0 132.5 jit_solution(2229986121733117567)
XLA Ops:
  0.0 1.7 %broadcast_in_dim.46 = bf16[8,16,2048]{2,1,0:T(8,128)(2,1)} broadcast(bf16[16,2048]{1,0:T(8,128)(2,1)} %param.13), dimensions={1,2} | broadcast | bytes 589824 | tf_op jit(solution)/shard_map/broadcast_in_dim | solution.py:81
  1.7 7.6 %all-to-all-start = ((bf16[8,16,2048]{2,1,0:T(8,128)(2,1)}), bf16[8,16,2048]{2,1,0:T(8,128)(2,1)S(1)}, u32[]{:S(2)}, u32[]{:S(2)}) async-start(bf16[8,16,2048]{2,1,0:T(8,128)(2,1)} %broadcast_in_dim.46), calls=%async_computation | async-start | bytes 1048576 | tf_op jit(solution)/shard_map/all_to_all | solution.py:80
  9.4 2.1 %copy.142 = bf16[256,8,2,256]{3,1,2,0:T(8,128)(2,1)S(1)} copy(bf16[256,8,2,256]{3,2,1,0:T(2,128)(2,1)} %bitcast.139) | data formatting | bytes 4194304
  11.9 1.1 copy.119
  13.0 0.8 dynamic_slice.26
  13.8 10.5 %all-to-all-done = bf16[8,16,2048]{2,1,0:T(8,128)(2,1)S(1)} async-done(((bf16[8,16,2048]{2,1,0:T(8,128)(2,1)}), bf16[8,16,2048]{2,1,0:T(8,128)(2,1)S(1)}, u32[]{:S(2)}, u32[]{:S(2)}) %all-to-all-start) | async-done | bytes 524320 | tf_op jit(solution)/shard_map/all_to_all | solution.py:80
  24.3 5.4 %collective-permute-start = (bf16[8,16,2048]{2,1,0:T(8,128)(2,1)S(1)}, bf16[8,16,2048]{2,1,0:T(8,128)(2,1)S(1)}, u32[]{:S(2)}, u32[]{:S(2)}) collective-permute-start(bf16[8,16,2048]{2,1,0:T(8,128)(2,1)S(1)} %all-to-all-done), channel_id=1, source_target_pairs={{0,1},{1,0},{2,3},{3,2},{4,5},{5,4},{6,7},{7,6},{8,9},{9,8},{10,11... | collective-permute-start | bytes 1572872 | tf_op jit(solution)/shard_map/ppermute | solution.py:83
  29.7 0.9 constant_dynamic-slice_fusion
  31.3 2.5 %fusion.14 = bf16[256,580]{0,1:T(8,128)(2,1)S(1)} fusion(bf16[256,2048]{1,0:T(8,128)(2,1)S(1)} %bitcast.141, bf16[2048,64]{1,0:T(8,128)(2,1)S(1)} %copy.120, bf16[2048,4]{1,0:T(8,128)(2,1)} %copy.119, bf16[2048,512]{1,0:T(8,128)(2,1)S(1)} %bitcast.140), kind=kOutput, calls=%fused_computation.14 | convolution fusion | flops 615449600 | bytes 3721216 | tf_op jit(solution)/shard_map/...d,dn->...n/dot_general | solution.py:95
  33.9 1.2 reduce-window.6
  35.3 0.6 broadcast_in_dim.47
  35.9 3.7 %all-to-all-start.1 = ((bf16[16,256,16]{1,2,0:T(8,128)(2,1)}), bf16[16,256,16]{1,2,0:T(8,128)(2,1)S(1)}, u32[]{:S(2)}, u32[]{:S(2)}) async-start(bf16[16,256,16]{1,2,0:T(8,128)(2,1)} %bitcast.8), calls=%async_computation.1 | async-start | bytes 262144 | tf_op jit(solution)/shard_map/all_to_all | solution.py:104
  40.3 8.5 %all-to-all-done.1 = bf16[16,256,16]{1,2,0:T(8,128)(2,1)S(1)} async-done(((bf16[16,256,16]{1,2,0:T(8,128)(2,1)}), bf16[16,256,16]{1,2,0:T(8,128)(2,1)S(1)}, u32[]{:S(2)}, u32[]{:S(2)}) %all-to-all-start.1) | async-done | bytes 131104 | tf_op jit(solution)/shard_map/all_to_all | solution.py:104
  48.9 3.1 %collective-permute-start.1 = (bf16[3,512]{0,1:T(8,128)(2,1)S(1)}, bf16[3,512]{0,1:T(8,128)(2,1)S(1)}, u32[]{:S(2)}, u32[]{:S(2)}) collective-permute-start(bf16[3,512]{0,1:T(8,128)(2,1)S(1)} %pad_maximum_fusion.1), channel_id=1, source_target_pairs={{0,16},{16,32},{32,48},{48,64},{64,80},{80,96},{96,112},{112,128},... | collective-permute-start | bytes 9224 | tf_op jit(solution)/shard_map/ppermute | solution.py:17
  52.1 3.1 %collective-permute-done.1 = bf16[3,512]{0,1:T(8,128)(2,1)S(1)} collective-permute-done((bf16[3,512]{0,1:T(8,128)(2,1)S(1)}, bf16[3,512]{0,1:T(8,128)(2,1)S(1)}, u32[]{:S(2)}, u32[]{:S(2)}) %collective-permute-start.1) | collective-permute-done | bytes 3104 | tf_op jit(solution)/shard_map/ppermute | solution.py:17
  56.7 0.8 broadcast_in_dim.52
  57.5 5.0 %all-to-all-start.2 = ((bf16[4,4,65,128]{3,1,2,0:T(4,128)(2,1)}), bf16[4,4,65,128]{3,1,2,0:T(4,128)(2,1)S(1)}, u32[]{:S(2)}, u32[]{:S(2)}) async-start(bf16[4,4,65,128]{3,1,2,0:T(4,128)(2,1)} %broadcast_in_dim.52), calls=%async_computation.2 | async-start | bytes 532480 | tf_op jit(solution)/shard_map/all_to_all | solution.py:156
  62.6 5.7 %all-to-all-done.2 = bf16[4,4,65,128]{3,1,2,0:T(4,128)(2,1)S(1)} async-done(((bf16[4,4,65,128]{3,1,2,0:T(4,128)(2,1)}), bf16[4,4,65,128]{3,1,2,0:T(4,128)(2,1)S(1)}, u32[]{:S(2)}, u32[]{:S(2)}) %all-to-all-start.2) | async-done | bytes 266272 | tf_op jit(solution)/shard_map/all_to_all | solution.py:156
  68.7 5.8 %collective-permute-start.2 = (bf16[4,65,128]{2,0,1:T(4,128)(2,1)S(1)}, bf16[4,65,128]{2,0,1:T(4,128)(2,1)S(1)}, u32[]{:S(2)}, u32[]{:S(2)}) collective-permute-start(bf16[4,65,128]{2,0,1:T(4,128)(2,1)S(1)} %pad_maximum_fusion.3), channel_id=1, source_target_pairs={{0,64},{64,128},{128,192},{192,256},{256,320},{320,384},{384,448},... | collective-permute-start | bytes 199688 | tf_op jit(solution)/shard_map/ppermute | solution.py:17
  74.5 1.3 collective-permute-done.2
  76.2 5.8 %collective-permute-start.3 = (bf16[4,65,128]{2,0,1:T(4,128)(2,1)S(1)}, bf16[4,65,128]{2,0,1:T(4,128)(2,1)S(1)}, u32[]{:S(2)}, u32[]{:S(2)}) collective-permute-start(bf16[4,65,128]{2,0,1:T(4,128)(2,1)S(1)} %pad_maximum_fusion.4), channel_id=1, source_target_pairs={{0,128},{64,192},{128,256},{192,320},{256,384},{320,448},{1,129},{... | collective-permute-start | bytes 199688 | tf_op jit(solution)/shard_map/ppermute | solution.py:17
  82.1 1.2 collective-permute-done.3
  83.9 12.7 %collective-permute-start.4 = (bf16[4,65,128]{2,0,1:T(4,128)(2,1)S(1)}, bf16[4,65,128]{2,0,1:T(4,128)(2,1)S(1)}, u32[]{:S(2)}, u32[]{:S(2)}) collective-permute-start(bf16[4,65,128]{2,0,1:T(4,128)(2,1)S(1)} %pad_maximum_fusion.5), channel_id=1, source_target_pairs={{0,256},{64,320},{128,384},{192,448},{1,257},{65,321},{129,385},{1... | collective-permute-start | bytes 199688 | tf_op jit(solution)/shard_map/ppermute | solution.py:17
  96.9 1.1 collective-permute-done.4
  99.2 2.0 %fusion.9 = f32[2,2,4,16,2176]{4,3,2,1,0:T(8,128)S(1)} fusion(bf16[256,2048]{1,0:T(8,128)(2,1)} %param.25, bf16[256,2176]{1,0:T(8,128)(2,1)S(1)} %concatenate.57, bf16[4,2,2,16,512]{4,3,2,1,0:T(8,128)(2,1)S(1)} %bitcast.147), kind=kOutput, calls=%fused_computation.10 | convolution fusion | flops 577110016 | bytes 4653056 | tf_op jit(solution)/shard_map/...c,cn->...n/dot_general | solution.py:222
  101.3 6.7 %collective-permute-start.5 = (bf16[2,4,16,2176]{3,2,1,0:T(8,128)(2,1)S(1)}, bf16[2,4,16,2176]{3,2,1,0:T(8,128)(2,1)}, u32[]{:S(2)}, u32[]{:S(2)}) collective-permute-start(bf16[2,4,16,2176]{3,2,1,0:T(8,128)(2,1)S(1)} %fusion.22), channel_id=1, source_target_pairs={{0,1},{1,0},{2,3},{3,2},{4,5},{5,4},{6,7},{7,6},{8,9},{9,8},{10,11... | collective-permute-start | bytes 1671176 | tf_op jit(solution)/shard_map/ppermute | solution.py:227
  108.0 1.7 %collective-permute-done.5 = bf16[2,4,16,2176]{3,2,1,0:T(8,128)(2,1)} collective-permute-done((bf16[2,4,16,2176]{3,2,1,0:T(8,128)(2,1)S(1)}, bf16[2,4,16,2176]{3,2,1,0:T(8,128)(2,1)}, u32[]{:S(2)}, u32[]{:S(2)}) %collective-permute-start.5) | collective-permute-done | bytes 557088 | tf_op jit(solution)/shard_map/ppermute | solution.py:227
  109.7 1.1 bitcast_add_fusion
  110.9 1.9 %collective-permute-start.6 = (bf16[4,16,2176]{2,1,0:T(8,128)(2,1)S(1)}, bf16[4,16,2176]{2,1,0:T(8,128)(2,1)S(1)}, u32[]{:S(2)}, u32[]{:S(2)}) collective-permute-start(bf16[4,16,2176]{2,1,0:T(8,128)(2,1)S(1)} %fusion.30), channel_id=1, source_target_pairs={{0,2},{2,0},{1,3},{3,1},{4,6},{6,4},{5,7},{7,5},{8,10},{10,8},{9,1... | collective-permute-start | bytes 835592 | tf_op jit(solution)/shard_map/ppermute | solution.py:227
  112.8 7.8 %collective-permute-done.6 = bf16[4,16,2176]{2,1,0:T(8,128)(2,1)S(1)} collective-permute-done((bf16[4,16,2176]{2,1,0:T(8,128)(2,1)S(1)}, bf16[4,16,2176]{2,1,0:T(8,128)(2,1)S(1)}, u32[]{:S(2)}, u32[]{:S(2)}) %collective-permute-start.6) | collective-permute-done | bytes 278560 | tf_op jit(solution)/shard_map/ppermute | solution.py:227
  120.9 10.9 %all_to_all.20 = bf16[4,16,2048]{2,1,0:T(8,128)(2,1)S(1)} all-to-all(bf16[4,16,2048]{2,1,0:T(8,128)(2,1)S(1)} %fusion.23), channel_id=1, replica_groups=mesh['z'=8,'x'=4,'tg'=4,'yl'=2,'tc'=2] {'tg'}, dimensions={0} | all-to-all | bytes 524288 | tf_op jit(solution)/shard_map/all_to_all | solution.py:230
  131.8 0.7 reduce_sum.12
  (91 shorter events, 6.8 us)
Async XLA Ops:
  1.7 22.6 %all-to-all-start = ((bf16[8,16,2048]{2,1,0:T(8,128)(2,1)}), bf16[8,16,2048]{2,1,0:T(8,128)(2,1)S(1)}, u32[]{:S(2)}, u32[]{:S(2)}) async-start(bf16[8,16,2048]{2,1,0:T(8,128)(2,1)} %broadcast_in_dim.46), calls=%async_computation | async-start | bytes 1048576 | tf_op jit(solution)/shard_map/all_to_all | solution.py:80
  9.3 2.2 %copy-start = (bf16[16,4,2048]{2,1,0:T(4,128)(2,1)S(1)}, bf16[16,4,2048]{2,1,0:T(4,128)(2,1)}, u32[]{:S(2)}) copy-start(bf16[16,4,2048]{2,1,0:T(4,128)(2,1)} %param.16) | copy-start | bytes 786436
  9.3 2.6 %copy-start.1 = (bf16[2048,4]{0,1:T(4,128)(2,1)S(1)}, bf16[2048,4]{0,1:T(4,128)(2,1)}, u32[]{:S(2)}) copy-start(bf16[2048,4]{0,1:T(4,128)(2,1)} %param.15) | copy-start | bytes 49156
  9.4 21.2 %copy-start.7 = (f32[4]{0:T(128)S(1)}, f32[4]{0:T(128)}, u32[]{:S(2)}) copy-start(f32[4]{0:T(128)} %param.22) | copy-start | bytes 52
  9.4 21.2 %copy-start.3 = (f32[4,256]{1,0:T(4,128)S(1)}, f32[4,256]{1,0:T(4,128)}, u32[]{:S(2)}) copy-start(f32[4,256]{1,0:T(4,128)} %param.17) | copy-start | bytes 12292
  24.3 6.9 %collective-permute-start = (bf16[8,16,2048]{2,1,0:T(8,128)(2,1)S(1)}, bf16[8,16,2048]{2,1,0:T(8,128)(2,1)S(1)}, u32[]{:S(2)}, u32[]{:S(2)}) collective-permute-start(bf16[8,16,2048]{2,1,0:T(8,128)(2,1)S(1)} %all-to-all-done), channel_id=1, source_target_pairs={{0,1},{1,0},{2,3},{3,2},{4,5},{5,4},{6,7},{7,6},{8,9},{9,8},{10,11... | collective-permute-start | bytes 1572872 | tf_op jit(solution)/shard_map/ppermute | solution.py:83
  31.3 2.5 %copy-start.2 = (f32[4]{0:T(128)S(1)}, f32[4]{0:T(128)}, u32[]{:S(2)}) copy-start(f32[4]{0:T(128)} %param.21) | copy-start | bytes 52
  33.8 22.1 %copy-start.4 = (f32[1,256]{1,0:T(1,128)S(1)}, f32[1,256]{1,0:T(1,128)}, u32[]{:S(2)}) copy-start(f32[1,256]{1,0:T(1,128)} %get-tuple-element.59) | copy-start | bytes 3076
  33.8 22.1 %copy-start.6 = (f32[256]{0:T(256)S(1)}, f32[256]{0:T(256)}, u32[]{:S(2)}) copy-start(f32[256]{0:T(256)} %param.18) | copy-start | bytes 3076
  35.9 12.9 %all-to-all-start.1 = ((bf16[16,256,16]{1,2,0:T(8,128)(2,1)}), bf16[16,256,16]{1,2,0:T(8,128)(2,1)S(1)}, u32[]{:S(2)}, u32[]{:S(2)}) async-start(bf16[16,256,16]{1,2,0:T(8,128)(2,1)} %bitcast.8), calls=%async_computation.1 | async-start | bytes 262144 | tf_op jit(solution)/shard_map/all_to_all | solution.py:104
  48.9 6.3 %collective-permute-start.1 = (bf16[3,512]{0,1:T(8,128)(2,1)S(1)}, bf16[3,512]{0,1:T(8,128)(2,1)S(1)}, u32[]{:S(2)}, u32[]{:S(2)}) collective-permute-start(bf16[3,512]{0,1:T(8,128)(2,1)S(1)} %pad_maximum_fusion.1), channel_id=1, source_target_pairs={{0,16},{16,32},{32,48},{48,64},{64,80},{80,96},{96,112},{112,128},... | collective-permute-start | bytes 9224 | tf_op jit(solution)/shard_map/ppermute | solution.py:17
  57.5 10.7 %all-to-all-start.2 = ((bf16[4,4,65,128]{3,1,2,0:T(4,128)(2,1)}), bf16[4,4,65,128]{3,1,2,0:T(4,128)(2,1)S(1)}, u32[]{:S(2)}, u32[]{:S(2)}) async-start(bf16[4,4,65,128]{3,1,2,0:T(4,128)(2,1)} %broadcast_in_dim.52), calls=%async_computation.2 | async-start | bytes 532480 | tf_op jit(solution)/shard_map/all_to_all | solution.py:156
  68.4 29.9 %copy-start.8 = (f32[4]{0:T(128)S(1)}, f32[4]{0:T(128)}, u32[]{:S(2)}) copy-start(f32[4]{0:T(128)} %param.23) | copy-start | bytes 52
  68.7 7.1 %collective-permute-start.2 = (bf16[4,65,128]{2,0,1:T(4,128)(2,1)S(1)}, bf16[4,65,128]{2,0,1:T(4,128)(2,1)S(1)}, u32[]{:S(2)}, u32[]{:S(2)}) collective-permute-start(bf16[4,65,128]{2,0,1:T(4,128)(2,1)S(1)} %pad_maximum_fusion.3), channel_id=1, source_target_pairs={{0,64},{64,128},{128,192},{192,256},{256,320},{320,384},{384,448},... | collective-permute-start | bytes 199688 | tf_op jit(solution)/shard_map/ppermute | solution.py:17
  76.2 7.1 %collective-permute-start.3 = (bf16[4,65,128]{2,0,1:T(4,128)(2,1)S(1)}, bf16[4,65,128]{2,0,1:T(4,128)(2,1)S(1)}, u32[]{:S(2)}, u32[]{:S(2)}) collective-permute-start(bf16[4,65,128]{2,0,1:T(4,128)(2,1)S(1)} %pad_maximum_fusion.4), channel_id=1, source_target_pairs={{0,128},{64,192},{128,256},{192,320},{256,384},{320,448},{1,129},{... | collective-permute-start | bytes 199688 | tf_op jit(solution)/shard_map/ppermute | solution.py:17
  83.5 15.3 %copy-start.5 = (f32[256]{0:T(256)S(1)}, f32[256]{0:T(256)}, u32[]{:S(2)}) copy-start(f32[256]{0:T(256)} %param.24) | copy-start | bytes 3076
  83.9 14.1 %collective-permute-start.4 = (bf16[4,65,128]{2,0,1:T(4,128)(2,1)S(1)}, bf16[4,65,128]{2,0,1:T(4,128)(2,1)S(1)}, u32[]{:S(2)}, u32[]{:S(2)}) collective-permute-start(bf16[4,65,128]{2,0,1:T(4,128)(2,1)S(1)} %pad_maximum_fusion.5), channel_id=1, source_target_pairs={{0,256},{64,320},{128,384},{192,448},{1,257},{65,321},{129,385},{1... | collective-permute-start | bytes 199688 | tf_op jit(solution)/shard_map/ppermute | solution.py:17
  101.3 8.4 %collective-permute-start.5 = (bf16[2,4,16,2176]{3,2,1,0:T(8,128)(2,1)S(1)}, bf16[2,4,16,2176]{3,2,1,0:T(8,128)(2,1)}, u32[]{:S(2)}, u32[]{:S(2)}) collective-permute-start(bf16[2,4,16,2176]{3,2,1,0:T(8,128)(2,1)S(1)} %fusion.22), channel_id=1, source_target_pairs={{0,1},{1,0},{2,3},{3,2},{4,5},{5,4},{6,7},{7,6},{8,9},{9,8},{10,11... | collective-permute-start | bytes 1671176 | tf_op jit(solution)/shard_map/ppermute | solution.py:227
  110.9 9.7 %collective-permute-start.6 = (bf16[4,16,2176]{2,1,0:T(8,128)(2,1)S(1)}, bf16[4,16,2176]{2,1,0:T(8,128)(2,1)S(1)}, u32[]{:S(2)}, u32[]{:S(2)}) collective-permute-start(bf16[4,16,2176]{2,1,0:T(8,128)(2,1)S(1)} %fusion.30), channel_id=1, source_target_pairs={{0,2},{2,0},{1,3},{3,1},{4,6},{6,4},{5,7},{7,5},{8,10},{10,8},{9,1... | collective-permute-start | bytes 835592 | tf_op jit(solution)/shard_map/ppermute | solution.py:227

commit v11 on v10

--- a/solution.py
+++ b/solution.py
@@ -106,7 +106,7 @@
     border_rows = KERNEL - 1
     prior = shifted(
         jnp.concatenate([inner_raw[length - border_rows :], map_part[length - border_rows :]], axis=1),
-        ("z", "x"),
+        ("zh", "zl", "x"),
         1,
     )
     inner_prior = prior[:, :inner_dev]
@@ -148,47 +148,34 @@
     (dev_state, dev_decay), (local_starts, prefixes) = lax.scan(
         advance, (empty_state, jnp.ones((heads_dev,), jnp.float32)), (block_decay, block_state)
     )
-    x_peers = lax.axis_size("x")
-    x_place = lax.axis_index("x")
-    packed = jnp.concatenate(
-        [dev_state, jnp.broadcast_to(dev_decay[:, None, None], (heads_dev, 1, STATE))], axis=1
-    ).astype(jnp.bfloat16)
-    row = lax.all_to_all(
-        jnp.broadcast_to(packed[None], (x_peers,) + packed.shape), "x", 0, 0, tiled=True
-    ).astype(jnp.float32)
-    row_decay = jnp.ones_like(dev_decay)
-    row_state = jnp.zeros_like(dev_state)
-    in_decay = jnp.ones_like(dev_decay)
-    in_state = jnp.zeros_like(dev_state)
-    for k in reversed(range(x_peers)):
-        got_state = row[k, :, :HEAD_DIM]
-        got_decay = row[k, :, HEAD_DIM, 0]
-        earlier = k < x_place
-        in_state = jnp.where(earlier, in_decay[:, None, None] * got_state + in_state, in_state)
-        in_decay = jnp.where(earlier, got_decay * in_decay, in_decay)
-        row_state = row_decay[:, None, None] * got_state + row_state
-        row_decay = got_decay * row_decay
-    z_peers = lax.axis_size("z")
-    z_place = lax.axis_index("z")
-    pre_decay = jnp.ones_like(dev_decay)
-    pre_state = jnp.zeros_like(dev_state)
-    run_decay = row_decay
-    run_state = row_state
-    reach = 1
-    while reach < z_peers:
+    def level(decay, state, axis):
+        peers = lax.axis_size(axis)
+        place = lax.axis_index(axis)
         packed = jnp.concatenate(
-            [run_state, jnp.broadcast_to(run_decay[:, None, None], (heads_dev, 1, STATE))], axis=1
-        )
-        got = shifted(packed.astype(jnp.bfloat16), "z", reach).astype(jnp.float32)
-        valid = z_place >= reach
-        got_state = jnp.where(valid, got[:, :HEAD_DIM], 0.0)
-        got_decay = jnp.where(valid, got[:, HEAD_DIM, 0], 1.0)
-        pre_state = pre_decay[:, None, None] * got_state + pre_state
-        pre_decay = got_decay * pre_decay
-        run_state = run_decay[:, None, None] * got_state + run_state
-        run_decay = got_decay * run_decay
-        reach *= 2
-    in_state = in_decay[:, None, None] * pre_state + in_state
+            [state, jnp.broadcast_to(decay[:, None, None], (heads_dev, 1, STATE))], axis=1
+        ).astype(jnp.bfloat16)
+        got = lax.all_to_all(
+            jnp.broadcast_to(packed[None], (peers,) + packed.shape), axis, 0, 0, tiled=True
+        ).astype(jnp.float32)
+        tot_decay = jnp.ones_like(decay)
+        tot_state = jnp.zeros_like(state)
+        ex_decay = jnp.ones_like(decay)
+        ex_state = jnp.zeros_like(state)
+        for k in reversed(range(peers)):
+            got_state = got[k, :, :HEAD_DIM]
+            got_decay = got[k, :, HEAD_DIM, 0]
+            earlier = k < place
+            ex_state = jnp.where(earlier, ex_decay[:, None, None] * got_state + ex_state, ex_state)
+            ex_decay = jnp.where(earlier, got_decay * ex_decay, ex_decay)
+            tot_state = tot_decay[:, None, None] * got_state + tot_state
+            tot_decay = got_decay * tot_decay
+        return ex_decay, ex_state, tot_decay, tot_state
+
+    in_decay, in_state, row_decay, row_state = level(dev_decay, dev_state, "x")
+    mid_decay, mid_state, part_decay, part_state = level(row_decay, row_state, "zl")
+    top_decay, top_state, _, _ = level(part_decay, part_state, "zh")
+    before_state = mid_decay[:, None, None] * top_state + mid_state
+    in_state = in_decay[:, None, None] * before_state + in_state
     incoming = in_state
     starting = local_starts + prefixes[:, :, None, None] * incoming[None]
     carried = jnp.einsum(
@@ -239,10 +226,13 @@
     ctx_size = mesh.shape["ctx"]
     tp_size = mesh.shape["tp"]
     x_size = 4 if ctx_size % 4 == 0 else ctx_size
+    z_size = ctx_size // x_size
+    zl_size = 4 if z_size % 4 == 0 else z_size
     fine = Mesh(
-        mesh.devices.reshape(ctx_size // x_size, x_size, tp_size // 4, 2, 2), ("z", "x") + TP_AXES
-    )
-    rows = ("z", "x") + TP_AXES
+        mesh.devices.reshape(z_size // zl_size, zl_size, x_size, tp_size // 4, 2, 2),
+        ("zh", "zl", "x") + TP_AXES,
+    )
+    rows = ("zh", "zl", "x") + TP_AXES
     tp = TP_AXES
     placed = (
         P(rows, None),

time: 134 us -> 137 us (1.022)
  waiting for transfers between devices: 40.9 us -> 50.4 us
  starting transfers between devices: 57.8 us -> 50.7 us
    ppermute x4 -> x1, starting transfers between devices: 27.5 us -> 3.12 us  [shifted(): return lax.ppermute(x, axis, pairs)]
    all_to_all x1 -> x3, starting transfers between devices: 5 us -> 21.5 us  [level(): lax.all_to_all(jnp.broadcast_to(packed[None], (peers,) + packed.shape), a...]
    all_to_all x1 -> x3, waiting for transfers between devices: 5.66 us -> 18.3 us  [level(): lax.all_to_all(jnp.broadcast_to(packed[None], (peers,) + packed.shape), a...]
    ppermute x4 -> x1, waiting for transfers between devices: 6.8 us -> 3.14 us  [shifted(): return lax.ppermute(x, axis, pairs)]
    broadcast_in_dim x5 -> x6, local copies, waits for them, and re-layouts: 1.07 us -> 2.45 us  [the longest x3 2.23 us: level(): jnp.broadcast_to(packed[None], (peers,) + packed.shape)]
    unnamed x22 -> x20, local copies, waits for them, and re-layouts: 3.44 us -> 3.43 us
  transfers between devices with their start and end apart: 10 -> 9, of which waited for: 9 -> 9; matrix products, arithmetic and copies ran while one was open for 5% -> 5% of each run, Pallas kernels for 0% -> 0%
where the time goes in v11:
time: 137 us; the launch traced here: 136 us
  starting transfers between devices  50.7 us (37%)
  waiting for transfers between devices  50.4 us (37%)
  local copies, waits for them, and re-layouts  11.6 us (8%)
  blocking collectives  10.9 us (8%)
  other arithmetic  5.92 us (4%)
  matrix products  5.54 us (4%)
    all_to_all x3, starting transfers between devices, level(): lax.all_to_all(jnp.broadcast_to(packed[None], (peers,) + packed.shape), a...  21.5 us
    all_to_all x3, waiting for transfers between devices, level(): lax.all_to_all(jnp.broadcast_to(packed[None], (peers,) + packed.shape), a...  18.3 us
    all_to_all x1, blocking collectives, body(): arrived = lax.all_to_all(held, 'tg', 0, 0, tiled=True)  10.9 us
    all_to_all x1, waiting for transfers between devices, body(): lax.all_to_all(jnp.broadcast_to(hidden[None], (ring_size,) + hidden.shape...  10.5 us
    ppermute x2, waiting for transfers between devices, body(): lax.ppermute(give.astype(jnp.bfloat16), axis, [(0, 1), (1, 0)])  9.5 us
    ppermute x2, starting transfers between devices, body(): lax.ppermute(give.astype(jnp.bfloat16), axis, [(0, 1), (1, 0)])  9.42 us
    all_to_all x1, waiting for transfers between devices, body(): got_maps = lax.all_to_all(own_maps, TP_AXES, 0, 0, tiled=True)  8.48 us
    all_to_all x1, starting transfers between devices, body(): lax.all_to_all(jnp.broadcast_to(hidden[None], (ring_size,) + hidden.shape...  7.64 us
  transfers between devices with their start and end apart: 9, of which 9 were waited for; matrix products, arithmetic and copies ran while one was open for 5% of the time, Pallas kernels for 0%

profile of v11, /device:TPU:1, one launch (start us, length us, event | category | flops | bytes accessed | tf_op | source)
XLA Modules:
  0.0 135.6 jit_solution(13269399680985179652)
XLA Ops:
  0.0 1.7 %broadcast_in_dim.39 = bf16[8,16,2048]{2,1,0:T(8,128)(2,1)} broadcast(bf16[16,2048]{1,0:T(8,128)(2,1)} %param.13), dimensions={1,2} | broadcast | bytes 589824 | tf_op jit(solution)/shard_map/broadcast_in_dim | solution.py:81
  1.7 7.6 %all-to-all-start = ((bf16[8,16,2048]{2,1,0:T(8,128)(2,1)}), bf16[8,16,2048]{2,1,0:T(8,128)(2,1)S(1)}, u32[]{:S(2)}, u32[]{:S(2)}) async-start(bf16[8,16,2048]{2,1,0:T(8,128)(2,1)} %broadcast_in_dim.39), calls=%async_computation | async-start | bytes 1048576 | tf_op jit(solution)/shard_map/all_to_all | solution.py:80
  9.4 2.1 %copy.77 = bf16[256,8,2,256]{3,1,2,0:T(8,128)(2,1)S(1)} copy(bf16[256,8,2,256]{3,2,1,0:T(2,128)(2,1)} %bitcast.110) | data formatting | bytes 4194304
  11.9 1.1 copy.62
  13.0 0.8 dynamic_slice.26
  13.8 10.5 %all-to-all-done = bf16[8,16,2048]{2,1,0:T(8,128)(2,1)S(1)} async-done(((bf16[8,16,2048]{2,1,0:T(8,128)(2,1)}), bf16[8,16,2048]{2,1,0:T(8,128)(2,1)S(1)}, u32[]{:S(2)}, u32[]{:S(2)}) %all-to-all-start) | async-done | bytes 524320 | tf_op jit(solution)/shard_map/all_to_all | solution.py:80
  24.3 5.4 %collective-permute-start = (bf16[8,16,2048]{2,1,0:T(8,128)(2,1)S(1)}, bf16[8,16,2048]{2,1,0:T(8,128)(2,1)S(1)}, u32[]{:S(2)}, u32[]{:S(2)}) collective-permute-start(bf16[8,16,2048]{2,1,0:T(8,128)(2,1)S(1)} %all-to-all-done), channel_id=1, source_target_pairs={{0,1},{1,0},{2,3},{3,2},{4,5},{5,4},{6,7},{7,6},{8,9},{9,8},{10,11... | collective-permute-start | bytes 1572872 | tf_op jit(solution)/shard_map/ppermute | solution.py:83
  29.7 0.9 constant_dynamic-slice_fusion
  31.3 2.5 %fusion.14 = bf16[256,580]{0,1:T(8,128)(2,1)S(1)} fusion(bf16[256,2048]{1,0:T(8,128)(2,1)S(1)} %bitcast.112, bf16[2048,64]{1,0:T(8,128)(2,1)S(1)} %copy.63, bf16[2048,4]{1,0:T(8,128)(2,1)} %copy.62, bf16[2048,512]{1,0:T(8,128)(2,1)S(1)} %bitcast.111), kind=kOutput, calls=%fused_computation.14 | convolution fusion | flops 615449600 | bytes 3721216 | tf_op jit(solution)/shard_map/...d,dn->...n/dot_general | solution.py:95
  33.9 1.2 reduce-window.6
  35.2 0.6 broadcast_in_dim.40
  35.9 3.7 %all-to-all-start.1 = ((bf16[16,256,16]{1,2,0:T(8,128)(2,1)}), bf16[16,256,16]{1,2,0:T(8,128)(2,1)S(1)}, u32[]{:S(2)}, u32[]{:S(2)}) async-start(bf16[16,256,16]{1,2,0:T(8,128)(2,1)} %bitcast.8), calls=%async_computation.1 | async-start | bytes 262144 | tf_op jit(solution)/shard_map/all_to_all | solution.py:104
  40.3 8.5 %all-to-all-done.1 = bf16[16,256,16]{1,2,0:T(8,128)(2,1)S(1)} async-done(((bf16[16,256,16]{1,2,0:T(8,128)(2,1)}), bf16[16,256,16]{1,2,0:T(8,128)(2,1)S(1)}, u32[]{:S(2)}, u32[]{:S(2)}) %all-to-all-start.1) | async-done | bytes 131104 | tf_op jit(solution)/shard_map/all_to_all | solution.py:104
  48.9 3.1 %collective-permute-start.1 = (bf16[3,512]{0,1:T(8,128)(2,1)S(1)}, bf16[3,512]{0,1:T(8,128)(2,1)S(1)}, u32[]{:S(2)}, u32[]{:S(2)}) collective-permute-start(bf16[3,512]{0,1:T(8,128)(2,1)S(1)} %pad_maximum_fusion.1), channel_id=1, source_target_pairs={{0,16},{16,32},{32,48},{48,64},{64,80},{80,96},{96,112},{112,128},... | collective-permute-start | bytes 9224 | tf_op jit(solution)/shard_map/ppermute | solution.py:17
  52.0 3.1 %collective-permute-done.1 = bf16[3,512]{0,1:T(8,128)(2,1)S(1)} collective-permute-done((bf16[3,512]{0,1:T(8,128)(2,1)S(1)}, bf16[3,512]{0,1:T(8,128)(2,1)S(1)}, u32[]{:S(2)}, u32[]{:S(2)}) %collective-permute-start.1) | collective-permute-done | bytes 3104 | tf_op jit(solution)/shard_map/ppermute | solution.py:17
  56.7 0.8 broadcast_in_dim.45
  57.5 5.0 %all-to-all-start.2 = ((bf16[4,4,65,128]{3,1,2,0:T(4,128)(2,1)}), bf16[4,4,65,128]{3,1,2,0:T(4,128)(2,1)S(1)}, u32[]{:S(2)}, u32[]{:S(2)}) async-start(bf16[4,4,65,128]{3,1,2,0:T(4,128)(2,1)} %broadcast_in_dim.45), calls=%async_computation.2 | async-start | bytes 532480 | tf_op jit(solution)/shard_map/all_to_all | solution.py:157
  62.5 5.6 %all-to-all-done.2 = bf16[4,4,65,128]{3,1,2,0:T(4,128)(2,1)S(1)} async-done(((bf16[4,4,65,128]{3,1,2,0:T(4,128)(2,1)}), bf16[4,4,65,128]{3,1,2,0:T(4,128)(2,1)S(1)}, u32[]{:S(2)}, u32[]{:S(2)}) %all-to-all-start.2) | async-done | bytes 266272 | tf_op jit(solution)/shard_map/all_to_all | solution.py:157
  68.6 0.8 broadcast_in_dim.47
  69.4 8.8 %all-to-all-start.3 = ((bf16[4,4,65,128]{3,1,2,0:T(4,128)(2,1)}), bf16[4,4,65,128]{3,1,2,0:T(4,128)(2,1)S(1)}, u32[]{:S(2)}, u32[]{:S(2)}) async-start(bf16[4,4,65,128]{3,1,2,0:T(4,128)(2,1)} %broadcast_in_dim.47), calls=%async_computation.3 | async-start | bytes 532480 | tf_op jit(solution)/shard_map/all_to_all | solution.py:157
  78.3 5.6 %all-to-all-done.3 = bf16[4,4,65,128]{3,1,2,0:T(4,128)(2,1)S(1)} async-done(((bf16[4,4,65,128]{3,1,2,0:T(4,128)(2,1)}), bf16[4,4,65,128]{3,1,2,0:T(4,128)(2,1)S(1)}, u32[]{:S(2)}, u32[]{:S(2)}) %all-to-all-start.3) | async-done | bytes 266272 | tf_op jit(solution)/shard_map/all_to_all | solution.py:157
  84.4 0.7 broadcast_in_dim.49
  85.1 7.7 %all-to-all-start.4 = ((bf16[2,4,65,128]{3,1,2,0:T(4,128)(2,1)}), bf16[2,4,65,128]{3,1,2,0:T(4,128)(2,1)S(1)}, u32[]{:S(2)}, u32[]{:S(2)}) async-start(bf16[2,4,65,128]{3,1,2,0:T(4,128)(2,1)} %broadcast_in_dim.49), calls=%async_computation.4 | async-start | bytes 266240 | tf_op jit(solution)/shard_map/all_to_all | solution.py:157
  92.9 7.0 %all-to-all-done.4 = bf16[2,4,65,128]{3,1,2,0:T(4,128)(2,1)S(1)} async-done(((bf16[2,4,65,128]{3,1,2,0:T(4,128)(2,1)}), bf16[2,4,65,128]{3,1,2,0:T(4,128)(2,1)S(1)}, u32[]{:S(2)}, u32[]{:S(2)}) %all-to-all-start.4) | async-done | bytes 133152 | tf_op jit(solution)/shard_map/all_to_all | solution.py:157
  101.5 2.0 %fusion.9 = f32[2,2,4,16,2176]{4,3,2,1,0:T(8,128)S(1)} fusion(bf16[256,2048]{1,0:T(8,128)(2,1)} %param.25, bf16[256,2176]{1,0:T(8,128)(2,1)S(1)} %concatenate.66, bf16[4,2,2,16,512]{4,3,2,1,0:T(8,128)(2,1)S(1)} %bitcast.118), kind=kOutput, calls=%fused_computation.10 | convolution fusion | flops 577110016 | bytes 4653056 | tf_op jit(solution)/shard_map/...c,cn->...n/dot_general | solution.py:209
  103.6 7.5 %collective-permute-start.2 = (bf16[2,4,16,2176]{3,2,1,0:T(8,128)(2,1)S(1)}, bf16[2,4,16,2176]{3,2,1,0:T(8,128)(2,1)}, u32[]{:S(2)}, u32[]{:S(2)}) collective-permute-start(bf16[2,4,16,2176]{3,2,1,0:T(8,128)(2,1)S(1)} %fusion.22), channel_id=1, source_target_pairs={{0,1},{1,0},{2,3},{3,2},{4,5},{5,4},{6,7},{7,6},{8,9},{9,8},{10,11... | collective-permute-start | bytes 1671176 | tf_op jit(solution)/shard_map/ppermute | solution.py:214
  111.1 1.7 %collective-permute-done.2 = bf16[2,4,16,2176]{3,2,1,0:T(8,128)(2,1)} collective-permute-done((bf16[2,4,16,2176]{3,2,1,0:T(8,128)(2,1)S(1)}, bf16[2,4,16,2176]{3,2,1,0:T(8,128)(2,1)}, u32[]{:S(2)}, u32[]{:S(2)}) %collective-permute-start.2) | collective-permute-done | bytes 557088 | tf_op jit(solution)/shard_map/ppermute | solution.py:214
  112.8 1.1 bitcast_add_fusion
  114.0 1.9 %collective-permute-start.3 = (bf16[4,16,2176]{2,1,0:T(8,128)(2,1)S(1)}, bf16[4,16,2176]{2,1,0:T(8,128)(2,1)S(1)}, u32[]{:S(2)}, u32[]{:S(2)}) collective-permute-start(bf16[4,16,2176]{2,1,0:T(8,128)(2,1)S(1)} %fusion.30), channel_id=1, source_target_pairs={{0,2},{2,0},{1,3},{3,1},{4,6},{6,4},{5,7},{7,5},{8,10},{10,8},{9,1... | collective-permute-start | bytes 835592 | tf_op jit(solution)/shard_map/ppermute | solution.py:214
  115.9 7.8 %collective-permute-done.3 = bf16[4,16,2176]{2,1,0:T(8,128)(2,1)S(1)} collective-permute-done((bf16[4,16,2176]{2,1,0:T(8,128)(2,1)S(1)}, bf16[4,16,2176]{2,1,0:T(8,128)(2,1)S(1)}, u32[]{:S(2)}, u32[]{:S(2)}) %collective-permute-start.3) | collective-permute-done | bytes 278560 | tf_op jit(solution)/shard_map/ppermute | solution.py:214
  124.0 10.9 %all_to_all.30 = bf16[4,16,2048]{2,1,0:T(8,128)(2,1)S(1)} all-to-all(bf16[4,16,2048]{2,1,0:T(8,128)(2,1)S(1)} %fusion.23), channel_id=1, replica_groups=mesh['zh'=2,'zl'=4,'x'=4,'tg'=4,'yl'=2,'tc'=2] {'tg'}, dimensions={0} | all-to-all | bytes 524288 | tf_op jit(solution)/shard_map/all_to_all | solution.py:217
  134.9 0.7 reduce_sum.12
  (82 shorter events, 6.7 us)
Async XLA Ops:
  1.7 22.6 %all-to-all-start = ((bf16[8,16,2048]{2,1,0:T(8,128)(2,1)}), bf16[8,16,2048]{2,1,0:T(8,128)(2,1)S(1)}, u32[]{:S(2)}, u32[]{:S(2)}) async-start(bf16[8,16,2048]{2,1,0:T(8,128)(2,1)} %broadcast_in_dim.39), calls=%async_computation | async-start | bytes 1048576 | tf_op jit(solution)/shard_map/all_to_all | solution.py:80
  9.3 2.2 %copy-start = (bf16[16,4,2048]{2,1,0:T(4,128)(2,1)S(1)}, bf16[16,4,2048]{2,1,0:T(4,128)(2,1)}, u32[]{:S(2)}) copy-start(bf16[16,4,2048]{2,1,0:T(4,128)(2,1)} %param.16) | copy-start | bytes 786436
  9.4 2.6 %copy-start.1 = (bf16[2048,4]{0,1:T(4,128)(2,1)S(1)}, bf16[2048,4]{0,1:T(4,128)(2,1)}, u32[]{:S(2)}) copy-start(bf16[2048,4]{0,1:T(4,128)(2,1)} %param.15) | copy-start | bytes 49156
  9.4 21.2 %copy-start.6 = (f32[4]{0:T(128)S(1)}, f32[4]{0:T(128)}, u32[]{:S(2)}) copy-start(f32[4]{0:T(128)} %param.22) | copy-start | bytes 52
  9.4 21.2 %copy-start.3 = (f32[4,256]{1,0:T(4,128)S(1)}, f32[4,256]{1,0:T(4,128)}, u32[]{:S(2)}) copy-start(f32[4,256]{1,0:T(4,128)} %param.17) | copy-start | bytes 12292
  24.3 6.9 %collective-permute-start = (bf16[8,16,2048]{2,1,0:T(8,128)(2,1)S(1)}, bf16[8,16,2048]{2,1,0:T(8,128)(2,1)S(1)}, u32[]{:S(2)}, u32[]{:S(2)}) collective-permute-start(bf16[8,16,2048]{2,1,0:T(8,128)(2,1)S(1)} %all-to-all-done), channel_id=1, source_target_pairs={{0,1},{1,0},{2,3},{3,2},{4,5},{5,4},{6,7},{7,6},{8,9},{9,8},{10,11... | collective-permute-start | bytes 1572872 | tf_op jit(solution)/shard_map/ppermute | solution.py:83
  31.3 2.5 %copy-start.2 = (f32[4]{0:T(128)S(1)}, f32[4]{0:T(128)}, u32[]{:S(2)}) copy-start(f32[4]{0:T(128)} %param.21) | copy-start | bytes 52
  33.8 22.1 %copy-start.5 = (f32[256]{0:T(256)S(1)}, f32[256]{0:T(256)}, u32[]{:S(2)}) copy-start(f32[256]{0:T(256)} %param.18) | copy-start | bytes 3076
  35.9 12.9 %all-to-all-start.1 = ((bf16[16,256,16]{1,2,0:T(8,128)(2,1)}), bf16[16,256,16]{1,2,0:T(8,128)(2,1)S(1)}, u32[]{:S(2)}, u32[]{:S(2)}) async-start(bf16[16,256,16]{1,2,0:T(8,128)(2,1)} %bitcast.8), calls=%async_computation.1 | async-start | bytes 262144 | tf_op jit(solution)/shard_map/all_to_all | solution.py:104
  48.9 6.3 %collective-permute-start.1 = (bf16[3,512]{0,1:T(8,128)(2,1)S(1)}, bf16[3,512]{0,1:T(8,128)(2,1)S(1)}, u32[]{:S(2)}, u32[]{:S(2)}) collective-permute-start(bf16[3,512]{0,1:T(8,128)(2,1)S(1)} %pad_maximum_fusion.1), channel_id=1, source_target_pairs={{0,16},{16,32},{32,48},{48,64},{64,80},{80,96},{96,112},{112,128},... | collective-permute-start | bytes 9224 | tf_op jit(solution)/shard_map/ppermute | solution.py:17
  57.5 10.7 %all-to-all-start.2 = ((bf16[4,4,65,128]{3,1,2,0:T(4,128)(2,1)}), bf16[4,4,65,128]{3,1,2,0:T(4,128)(2,1)S(1)}, u32[]{:S(2)}, u32[]{:S(2)}) async-start(bf16[4,4,65,128]{3,1,2,0:T(4,128)(2,1)} %broadcast_in_dim.45), calls=%async_computation.2 | async-start | bytes 532480 | tf_op jit(solution)/shard_map/all_to_all | solution.py:157
  69.4 14.5 %all-to-all-start.3 = ((bf16[4,4,65,128]{3,1,2,0:T(4,128)(2,1)}), bf16[4,4,65,128]{3,1,2,0:T(4,128)(2,1)S(1)}, u32[]{:S(2)}, u32[]{:S(2)}) async-start(bf16[4,4,65,128]{3,1,2,0:T(4,128)(2,1)} %broadcast_in_dim.47), calls=%async_computation.3 | async-start | bytes 532480 | tf_op jit(solution)/shard_map/all_to_all | solution.py:157
  78.3 22.4 %copy-start.7 = (f32[4]{0:T(128)S(1)}, f32[4]{0:T(128)}, u32[]{:S(2)}) copy-start(f32[4]{0:T(128)} %param.23) | copy-start | bytes 52
  85.1 14.9 %all-to-all-start.4 = ((bf16[2,4,65,128]{3,1,2,0:T(4,128)(2,1)}), bf16[2,4,65,128]{3,1,2,0:T(4,128)(2,1)S(1)}, u32[]{:S(2)}, u32[]{:S(2)}) async-start(bf16[2,4,65,128]{3,1,2,0:T(4,128)(2,1)} %broadcast_in_dim.49), calls=%async_computation.4 | async-start | bytes 266240 | tf_op jit(solution)/shard_map/all_to_all | solution.py:157
  92.9 8.2 %copy-start.4 = (f32[256]{0:T(256)S(1)}, f32[256]{0:T(256)}, u32[]{:S(2)}) copy-start(f32[256]{0:T(256)} %param.24) | copy-start | bytes 3076
  103.6 9.2 %collective-permute-start.2 = (bf16[2,4,16,2176]{3,2,1,0:T(8,128)(2,1)S(1)}, bf16[2,4,16,2176]{3,2,1,0:T(8,128)(2,1)}, u32[]{:S(2)}, u32[]{:S(2)}) collective-permute-start(bf16[2,4,16,2176]{3,2,1,0:T(8,128)(2,1)S(1)} %fusion.22), channel_id=1, source_target_pairs={{0,1},{1,0},{2,3},{3,2},{4,5},{5,4},{6,7},{7,6},{8,9},{9,8},{10,11... | collective-permute-start | bytes 1671176 | tf_op jit(solution)/shard_map/ppermute | solution.py:214
  114.0 9.7 %collective-permute-start.3 = (bf16[4,16,2176]{2,1,0:T(8,128)(2,1)S(1)}, bf16[4,16,2176]{2,1,0:T(8,128)(2,1)S(1)}, u32[]{:S(2)}, u32[]{:S(2)}) collective-permute-start(bf16[4,16,2176]{2,1,0:T(8,128)(2,1)S(1)} %fusion.30), channel_id=1, source_target_pairs={{0,2},{2,0},{1,3},{3,1},{4,6},{6,4},{5,7},{7,5},{8,10},{10,8},{9,1... | collective-permute-start | bytes 835592 | tf_op jit(solution)/shard_map/ppermute | solution.py:214

commit v12 on v10

--- a/solution.py
+++ b/solution.py
@@ -218,17 +218,18 @@
     groups_here = lax.axis_size("tg")
     per = length // tp_size
     scaled = scaled.reshape((groups_here, 2, 2, per, 2 * inner_dev))
-    scaled = jnp.transpose(scaled, (2, 1, 0, 3, 4))
+    scaled = jnp.transpose(scaled, (2, 0, 1, 3, 4))
     partial = jnp.einsum("...c,cn->...n", scaled, extended, preferred_element_type=jnp.float32)
-    for axis in ("tc", "yl"):
-        mine = lax.axis_index(axis)
-        keep = lax.dynamic_index_in_dim(partial, mine, 0, keepdims=False)
-        give = lax.dynamic_index_in_dim(partial, 1 - mine, 0, keepdims=False)
-        partial = keep + lax.ppermute(give.astype(jnp.bfloat16), axis, [(0, 1), (1, 0)]).astype(jnp.float32)
-    inverse = lax.rsqrt(partial[..., width] / (HEADS * HEAD_DIM // GROUPS) + 1e-05)
-    held = (partial[..., :width] * inverse[..., None]).astype(jnp.bfloat16)
-    arrived = lax.all_to_all(held, "tg", 0, 0, tiled=True)
-    mixed = jnp.sum(arrived.astype(jnp.float32), axis=0)
+    mine = lax.axis_index("tc")
+    keep = lax.dynamic_index_in_dim(partial, mine, 0, keepdims=False)
+    give = lax.dynamic_index_in_dim(partial, 1 - mine, 0, keepdims=False)
+    partial = keep + lax.ppermute(give.astype(jnp.bfloat16), "tc", [(0, 1), (1, 0)]).astype(jnp.float32)
+    partial = partial.reshape((ring_size,) + partial.shape[2:])
+    arrived = lax.all_to_all(partial.astype(jnp.bfloat16), ring, 0, 0, tiled=True)
+    arrived = arrived.astype(jnp.float32).reshape((groups_here, ring_size // groups_here) + arrived.shape[1:])
+    per_group = jnp.sum(arrived, axis=1)
+    inverse = lax.rsqrt(per_group[..., width] / (HEADS * HEAD_DIM // GROUPS) + 1e-05)
+    mixed = jnp.sum(per_group[..., :width] * inverse[..., None], axis=0)
     return mixed.astype(jnp.bfloat16)
 
 

time: 134 us -> 132 us (0.985)
  blocking collectives: 10.9 us -> 20.6 us
  waiting for transfers between devices: 40.9 us -> 32.9 us
  starting transfers between devices: 57.8 us -> 55.9 us
    all_to_all x1, blocking collectives: 10.9 us -> 20.6 us  [body(): lax.all_to_all(partial.astype(jnp.bfloat16), ring, 0, 0, tiled=True)]
    ppermute x2 -> x1, waiting for transfers between devices: 9.5 us -> 1.56 us  [body(): lax.ppermute(give.astype(jnp.bfloat16), 'tc', [(0, 1), (1, 0)])]
    ppermute x2 -> x1, starting transfers between devices: 8.64 us -> 6.72 us  [body(): lax.ppermute(give.astype(jnp.bfloat16), 'tc', [(0, 1), (1, 0)])]
  transfers between devices with their start and end apart: 10 -> 9, of which waited for: 9 -> 8; matrix products, arithmetic and copies ran while one was open for 5% -> 5% of each run, Pallas kernels for 0% -> 0%
where the time goes in v12:
time: 132 us; the launch traced here: 131 us
  starting transfers between devices  55.9 us (42%)
  waiting for transfers between devices  32.9 us (25%)
  blocking collectives  20.6 us (16%)
  local copies, waits for them, and re-layouts  10.8 us (8%)
  matrix products  5.65 us (4%)
  other arithmetic  4.81 us (4%)
    ppermute x4, starting transfers between devices, shifted(): return lax.ppermute(x, axis, pairs)  27.5 us
    all_to_all x1, blocking collectives, body(): lax.all_to_all(partial.astype(jnp.bfloat16), ring, 0, 0, tiled=True)  20.6 us
    all_to_all x1, waiting for transfers between devices, body(): lax.all_to_all(jnp.broadcast_to(hidden[None], (ring_size,) + hidden.shape...  10.5 us
    all_to_all x1, waiting for transfers between devices, body(): got_maps = lax.all_to_all(own_maps, TP_AXES, 0, 0, tiled=True)  8.48 us
    all_to_all x1, starting transfers between devices, body(): lax.all_to_all(jnp.broadcast_to(hidden[None], (ring_size,) + hidden.shape...  7.64 us
    ppermute x4, waiting for transfers between devices, shifted(): return lax.ppermute(x, axis, pairs)  6.8 us
    ppermute x1, starting transfers between devices, body(): lax.ppermute(give.astype(jnp.bfloat16), 'tc', [(0, 1), (1, 0)])  6.72 us
    all_to_all x1, waiting for transfers between devices, body(): lax.all_to_all(jnp.broadcast_to(packed[None], (x_peers,) + packed.shape),...  5.66 us
  transfers between devices with their start and end apart: 9, of which 8 were waited for; matrix products, arithmetic and copies ran while one was open for 5% of the time, Pallas kernels for 0%

profile of v12, /device:TPU:1, one launch (start us, length us, event | category | flops | bytes accessed | tf_op | source)
XLA Modules:
  0.0 131.2 jit_solution(12843837641368321949)
XLA Ops:
  0.0 1.7 %broadcast_in_dim.46 = bf16[8,16,2048]{2,1,0:T(8,128)(2,1)} broadcast(bf16[16,2048]{1,0:T(8,128)(2,1)} %param.13), dimensions={1,2} | broadcast | bytes 589824 | tf_op jit(solution)/shard_map/broadcast_in_dim | solution.py:81
  1.7 7.6 %all-to-all-start = ((bf16[8,16,2048]{2,1,0:T(8,128)(2,1)}), bf16[8,16,2048]{2,1,0:T(8,128)(2,1)S(1)}, u32[]{:S(2)}, u32[]{:S(2)}) async-start(bf16[8,16,2048]{2,1,0:T(8,128)(2,1)} %broadcast_in_dim.46), calls=%async_computation | async-start | bytes 1048576 | tf_op jit(solution)/shard_map/all_to_all | solution.py:80
  9.4 2.1 %copy.188 = bf16[256,8,2,256]{3,1,2,0:T(8,128)(2,1)S(1)} copy(bf16[256,8,2,256]{3,2,1,0:T(2,128)(2,1)} %bitcast.142) | data formatting | bytes 4194304
  11.9 1.1 copy.162
  13.0 0.8 dynamic_slice.19
  13.8 10.5 %all-to-all-done = bf16[8,16,2048]{2,1,0:T(8,128)(2,1)S(1)} async-done(((bf16[8,16,2048]{2,1,0:T(8,128)(2,1)}), bf16[8,16,2048]{2,1,0:T(8,128)(2,1)S(1)}, u32[]{:S(2)}, u32[]{:S(2)}) %all-to-all-start) | async-done | bytes 524320 | tf_op jit(solution)/shard_map/all_to_all | solution.py:80
  24.3 5.4 %collective-permute-start = (bf16[8,16,2048]{2,1,0:T(8,128)(2,1)S(1)}, bf16[8,16,2048]{2,1,0:T(8,128)(2,1)S(1)}, u32[]{:S(2)}, u32[]{:S(2)}) collective-permute-start(bf16[8,16,2048]{2,1,0:T(8,128)(2,1)S(1)} %all-to-all-done), channel_id=1, source_target_pairs={{0,1},{1,0},{2,3},{3,2},{4,5},{5,4},{6,7},{7,6},{8,9},{9,8},{10,11... | collective-permute-start | bytes 1572872 | tf_op jit(solution)/shard_map/ppermute | solution.py:83
  29.7 0.9 constant_dynamic-slice_fusion
  30.6 0.6 fusion.87
  31.3 2.5 %fusion.14 = bf16[256,580]{0,1:T(8,128)(2,1)S(1)} fusion(bf16[256,2048]{1,0:T(8,128)(2,1)S(1)} %bitcast.144, bf16[2048,64]{1,0:T(8,128)(2,1)S(1)} %copy.163, bf16[2048,4]{1,0:T(8,128)(2,1)} %copy.162, bf16[2048,512]{1,0:T(8,128)(2,1)S(1)} %bitcast.143), kind=kOutput, calls=%fused_computation.14 | convolution fusion | flops 615449600 | bytes 3721216 | tf_op jit(solution)/shard_map/...d,dn->...n/dot_general | solution.py:95
  33.9 1.2 reduce-window.6
  35.3 0.6 broadcast_in_dim.47
  35.9 3.7 %all-to-all-start.1 = ((bf16[16,256,16]{1,2,0:T(8,128)(2,1)}), bf16[16,256,16]{1,2,0:T(8,128)(2,1)S(1)}, u32[]{:S(2)}, u32[]{:S(2)}) async-start(bf16[16,256,16]{1,2,0:T(8,128)(2,1)} %bitcast.8), calls=%async_computation.1 | async-start | bytes 262144 | tf_op jit(solution)/shard_map/all_to_all | solution.py:104
  40.3 8.5 %all-to-all-done.1 = bf16[16,256,16]{1,2,0:T(8,128)(2,1)S(1)} async-done(((bf16[16,256,16]{1,2,0:T(8,128)(2,1)}), bf16[16,256,16]{1,2,0:T(8,128)(2,1)S(1)}, u32[]{:S(2)}, u32[]{:S(2)}) %all-to-all-start.1) | async-done | bytes 131104 | tf_op jit(solution)/shard_map/all_to_all | solution.py:104
  48.9 3.1 %collective-permute-start.1 = (bf16[3,512]{0,1:T(8,128)(2,1)S(1)}, bf16[3,512]{0,1:T(8,128)(2,1)S(1)}, u32[]{:S(2)}, u32[]{:S(2)}) collective-permute-start(bf16[3,512]{0,1:T(8,128)(2,1)S(1)} %pad_maximum_fusion.1), channel_id=1, source_target_pairs={{0,16},{16,32},{32,48},{48,64},{64,80},{80,96},{96,112},{112,128},... | collective-permute-start | bytes 9224 | tf_op jit(solution)/shard_map/ppermute | solution.py:17
  52.1 3.1 %collective-permute-done.1 = bf16[3,512]{0,1:T(8,128)(2,1)S(1)} collective-permute-done((bf16[3,512]{0,1:T(8,128)(2,1)S(1)}, bf16[3,512]{0,1:T(8,128)(2,1)S(1)}, u32[]{:S(2)}, u32[]{:S(2)}) %collective-permute-start.1) | collective-permute-done | bytes 3104 | tf_op jit(solution)/shard_map/ppermute | solution.py:17
  55.4 0.5 multiply_convert_fusion.4
  56.7 0.8 broadcast_in_dim.52
  57.5 5.0 %all-to-all-start.2 = ((bf16[4,4,65,128]{3,1,2,0:T(4,128)(2,1)}), bf16[4,4,65,128]{3,1,2,0:T(4,128)(2,1)S(1)}, u32[]{:S(2)}, u32[]{:S(2)}) async-start(bf16[4,4,65,128]{3,1,2,0:T(4,128)(2,1)} %broadcast_in_dim.52), calls=%async_computation.2 | async-start | bytes 532480 | tf_op jit(solution)/shard_map/all_to_all | solution.py:156
  62.6 5.7 %all-to-all-done.2 = bf16[4,4,65,128]{3,1,2,0:T(4,128)(2,1)S(1)} async-done(((bf16[4,4,65,128]{3,1,2,0:T(4,128)(2,1)}), bf16[4,4,65,128]{3,1,2,0:T(4,128)(2,1)S(1)}, u32[]{:S(2)}, u32[]{:S(2)}) %all-to-all-start.2) | async-done | bytes 266272 | tf_op jit(solution)/shard_map/all_to_all | solution.py:156
  68.7 5.8 %collective-permute-start.2 = (bf16[4,65,128]{2,0,1:T(4,128)(2,1)S(1)}, bf16[4,65,128]{2,0,1:T(4,128)(2,1)S(1)}, u32[]{:S(2)}, u32[]{:S(2)}) collective-permute-start(bf16[4,65,128]{2,0,1:T(4,128)(2,1)S(1)} %pad_maximum_fusion.3), channel_id=1, source_target_pairs={{0,64},{64,128},{128,192},{192,256},{256,320},{320,384},{384,448},... | collective-permute-start | bytes 199688 | tf_op jit(solution)/shard_map/ppermute | solution.py:17
  74.5 1.3 collective-permute-done.2
  76.2 5.8 %collective-permute-start.3 = (bf16[4,65,128]{2,0,1:T(4,128)(2,1)S(1)}, bf16[4,65,128]{2,0,1:T(4,128)(2,1)S(1)}, u32[]{:S(2)}, u32[]{:S(2)}) collective-permute-start(bf16[4,65,128]{2,0,1:T(4,128)(2,1)S(1)} %pad_maximum_fusion.4), channel_id=1, source_target_pairs={{0,128},{64,192},{128,256},{192,320},{256,384},{320,448},{1,129},{... | collective-permute-start | bytes 199688 | tf_op jit(solution)/shard_map/ppermute | solution.py:17
  82.1 1.2 collective-permute-done.3
  83.9 12.7 %collective-permute-start.4 = (bf16[4,65,128]{2,0,1:T(4,128)(2,1)S(1)}, bf16[4,65,128]{2,0,1:T(4,128)(2,1)S(1)}, u32[]{:S(2)}, u32[]{:S(2)}) collective-permute-start(bf16[4,65,128]{2,0,1:T(4,128)(2,1)S(1)} %pad_maximum_fusion.5), channel_id=1, source_target_pairs={{0,256},{64,320},{128,384},{192,448},{1,257},{65,321},{129,385},{1... | collective-permute-start | bytes 199688 | tf_op jit(solution)/shard_map/ppermute | solution.py:17
  96.9 1.1 collective-permute-done.4
  98.3 0.5 fusion.19
  99.2 2.0 %fusion.9 = f32[2,4,2,16,2176]{4,3,2,1,0:T(8,128)S(1)} fusion(bf16[256,2048]{1,0:T(8,128)(2,1)} %param.25, bf16[256,2176]{1,0:T(8,128)(2,1)S(1)} %concatenate.57, bf16[4,2,2,16,512]{4,3,2,1,0:T(8,128)(2,1)S(1)} %bitcast.150), kind=kOutput, calls=%fused_computation.10 | convolution fusion | flops 577110016 | bytes 4653056 | tf_op jit(solution)/shard_map/...c,cn->...n/dot_general | solution.py:222
  101.3 6.7 %collective-permute-start.5 = (bf16[4,2,16,2176]{3,2,1,0:T(8,128)(2,1)S(1)}, bf16[4,2,16,2176]{3,2,1,0:T(8,128)(2,1)S(1)}, u32[]{:S(2)}, u32[]{:S(2)}) collective-permute-start(bf16[4,2,16,2176]{3,2,1,0:T(8,128)(2,1)S(1)} %fusion.23), channel_id=1, source_target_pairs={{0,1},{1,0},{2,3},{3,2},{4,5},{5,4},{6,7},{7,6},{8,9},{9,8},{10,11... | collective-permute-start | bytes 1671176 | tf_op jit(solution)/shard_map/ppermute | solution.py:226
  108.0 1.6 %collective-permute-done.5 = bf16[4,2,16,2176]{3,2,1,0:T(8,128)(2,1)S(1)} collective-permute-done((bf16[4,2,16,2176]{3,2,1,0:T(8,128)(2,1)S(1)}, bf16[4,2,16,2176]{3,2,1,0:T(8,128)(2,1)S(1)}, u32[]{:S(2)}, u32[]{:S(2)}) %collective-permute-start.5) | collective-permute-done | bytes 557088 | tf_op jit(solution)/shard_map/ppermute | solution.py:226
  109.7 20.6 %all_to_all.20 = bf16[8,16,2176]{2,1,0:T(8,128)(2,1)S(1)} all-to-all(bf16[8,16,2176]{2,1,0:T(8,128)(2,1)S(1)} %bitcast.140), channel_id=1, replica_groups=mesh['z'=8,'x'=4,'tg'=4,'yl'=2,'tc'=2] {'tg','yl'}, dimensions={0} | all-to-all | bytes 1114112 | tf_op jit(solution)/shard_map/all_to_all | solution.py:228
  130.5 0.7 fusion.24
  (87 shorter events, 5.3 us)
Async XLA Ops:
  1.7 22.6 %all-to-all-start = ((bf16[8,16,2048]{2,1,0:T(8,128)(2,1)}), bf16[8,16,2048]{2,1,0:T(8,128)(2,1)S(1)}, u32[]{:S(2)}, u32[]{:S(2)}) async-start(bf16[8,16,2048]{2,1,0:T(8,128)(2,1)} %broadcast_in_dim.46), calls=%async_computation | async-start | bytes 1048576 | tf_op jit(solution)/shard_map/all_to_all | solution.py:80
  9.3 2.2 %copy-start = (bf16[16,4,2048]{2,1,0:T(4,128)(2,1)S(1)}, bf16[16,4,2048]{2,1,0:T(4,128)(2,1)}, u32[]{:S(2)}) copy-start(bf16[16,4,2048]{2,1,0:T(4,128)(2,1)} %param.16) | copy-start | bytes 786436
  9.3 2.6 %copy-start.1 = (bf16[2048,4]{0,1:T(4,128)(2,1)S(1)}, bf16[2048,4]{0,1:T(4,128)(2,1)}, u32[]{:S(2)}) copy-start(bf16[2048,4]{0,1:T(4,128)(2,1)} %param.15) | copy-start | bytes 49156
  9.4 21.2 %copy-start.7 = (f32[4]{0:T(128)S(1)}, f32[4]{0:T(128)}, u32[]{:S(2)}) copy-start(f32[4]{0:T(128)} %param.22) | copy-start | bytes 52
  9.4 21.2 %copy-start.3 = (f32[4,256]{1,0:T(4,128)S(1)}, f32[4,256]{1,0:T(4,128)}, u32[]{:S(2)}) copy-start(f32[4,256]{1,0:T(4,128)} %param.17) | copy-start | bytes 12292
  24.3 6.9 %collective-permute-start = (bf16[8,16,2048]{2,1,0:T(8,128)(2,1)S(1)}, bf16[8,16,2048]{2,1,0:T(8,128)(2,1)S(1)}, u32[]{:S(2)}, u32[]{:S(2)}) collective-permute-start(bf16[8,16,2048]{2,1,0:T(8,128)(2,1)S(1)} %all-to-all-done), channel_id=1, source_target_pairs={{0,1},{1,0},{2,3},{3,2},{4,5},{5,4},{6,7},{7,6},{8,9},{9,8},{10,11... | collective-permute-start | bytes 1572872 | tf_op jit(solution)/shard_map/ppermute | solution.py:83
  31.3 2.5 %copy-start.2 = (f32[4]{0:T(128)S(1)}, f32[4]{0:T(128)}, u32[]{:S(2)}) copy-start(f32[4]{0:T(128)} %param.21) | copy-start | bytes 52
  33.8 22.1 %copy-start.4 = (f32[1,256]{1,0:T(1,128)S(1)}, f32[1,256]{1,0:T(1,128)}, u32[]{:S(2)}) copy-start(f32[1,256]{1,0:T(1,128)} %get-tuple-element.59) | copy-start | bytes 3076
  33.8 22.1 %copy-start.6 = (f32[256]{0:T(256)S(1)}, f32[256]{0:T(256)}, u32[]{:S(2)}) copy-start(f32[256]{0:T(256)} %param.18) | copy-start | bytes 3076
  35.9 12.9 %all-to-all-start.1 = ((bf16[16,256,16]{1,2,0:T(8,128)(2,1)}), bf16[16,256,16]{1,2,0:T(8,128)(2,1)S(1)}, u32[]{:S(2)}, u32[]{:S(2)}) async-start(bf16[16,256,16]{1,2,0:T(8,128)(2,1)} %bitcast.8), calls=%async_computation.1 | async-start | bytes 262144 | tf_op jit(solution)/shard_map/all_to_all | solution.py:104
  48.9 6.3 %collective-permute-start.1 = (bf16[3,512]{0,1:T(8,128)(2,1)S(1)}, bf16[3,512]{0,1:T(8,128)(2,1)S(1)}, u32[]{:S(2)}, u32[]{:S(2)}) collective-permute-start(bf16[3,512]{0,1:T(8,128)(2,1)S(1)} %pad_maximum_fusion.1), channel_id=1, source_target_pairs={{0,16},{16,32},{32,48},{48,64},{64,80},{80,96},{96,112},{112,128},... | collective-permute-start | bytes 9224 | tf_op jit(solution)/shard_map/ppermute | solution.py:17
  57.5 10.7 %all-to-all-start.2 = ((bf16[4,4,65,128]{3,1,2,0:T(4,128)(2,1)}), bf16[4,4,65,128]{3,1,2,0:T(4,128)(2,1)S(1)}, u32[]{:S(2)}, u32[]{:S(2)}) async-start(bf16[4,4,65,128]{3,1,2,0:T(4,128)(2,1)} %broadcast_in_dim.52), calls=%async_computation.2 | async-start | bytes 532480 | tf_op jit(solution)/shard_map/all_to_all | solution.py:156
  68.4 29.9 %copy-start.8 = (f32[4]{0:T(128)S(1)}, f32[4]{0:T(128)}, u32[]{:S(2)}) copy-start(f32[4]{0:T(128)} %param.23) | copy-start | bytes 52
  68.7 7.1 %collective-permute-start.2 = (bf16[4,65,128]{2,0,1:T(4,128)(2,1)S(1)}, bf16[4,65,128]{2,0,1:T(4,128)(2,1)S(1)}, u32[]{:S(2)}, u32[]{:S(2)}) collective-permute-start(bf16[4,65,128]{2,0,1:T(4,128)(2,1)S(1)} %pad_maximum_fusion.3), channel_id=1, source_target_pairs={{0,64},{64,128},{128,192},{192,256},{256,320},{320,384},{384,448},... | collective-permute-start | bytes 199688 | tf_op jit(solution)/shard_map/ppermute | solution.py:17
  76.2 7.1 %collective-permute-start.3 = (bf16[4,65,128]{2,0,1:T(4,128)(2,1)S(1)}, bf16[4,65,128]{2,0,1:T(4,128)(2,1)S(1)}, u32[]{:S(2)}, u32[]{:S(2)}) collective-permute-start(bf16[4,65,128]{2,0,1:T(4,128)(2,1)S(1)} %pad_maximum_fusion.4), channel_id=1, source_target_pairs={{0,128},{64,192},{128,256},{192,320},{256,384},{320,448},{1,129},{... | collective-permute-start | bytes 199688 | tf_op jit(solution)/shard_map/ppermute | solution.py:17
  83.5 15.3 %copy-start.5 = (f32[256]{0:T(256)S(1)}, f32[256]{0:T(256)}, u32[]{:S(2)}) copy-start(f32[256]{0:T(256)} %param.24) | copy-start | bytes 3076
  83.9 14.1 %collective-permute-start.4 = (bf16[4,65,128]{2,0,1:T(4,128)(2,1)S(1)}, bf16[4,65,128]{2,0,1:T(4,128)(2,1)S(1)}, u32[]{:S(2)}, u32[]{:S(2)}) collective-permute-start(bf16[4,65,128]{2,0,1:T(4,128)(2,1)S(1)} %pad_maximum_fusion.5), channel_id=1, source_target_pairs={{0,256},{64,320},{128,384},{192,448},{1,257},{65,321},{129,385},{1... | collective-permute-start | bytes 199688 | tf_op jit(solution)/shard_map/ppermute | solution.py:17
  101.3 8.3 %collective-permute-start.5 = (bf16[4,2,16,2176]{3,2,1,0:T(8,128)(2,1)S(1)}, bf16[4,2,16,2176]{3,2,1,0:T(8,128)(2,1)S(1)}, u32[]{:S(2)}, u32[]{:S(2)}) collective-permute-start(bf16[4,2,16,2176]{3,2,1,0:T(8,128)(2,1)S(1)} %fusion.23), channel_id=1, source_target_pairs={{0,1},{1,0},{2,3},{3,2},{4,5},{5,4},{6,7},{7,6},{8,9},{9,8},{10,11... | collective-permute-start | bytes 1671176 | tf_op jit(solution)/shard_map/ppermute | solution.py:226

commit v13 on v12

--- a/solution.py
+++ b/solution.py
@@ -99,9 +99,14 @@
     step_raw = projected[:, 2 * inner_dev : 2 * inner_dev + heads_dev]
     own_maps = projected[:, 2 * inner_dev + heads_dev :].reshape(length, GROUPS, -1)
     own_maps = jnp.moveaxis(own_maps, 1, 0)
-    own_maps = jnp.broadcast_to(own_maps[:, None], (GROUPS, per_group_dev) + own_maps.shape[1:])
-    own_maps = own_maps.reshape((tp_size,) + own_maps.shape[2:])
-    got_maps = lax.all_to_all(own_maps, TP_AXES, 0, 0, tiled=True)
+    partner_maps = lax.ppermute(own_maps, "tc", [(0, 1), (1, 0)])
+    chip_maps = jnp.where(
+        first, jnp.stack([own_maps, partner_maps], axis=2), jnp.stack([partner_maps, own_maps], axis=2)
+    ).reshape(own_maps.shape[:2] + (-1,))
+    chip_maps = jnp.broadcast_to(
+        chip_maps[:, None], (GROUPS, ring_size // GROUPS) + chip_maps.shape[1:]
+    ).reshape((ring_size,) + chip_maps.shape[1:])
+    got_maps = lax.all_to_all(chip_maps, ring, 0, 0, tiled=True)
     map_part = jnp.transpose(got_maps, (1, 0, 2)).reshape(length, group_cols)
     border_rows = KERNEL - 1
     prior = shifted(

time: 132 us -> 134 us (1.015)
  starting transfers between devices: 55.9 us -> 59.5 us
  waiting for transfers between devices: 32.9 us -> 31.5 us
    ppermute x0 -> x1, starting transfers between devices: none -> 2.27 us  [body(): partner_maps = lax.ppermute(own_maps, 'tc', [(0, 1), (1, 0)])]
    ppermute x1, starting transfers between devices: 6.72 us -> 8.98 us  [body(): lax.ppermute(give.astype(jnp.bfloat16), 'tc', [(0, 1), (1, 0)])]
  transfers between devices with their start and end apart: 9 -> 10, of which waited for: 8 -> 9; matrix products, arithmetic and copies ran while one was open for 5% -> 5% of each run, Pallas kernels for 0% -> 0%
where the time goes in v13:
time: 134 us; the launch traced here: 133 us
  starting transfers between devices  59.5 us (44%)
  waiting for transfers between devices  31.5 us (24%)
  blocking collectives  20.6 us (15%)
  local copies, waits for them, and re-layouts  10.8 us (8%)
  matrix products  5.65 us (4%)
  other arithmetic  4.82 us (4%)
    ppermute x4, starting transfers between devices, shifted(): return lax.ppermute(x, axis, pairs)  27.2 us
    all_to_all x1, blocking collectives, body(): lax.all_to_all(partial.astype(jnp.bfloat16), ring, 0, 0, tiled=True)  20.6 us
    all_to_all x1, waiting for transfers between devices, body(): lax.all_to_all(jnp.broadcast_to(hidden[None], (ring_size,) + hidden.shape...  10.5 us
    ppermute x1, starting transfers between devices, body(): lax.ppermute(give.astype(jnp.bfloat16), 'tc', [(0, 1), (1, 0)])  8.98 us
    all_to_all x1, waiting for transfers between devices, body(): got_maps = lax.all_to_all(chip_maps, ring, 0, 0, tiled=True)  7.94 us
    all_to_all x1, starting transfers between devices, body(): lax.all_to_all(jnp.broadcast_to(hidden[None], (ring_size,) + hidden.shape...  7.64 us
    ppermute x4, waiting for transfers between devices, shifted(): return lax.ppermute(x, axis, pairs)  5.55 us
    all_to_all x1, waiting for transfers between devices, body(): lax.all_to_all(jnp.broadcast_to(packed[None], (x_peers,) + packed.shape),...  5.48 us
  transfers between devices with their start and end apart: 10, of which 9 were waited for; matrix products, arithmetic and copies ran while one was open for 5% of the time, Pallas kernels for 0%

profile of v13, /device:TPU:1, one launch (start us, length us, event | category | flops | bytes accessed | tf_op | source)
XLA Modules:
  0.0 133.4 jit_solution(15288197902655204868)
XLA Ops:
  0.0 1.7 %broadcast_in_dim.46 = bf16[8,16,2048]{2,1,0:T(8,128)(2,1)} broadcast(bf16[16,2048]{1,0:T(8,128)(2,1)} %param.13), dimensions={1,2} | broadcast | bytes 589824 | tf_op jit(solution)/shard_map/broadcast_in_dim | solution.py:81
  1.7 7.6 %all-to-all-start = ((bf16[8,16,2048]{2,1,0:T(8,128)(2,1)}), bf16[8,16,2048]{2,1,0:T(8,128)(2,1)S(1)}, u32[]{:S(2)}, u32[]{:S(2)}) async-start(bf16[8,16,2048]{2,1,0:T(8,128)(2,1)} %broadcast_in_dim.46), calls=%async_computation | async-start | bytes 1048576 | tf_op jit(solution)/shard_map/all_to_all | solution.py:80
  9.4 2.1 %copy.188 = bf16[256,8,2,256]{3,1,2,0:T(8,128)(2,1)S(1)} copy(bf16[256,8,2,256]{3,2,1,0:T(2,128)(2,1)} %bitcast.146) | data formatting | bytes 4194304
  11.9 1.1 copy.162
  13.0 0.8 dynamic_slice.19
  13.8 10.5 %all-to-all-done = bf16[8,16,2048]{2,1,0:T(8,128)(2,1)S(1)} async-done(((bf16[8,16,2048]{2,1,0:T(8,128)(2,1)}), bf16[8,16,2048]{2,1,0:T(8,128)(2,1)S(1)}, u32[]{:S(2)}, u32[]{:S(2)}) %all-to-all-start) | async-done | bytes 524320 | tf_op jit(solution)/shard_map/all_to_all | solution.py:80
  24.3 5.4 %collective-permute-start = (bf16[8,16,2048]{2,1,0:T(8,128)(2,1)S(1)}, bf16[8,16,2048]{2,1,0:T(8,128)(2,1)S(1)}, u32[]{:S(2)}, u32[]{:S(2)}) collective-permute-start(bf16[8,16,2048]{2,1,0:T(8,128)(2,1)S(1)} %all-to-all-done), channel_id=1, source_target_pairs={{0,1},{1,0},{2,3},{3,2},{4,5},{5,4},{6,7},{7,6},{8,9},{9,8},{10,11... | collective-permute-start | bytes 1572872 | tf_op jit(solution)/shard_map/ppermute | solution.py:83
  29.7 0.9 constant_dynamic-slice_fusion
  30.6 0.6 fusion.87
  31.3 2.5 %fusion.14 = bf16[256,580]{0,1:T(8,128)(2,1)S(1)} fusion(bf16[256,2048]{1,0:T(8,128)(2,1)S(1)} %bitcast.148, bf16[2048,64]{1,0:T(8,128)(2,1)S(1)} %copy.163, bf16[2048,4]{1,0:T(8,128)(2,1)} %copy.162, bf16[2048,512]{1,0:T(8,128)(2,1)S(1)} %bitcast.147), kind=kOutput, calls=%fused_computation.14 | convolution fusion | flops 615449600 | bytes 3721216 | tf_op jit(solution)/shard_map/...d,dn->...n/dot_general | solution.py:95
  33.9 1.2 reduce-window.6
  35.3 2.3 %collective-permute-start.1 = (bf16[4,256,16]{1,2,0:T(8,128)(2,1)S(1)}, bf16[4,256,16]{1,2,0:T(8,128)(2,1)S(1)}, u32[]{:S(2)}, u32[]{:S(2)}) collective-permute-start(bf16[4,256,16]{1,2,0:T(8,128)(2,1)S(1)} %bitcast.159), channel_id=1, source_target_pairs={{0,1},{1,0},{2,3},{3,2},{4,5},{5,4},{6,7},{7,6},{8,9},{9,8},{10,11... | collective-permute-start | bytes 98312 | tf_op jit(solution)/shard_map/ppermute | solution.py:102
  37.9 0.5 collective-permute-done.1
  38.4 0.6 broadcast_in_dim.47
  39.0 3.4 %all-to-all-start.1 = ((bf16[8,256,32]{1,2,0:T(8,128)(2,1)}), bf16[8,256,32]{1,2,0:T(8,128)(2,1)S(1)}, u32[]{:S(2)}, u32[]{:S(2)}) async-start(bf16[8,256,32]{1,2,0:T(8,128)(2,1)} %bitcast.13), calls=%async_computation.1 | async-start | bytes 262144 | tf_op jit(solution)/shard_map/all_to_all | solution.py:109
  42.8 7.9 %all-to-all-done.1 = bf16[8,256,32]{1,2,0:T(8,128)(2,1)S(1)} async-done(((bf16[8,256,32]{1,2,0:T(8,128)(2,1)}), bf16[8,256,32]{1,2,0:T(8,128)(2,1)S(1)}, u32[]{:S(2)}, u32[]{:S(2)}) %all-to-all-start.1) | async-done | bytes 131104 | tf_op jit(solution)/shard_map/all_to_all | solution.py:109
  50.8 3.1 %collective-permute-start.2 = (bf16[3,512]{0,1:T(8,128)(2,1)S(1)}, bf16[3,512]{0,1:T(8,128)(2,1)S(1)}, u32[]{:S(2)}, u32[]{:S(2)}) collective-permute-start(bf16[3,512]{0,1:T(8,128)(2,1)S(1)} %pad_maximum_fusion.1), channel_id=1, source_target_pairs={{0,16},{16,32},{32,48},{48,64},{64,80},{80,96},{96,112},{112,128},... | collective-permute-start | bytes 9224 | tf_op jit(solution)/shard_map/ppermute | solution.py:17
  54.0 1.9 %collective-permute-done.2 = bf16[3,512]{0,1:T(8,128)(2,1)S(1)} collective-permute-done((bf16[3,512]{0,1:T(8,128)(2,1)S(1)}, bf16[3,512]{0,1:T(8,128)(2,1)S(1)}, u32[]{:S(2)}, u32[]{:S(2)}) %collective-permute-start.2) | collective-permute-done | bytes 3104 | tf_op jit(solution)/shard_map/ppermute | solution.py:17
  57.4 0.8 broadcast_in_dim.52
  58.2 4.7 %all-to-all-start.2 = ((bf16[4,4,65,128]{3,1,2,0:T(4,128)(2,1)}), bf16[4,4,65,128]{3,1,2,0:T(4,128)(2,1)S(1)}, u32[]{:S(2)}, u32[]{:S(2)}) async-start(bf16[4,4,65,128]{3,1,2,0:T(4,128)(2,1)} %broadcast_in_dim.52), calls=%async_computation.2 | async-start | bytes 532480 | tf_op jit(solution)/shard_map/all_to_all | solution.py:161
  62.9 5.5 %all-to-all-done.2 = bf16[4,4,65,128]{3,1,2,0:T(4,128)(2,1)S(1)} async-done(((bf16[4,4,65,128]{3,1,2,0:T(4,128)(2,1)}), bf16[4,4,65,128]{3,1,2,0:T(4,128)(2,1)S(1)}, u32[]{:S(2)}, u32[]{:S(2)}) %all-to-all-start.2) | async-done | bytes 266272 | tf_op jit(solution)/shard_map/all_to_all | solution.py:161
  68.9 5.5 %collective-permute-start.3 = (bf16[4,65,128]{2,0,1:T(4,128)(2,1)S(1)}, bf16[4,65,128]{2,0,1:T(4,128)(2,1)S(1)}, u32[]{:S(2)}, u32[]{:S(2)}) collective-permute-start(bf16[4,65,128]{2,0,1:T(4,128)(2,1)S(1)} %pad_maximum_fusion.3), channel_id=1, source_target_pairs={{0,64},{64,128},{128,192},{192,256},{256,320},{320,384},{384,448},... | collective-permute-start | bytes 199688 | tf_op jit(solution)/shard_map/ppermute | solution.py:17
  74.4 1.3 collective-permute-done.3
  76.1 5.8 %collective-permute-start.4 = (bf16[4,65,128]{2,0,1:T(4,128)(2,1)S(1)}, bf16[4,65,128]{2,0,1:T(4,128)(2,1)S(1)}, u32[]{:S(2)}, u32[]{:S(2)}) collective-permute-start(bf16[4,65,128]{2,0,1:T(4,128)(2,1)S(1)} %pad_maximum_fusion.4), channel_id=1, source_target_pairs={{0,128},{64,192},{128,256},{192,320},{256,384},{320,448},{1,129},{... | collective-permute-start | bytes 199688 | tf_op jit(solution)/shard_map/ppermute | solution.py:17
  82.0 1.2 collective-permute-done.4
  83.8 12.7 %collective-permute-start.5 = (bf16[4,65,128]{2,0,1:T(4,128)(2,1)S(1)}, bf16[4,65,128]{2,0,1:T(4,128)(2,1)S(1)}, u32[]{:S(2)}, u32[]{:S(2)}) collective-permute-start(bf16[4,65,128]{2,0,1:T(4,128)(2,1)S(1)} %pad_maximum_fusion.5), channel_id=1, source_target_pairs={{0,256},{64,320},{128,384},{192,448},{1,257},{65,321},{129,385},{1... | collective-permute-start | bytes 199688 | tf_op jit(solution)/shard_map/ppermute | solution.py:17
  96.8 1.1 collective-permute-done.5
  99.1 2.0 %fusion.9 = f32[2,4,2,16,2176]{4,3,2,1,0:T(8,128)S(1)} fusion(bf16[256,2048]{1,0:T(8,128)(2,1)} %param.25, bf16[256,2176]{1,0:T(8,128)(2,1)S(1)} %concatenate.57, bf16[4,2,2,16,512]{4,3,2,1,0:T(8,128)(2,1)S(1)} %bitcast.155), kind=kOutput, calls=%fused_computation.10 | convolution fusion | flops 577110016 | bytes 4653056 | tf_op jit(solution)/shard_map/...c,cn->...n/dot_general | solution.py:227
  101.2 9.0 %collective-permute-start.6 = (bf16[4,2,16,2176]{3,2,1,0:T(8,128)(2,1)S(1)}, bf16[4,2,16,2176]{3,2,1,0:T(8,128)(2,1)S(1)}, u32[]{:S(2)}, u32[]{:S(2)}) collective-permute-start(bf16[4,2,16,2176]{3,2,1,0:T(8,128)(2,1)S(1)} %fusion.23), channel_id=1, source_target_pairs={{0,1},{1,0},{2,3},{3,2},{4,5},{5,4},{6,7},{7,6},{8,9},{9,8},{10,11... | collective-permute-start | bytes 1671176 | tf_op jit(solution)/shard_map/ppermute | solution.py:231
  110.2 1.6 %collective-permute-done.6 = bf16[4,2,16,2176]{3,2,1,0:T(8,128)(2,1)S(1)} collective-permute-done((bf16[4,2,16,2176]{3,2,1,0:T(8,128)(2,1)S(1)}, bf16[4,2,16,2176]{3,2,1,0:T(8,128)(2,1)S(1)}, u32[]{:S(2)}, u32[]{:S(2)}) %collective-permute-start.6) | collective-permute-done | bytes 557088 | tf_op jit(solution)/shard_map/ppermute | solution.py:231
  111.8 20.6 %all_to_all.20 = bf16[8,16,2176]{2,1,0:T(8,128)(2,1)S(1)} all-to-all(bf16[8,16,2176]{2,1,0:T(8,128)(2,1)S(1)} %bitcast.144), channel_id=1, replica_groups=mesh['z'=8,'x'=4,'tg'=4,'yl'=2,'tc'=2] {'tg','yl'}, dimensions={0} | all-to-all | bytes 1114112 | tf_op jit(solution)/shard_map/all_to_all | solution.py:233
  132.6 0.7 fusion.24
  (90 shorter events, 6.3 us)
Async XLA Ops:
  1.7 22.6 %all-to-all-start = ((bf16[8,16,2048]{2,1,0:T(8,128)(2,1)}), bf16[8,16,2048]{2,1,0:T(8,128)(2,1)S(1)}, u32[]{:S(2)}, u32[]{:S(2)}) async-start(bf16[8,16,2048]{2,1,0:T(8,128)(2,1)} %broadcast_in_dim.46), calls=%async_computation | async-start | bytes 1048576 | tf_op jit(solution)/shard_map/all_to_all | solution.py:80
  9.3 2.2 %copy-start = (bf16[16,4,2048]{2,1,0:T(4,128)(2,1)S(1)}, bf16[16,4,2048]{2,1,0:T(4,128)(2,1)}, u32[]{:S(2)}) copy-start(bf16[16,4,2048]{2,1,0:T(4,128)(2,1)} %param.16) | copy-start | bytes 786436
  9.3 2.6 %copy-start.1 = (bf16[2048,4]{0,1:T(4,128)(2,1)S(1)}, bf16[2048,4]{0,1:T(4,128)(2,1)}, u32[]{:S(2)}) copy-start(bf16[2048,4]{0,1:T(4,128)(2,1)} %param.15) | copy-start | bytes 49156
  9.4 21.2 %copy-start.7 = (f32[4]{0:T(128)S(1)}, f32[4]{0:T(128)}, u32[]{:S(2)}) copy-start(f32[4]{0:T(128)} %param.22) | copy-start | bytes 52
  9.4 21.2 %copy-start.3 = (f32[4,256]{1,0:T(4,128)S(1)}, f32[4,256]{1,0:T(4,128)}, u32[]{:S(2)}) copy-start(f32[4,256]{1,0:T(4,128)} %param.17) | copy-start | bytes 12292
  24.3 6.9 %collective-permute-start = (bf16[8,16,2048]{2,1,0:T(8,128)(2,1)S(1)}, bf16[8,16,2048]{2,1,0:T(8,128)(2,1)S(1)}, u32[]{:S(2)}, u32[]{:S(2)}) collective-permute-start(bf16[8,16,2048]{2,1,0:T(8,128)(2,1)S(1)} %all-to-all-done), channel_id=1, source_target_pairs={{0,1},{1,0},{2,3},{3,2},{4,5},{5,4},{6,7},{7,6},{8,9},{9,8},{10,11... | collective-permute-start | bytes 1572872 | tf_op jit(solution)/shard_map/ppermute | solution.py:83
  31.3 2.5 %copy-start.2 = (f32[4]{0:T(128)S(1)}, f32[4]{0:T(128)}, u32[]{:S(2)}) copy-start(f32[4]{0:T(128)} %param.21) | copy-start | bytes 52
  33.8 22.8 %copy-start.4 = (f32[1,256]{1,0:T(1,128)S(1)}, f32[1,256]{1,0:T(1,128)}, u32[]{:S(2)}) copy-start(f32[1,256]{1,0:T(1,128)} %get-tuple-element.59) | copy-start | bytes 3076
  33.8 22.8 %copy-start.6 = (f32[256]{0:T(256)S(1)}, f32[256]{0:T(256)}, u32[]{:S(2)}) copy-start(f32[256]{0:T(256)} %param.18) | copy-start | bytes 3076
  35.3 3.1 %collective-permute-start.1 = (bf16[4,256,16]{1,2,0:T(8,128)(2,1)S(1)}, bf16[4,256,16]{1,2,0:T(8,128)(2,1)S(1)}, u32[]{:S(2)}, u32[]{:S(2)}) collective-permute-start(bf16[4,256,16]{1,2,0:T(8,128)(2,1)S(1)} %bitcast.159), channel_id=1, source_target_pairs={{0,1},{1,0},{2,3},{3,2},{4,5},{5,4},{6,7},{7,6},{8,9},{9,8},{10,11... | collective-permute-start | bytes 98312 | tf_op jit(solution)/shard_map/ppermute | solution.py:102
  39.0 11.7 %all-to-all-start.1 = ((bf16[8,256,32]{1,2,0:T(8,128)(2,1)}), bf16[8,256,32]{1,2,0:T(8,128)(2,1)S(1)}, u32[]{:S(2)}, u32[]{:S(2)}) async-start(bf16[8,256,32]{1,2,0:T(8,128)(2,1)} %bitcast.13), calls=%async_computation.1 | async-start | bytes 262144 | tf_op jit(solution)/shard_map/all_to_all | solution.py:109
  50.8 5.1 %collective-permute-start.2 = (bf16[3,512]{0,1:T(8,128)(2,1)S(1)}, bf16[3,512]{0,1:T(8,128)(2,1)S(1)}, u32[]{:S(2)}, u32[]{:S(2)}) collective-permute-start(bf16[3,512]{0,1:T(8,128)(2,1)S(1)} %pad_maximum_fusion.1), channel_id=1, source_target_pairs={{0,16},{16,32},{32,48},{48,64},{64,80},{80,96},{96,112},{112,128},... | collective-permute-start | bytes 9224 | tf_op jit(solution)/shard_map/ppermute | solution.py:17
  58.2 10.2 %all-to-all-start.2 = ((bf16[4,4,65,128]{3,1,2,0:T(4,128)(2,1)}), bf16[4,4,65,128]{3,1,2,0:T(4,128)(2,1)S(1)}, u32[]{:S(2)}, u32[]{:S(2)}) async-start(bf16[4,4,65,128]{3,1,2,0:T(4,128)(2,1)} %broadcast_in_dim.52), calls=%async_computation.2 | async-start | bytes 532480 | tf_op jit(solution)/shard_map/all_to_all | solution.py:161
  68.6 29.6 %copy-start.8 = (f32[4]{0:T(128)S(1)}, f32[4]{0:T(128)}, u32[]{:S(2)}) copy-start(f32[4]{0:T(128)} %param.23) | copy-start | bytes 52
  68.9 6.8 %collective-permute-start.3 = (bf16[4,65,128]{2,0,1:T(4,128)(2,1)S(1)}, bf16[4,65,128]{2,0,1:T(4,128)(2,1)S(1)}, u32[]{:S(2)}, u32[]{:S(2)}) collective-permute-start(bf16[4,65,128]{2,0,1:T(4,128)(2,1)S(1)} %pad_maximum_fusion.3), channel_id=1, source_target_pairs={{0,64},{64,128},{128,192},{192,256},{256,320},{320,384},{384,448},... | collective-permute-start | bytes 199688 | tf_op jit(solution)/shard_map/ppermute | solution.py:17
  76.1 7.1 %collective-permute-start.4 = (bf16[4,65,128]{2,0,1:T(4,128)(2,1)S(1)}, bf16[4,65,128]{2,0,1:T(4,128)(2,1)S(1)}, u32[]{:S(2)}, u32[]{:S(2)}) collective-permute-start(bf16[4,65,128]{2,0,1:T(4,128)(2,1)S(1)} %pad_maximum_fusion.4), channel_id=1, source_target_pairs={{0,128},{64,192},{128,256},{192,320},{256,384},{320,448},{1,129},{... | collective-permute-start | bytes 199688 | tf_op jit(solution)/shard_map/ppermute | solution.py:17
  83.4 15.3 %copy-start.5 = (f32[256]{0:T(256)S(1)}, f32[256]{0:T(256)}, u32[]{:S(2)}) copy-start(f32[256]{0:T(256)} %param.24) | copy-start | bytes 3076
  83.8 14.1 %collective-permute-start.5 = (bf16[4,65,128]{2,0,1:T(4,128)(2,1)S(1)}, bf16[4,65,128]{2,0,1:T(4,128)(2,1)S(1)}, u32[]{:S(2)}, u32[]{:S(2)}) collective-permute-start(bf16[4,65,128]{2,0,1:T(4,128)(2,1)S(1)} %pad_maximum_fusion.5), channel_id=1, source_target_pairs={{0,256},{64,320},{128,384},{192,448},{1,257},{65,321},{129,385},{1... | collective-permute-start | bytes 199688 | tf_op jit(solution)/shard_map/ppermute | solution.py:17
  101.2 10.6 %collective-permute-start.6 = (bf16[4,2,16,2176]{3,2,1,0:T(8,128)(2,1)S(1)}, bf16[4,2,16,2176]{3,2,1,0:T(8,128)(2,1)S(1)}, u32[]{:S(2)}, u32[]{:S(2)}) collective-permute-start(bf16[4,2,16,2176]{3,2,1,0:T(8,128)(2,1)S(1)} %fusion.23), channel_id=1, source_target_pairs={{0,1},{1,0},{2,3},{3,2},{4,5},{5,4},{6,7},{7,6},{8,9},{9,8},{10,11... | collective-permute-start | bytes 1671176 | tf_op jit(solution)/shard_map/ppermute | solution.py:231

commit v14 on v12

--- a/solution.py
+++ b/solution.py
@@ -82,18 +82,14 @@
     )
     other_rows = lax.ppermute(ring_rows, "tc", [(0, 1), (1, 0)])
     first = lax.axis_index("tc") == 0
-    stacked = jnp.where(
-        first, jnp.stack([ring_rows, other_rows], axis=1), jnp.stack([other_rows, ring_rows], axis=1)
-    ).reshape((length,) + hidden.shape[1:])
-
-    def in_order(rows):
-        return rows
 
     map_cols = jnp.transpose(group_weight, (2, 1, 0)).reshape(group_weight.shape[2], -1)
     joined = jnp.concatenate([zx_weight, step_weight, map_cols], axis=1)
-    projected = in_order(
-        jnp.einsum("...d,dn->...n", stacked, joined, preferred_element_type=jnp.float32)
-    ).astype(jnp.bfloat16)
+    own_proj = jnp.einsum("...d,dn->...n", ring_rows, joined, preferred_element_type=jnp.float32)
+    other_proj = jnp.einsum("...d,dn->...n", other_rows, joined, preferred_element_type=jnp.float32)
+    projected = jnp.where(
+        first, jnp.stack([own_proj, other_proj], axis=1), jnp.stack([other_proj, own_proj], axis=1)
+    ).reshape((length, joined.shape[1])).astype(jnp.bfloat16)
     gate_raw = projected[:, :inner_dev]
     inner_raw = projected[:, inner_dev : 2 * inner_dev]
     step_raw = projected[:, 2 * inner_dev : 2 * inner_dev + heads_dev]

time: 132 us -> 127 us (0.962)
  waiting for transfers between devices: 32.9 us -> 28.5 us
  local copies, waits for them, and re-layouts: 10.8 us -> 12.4 us
    ppermute x4, waiting for transfers between devices: 6.8 us -> 3.88 us  [shifted(): return lax.ppermute(x, axis, pairs)]
    all_to_all x1, waiting for transfers between devices: 10.5 us -> 8.17 us  [body(): lax.all_to_all(jnp.broadcast_to(hidden[None], (ring_size,) + hidden.shape...]
    unnamed x22 -> x19, local copies, waits for them, and re-layouts: 3.44 us -> 4.99 us
  transfers between devices with their start and end apart: 9 -> 9, of which waited for: 8 -> 9; matrix products, arithmetic and copies ran while one was open for 5% -> 7% of each run, Pallas kernels for 0% -> 0%
where the time goes in v14:
time: 127 us; the launch traced here: 126 us
  starting transfers between devices  55.6 us (44%)
  waiting for transfers between devices  28.5 us (22%)
  blocking collectives  20.3 us (16%)
  local copies, waits for them, and re-layouts  12.4 us (10%)
  matrix products  5.07 us (4%)
  other arithmetic  4.11 us (3%)
    ppermute x4, starting transfers between devices, shifted(): return lax.ppermute(x, axis, pairs)  27.3 us
    all_to_all x1, blocking collectives, body(): lax.all_to_all(partial.astype(jnp.bfloat16), ring, 0, 0, tiled=True)  20.3 us
    all_to_all x1, waiting for transfers between devices, body(): got_maps = lax.all_to_all(own_maps, TP_AXES, 0, 0, tiled=True)  8.9 us
    all_to_all x1, waiting for transfers between devices, body(): lax.all_to_all(jnp.broadcast_to(hidden[None], (ring_size,) + hidden.shape...  8.17 us
    all_to_all x1, starting transfers between devices, body(): lax.all_to_all(jnp.broadcast_to(hidden[None], (ring_size,) + hidden.shape...  7.64 us
    ppermute x1, starting transfers between devices, body(): lax.ppermute(give.astype(jnp.bfloat16), 'tc', [(0, 1), (1, 0)])  7.01 us
    all_to_all x1, waiting for transfers between devices, body(): lax.all_to_all(jnp.broadcast_to(packed[None], (x_peers,) + packed.shape),...  5.5 us
    ppermute x1, starting transfers between devices, body(): other_rows = lax.ppermute(ring_rows, 'tc', [(0, 1), (1, 0)])  5.4 us
  transfers between devices with their start and end apart: 9, of which 9 were waited for; matrix products, arithmetic and copies ran while one was open for 7% of the time, Pallas kernels for 0%

profile of v14, /device:TPU:1, one launch (start us, length us, event | category | flops | bytes accessed | tf_op | source)
XLA Modules:
  0.0 126.5 jit_solution(5106976011633546739)
XLA Ops:
  0.0 1.7 %broadcast_in_dim.46 = bf16[8,16,2048]{2,1,0:T(8,128)(2,1)} broadcast(bf16[16,2048]{1,0:T(8,128)(2,1)} %param.13), dimensions={1,2} | broadcast | bytes 589824 | tf_op jit(solution)/shard_map/broadcast_in_dim | solution.py:81
  1.7 7.6 %all-to-all-start = ((bf16[8,16,2048]{2,1,0:T(8,128)(2,1)}), bf16[8,16,2048]{2,1,0:T(8,128)(2,1)S(1)}, u32[]{:S(2)}, u32[]{:S(2)}) async-start(bf16[8,16,2048]{2,1,0:T(8,128)(2,1)} %broadcast_in_dim.46), calls=%async_computation | async-start | bytes 1048576 | tf_op jit(solution)/shard_map/all_to_all | solution.py:80
  9.4 4.8 %copy.164 = bf16[2048,2,256]{0,2,1:T(8,128)(2,1)S(1)} copy(bf16[2048,2,256]{2,1,0:T(2,128)(2,1)} %param.14) | data formatting | bytes 4194304 | tf_op args[1]
  14.4 0.8 dynamic_slice.19
  15.1 0.9 constant_dynamic-slice_fusion
  16.1 8.2 %all-to-all-done = bf16[8,16,2048]{2,1,0:T(8,128)(2,1)S(1)} async-done(((bf16[8,16,2048]{2,1,0:T(8,128)(2,1)}), bf16[8,16,2048]{2,1,0:T(8,128)(2,1)S(1)}, u32[]{:S(2)}, u32[]{:S(2)}) %all-to-all-start) | async-done | bytes 524320 | tf_op jit(solution)/shard_map/all_to_all | solution.py:80
  24.3 5.4 %collective-permute-start = (bf16[8,16,2048]{2,1,0:T(8,128)(2,1)S(1)}, bf16[8,16,2048]{2,1,0:T(8,128)(2,1)S(1)}, u32[]{:S(2)}, u32[]{:S(2)}) collective-permute-start(bf16[8,16,2048]{2,1,0:T(8,128)(2,1)S(1)} %all-to-all-done), channel_id=1, source_target_pairs={{0,1},{1,0},{2,3},{3,2},{4,5},{5,4},{6,7},{7,6},{8,9},{9,8},{10,11... | collective-permute-start | bytes 1572872 | tf_op jit(solution)/shard_map/ppermute | solution.py:83
  29.7 1.0 fusion.10
  30.7 0.5 collective-permute-done
  31.2 1.0 fusion.11
  32.5 1.2 reduce-window.6
  34.4 0.6 broadcast_in_dim.47
  35.0 3.7 %all-to-all-start.1 = ((bf16[16,256,16]{1,2,0:T(8,128)(2,1)}), bf16[16,256,16]{1,2,0:T(8,128)(2,1)S(1)}, u32[]{:S(2)}, u32[]{:S(2)}) async-start(bf16[16,256,16]{1,2,0:T(8,128)(2,1)} %bitcast.14), calls=%async_computation.1 | async-start | bytes 262144 | tf_op jit(solution)/shard_map/all_to_all | solution.py:100
  39.0 8.9 %all-to-all-done.1 = bf16[16,256,16]{1,2,0:T(8,128)(2,1)S(1)} async-done(((bf16[16,256,16]{1,2,0:T(8,128)(2,1)}), bf16[16,256,16]{1,2,0:T(8,128)(2,1)S(1)}, u32[]{:S(2)}, u32[]{:S(2)}) %all-to-all-start.1) | async-done | bytes 131104 | tf_op jit(solution)/shard_map/all_to_all | solution.py:100
  48.1 3.1 %collective-permute-start.1 = (bf16[3,512]{1,0:T(4,128)(2,1)S(1)}, bf16[3,512]{1,0:T(4,128)(2,1)S(1)}, u32[]{:S(2)}, u32[]{:S(2)}) collective-permute-start(bf16[3,512]{1,0:T(4,128)(2,1)S(1)} %pad_maximum_fusion.5), channel_id=1, source_target_pairs={{0,16},{16,32},{32,48},{48,64},{64,80},{80,96},{96,112},{112,128},... | collective-permute-start | bytes 9224 | tf_op jit(solution)/shard_map/ppermute | solution.py:17
  51.5 0.4 collective-permute-done.1
  52.8 0.8 broadcast_in_dim.52
  53.6 4.5 %all-to-all-start.2 = ((bf16[4,4,65,128]{3,1,2,0:T(4,128)(2,1)}), bf16[4,4,65,128]{3,1,2,0:T(4,128)(2,1)S(1)}, u32[]{:S(2)}, u32[]{:S(2)}) async-start(bf16[4,4,65,128]{3,1,2,0:T(4,128)(2,1)} %broadcast_in_dim.52), calls=%async_computation.2 | async-start | bytes 532480 | tf_op jit(solution)/shard_map/all_to_all | solution.py:152
  58.2 5.5 %all-to-all-done.2 = bf16[4,4,65,128]{3,1,2,0:T(4,128)(2,1)S(1)} async-done(((bf16[4,4,65,128]{3,1,2,0:T(4,128)(2,1)}), bf16[4,4,65,128]{3,1,2,0:T(4,128)(2,1)S(1)}, u32[]{:S(2)}, u32[]{:S(2)}) %all-to-all-start.2) | async-done | bytes 266272 | tf_op jit(solution)/shard_map/all_to_all | solution.py:152
  64.2 5.6 %collective-permute-start.2 = (bf16[4,65,128]{2,0,1:T(4,128)(2,1)S(1)}, bf16[4,65,128]{2,0,1:T(4,128)(2,1)S(1)}, u32[]{:S(2)}, u32[]{:S(2)}) collective-permute-start(bf16[4,65,128]{2,0,1:T(4,128)(2,1)S(1)} %pad_maximum_fusion.2), channel_id=1, source_target_pairs={{0,64},{64,128},{128,192},{192,256},{256,320},{320,384},{384,448},... | collective-permute-start | bytes 199688 | tf_op jit(solution)/shard_map/ppermute | solution.py:17
  69.8 1.3 %collective-permute-done.2 = bf16[4,65,128]{2,0,1:T(4,128)(2,1)S(1)} collective-permute-done((bf16[4,65,128]{2,0,1:T(4,128)(2,1)S(1)}, bf16[4,65,128]{2,0,1:T(4,128)(2,1)S(1)}, u32[]{:S(2)}, u32[]{:S(2)}) %collective-permute-start.2) | collective-permute-done | bytes 66592 | tf_op jit(solution)/shard_map/ppermute | solution.py:17
  71.5 5.8 %collective-permute-start.3 = (bf16[4,65,128]{2,0,1:T(4,128)(2,1)S(1)}, bf16[4,65,128]{2,0,1:T(4,128)(2,1)S(1)}, u32[]{:S(2)}, u32[]{:S(2)}) collective-permute-start(bf16[4,65,128]{2,0,1:T(4,128)(2,1)S(1)} %pad_maximum_fusion.3), channel_id=1, source_target_pairs={{0,128},{64,192},{128,256},{192,320},{256,384},{320,448},{1,129},{... | collective-permute-start | bytes 199688 | tf_op jit(solution)/shard_map/ppermute | solution.py:17
  77.4 1.2 collective-permute-done.3
  79.2 12.8 %collective-permute-start.4 = (bf16[4,65,128]{2,0,1:T(4,128)(2,1)S(1)}, bf16[4,65,128]{2,0,1:T(4,128)(2,1)S(1)}, u32[]{:S(2)}, u32[]{:S(2)}) collective-permute-start(bf16[4,65,128]{2,0,1:T(4,128)(2,1)S(1)} %pad_maximum_fusion.4), channel_id=1, source_target_pairs={{0,256},{64,320},{128,384},{192,448},{1,257},{65,321},{129,385},{1... | collective-permute-start | bytes 199688 | tf_op jit(solution)/shard_map/ppermute | solution.py:17
  92.4 0.9 collective-permute-done.4
  93.3 0.3 fusion.12
  93.6 0.5 fusion.14
  94.5 2.0 %fusion.3 = f32[2,4,2,16,2176]{4,3,2,1,0:T(8,128)S(1)} fusion(bf16[256,2048]{1,0:T(8,128)(2,1)} %param.25, bf16[256,2176]{1,0:T(8,128)(2,1)S(1)} %concatenate.57, bf16[4,2,2,16,512]{4,3,2,1,0:T(8,128)(2,1)S(1)} %bitcast.161), kind=kOutput, calls=%fused_computation.5 | convolution fusion | flops 577110016 | bytes 4653056 | tf_op jit(solution)/shard_map/...c,cn->...n/dot_general | solution.py:218
  96.6 7.0 %collective-permute-start.5 = (bf16[4,2,16,2176]{3,2,1,0:T(8,128)(2,1)S(1)}, bf16[4,2,16,2176]{3,2,1,0:T(8,128)(2,1)S(1)}, u32[]{:S(2)}, u32[]{:S(2)}) collective-permute-start(bf16[4,2,16,2176]{3,2,1,0:T(8,128)(2,1)S(1)} %fusion.19), channel_id=1, source_target_pairs={{0,1},{1,0},{2,3},{3,2},{4,5},{5,4},{6,7},{7,6},{8,9},{9,8},{10,11... | collective-permute-start | bytes 1671176 | tf_op jit(solution)/shard_map/ppermute | solution.py:222
  103.6 1.6 %collective-permute-done.5 = bf16[4,2,16,2176]{3,2,1,0:T(8,128)(2,1)S(1)} collective-permute-done((bf16[4,2,16,2176]{3,2,1,0:T(8,128)(2,1)S(1)}, bf16[4,2,16,2176]{3,2,1,0:T(8,128)(2,1)S(1)}, u32[]{:S(2)}, u32[]{:S(2)}) %collective-permute-start.5) | collective-permute-done | bytes 557088 | tf_op jit(solution)/shard_map/ppermute | solution.py:222
  105.2 20.3 %all_to_all.20 = bf16[8,16,2176]{2,1,0:T(8,128)(2,1)S(1)} all-to-all(bf16[8,16,2176]{2,1,0:T(8,128)(2,1)S(1)} %bitcast.144), channel_id=1, replica_groups=mesh['z'=8,'x'=4,'tg'=4,'yl'=2,'tc'=2] {'tg','yl'}, dimensions={0} | all-to-all | bytes 1114112 | tf_op jit(solution)/shard_map/all_to_all | solution.py:224
  125.7 0.7 fusion.20
  (95 shorter events, 5.3 us)
Async XLA Ops:
  1.7 22.6 %all-to-all-start = ((bf16[8,16,2048]{2,1,0:T(8,128)(2,1)}), bf16[8,16,2048]{2,1,0:T(8,128)(2,1)S(1)}, u32[]{:S(2)}, u32[]{:S(2)}) async-start(bf16[8,16,2048]{2,1,0:T(8,128)(2,1)} %broadcast_in_dim.46), calls=%async_computation | async-start | bytes 1048576 | tf_op jit(solution)/shard_map/all_to_all | solution.py:80
  9.3 4.9 %copy-start = (bf16[16,4,2048]{2,1,0:T(4,128)(2,1)S(1)}, bf16[16,4,2048]{2,1,0:T(4,128)(2,1)}, u32[]{:S(2)}) copy-start(bf16[16,4,2048]{2,1,0:T(4,128)(2,1)} %param.16) | copy-start | bytes 786436
  9.3 6.7 %copy-start.2 = (f32[4,256]{1,0:T(4,128)S(1)}, f32[4,256]{1,0:T(4,128)}, u32[]{:S(2)}) copy-start(f32[4,256]{1,0:T(4,128)} %param.17) | copy-start | bytes 12292
  9.4 20.3 %copy-start.6 = (f32[4]{0:T(128)S(1)}, f32[4]{0:T(128)}, u32[]{:S(2)}) copy-start(f32[4]{0:T(128)} %param.22) | copy-start | bytes 52
  9.4 20.3 %copy-start.5 = (bf16[2048,4]{0,1:T(4,128)(2,1)S(1)}, bf16[2048,4]{0,1:T(4,128)(2,1)}, u32[]{:S(2)}) copy-start(bf16[2048,4]{0,1:T(4,128)(2,1)} %param.15) | copy-start | bytes 49156
  24.3 6.9 %collective-permute-start = (bf16[8,16,2048]{2,1,0:T(8,128)(2,1)S(1)}, bf16[8,16,2048]{2,1,0:T(8,128)(2,1)S(1)}, u32[]{:S(2)}, u32[]{:S(2)}) collective-permute-start(bf16[8,16,2048]{2,1,0:T(8,128)(2,1)S(1)} %all-to-all-done), channel_id=1, source_target_pairs={{0,1},{1,0},{2,3},{3,2},{4,5},{5,4},{6,7},{7,6},{8,9},{9,8},{10,11... | collective-permute-start | bytes 1572872 | tf_op jit(solution)/shard_map/ppermute | solution.py:83
  30.7 1.7 %copy-start.1 = (f32[4]{0:T(128)S(1)}, f32[4]{0:T(128)}, u32[]{:S(2)}) copy-start(f32[4]{0:T(128)} %param.21) | copy-start | bytes 52
  32.2 19.8 %copy-start.4 = (f32[256]{0:T(256)S(1)}, f32[256]{0:T(256)}, u32[]{:S(2)}) copy-start(f32[256]{0:T(256)} %param.18) | copy-start | bytes 3076
  35.0 12.9 %all-to-all-start.1 = ((bf16[16,256,16]{1,2,0:T(8,128)(2,1)}), bf16[16,256,16]{1,2,0:T(8,128)(2,1)S(1)}, u32[]{:S(2)}, u32[]{:S(2)}) async-start(bf16[16,256,16]{1,2,0:T(8,128)(2,1)} %bitcast.14), calls=%async_computation.1 | async-start | bytes 262144 | tf_op jit(solution)/shard_map/all_to_all | solution.py:100
  48.1 3.9 %collective-permute-start.1 = (bf16[3,512]{1,0:T(4,128)(2,1)S(1)}, bf16[3,512]{1,0:T(4,128)(2,1)S(1)}, u32[]{:S(2)}, u32[]{:S(2)}) collective-permute-start(bf16[3,512]{1,0:T(4,128)(2,1)S(1)} %pad_maximum_fusion.5), channel_id=1, source_target_pairs={{0,16},{16,32},{32,48},{48,64},{64,80},{80,96},{96,112},{112,128},... | collective-permute-start | bytes 9224 | tf_op jit(solution)/shard_map/ppermute | solution.py:17
  53.6 10.1 %all-to-all-start.2 = ((bf16[4,4,65,128]{3,1,2,0:T(4,128)(2,1)}), bf16[4,4,65,128]{3,1,2,0:T(4,128)(2,1)S(1)}, u32[]{:S(2)}, u32[]{:S(2)}) async-start(bf16[4,4,65,128]{3,1,2,0:T(4,128)(2,1)} %broadcast_in_dim.52), calls=%async_computation.2 | async-start | bytes 532480 | tf_op jit(solution)/shard_map/all_to_all | solution.py:152
  64.0 29.6 %copy-start.7 = (f32[4]{0:T(128)S(1)}, f32[4]{0:T(128)}, u32[]{:S(2)}) copy-start(f32[4]{0:T(128)} %param.23) | copy-start | bytes 52
  64.2 6.9 %collective-permute-start.2 = (bf16[4,65,128]{2,0,1:T(4,128)(2,1)S(1)}, bf16[4,65,128]{2,0,1:T(4,128)(2,1)S(1)}, u32[]{:S(2)}, u32[]{:S(2)}) collective-permute-start(bf16[4,65,128]{2,0,1:T(4,128)(2,1)S(1)} %pad_maximum_fusion.2), channel_id=1, source_target_pairs={{0,64},{64,128},{128,192},{192,256},{256,320},{320,384},{384,448},... | collective-permute-start | bytes 199688 | tf_op jit(solution)/shard_map/ppermute | solution.py:17
  71.5 7.1 %collective-permute-start.3 = (bf16[4,65,128]{2,0,1:T(4,128)(2,1)S(1)}, bf16[4,65,128]{2,0,1:T(4,128)(2,1)S(1)}, u32[]{:S(2)}, u32[]{:S(2)}) collective-permute-start(bf16[4,65,128]{2,0,1:T(4,128)(2,1)S(1)} %pad_maximum_fusion.3), channel_id=1, source_target_pairs={{0,128},{64,192},{128,256},{192,320},{256,384},{320,448},{1,129},{... | collective-permute-start | bytes 199688 | tf_op jit(solution)/shard_map/ppermute | solution.py:17
  79.2 14.1 %collective-permute-start.4 = (bf16[4,65,128]{2,0,1:T(4,128)(2,1)S(1)}, bf16[4,65,128]{2,0,1:T(4,128)(2,1)S(1)}, u32[]{:S(2)}, u32[]{:S(2)}) collective-permute-start(bf16[4,65,128]{2,0,1:T(4,128)(2,1)S(1)} %pad_maximum_fusion.4), channel_id=1, source_target_pairs={{0,256},{64,320},{128,384},{192,448},{1,257},{65,321},{129,385},{1... | collective-permute-start | bytes 199688 | tf_op jit(solution)/shard_map/ppermute | solution.py:17
  92.2 2.1 %copy-start.3 = (f32[256]{0:T(256)S(1)}, f32[256]{0:T(256)}, u32[]{:S(2)}) copy-start(f32[256]{0:T(256)} %param.24) | copy-start | bytes 3076
  96.6 8.6 %collective-permute-start.5 = (bf16[4,2,16,2176]{3,2,1,0:T(8,128)(2,1)S(1)}, bf16[4,2,16,2176]{3,2,1,0:T(8,128)(2,1)S(1)}, u32[]{:S(2)}, u32[]{:S(2)}) collective-permute-start(bf16[4,2,16,2176]{3,2,1,0:T(8,128)(2,1)S(1)} %fusion.19), channel_id=1, source_target_pairs={{0,1},{1,0},{2,3},{3,2},{4,5},{5,4},{6,7},{7,6},{8,9},{9,8},{10,11... | collective-permute-start | bytes 1671176 | tf_op jit(solution)/shard_map/ppermute | solution.py:222
